TPU v7x, 32 devices: a whole 2x2x4 slice. The times are simulated.
32 devices in a mesh: section: 4 (over z), ctx: 8 (over y, x, core).
Axes of the slice: x: 2, y: 2, z: 4, core: 2. Of those that a mesh axis runs over, the one named last changes fastest.
Arguments:
- inputs: bfloat16 [4, 1024, 2048], P('section', 'ctx'), may hold values from -6 to 6
- out_grad: bfloat16 [4, 1024, 2048], P('section', 'ctx'), may hold values from -6 to 6
- gains: float32 [4, 3, 2048], P('section'), may hold values from 0.25 to 1.75
- exponent: int32 [4, 16, 16], P('section', 'ctx'), may hold values from 1 to 2048, as said below
- boundary: int32 [4, 16], P('section', 'ctx'), may hold values 0 or 1
Outputs:
- passed: bfloat16 [4, 1024, 2048], P('section', 'ctx')
Inputs may be any that keep to these rules, and one draw needn't show every extreme that they name: Every group's tokens of head h decay by 1 - exponent / 65536 a token; every exponent is a power of two or twice one.
All inputs are finite; a program needn't handle non-finite values. No bound on the sum of `boundary` on one device may be relied on, other than what follows from the above.
Results may differ from a plain program's by a relative error of at most 0.0053.
Values may be sent and summed in bfloat16 or wider, within the bound.
No kernel may reach another device: no remote copies, remote signals or barrier semaphores. Data moves between devices by JAX's collectives and lax.ppermute only.
A program may use at most 192 MiB of HBM per device.

v0:
```python
import math

import jax
import jax.numpy as jnp
from jax import lax
from jax.sharding import PartitionSpec as P

CH = 64


HIGH = lax.Precision.HIGHEST


def carried_in(array, axis, combine, identity, reverse):
    peers, here = (lax.axis_size(axis), lax.axis_index(axis))
    everything = jax.tree.map(lambda part: lax.all_gather(part, axis), array)
    start = jax.tree.map(
        lambda part, zero: jnp.broadcast_to(jnp.asarray(zero, part.dtype), part.shape),
        array,
        identity,
    )

    def lap(k, before):
        at = peers - 1 - k if reverse else k
        reached = at > here if reverse else at < here
        new = combine(before, jax.tree.map(lambda part: part[at], everything))
        return jax.tree.map(lambda a, b: jnp.where(reached, a, b), new, before)

    return lax.fori_loop(0, peers, lap, start)


def passed_along(value, axis, steps):
    count = lax.axis_size(axis)
    pairs = [(source, (source + steps) % count) for source in range(count)]
    return lax.ppermute(value, axis, pairs)


def decay_logs(exponent, boundary, length):
    count, heads = exponent.shape
    rate = jnp.log(1.0 - exponent.astype(jnp.float32) / 65536.0)
    spread = jnp.broadcast_to(rate[:, None, :], (count, length, heads))
    opening = (jnp.arange(length) == 0)[None, :, None] & (boundary == 1)[:, None, None]
    return spread + jnp.where(opening, math.log(0.5), 0.0).astype(spread.dtype)


def projections(inputs, gain, heads):
    rows = inputs.shape[0]
    widened = inputs.astype(jnp.float32)
    result = []
    for index in range(3):
        rounded = lax.optimization_barrier((widened * gain[index]).astype(jnp.bfloat16))
        result.append(rounded.reshape(rows, heads, -1))
    return result


def combine(earlier, later):
    return (earlier[0] * later[0], later[0][:, None, None] * earlier[1] + later[1])


def local(inputs, out_grad, gains, exponent, boundary):
    block = inputs[0]
    grad_block = out_grad[0]
    gain = gains[0]
    rows, width = block.shape
    heads = exponent.shape[2]
    head_dim = width // heads
    scale = 1.0 / head_dim
    query_half, key_half, value_half = projections(block, gain, heads)
    grad_half = grad_block.reshape(rows, heads, head_dim)
    queries = query_half.astype(jnp.float32)
    key_rows = key_half.astype(jnp.float32)
    value_rows = value_half.astype(jnp.float32)
    grad_rows = grad_half.astype(jnp.float32)
    logs = decay_logs(exponent[0], boundary[0], CH).reshape(rows, heads)
    cumul = jnp.cumsum(logs, axis=0)
    cum_heads = cumul.T
    gap = cum_heads[:, :, None] - cum_heads[:, None, :]
    lower = jnp.arange(rows)[:, None] >= jnp.arange(rows)[None, :]
    decay = jnp.where(lower[None], jnp.exp(jnp.minimum(gap, 0.0)), 0.0)
    mixing = (
        jnp.einsum("thd,shd->hts", grad_half, value_half, preferred_element_type=jnp.float32)
        * decay
    )
    query_near = scale * jnp.einsum("hts,shd->thd", mixing, key_rows, precision=HIGH)
    key_near = scale * jnp.einsum("hts,thd->shd", mixing, queries, precision=HIGH)
    attention = (
        jnp.einsum("thd,shd->hts", query_half, key_half, preferred_element_type=jnp.float32) * decay
    )
    value_near = scale * jnp.einsum("hts,the->she", attention, grad_rows, precision=HIGH)
    near_total = grad_block.astype(jnp.float32)
    near_total = near_total + gain[0] * query_near.reshape(rows, width)
    near_total = near_total + gain[1] * key_near.reshape(rows, width)
    near_total = near_total + gain[2] * value_near.reshape(rows, width)
    near_round = near_total.astype(jnp.bfloat16)
    whole_decay = jnp.exp(cumul[-1])
    growth = jnp.exp(cumul)
    tail = jnp.exp(cumul[-1][None, :] - cumul)
    forward_part = jnp.einsum(
        "shd,she->hde", key_rows * tail[:, :, None], value_rows, precision=HIGH
    )
    adjoint_part = scale * jnp.einsum(
        "shd,she->hde", queries * growth[:, :, None], grad_rows, precision=HIGH
    )
    identity = (
        jnp.ones((heads,), jnp.float32),
        jnp.zeros((heads, head_dim, head_dim), jnp.float32),
    )
    state_in = carried_in((whole_decay, forward_part), "ctx", combine, identity, False)[1]
    adjoint_in = carried_in((whole_decay, adjoint_part), "ctx", combine, identity, True)[1]
    query_far = (
        scale * growth[:, :, None] * jnp.einsum("the,hde->thd", grad_rows, state_in, precision=HIGH)
    )
    key_far = tail[:, :, None] * jnp.einsum("she,hde->shd", value_rows, adjoint_in, precision=HIGH)
    value_far = tail[:, :, None] * jnp.einsum("shd,hde->she", key_rows, adjoint_in, precision=HIGH)
    far_total = gain[0] * query_far.reshape(rows, width)
    far_total = far_total + gain[1] * key_far.reshape(rows, width)
    far_total = far_total + gain[2] * value_far.reshape(rows, width)
    far_round = far_total.astype(jnp.bfloat16)
    near_kept, far_kept = lax.optimization_barrier((near_round, far_round))
    outgoing = (near_kept.astype(jnp.float32) + far_kept.astype(jnp.float32)).astype(jnp.bfloat16)
    received = passed_along(outgoing, "section", -1)
    return received[None]


def solution(mesh):
    in_specs = (
        P("section", "ctx", None),
        P("section", "ctx", None),
        P("section", None, None),
        P("section", "ctx", None),
        P("section", "ctx"),
    )
    out_specs = P("section", "ctx", None)
    return jax.shard_map(local, mesh=mesh, in_specs=in_specs, out_specs=out_specs, check_vma=False)
```

profile of v0, /device:TPU:0, one launch (start us, length us, event | category | flops | bytes accessed | tf_op | source)
XLA Modules:
  0.0 167.4 jit_solution(4476700048254603723)
XLA Ops:
  13.0 1.7 %convolution_multiply_fusion = f32[16,128,128]{2,1,0:T(8,128)} fusion(bf16[128,16,128]{0,2,1:T(8,128)(2,1)S(1)} %bitcast.135, f32[128,16]{0,1:T(8,128)S(1)} %copy.73, bf16[128,16,128]{2,1,0:T(8,128)(2,1)S(1)} %bitcast.124), kind=kOutput, calls=%fused_computation.9 | convolution fusion | flops 403439616 | bytes 2105344 | tf_op jit(solution)/shard_map/shd,she->hde/dot_general | solution.py:101
  14.8 2.2 %fusion.19 = f32[16,128,128]{2,1,0:T(8,128)} fusion(bf16[128,16,128]{0,2,1:T(8,128)(2,1)S(1)} %bitcast.132, bf16[128,16,128]{0,2,1:T(8,128)(2,1)S(1)} %bitcast.128, f32[128,16]{0,1:T(8,128)S(1)} %copy.70), kind=kOutput, calls=%fused_computation.42 | convolution fusion | flops 403177472 | bytes 2105344 | tf_op jit(solution)/shard_map/shd,she->hde/dot_general | solution.py:98
  17.1 2.1 %copy.54 = bf16[1,128,2048]{1,2,0:T(8,128)(2,1)} copy(bf16[1,128,2048]{2,1,0:T(8,128)(2,1)} %param.10) | data formatting | bytes 1048576 | tf_op args[1]
  19.4 1.6 convolution_multiply_fusion.2
  21.0 1.7 %fusion.2 = f32[128,16,128]{2,0,1:T(8,128)} fusion(f32[16,128,128]{1,2,0:T(8,128)S(1)} %convolution_multiply_fusion.2, bf16[128,16,128]{2,1,0:T(8,128)(2,1)S(1)} %bitcast.125), kind=kOutput, calls=%fused_computation.11 | convolution fusion | flops 402915328 | bytes 2621440 | tf_op jit(solution)/shard_map/hts,the->she/dot_general | solution.py:89
  22.6 2.5 %copy.68 = f32[128,16,128]{0,2,1:T(8,128)} copy(f32[128,16,128]{2,0,1:T(8,128)} %fusion.2) | data formatting | bytes 2097152 | tf_op jit(solution)/shard_map/mul | solution.py:89
  25.2 10.3 %all-gather.2 = f32[8,1,16]{2,1,0:T(1,128)S(1)} all-gather(f32[1,1,16]{2,1,0:T(1,128)S(1)} %get-tuple-element.300), channel_id=1, replica_groups=mesh['section'=4,'ctx'=8] {'ctx'}, dimensions={0}, use_global_device_ids=true | all-gather | bytes 576 | tf_op jit(solution)/shard_map/all_gather | solution.py:16
  35.5 1.6 fusion.3
  37.1 3.3 %convolution_multiply_fusion.3 = f32[16,128,128]{2,1,0:T(8,128)} fusion(bf16[128,16,128]{0,2,1:T(8,128)(2,1)} %bitcast.137, f32[16,128,128]{1,2,0:T(8,128)S(1)} %fusion.3), kind=kOutput, calls=%fused_computation.13 | convolution fusion | flops 402915328 | bytes 2621440 | tf_op jit(solution)/shard_map/hts,thd->shd/dot_general | solution.py:85
  40.4 1.6 convolution_multiply_fusion.4
  42.0 30.0 %all-gather.8.cloned.1.call-done = f32[128,128,128]{2,1,0:T(8,128)} async-done(((f32[16,128,128]{2,1,0:T(8,128)}), f32[128,128,128]{2,1,0:T(8,128)}) %all-gather.8.cloned.1.call-update) | async-done | bytes 8388624 | tf_op jit(solution)/shard_map/all_gather | solution.py:16
  72.0 12.4 %while.31 = (s32[]{:T(128)}, f32[16,128,128]{2,1,0:T(8,128)S(1)}, s32[]{:T(128)}, f32[8,16]{1,0:T(8,128)S(1)}, f32[8,16,128,128]{3,2,1,0:T(8,128)}, /*index=5*/s32[]{:T(128)}, s32[]{:T(128)}, s32[]{:T(128)}, s32[]{:T(128)}) while((s32[]{:T(128)}, f32[16,128,128]{2,1,0:T(8,128)S(1)}, s32[]{:T(128)}, f32[8,16]{1,0:T(8,128)S(1)}, ...), condition=%wide.region_4.5_spmd.clone, body=%wide.region_3.4_spmd.clone.sunk | while | flops 1048584 | bytes 3146095 | solution.py:29
  73.5 1.5 fusion.46
  75.0 1.5 fusion.46
  76.5 1.5 fusion.46
  78.0 1.5 fusion.46
  79.5 1.6 fusion.46
  81.2 1.6 fusion.46
  82.8 1.6 fusion.46
  84.4 2.1 %fusion.4 = f32[128,16,128]{0,2,1:T(8,128)} fusion(f32[16,128,128]{2,1,0:T(8,128)S(1)} %get-tuple-element.234, bf16[128,16,128]{0,2,1:T(8,128)(2,1)S(1)} %bitcast.131, f32[128,16]{0,1:T(8,128)S(1)} %copy.70), kind=kOutput, calls=%fused_computation.18 | convolution fusion | flops 402915328 | bytes 2629632 | tf_op jit(solution)/shard_map/shd,hde->she/dot_general | solution.py:114
  86.5 2.6 %fusion.5 = f32[128,16,128]{0,2,1:T(8,128)} fusion(f32[16,128,128]{2,1,0:T(8,128)S(1)} %get-tuple-element.234, bf16[128,16,128]{0,2,1:T(8,128)(2,1)} %bitcast.134, f32[128,16]{0,1:T(8,128)S(1)} %copy.70), kind=kOutput, calls=%fused_computation.20 | convolution fusion | flops 402915328 | bytes 2629632 | tf_op jit(solution)/shard_map/she,hde->shd/dot_general | solution.py:113
  89.1 39.2 %all-gather.6.cloned.1.call-done = f32[128,128,128]{2,1,0:T(8,128)} async-done(((f32[16,128,128]{2,1,0:T(8,128)}), f32[128,128,128]{2,1,0:T(8,128)}) %all-gather.6.cloned.1.call-update) | async-done | bytes 8388624 | tf_op jit(solution)/shard_map/all_gather | solution.py:16
  128.3 12.1 %while.30 = (s32[]{:T(128)}, f32[16,128,128]{2,1,0:T(8,128)S(1)}, s32[]{:T(128)}, f32[8,16]{1,0:T(8,128)S(1)}, f32[8,16,128,128]{3,2,1,0:T(8,128)}, /*index=5*/s32[]{:T(128)}, s32[]{:T(128)}) while((s32[]{:T(128)}, f32[16,128,128]{2,1,0:T(8,128)S(1)}, s32[]{:T(128)}, f32[8,16]{1,0:T(8,128)S(1)}, f32[8,16,128,128]{3,2,1,0:T(8,128)}, ...), condition=%wide.region_2.3_spmd.clone, body=%wide.region_1.2_spmd.clone.sunk | while | flops 1048580 | bytes 3146033 | solution.py:29
  128.3 1.5 fusion.45
  129.9 1.5 fusion.45
  132.9 1.5 fusion.45
  134.4 1.5 fusion.45
  137.4 1.5 fusion.45
  138.9 1.5 fusion.45
  141.6 2.8 %fusion.15 = (bf16[128,2048]{0,1:T(8,128)(2,1)S(1)}, bf16[128,2048]{0,1:T(8,128)(2,1)S(1)}) fusion(f32[128,16,128]{0,2,1:T(8,128)} %fusion.4, f32[128,16,128]{0,2,1:T(8,128)} %fusion.5, f32[128,16,128]{0,2,1:T(8,128)S(1)} %fusion.6, f32[2048]{0:T(1024)S(1)} %bitcast.148, f32[2048]{0:T(1024)S(1)} %bitcast.144, f32[2048]{0:T(1024)S(1)} %bitcast.146, ...), kind=kLoop, calls=%fused_computation.34 | loop fusion | flops 3670016 | bytes 7888896 | tf_op jit(solution)/shard_map/convert_element_type | solution.py:118
  144.6 3.4 %collective-permute-start = (bf16[128,2048]{0,1:T(8,128)(2,1)S(1)}, bf16[128,2048]{0,1:T(8,128)(2,1)S(1)}, u32[]{:S(2)}, u32[]{:S(2)}) collective-permute-start(bf16[128,2048]{0,1:T(8,128)(2,1)S(1)} %add_convert_fusion), channel_id=1, source_target_pairs={{0,24},{8,0},{16,8},{24,16},{1,25},{9,1},{17,9},{25,17},{2,26},{10... | collective-permute-start | bytes 1572872 | tf_op jit(solution)/shard_map/ppermute | solution.py:35
  148.0 11.6 %collective-permute-done = bf16[128,2048]{0,1:T(8,128)(2,1)S(1)} collective-permute-done((bf16[128,2048]{0,1:T(8,128)(2,1)S(1)}, bf16[128,2048]{0,1:T(8,128)(2,1)S(1)}, u32[]{:S(2)}, u32[]{:S(2)}) %collective-permute-start) | collective-permute-done | bytes 524320 | tf_op jit(solution)/shard_map/ppermute | solution.py:35
  (55 shorter events, 13.6 us)
Async XLA Ops:
  6.5 65.5 %all-gather.8.cloned.1.call-start = ((), (), s32[]{:S(2)}) async-start(), calls=%async_computation.1 | async-start | bytes 9437184 | tf_op jit(solution)/shard_map/all_gather | solution.py:16
  11.5 5.6 %copy-start = (bf16[128,2048]{0,1:T(8,128)(2,1)}, bf16[128,2048]{0,1:T(8,128)(2,1)S(1)}, u32[]{:S(2)}) copy-start(bf16[128,2048]{0,1:T(8,128)(2,1)S(1)} %get-tuple-element.295) | copy-start | bytes 1572868
  11.5 5.6 %copy-start.1 = (bf16[128,2048]{0,1:T(8,128)(2,1)}, bf16[128,2048]{0,1:T(8,128)(2,1)S(1)}, u32[]{:S(2)}) copy-start(bf16[128,2048]{0,1:T(8,128)(2,1)S(1)} %get-tuple-element.294) | copy-start | bytes 1572868
  14.7 113.6 %all-gather.6.cloned.1.call-start = ((), (), s32[]{:S(2)}) async-start(), calls=%async_computation | async-start | bytes 9437184 | tf_op jit(solution)/shard_map/all_gather | solution.py:16
  128.3 13.3 %copy-start.2 = (f32[128,16,128]{0,2,1:T(8,128)S(1)}, f32[128,16,128]{0,2,1:T(8,128)}, u32[]{:S(2)}) copy-start(f32[128,16,128]{0,2,1:T(8,128)} %copy.68) | copy-start | bytes 3145732
  144.6 15.0 %collective-permute-start = (bf16[128,2048]{0,1:T(8,128)(2,1)S(1)}, bf16[128,2048]{0,1:T(8,128)(2,1)S(1)}, u32[]{:S(2)}, u32[]{:S(2)}) collective-permute-start(bf16[128,2048]{0,1:T(8,128)(2,1)S(1)} %add_convert_fusion), channel_id=1, source_target_pairs={{0,24},{8,0},{16,8},{24,16},{1,25},{9,1},{17,9},{25,17},{2,26},{10... | collective-permute-start | bytes 1572872 | tf_op jit(solution)/shard_map/ppermute | solution.py:35
Sparse Core Ops, SparseCore 0:
  14.9 57.0 all-gather.7
  73.9 54.3 all-gather.5
where the time goes:
time: 169 us; the launch traced here: 167 us
  waiting for transfers between devices  80.8 us (48%)
  other arithmetic  29.4 us (17%)
  matrix products  19.6 us (12%)
  between operations  13.6 us (8%)
  blocking collectives  10.3 us (6%)
  local copies, waits for them, and re-layouts  9.74 us (6%)
  starting transfers between devices  3.42 us (2%)
    all_gather x2, waiting for transfers between devices, carried_in(): everything = jax.tree.map(lambda part: lax.all_gather(part, axis), array)  69.2 us
    select_n x16, other arithmetic, lap(): return jax.tree.map(lambda a, b: jnp.where(reached, a, b), new, before)  23.8 us
    ppermute x1, waiting for transfers between devices, passed_along(): return lax.ppermute(value, axis, pairs)  11.6 us
    all_gather x1, blocking collectives, carried_in(): everything = jax.tree.map(lambda part: lax.all_gather(part, axis), array)  10.3 us
    unnamed x9, local copies, waits for them, and re-layouts  4.84 us
  transfers between devices with their start and end apart: 3, of which 3 were waited for; matrix products, arithmetic and copies ran while one was open for 20% of the time, Pallas kernels for 0%

commit v1 on v0

--- a/solution.py
+++ b/solution.py
@@ -11,22 +11,33 @@
 HIGH = lax.Precision.HIGHEST
 
 
-def carried_in(array, axis, combine, identity, reverse):
-    peers, here = (lax.axis_size(axis), lax.axis_index(axis))
-    everything = jax.tree.map(lambda part: lax.all_gather(part, axis), array)
-    start = jax.tree.map(
-        lambda part, zero: jnp.broadcast_to(jnp.asarray(zero, part.dtype), part.shape),
-        array,
-        identity,
-    )
+def shifted(value, axis, steps):
+    count = lax.axis_size(axis)
+    if steps >= 0:
+        pairs = [(source, source + steps) for source in range(count - steps)]
+    else:
+        pairs = [(source, source + steps) for source in range(-steps, count)]
+    return lax.ppermute(value, axis, pairs)
 
-    def lap(k, before):
-        at = peers - 1 - k if reverse else k
-        reached = at > here if reverse else at < here
-        new = combine(before, jax.tree.map(lambda part: part[at], everything))
-        return jax.tree.map(lambda a, b: jnp.where(reached, a, b), new, before)
 
-    return lax.fori_loop(0, peers, lap, start)
+def merge(farther, nearer):
+    return (farther[0] * nearer[0], nearer[0][:, None, None] * farther[1] + nearer[1])
+
+
+def scan_in(item, axis, direction):
+    count = lax.axis_size(axis)
+    if count == 1:
+        return jnp.zeros_like(item[1])
+    window = item
+    covered = 1
+    while 2 * covered < count:
+        window = merge(shifted(window, axis, direction * covered), window)
+        covered *= 2
+    nearer = shifted(window, axis, direction)
+    if 1 + covered >= count:
+        return nearer[1]
+    farther = shifted(window[1], axis, direction * (1 + covered))
+    return nearer[0][:, None, None] * farther + nearer[1]
 
 
 def passed_along(value, axis, steps):
@@ -53,10 +64,6 @@
     return result
 
 
-def combine(earlier, later):
-    return (earlier[0] * later[0], later[0][:, None, None] * earlier[1] + later[1])
-
-
 def local(inputs, out_grad, gains, exponent, boundary):
     block = inputs[0]
     grad_block = out_grad[0]
@@ -73,6 +80,17 @@
     grad_rows = grad_half.astype(jnp.float32)
     logs = decay_logs(exponent[0], boundary[0], CH).reshape(rows, heads)
     cumul = jnp.cumsum(logs, axis=0)
+    whole_decay = jnp.exp(cumul[-1])
+    growth = jnp.exp(cumul)
+    tail = jnp.exp(cumul[-1][None, :] - cumul)
+    forward_part = jnp.einsum(
+        "shd,she->hde", key_rows * tail[:, :, None], value_rows, precision=HIGH
+    )
+    adjoint_part = scale * jnp.einsum(
+        "shd,she->hde", queries * growth[:, :, None], grad_rows, precision=HIGH
+    )
+    state_in = scan_in((whole_decay, forward_part), "ctx", 1)
+    adjoint_in = scan_in((whole_decay, adjoint_part), "ctx", -1)
     cum_heads = cumul.T
     gap = cum_heads[:, :, None] - cum_heads[:, None, :]
     lower = jnp.arange(rows)[:, None] >= jnp.arange(rows)[None, :]
@@ -92,21 +110,7 @@
     near_total = near_total + gain[1] * key_near.reshape(rows, width)
     near_total = near_total + gain[2] * value_near.reshape(rows, width)
     near_round = near_total.astype(jnp.bfloat16)
-    whole_decay = jnp.exp(cumul[-1])
-    growth = jnp.exp(cumul)
-    tail = jnp.exp(cumul[-1][None, :] - cumul)
-    forward_part = jnp.einsum(
-        "shd,she->hde", key_rows * tail[:, :, None], value_rows, precision=HIGH
-    )
-    adjoint_part = scale * jnp.einsum(
-        "shd,she->hde", queries * growth[:, :, None], grad_rows, precision=HIGH
-    )
-    identity = (
-        jnp.ones((heads,), jnp.float32),
-        jnp.zeros((heads, head_dim, head_dim), jnp.float32),
-    )
-    state_in = carried_in((whole_decay, forward_part), "ctx", combine, identity, False)[1]
-    adjoint_in = carried_in((whole_decay, adjoint_part), "ctx", combine, identity, True)[1]
+    near_received = passed_along(near_round, "section", -1)
     query_far = (
         scale * growth[:, :, None] * jnp.einsum("the,hde->thd", grad_rows, state_in, precision=HIGH)
     )
@@ -116,9 +120,9 @@
     far_total = far_total + gain[1] * key_far.reshape(rows, width)
     far_total = far_total + gain[2] * value_far.reshape(rows, width)
     far_round = far_total.astype(jnp.bfloat16)
-    near_kept, far_kept = lax.optimization_barrier((near_round, far_round))
-    outgoing = (near_kept.astype(jnp.float32) + far_kept.astype(jnp.float32)).astype(jnp.bfloat16)
-    received = passed_along(outgoing, "section", -1)
+    far_received = passed_along(far_round, "section", -1)
+    near_kept, far_kept = lax.optimization_barrier((near_received, far_received))
+    received = (near_kept.astype(jnp.float32) + far_kept.astype(jnp.float32)).astype(jnp.bfloat16)
     return received[None]
 
 

time: 169 us -> 159 us (0.941)
  starting transfers between devices: 3.42 us -> 71.4 us
  waiting for transfers between devices: 80.8 us -> 47.2 us
  other arithmetic: 29.4 us -> 11 us
  between operations: 13.6 us -> 0.37 us
  blocking collectives: 10.3 us -> 0 us
  matrix products: 19.6 us -> 17.8 us
    all_gather x2 -> x0, waiting for transfers between devices: 69.2 us -> none  [carried_in(): everything = jax.tree.map(lambda part: lax.all_gather(part, axis), array)]
    ppermute x0 -> x14, starting transfers between devices: none -> 67.3 us  [shifted(): return lax.ppermute(value, axis, pairs)]
    ppermute x0 -> x14, waiting for transfers between devices: none -> 25 us  [shifted(): return lax.ppermute(value, axis, pairs)]
    select_n x16 -> x0, other arithmetic: 23.8 us -> none  [lap(): return jax.tree.map(lambda a, b: jnp.where(reached, a, b), new, before)]
    ppermute x1 -> x2, waiting for transfers between devices: 11.6 us -> 22.2 us  [passed_along(): return lax.ppermute(value, axis, pairs)]
    all_gather x1 -> x0, blocking collectives: 10.3 us -> none  [carried_in(): everything = jax.tree.map(lambda part: lax.all_gather(part, axis), array)]
    add x0 -> x3, other arithmetic: none -> 8.08 us  [merge(): nearer[0][:, None, None] * farther[1] + nearer[1]]
    dot_general x1, matrix products: 3.26 us -> 1.21 us  [local(): jnp.einsum('hts,thd->shd', mixing, queries, precision=HIGH)]
  transfers between devices with their start and end apart: 3 -> 16, of which waited for: 3 -> 8; matrix products, arithmetic and copies ran while one was open for 20% -> 16% of each run, Pallas kernels for 0% -> 0%
where the time goes in v1:
time: 159 us; the launch traced here: 158 us
  starting transfers between devices  71.4 us (45%)
  waiting for transfers between devices  47.2 us (30%)
  matrix products  17.8 us (11%)
  other arithmetic  11 us (7%)
  local copies, waits for them, and re-layouts  9.8 us (6%)
    ppermute x14, starting transfers between devices, shifted(): return lax.ppermute(value, axis, pairs)  67.3 us
    ppermute x14, waiting for transfers between devices, shifted(): return lax.ppermute(value, axis, pairs)  25 us
    ppermute x2, waiting for transfers between devices, passed_along(): return lax.ppermute(value, axis, pairs)  22.2 us
    add x3, other arithmetic, merge(): nearer[0][:, None, None] * farther[1] + nearer[1]  8.08 us
    unnamed x15, local copies, waits for them, and re-layouts  5.7 us
    ppermute x2, starting transfers between devices, passed_along(): return lax.ppermute(value, axis, pairs)  4.1 us
  transfers between devices with their start and end apart: 16, of which 8 were waited for; matrix products, arithmetic and copies ran while one was open for 16% of the time, Pallas kernels for 0%

profile of v1, /device:TPU:0, one launch (start us, length us, event | category | flops | bytes accessed | tf_op | source)
XLA Modules:
  0.0 157.6 jit_solution(10052880029889207268)
XLA Ops:
  0.0 1.3 copy.33
  5.4 3.3 %collective-permute-start.4 = (f32[16,128,128]{2,1,0:T(8,128)S(1)}, f32[16,128,128]{2,1,0:T(8,128)}, u32[]{:S(2)}, u32[]{:S(2)}) collective-permute-start(f32[16,128,128]{2,1,0:T(8,128)S(1)} %fusion.19), channel_id=1, source_target_pairs={{0,1},{1,2},{2,3},{3,4},{4,5},{5,6},{6,7},{8,9},{9,10},{10,11},{11... | collective-permute-start | bytes 3145736 | tf_op jit(solution)/shard_map/ppermute | solution.py:20
  10.7 1.3 collective-permute-start.11
  12.0 4.4 %collective-permute-done.11 = f32[16,128,128]{2,1,0:T(8,128)S(1)} collective-permute-done((f32[16,128,128]{2,1,0:T(8,128)S(1)}, f32[16,128,128]{2,1,0:T(8,128)S(1)}, u32[]{:S(2)}, u32[]{:S(2)}) %collective-permute-start.11) | collective-permute-done | bytes 1048608 | tf_op jit(solution)/shard_map/ppermute | solution.py:20
  16.4 3.0 %multiply_add_fusion.4 = (f32[16,128,128]{2,1,0:T(8,128)}, f32[16,128,128]{2,1,0:T(8,128)}) fusion(f32[16,128,128]{2,1,0:T(8,128)S(1)} %fusion.19, f32[16,128,128]{2,1,0:T(8,128)} %collective-permute-done.4, f32[16]{0:T(128)S(1)} %fusion.30, f32[16,128,128]{2,1,0:T(8,128)S(1)} %convolution_multiply_fusion, f32[16,128,128]{2,1,0:T(8,128)S(1)} %collective-permute-done.11), kind=kLoop, calls=%fused_computation.42 | loop fusion | flops 1048576 | bytes 6291520 | tf_op jit(solution)/shard_map/add | solution.py:24
  19.3 1.3 collective-permute-start.12
  20.6 20.5 %collective-permute-start.1 = (f32[16]{0:T(128)S(1)}, f32[16]{0:T(128)S(1)}, u32[]{:S(2)}, u32[]{:S(2)}) collective-permute-start(f32[16]{0:T(128)S(1)} %fusion.30), channel_id=1, source_target_pairs={{0,1},{1,2},{2,3},{3,4},{4,5},{5,6},{6,7},{8,9},{9,10},{10,11},{11... | collective-permute-start | bytes 200 | tf_op jit(solution)/shard_map/ppermute | solution.py:20
  41.1 1.3 collective-permute-start.8
  43.1 5.0 %collective-permute-start.5 = (f32[16,128,128]{2,1,0:T(8,128)}, f32[16,128,128]{2,1,0:T(8,128)S(1)}, u32[]{:S(2)}, u32[]{:S(2)}) collective-permute-start(f32[16,128,128]{2,1,0:T(8,128)} %get-tuple-element.22), channel_id=1, source_target_pairs={{0,2},{1,3},{2,4},{3,5},{4,6},{5,7},{8,10},{9,11},{10,12},{11,13},... | collective-permute-start | bytes 3145736 | tf_op jit(solution)/shard_map/ppermute | solution.py:20
  49.4 13.2 %collective-permute-done.12 = f32[16,128,128]{2,1,0:T(8,128)} collective-permute-done((f32[16,128,128]{2,1,0:T(8,128)}, f32[16,128,128]{2,1,0:T(8,128)}, u32[]{:S(2)}, u32[]{:S(2)}) %collective-permute-start.12) | collective-permute-done | bytes 1048608 | tf_op jit(solution)/shard_map/ppermute | solution.py:20
  62.5 2.7 %multiply_add_fusion.1 = f32[16,128,128]{2,1,0:T(8,128)} fusion(f32[16,128,128]{2,1,0:T(8,128)} %get-tuple-element.23, f32[16,128,128]{2,1,0:T(8,128)} %collective-permute-done.12, f32[16]{0:T(128)S(1)} %get-tuple-element.16), kind=kLoop, calls=%fused_computation.35 | loop fusion | flops 524288 | bytes 3145792 | tf_op jit(solution)/shard_map/add | solution.py:24
  66.5 1.3 collective-permute-start.13
  67.8 1.7 %convolution_multiply_fusion.4 = f32[16,128,128]{2,1,0:T(8,128)} fusion(bf16[128,16,128]{0,2,1:T(8,128)(2,1)S(1)} %bitcast.108, f32[16,128,128]{1,2,0:T(8,128)S(1)} %fusion.1), kind=kOutput, calls=%fused_computation.8 | convolution fusion | flops 402915328 | bytes 2621440 | tf_op jit(solution)/shard_map/hts,shd->thd/dot_general | solution.py:102
  69.5 2.4 %collective-permute-done.5 = f32[16,128,128]{2,1,0:T(8,128)S(1)} collective-permute-done((f32[16,128,128]{2,1,0:T(8,128)}, f32[16,128,128]{2,1,0:T(8,128)S(1)}, u32[]{:S(2)}, u32[]{:S(2)}) %collective-permute-start.5) | collective-permute-done | bytes 1048608 | tf_op jit(solution)/shard_map/ppermute | solution.py:20
  71.8 2.4 %multiply_add_fusion.3 = f32[16,128,128]{2,1,0:T(8,128)} fusion(f32[16,128,128]{2,1,0:T(8,128)} %get-tuple-element.22, f32[16,128,128]{2,1,0:T(8,128)S(1)} %collective-permute-done.5, f32[16]{0:T(128)S(1)} %get-tuple-element.15), kind=kLoop, calls=%fused_computation.41 | loop fusion | flops 524288 | bytes 3145792 | tf_op jit(solution)/shard_map/add | solution.py:24
  74.3 3.7 %collective-permute-start.7 = (f32[16,128,128]{2,1,0:T(8,128)}, f32[16,128,128]{2,1,0:T(8,128)}, u32[]{:S(2)}, u32[]{:S(2)}) collective-permute-start(f32[16,128,128]{2,1,0:T(8,128)} %multiply_add_fusion.3), channel_id=1, source_target_pairs={{0,1},{1,2},{2,3},{3,4},{4,5},{5,6},{6,7},{8,9},{9,10},{10,11},{11... | collective-permute-start | bytes 3145736 | tf_op jit(solution)/shard_map/ppermute | solution.py:20
  78.0 17.9 %collective-permute-start.6 = (f32[16,128,128]{2,1,0:T(8,128)}, f32[16,128,128]{2,1,0:T(8,128)}, u32[]{:S(2)}, u32[]{:S(2)}) collective-permute-start(f32[16,128,128]{2,1,0:T(8,128)} %multiply_add_fusion.3), channel_id=1, source_target_pairs={{0,5},{1,6},{2,7},{8,13},{9,14},{10,15},{16,21},{17,22},{18,23},{2... | collective-permute-start | bytes 3145736 | tf_op jit(solution)/shard_map/ppermute | solution.py:20
  95.9 1.6 %convolution_multiply_fusion.2 = f32[16,128,128]{1,2,0:T(8,128)} fusion(bf16[128,16,128]{0,2,1:T(8,128)(2,1)S(1)} %bitcast.113, bf16[128,16,128]{0,2,1:T(8,128)(2,1)S(1)} %bitcast.109, f32[16,128]{1,0:T(8,128)S(1)} %copy.36, pred[128,128]{0,1:T(8,128)(4,1)S(1)} %iota_compare_fusion), kind=kOutput, calls=%fused_computation.6 | convolution fusion | flops 68157440 | bytes 2121728 | tf_op jit(solution)/shard_map/thd,shd->hts/dot_general | solution.py:105
  97.5 2.0 %copy.32 = bf16[1,128,2048]{1,2,0:T(8,128)(2,1)} copy(bf16[1,128,2048]{2,1,0:T(8,128)(2,1)} %param.6) | data formatting | bytes 1048576 | tf_op args[1]
  99.6 3.0 %fusion = f32[128,16,128]{2,0,1:T(8,128)} fusion(f32[16,128,128]{1,2,0:T(8,128)} %convolution_multiply_fusion.2, bf16[128,16,128]{2,1,0:T(8,128)(2,1)S(1)} %bitcast.105), kind=kOutput, calls=%fused_computation.5 | convolution fusion | flops 402915328 | bytes 2621440 | tf_op jit(solution)/shard_map/hts,the->she/dot_general | solution.py:107
  103.9 2.6 %copy.43 = f32[128,16,128]{0,2,1:T(8,128)} copy(f32[128,16,128]{2,0,1:T(8,128)} %fusion) | data formatting | bytes 2097152 | tf_op jit(solution)/shard_map/mul | solution.py:107
  106.5 1.6 collective-permute-done.9
  108.1 3.4 %collective-permute-start.2 = (f32[16]{0:T(128)S(1)}, f32[16]{0:T(128)S(1)}, u32[]{:S(2)}, u32[]{:S(2)}) collective-permute-start(f32[16]{0:T(128)S(1)} %get-tuple-element.15), channel_id=1, source_target_pairs={{0,2},{1,3},{2,4},{3,5},{4,6},{5,7},{8,10},{9,11},{10,12},{11,13},... | collective-permute-start | bytes 200 | tf_op jit(solution)/shard_map/ppermute | solution.py:20
  114.1 2.2 %collective-permute-done.10 = f32[16]{0:T(128)S(1)} collective-permute-done((f32[16]{0:T(128)S(1)}, f32[16]{0:T(128)S(1)}, u32[]{:S(2)}, u32[]{:S(2)}) %collective-permute-start.10) | collective-permute-done | bytes 96 | tf_op jit(solution)/shard_map/ppermute | solution.py:20
  116.3 4.4 %collective-permute-start.3 = (f32[16]{0:T(128)S(1)}, f32[16]{0:T(128)S(1)}, u32[]{:S(2)}, u32[]{:S(2)}) collective-permute-start(f32[16]{0:T(128)S(1)} %mul.223), channel_id=1, source_target_pairs={{0,1},{1,2},{2,3},{3,4},{4,5},{5,6},{6,7},{8,9},{9,10},{10,11},{11... | collective-permute-start | bytes 200 | tf_op jit(solution)/shard_map/ppermute | solution.py:20
  120.7 2.6 %fusion.2 = f32[128,16,128]{0,2,1:T(8,128)S(1)} fusion(bf16[128,16,128]{0,2,1:T(8,128)(2,1)S(1)} %bitcast.110, f32[128,16]{0,1:T(8,128)S(1)} %copy.45, f32[16,128,128]{2,1,0:T(8,128)} %collective-permute-done.14, f32[16,128,128]{2,1,0:T(8,128)} %collective-permute-done.13, f32[16]{0:T(128)S(1)} %collective-permute-done.10), kind=kOutput, calls=%fused_computation.12 | convolution fusion | flops 403439616 | bytes 3678272 | tf_op jit(solution)/shard_map/shd,hde->she/dot_general | solution.py:118
  123.3 2.3 %fusion.3 = f32[128,16,128]{0,2,1:T(8,128)S(1)} fusion(bf16[128,16,128]{0,2,1:T(8,128)(2,1)S(1)} %bitcast.116, f32[128,16]{0,1:T(8,128)S(1)} %copy.45, f32[16,128,128]{2,1,0:T(8,128)} %collective-permute-done.14, f32[16,128,128]{2,1,0:T(8,128)} %collective-permute-done.13, f32[16]{0:T(128)S(1)} %collective-permute-done.10), kind=kOutput, calls=%fused_computation.14 | convolution fusion | flops 403439616 | bytes 3678272 | tf_op jit(solution)/shard_map/she,hde->shd/dot_general | solution.py:117
  125.7 2.9 %fusion.4 = f32[128,16,128]{0,2,1:T(8,128)S(1)} fusion(f32[16,128,128]{2,1,0:T(8,128)} %collective-permute-done.7, f32[16,128,128]{2,1,0:T(8,128)} %collective-permute-done.6, f32[16]{0:T(128)S(1)} %collective-permute-done.3, f32[128,16]{0,1:T(8,128)S(1)} %copy.44, bf16[128,16,128]{2,1,0:T(8,128)(2,1)S(1)} %bitcast.106), kind=kOutput, calls=%fused_computation.16 | convolution fusion | flops 403439616 | bytes 3678272 | tf_op jit(solution)/shard_map/the,hde->thd/dot_general | solution.py:115
  128.6 1.4 fusion.13
  130.1 3.7 %collective-permute-start = (bf16[128,2048]{0,1:T(8,128)(2,1)S(1)}, bf16[128,2048]{0,1:T(8,128)(2,1)S(1)}, u32[]{:S(2)}, u32[]{:S(2)}) collective-permute-start(bf16[128,2048]{0,1:T(8,128)(2,1)S(1)} %get-tuple-element.18), channel_id=1, source_target_pairs={{0,24},{8,0},{16,8},{24,16},{1,25},{9,1},{17,9},{25,17},{2,26},{10... | collective-permute-start | bytes 1572872 | tf_op jit(solution)/shard_map/ppermute | solution.py:46
  134.2 11.8 %collective-permute-done = bf16[128,2048]{0,1:T(8,128)(2,1)S(1)} collective-permute-done((bf16[128,2048]{0,1:T(8,128)(2,1)S(1)}, bf16[128,2048]{0,1:T(8,128)(2,1)S(1)}, u32[]{:S(2)}, u32[]{:S(2)}) %collective-permute-start) | collective-permute-done | bytes 524320 | tf_op jit(solution)/shard_map/ppermute | solution.py:46
  146.0 10.4 %collective-permute-done.15 = bf16[128,2048]{0,1:T(8,128)(2,1)S(1)} collective-permute-done((bf16[128,2048]{0,1:T(8,128)(2,1)S(1)}, bf16[128,2048]{0,1:T(8,128)(2,1)S(1)}, u32[]{:S(2)}, u32[]{:S(2)}) %collective-permute-start.15) | collective-permute-done | bytes 524320 | tf_op jit(solution)/shard_map/ppermute | solution.py:46
  (55 shorter events, 14.6 us)
Async XLA Ops:
  0.0 1.3 copy-start.3
  2.4 0.7 copy-start.5
  3.1 0.7 copy-start.4
  5.4 6.6 %collective-permute-start.4 = (f32[16,128,128]{2,1,0:T(8,128)S(1)}, f32[16,128,128]{2,1,0:T(8,128)}, u32[]{:S(2)}, u32[]{:S(2)}) collective-permute-start(f32[16,128,128]{2,1,0:T(8,128)S(1)} %fusion.19), channel_id=1, source_target_pairs={{0,1},{1,2},{2,3},{3,4},{4,5},{5,6},{6,7},{8,9},{9,10},{10,11},{11... | collective-permute-start | bytes 3145736 | tf_op jit(solution)/shard_map/ppermute | solution.py:20
  10.7 5.7 %collective-permute-start.11 = (f32[16,128,128]{2,1,0:T(8,128)S(1)}, f32[16,128,128]{2,1,0:T(8,128)S(1)}, u32[]{:S(2)}, u32[]{:S(2)}) collective-permute-start(f32[16,128,128]{2,1,0:T(8,128)S(1)} %convolution_multiply_fusion), channel_id=1, source_target_pairs={{1,0},{2,1},{3,2},{4,3},{5,4},{6,5},{7,6},{9,8},{10,9},{11,10},{12... | collective-permute-start | bytes 3145736 | tf_op jit(solution)/shard_map/ppermute | solution.py:20
  19.3 43.2 %collective-permute-start.12 = (f32[16,128,128]{2,1,0:T(8,128)}, f32[16,128,128]{2,1,0:T(8,128)}, u32[]{:S(2)}, u32[]{:S(2)}) collective-permute-start(f32[16,128,128]{2,1,0:T(8,128)} %get-tuple-element.23), channel_id=1, source_target_pairs={{2,0},{3,1},{4,2},{5,3},{6,4},{7,5},{10,8},{11,9},{12,10},{13,11},... | collective-permute-start | bytes 3145736 | tf_op jit(solution)/shard_map/ppermute | solution.py:20
  20.6 28.7 %collective-permute-start.1 = (f32[16]{0:T(128)S(1)}, f32[16]{0:T(128)S(1)}, u32[]{:S(2)}, u32[]{:S(2)}) collective-permute-start(f32[16]{0:T(128)S(1)} %fusion.30), channel_id=1, source_target_pairs={{0,1},{1,2},{2,3},{3,4},{4,5},{5,6},{6,7},{8,9},{9,10},{10,11},{11... | collective-permute-start | bytes 200 | tf_op jit(solution)/shard_map/ppermute | solution.py:20
  41.1 8.2 %collective-permute-start.8 = (f32[16]{0:T(128)S(1)}, f32[16]{0:T(128)S(1)}, u32[]{:S(2)}, u32[]{:S(2)}) collective-permute-start(f32[16]{0:T(128)S(1)} %fusion.30), channel_id=1, source_target_pairs={{1,0},{2,1},{3,2},{4,3},{5,4},{6,5},{7,6},{9,8},{10,9},{11,10},{12... | collective-permute-start | bytes 200 | tf_op jit(solution)/shard_map/ppermute | solution.py:20
  43.1 28.7 %collective-permute-start.5 = (f32[16,128,128]{2,1,0:T(8,128)}, f32[16,128,128]{2,1,0:T(8,128)S(1)}, u32[]{:S(2)}, u32[]{:S(2)}) collective-permute-start(f32[16,128,128]{2,1,0:T(8,128)} %get-tuple-element.22), channel_id=1, source_target_pairs={{0,2},{1,3},{2,4},{3,5},{4,6},{5,7},{8,10},{9,11},{10,12},{11,13},... | collective-permute-start | bytes 3145736 | tf_op jit(solution)/shard_map/ppermute | solution.py:20
  65.2 55.5 %collective-permute-start.14 = (f32[16,128,128]{2,1,0:T(8,128)}, f32[16,128,128]{2,1,0:T(8,128)}, u32[]{:S(2)}, u32[]{:S(2)}) collective-permute-start(f32[16,128,128]{2,1,0:T(8,128)} %multiply_add_fusion.1), channel_id=1, source_target_pairs={{1,0},{2,1},{3,2},{4,3},{5,4},{6,5},{7,6},{9,8},{10,9},{11,10},{12... | collective-permute-start | bytes 3145736 | tf_op jit(solution)/shard_map/ppermute | solution.py:20
  66.5 54.2 %collective-permute-start.13 = (f32[16,128,128]{2,1,0:T(8,128)}, f32[16,128,128]{2,1,0:T(8,128)}, u32[]{:S(2)}, u32[]{:S(2)}) collective-permute-start(f32[16,128,128]{2,1,0:T(8,128)} %multiply_add_fusion.1), channel_id=1, source_target_pairs={{5,0},{6,1},{7,2},{13,8},{14,9},{15,10},{21,16},{22,17},{23,18},{2... | collective-permute-start | bytes 3145736 | tf_op jit(solution)/shard_map/ppermute | solution.py:20
  74.3 51.4 %collective-permute-start.7 = (f32[16,128,128]{2,1,0:T(8,128)}, f32[16,128,128]{2,1,0:T(8,128)}, u32[]{:S(2)}, u32[]{:S(2)}) collective-permute-start(f32[16,128,128]{2,1,0:T(8,128)} %multiply_add_fusion.3), channel_id=1, source_target_pairs={{0,1},{1,2},{2,3},{3,4},{4,5},{5,6},{6,7},{8,9},{9,10},{10,11},{11... | collective-permute-start | bytes 3145736 | tf_op jit(solution)/shard_map/ppermute | solution.py:20
  78.0 47.7 %collective-permute-start.6 = (f32[16,128,128]{2,1,0:T(8,128)}, f32[16,128,128]{2,1,0:T(8,128)}, u32[]{:S(2)}, u32[]{:S(2)}) collective-permute-start(f32[16,128,128]{2,1,0:T(8,128)} %multiply_add_fusion.3), channel_id=1, source_target_pairs={{0,5},{1,6},{2,7},{8,13},{9,14},{10,15},{16,21},{17,22},{18,23},{2... | collective-permute-start | bytes 3145736 | tf_op jit(solution)/shard_map/ppermute | solution.py:20
  102.6 5.5 %collective-permute-start.9 = (f32[16]{0:T(128)S(1)}, f32[16]{0:T(128)S(1)}, u32[]{:S(2)}, u32[]{:S(2)}) collective-permute-start(f32[16]{0:T(128)S(1)} %get-tuple-element.16), channel_id=1, source_target_pairs={{2,0},{3,1},{4,2},{5,3},{6,4},{7,5},{10,8},{11,9},{12,10},{13,11},... | collective-permute-start | bytes 200 | tf_op jit(solution)/shard_map/ppermute | solution.py:20
  108.1 4.7 %collective-permute-start.2 = (f32[16]{0:T(128)S(1)}, f32[16]{0:T(128)S(1)}, u32[]{:S(2)}, u32[]{:S(2)}) collective-permute-start(f32[16]{0:T(128)S(1)} %get-tuple-element.15), channel_id=1, source_target_pairs={{0,2},{1,3},{2,4},{3,5},{4,6},{5,7},{8,10},{9,11},{10,12},{11,13},... | collective-permute-start | bytes 200 | tf_op jit(solution)/shard_map/ppermute | solution.py:20
  112.8 3.5 %collective-permute-start.10 = (f32[16]{0:T(128)S(1)}, f32[16]{0:T(128)S(1)}, u32[]{:S(2)}, u32[]{:S(2)}) collective-permute-start(f32[16]{0:T(128)S(1)} %mul.235), channel_id=1, source_target_pairs={{1,0},{2,1},{3,2},{4,3},{5,4},{6,5},{7,6},{9,8},{10,9},{11,10},{12... | collective-permute-start | bytes 200 | tf_op jit(solution)/shard_map/ppermute | solution.py:20
  116.3 9.4 %collective-permute-start.3 = (f32[16]{0:T(128)S(1)}, f32[16]{0:T(128)S(1)}, u32[]{:S(2)}, u32[]{:S(2)}) collective-permute-start(f32[16]{0:T(128)S(1)} %mul.223), channel_id=1, source_target_pairs={{0,1},{1,2},{2,3},{3,4},{4,5},{5,6},{6,7},{8,9},{9,10},{10,11},{11... | collective-permute-start | bytes 200 | tf_op jit(solution)/shard_map/ppermute | solution.py:20
  125.6 3.0 %copy-start = (f32[16,128,128]{2,1,0:T(8,128)S(1)}, f32[16,128,128]{2,1,0:T(8,128)}, u32[]{:S(2)}) copy-start(f32[16,128,128]{2,1,0:T(8,128)} %convolution_multiply_fusion.4) | copy-start | bytes 3145732
  125.6 3.0 %copy-start.1 = (f32[128,16,128]{0,2,1:T(8,128)S(1)}, f32[128,16,128]{0,2,1:T(8,128)}, u32[]{:S(2)}) copy-start(f32[128,16,128]{0,2,1:T(8,128)} %copy.43) | copy-start | bytes 3145732
  125.6 3.0 %copy-start.2 = (bf16[1,128,2048]{1,2,0:T(8,128)(2,1)S(1)}, bf16[1,128,2048]{1,2,0:T(8,128)(2,1)}, u32[]{:S(2)}) copy-start(bf16[1,128,2048]{1,2,0:T(8,128)(2,1)} %copy.32) | copy-start | bytes 1572868
  130.1 16.0 %collective-permute-start = (bf16[128,2048]{0,1:T(8,128)(2,1)S(1)}, bf16[128,2048]{0,1:T(8,128)(2,1)S(1)}, u32[]{:S(2)}, u32[]{:S(2)}) collective-permute-start(bf16[128,2048]{0,1:T(8,128)(2,1)S(1)} %get-tuple-element.18), channel_id=1, source_target_pairs={{0,24},{8,0},{16,8},{24,16},{1,25},{9,1},{17,9},{25,17},{2,26},{10... | collective-permute-start | bytes 1572872 | tf_op jit(solution)/shard_map/ppermute | solution.py:46
  133.7 22.7 %collective-permute-start.15 = (bf16[128,2048]{0,1:T(8,128)(2,1)S(1)}, bf16[128,2048]{0,1:T(8,128)(2,1)S(1)}, u32[]{:S(2)}, u32[]{:S(2)}) collective-permute-start(bf16[128,2048]{0,1:T(8,128)(2,1)S(1)} %get-tuple-element.17), channel_id=1, source_target_pairs={{0,24},{8,0},{16,8},{24,16},{1,25},{9,1},{17,9},{25,17},{2,26},{10... | collective-permute-start | bytes 1572872 | tf_op jit(solution)/shard_map/ppermute | solution.py:46

commit v2 on v1

--- a/solution.py
+++ b/solution.py
@@ -11,33 +11,58 @@
 HIGH = lax.Precision.HIGHEST
 
 
-def shifted(value, axis, steps):
+def ranked(value, axis, forward, moves):
     count = lax.axis_size(axis)
-    if steps >= 0:
-        pairs = [(source, source + steps) for source in range(count - steps)]
+    if forward:
+        pairs = list(moves)
     else:
-        pairs = [(source, source + steps) for source in range(-steps, count)]
+        pairs = [(count - 1 - source, count - 1 - target) for source, target in moves]
     return lax.ppermute(value, axis, pairs)
 
 
-def merge(farther, nearer):
-    return (farther[0] * nearer[0], nearer[0][:, None, None] * farther[1] + nearer[1])
+def span_decay(logs, low, high):
+    spots = jnp.arange(logs.shape[0])[:, None]
+    inside = (spots > low) & (spots < high)
+    return jnp.exp(jnp.sum(jnp.where(inside, logs, 0.0), axis=0))[:, None, None]
 
 
-def scan_in(item, axis, direction):
+def scan_in(part, block_logs, axis, forward):
     count = lax.axis_size(axis)
     if count == 1:
-        return jnp.zeros_like(item[1])
-    window = item
-    covered = 1
-    while 2 * covered < count:
-        window = merge(shifted(window, axis, direction * covered), window)
-        covered *= 2
-    nearer = shifted(window, axis, direction)
-    if 1 + covered >= count:
-        return nearer[1]
-    farther = shifted(window[1], axis, direction * (1 + covered))
-    return nearer[0][:, None, None] * farther + nearer[1]
+        return jnp.zeros_like(part)
+    assert count % 2 == 0
+    here = lax.axis_index(axis)
+    rank = here if forward else count - 1 - here
+    ordered = block_logs if forward else block_logs[::-1]
+    couples = count // 2
+    group = rank // 2
+    lower = ranked(part, axis, forward, [(2 * p, 2 * p + 1) for p in range(couples)])
+    own = jnp.exp(lax.dynamic_index_in_dim(ordered, rank, keepdims=False))[:, None, None]
+    window = own * lower + part
+    group_logs = ordered.reshape(couples, 2, -1).sum(axis=1)
+    if couples <= 4:
+        incoming = jnp.zeros_like(part)
+        for step in range(1, couples):
+            moves = [(2 * p + 1, 2 * (p + step) + 1) for p in range(couples - step)]
+            got = ranked(window, axis, forward, moves)
+            incoming = incoming + span_decay(group_logs, group - step, group) * got
+    else:
+        covered = 1
+        while 2 * covered < couples:
+            moves = [(2 * p + 1, 2 * (p + covered) + 1) for p in range(couples - covered)]
+            got = ranked(window, axis, forward, moves)
+            window = span_decay(group_logs, group - covered, group + 1) * got + window
+            covered *= 2
+        moves = [(2 * p + 1, 2 * p + 3) for p in range(couples - 1)]
+        incoming = ranked(window, axis, forward, moves)
+        if 1 + covered < couples:
+            moves = [(2 * p + 1, 2 * (p + 1 + covered) + 1) for p in range(couples - 1 - covered)]
+            got = ranked(window, axis, forward, moves)
+            incoming = incoming + span_decay(group_logs, group - covered - 1, group) * got
+    down = ranked(incoming, axis, forward, [(2 * p + 1, 2 * p) for p in range(couples)])
+    previous = jnp.exp(lax.dynamic_index_in_dim(ordered, jnp.maximum(rank - 1, 0), keepdims=False))
+    odd_value = previous[:, None, None] * incoming + lower
+    return jnp.where(rank % 2 == 0, down, odd_value)
 
 
 def passed_along(value, axis, steps):
@@ -80,7 +105,6 @@
     grad_rows = grad_half.astype(jnp.float32)
     logs = decay_logs(exponent[0], boundary[0], CH).reshape(rows, heads)
     cumul = jnp.cumsum(logs, axis=0)
-    whole_decay = jnp.exp(cumul[-1])
     growth = jnp.exp(cumul)
     tail = jnp.exp(cumul[-1][None, :] - cumul)
     forward_part = jnp.einsum(
@@ -89,8 +113,9 @@
     adjoint_part = scale * jnp.einsum(
         "shd,she->hde", queries * growth[:, :, None], grad_rows, precision=HIGH
     )
-    state_in = scan_in((whole_decay, forward_part), "ctx", 1)
-    adjoint_in = scan_in((whole_decay, adjoint_part), "ctx", -1)
+    block_logs = lax.all_gather(cumul[-1], "ctx")
+    state_in = scan_in(forward_part, block_logs, "ctx", True)
+    adjoint_in = scan_in(adjoint_part, block_logs, "ctx", False)
     cum_heads = cumul.T
     gap = cum_heads[:, :, None] - cum_heads[:, None, :]
     lower = jnp.arange(rows)[:, None] >= jnp.arange(rows)[None, :]
@@ -111,6 +136,9 @@
     near_total = near_total + gain[2] * value_near.reshape(rows, width)
     near_round = near_total.astype(jnp.bfloat16)
     near_received = passed_along(near_round, "section", -1)
+    near_received, state_in, adjoint_in = lax.optimization_barrier(
+        (near_received, state_in, adjoint_in)
+    )
     query_far = (
         scale * growth[:, :, None] * jnp.einsum("the,hde->thd", grad_rows, state_in, precision=HIGH)
     )
@@ -121,8 +149,9 @@
     far_total = far_total + gain[2] * value_far.reshape(rows, width)
     far_round = far_total.astype(jnp.bfloat16)
     far_received = passed_along(far_round, "section", -1)
-    near_kept, far_kept = lax.optimization_barrier((near_received, far_received))
-    received = (near_kept.astype(jnp.float32) + far_kept.astype(jnp.float32)).astype(jnp.bfloat16)
+    received = (near_received.astype(jnp.float32) + far_received.astype(jnp.float32)).astype(
+        jnp.bfloat16
+    )
     return received[None]
 
 

time: 159 us -> 104 us (0.65)
  the two profiles are of different devices: /device:TPU:0 before, /device:TPU:26 now
where the time goes in v2:
time: 104 us; the launch traced here: 103 us
  waiting for transfers between devices  37.4 us (36%)
  other arithmetic  19.7 us (19%)
  starting transfers between devices  18.3 us (18%)
  matrix products  10.5 us (10%)
  blocking collectives  9.3 us (9%)
  local copies, waits for them, and re-layouts  7.77 us (7%)
    ppermute x2, waiting for transfers between devices, passed_along(): return lax.ppermute(value, axis, pairs)  19.2 us
    ppermute x10, waiting for transfers between devices, ranked(): return lax.ppermute(value, axis, pairs)  18.1 us
    ppermute x10, starting transfers between devices, ranked(): return lax.ppermute(value, axis, pairs)  17.8 us
    all_gather x1, blocking collectives, local(): block_logs = lax.all_gather(cumul[-1], 'ctx')  9.3 us
    add x2, other arithmetic, scan_in(): window = own * lower + part  5.43 us
    add x2, other arithmetic, scan_in(): incoming = incoming + span_decay(group_logs, group - step, group) * got  5.26 us
    unnamed x14, local copies, waits for them, and re-layouts  4.16 us
    select_n x2, other arithmetic, scan_in(): return jnp.where(rank % 2 == 0, down, odd_value)  3.51 us
  transfers between devices with their start and end apart: 12, of which 3 were waited for; matrix products, arithmetic and copies ran while one was open for 26% of the time, Pallas kernels for 0%

profile of v2, /device:TPU:26, one launch (start us, length us, event | category | flops | bytes accessed | tf_op | source)
XLA Modules:
  0.0 103.2 jit_solution(3916959528643903139)
XLA Ops:
  3.0 1.0 fusion.5
  4.0 2.2 %fusion.17 = f32[16,128,128]{2,1,0:T(8,128)} fusion(bf16[128,16,128]{0,2,1:T(8,128)(2,1)S(1)} %bitcast.121, bf16[128,16,128]{0,2,1:T(8,128)(2,1)S(1)} %bitcast.117, f32[128,16]{0,1:T(8,128)S(1)} %copy.94), kind=kOutput, calls=%fused_computation.42 | convolution fusion | flops 403177472 | bytes 2105344 | tf_op jit(solution)/shard_map/shd,she->hde/dot_general | solution.py:110
  6.2 1.8 %collective-permute-start.1 = (f32[16,128,128]{2,1,0:T(8,128)}, f32[16,128,128]{2,1,0:T(8,128)S(1)}, u32[]{:S(2)}, u32[]{:S(2)}) collective-permute-start(f32[16,128,128]{2,1,0:T(8,128)} %fusion.17), channel_id=1, source_target_pairs={{0,1},{2,3},{4,5},{6,7},{8,9},{10,11},{12,13},{14,15},{16,17},{18,... | collective-permute-start | bytes 3145736 | tf_op jit(solution)/shard_map/ppermute | solution.py:20
  8.0 1.2 %copy.116 = bf16[16,8,16,128]{3,2,1,0:T(8,128)(2,1)S(1)} copy(bf16[16,8,16,128]{3,1,2,0:T(8,128)(2,1)} %bitcast.127) | data formatting | bytes 1048576
  9.2 1.7 %convolution_multiply_fusion = f32[16,128,128]{2,1,0:T(8,128)} fusion(bf16[128,16,128]{0,2,1:T(8,128)(2,1)S(1)} %bitcast.124, f32[128,16]{0,1:T(8,128)S(1)} %copy.96, bf16[128,16,128]{2,1,0:T(8,128)(2,1)S(1)} %bitcast.113), kind=kOutput, calls=%fused_computation.3 | convolution fusion | flops 403439616 | bytes 2105344 | tf_op jit(solution)/shard_map/shd,she->hde/dot_general | solution.py:113
  10.9 1.3 %collective-permute-start.6 = (f32[16,128,128]{2,1,0:T(8,128)}, f32[16,128,128]{2,1,0:T(8,128)}, u32[]{:S(2)}, u32[]{:S(2)}) collective-permute-start(f32[16,128,128]{2,1,0:T(8,128)} %convolution_multiply_fusion), channel_id=1, source_target_pairs={{7,6},{5,4},{3,2},{1,0},{15,14},{13,12},{11,10},{9,8},{23,22},{21,... | collective-permute-start | bytes 3145736 | tf_op jit(solution)/shard_map/ppermute | solution.py:20
  12.2 9.3 %all-gather = f32[8,1,16]{2,1,0:T(1,128)S(1)} all-gather(f32[1,1,16]{2,1,0:T(1,128)S(1)} %get-tuple-element.23), channel_id=1, replica_groups=mesh['section'=4,'ctx'=8] {'ctx'}, dimensions={0}, use_global_device_ids=true | all-gather | bytes 576 | tf_op jit(solution)/shard_map/all_gather | solution.py:116
  21.7 2.7 %multiply_add_fusion.3 = f32[16,128,128]{2,1,0:T(8,128)} fusion(f32[16,128,128]{2,1,0:T(8,128)} %fusion.17, f32[16,128,128]{2,1,0:T(8,128)S(1)} %collective-permute-done.1, f32[16]{0:T(128)S(1)} %get-tuple-element.31), kind=kLoop, calls=%fused_computation.41 | loop fusion | flops 524288 | bytes 3145792 | tf_op jit(solution)/shard_map/add | solution.py:41
  24.4 1.7 %collective-permute-start.4 = (f32[16,128,128]{2,1,0:T(8,128)}, f32[16,128,128]{2,1,0:T(8,128)}, u32[]{:S(2)}, u32[]{:S(2)}) collective-permute-start(f32[16,128,128]{2,1,0:T(8,128)} %multiply_add_fusion.3), channel_id=1, source_target_pairs={{1,7},{9,15},{17,23},{25,31}} | collective-permute-start | bytes 3145736 | tf_op jit(solution)/shard_map/ppermute | solution.py:20
  26.1 2.0 %copy.79 = bf16[1,128,2048]{1,2,0:T(8,128)(2,1)} copy(bf16[1,128,2048]{2,1,0:T(8,128)(2,1)} %param.6) | data formatting | bytes 1048576 | tf_op args[1]
  29.0 1.7 %collective-permute-start.3 = (f32[16,128,128]{2,1,0:T(8,128)}, f32[16,128,128]{2,1,0:T(8,128)}, u32[]{:S(2)}, u32[]{:S(2)}) collective-permute-start(f32[16,128,128]{2,1,0:T(8,128)} %multiply_add_fusion.3), channel_id=1, source_target_pairs={{1,5},{3,7},{9,13},{11,15},{17,21},{19,23},{25,29},{27,31}} | collective-permute-start | bytes 3145736 | tf_op jit(solution)/shard_map/ppermute | solution.py:20
  30.7 1.7 %collective-permute-start.2 = (f32[16,128,128]{2,1,0:T(8,128)}, f32[16,128,128]{2,1,0:T(8,128)}, u32[]{:S(2)}, u32[]{:S(2)}) collective-permute-start(f32[16,128,128]{2,1,0:T(8,128)} %multiply_add_fusion.3), channel_id=1, source_target_pairs={{1,3},{3,5},{5,7},{9,11},{11,13},{13,15},{17,19},{19,21},{21,23},{... | collective-permute-start | bytes 3145736 | tf_op jit(solution)/shard_map/ppermute | solution.py:20
  32.4 2.7 %multiply_add_fusion.1 = f32[16,128,128]{2,1,0:T(8,128)} fusion(f32[16,128,128]{2,1,0:T(8,128)} %convolution_multiply_fusion, f32[16,128,128]{2,1,0:T(8,128)} %collective-permute-done.6, f32[16]{0:T(128)S(1)} %get-tuple-element.29), kind=kLoop, calls=%fused_computation.36 | loop fusion | flops 524288 | bytes 3145792 | tf_op jit(solution)/shard_map/add | solution.py:41
  35.1 1.6 %collective-permute-start.9 = (f32[16,128,128]{2,1,0:T(8,128)}, f32[16,128,128]{2,1,0:T(8,128)}, u32[]{:S(2)}, u32[]{:S(2)}) collective-permute-start(f32[16,128,128]{2,1,0:T(8,128)} %multiply_add_fusion.1), channel_id=1, source_target_pairs={{6,0},{14,8},{22,16},{30,24}} | collective-permute-start | bytes 3145736 | tf_op jit(solution)/shard_map/ppermute | solution.py:20
  36.7 1.3 %collective-permute-start.8 = (f32[16,128,128]{2,1,0:T(8,128)}, f32[16,128,128]{2,1,0:T(8,128)}, u32[]{:S(2)}, u32[]{:S(2)}) collective-permute-start(f32[16,128,128]{2,1,0:T(8,128)} %multiply_add_fusion.1), channel_id=1, source_target_pairs={{6,2},{4,0},{14,10},{12,8},{22,18},{20,16},{30,26},{28,24}} | collective-permute-start | bytes 3145736 | tf_op jit(solution)/shard_map/ppermute | solution.py:20
  38.0 3.1 %collective-permute-start.7 = (f32[16,128,128]{2,1,0:T(8,128)}, f32[16,128,128]{2,1,0:T(8,128)}, u32[]{:S(2)}, u32[]{:S(2)}) collective-permute-start(f32[16,128,128]{2,1,0:T(8,128)} %multiply_add_fusion.1), channel_id=1, source_target_pairs={{6,4},{4,2},{2,0},{14,12},{12,10},{10,8},{22,20},{20,18},{18,16},{... | collective-permute-start | bytes 3145736 | tf_op jit(solution)/shard_map/ppermute | solution.py:20
  41.8 1.3 %copy.93 = f32[128,16,128]{0,2,1:T(8,128)} copy(f32[128,16,128]{2,0,1:T(8,128)S(1)} %fusion) | data formatting | bytes 2097152 | tf_op jit(solution)/shard_map/mul | solution.py:132
  43.7 1.2 %convolution_multiply_fusion.3 = f32[16,128,128]{2,1,0:T(8,128)S(1)} fusion(bf16[128,16,128]{0,2,1:T(8,128)(2,1)S(1)} %bitcast.126, f32[16,128,128]{1,2,0:T(8,128)S(1)} %fusion.1), kind=kOutput, calls=%fused_computation.7 | convolution fusion | flops 402915328 | bytes 2621440 | tf_op jit(solution)/shard_map/hts,thd->shd/dot_general | solution.py:128
  44.9 2.1 %multiply_add_fusion.2 = f32[16,128,128]{2,1,0:T(8,128)S(1)} fusion(f32[16,128,128]{2,1,0:T(8,128)} %collective-permute-done.4, f32[16,128,128]{2,1,0:T(8,128)} %collective-permute-done.3, f32[16,128,128]{2,1,0:T(8,128)} %collective-permute-done.2, f32[16]{0:T(128)S(1)} %exp.108, f32[16]{0:T(128)S(1)} %exp.107, f32[16]{0:T(128)S(1)} %exp.103), kind=kLoop, calls=%fused_computation.40 | loop fusion | flops 1310720 | bytes 4194496 | tf_op jit(solution)/shard_map/add | solution.py:48
  47.1 1.3 %collective-permute-start.5 = (f32[16,128,128]{2,1,0:T(8,128)S(1)}, f32[16,128,128]{2,1,0:T(8,128)}, u32[]{:S(2)}, u32[]{:S(2)}) collective-permute-start(f32[16,128,128]{2,1,0:T(8,128)S(1)} %multiply_add_fusion.2), channel_id=1, source_target_pairs={{1,0},{3,2},{5,4},{7,6},{9,8},{11,10},{13,12},{15,14},{17,16},{19,... | collective-permute-start | bytes 3145736 | tf_op jit(solution)/shard_map/ppermute | solution.py:20
  48.4 18.1 %collective-permute-done.8 = f32[16,128,128]{2,1,0:T(8,128)} collective-permute-done((f32[16,128,128]{2,1,0:T(8,128)}, f32[16,128,128]{2,1,0:T(8,128)}, u32[]{:S(2)}, u32[]{:S(2)}) %collective-permute-start.8) | collective-permute-done | bytes 1048608 | tf_op jit(solution)/shard_map/ppermute | solution.py:20
  66.5 3.1 %multiply_add_fusion = f32[16,128,128]{2,1,0:T(8,128)} fusion(f32[16,128,128]{2,1,0:T(8,128)} %collective-permute-done.9, f32[16,128,128]{2,1,0:T(8,128)} %collective-permute-done.8, f32[16,128,128]{2,1,0:T(8,128)} %collective-permute-done.7, f32[16]{0:T(128)S(1)} %exp.116, f32[16]{0:T(128)S(1)} %exp.115, f32[16]{0:T(128)S(1)} %exp.111), kind=kLoop, calls=%fused_computation.35 | loop fusion | flops 1310720 | bytes 4194496 | tf_op jit(solution)/shard_map/add | solution.py:48
  69.6 2.4 %collective-permute-start.10 = (f32[16,128,128]{2,1,0:T(8,128)}, f32[16,128,128]{2,1,0:T(8,128)}, u32[]{:S(2)}, u32[]{:S(2)}) collective-permute-start(f32[16,128,128]{2,1,0:T(8,128)} %multiply_add_fusion), channel_id=1, source_target_pairs={{6,7},{4,5},{2,3},{0,1},{14,15},{12,13},{10,11},{8,9},{22,23},{20,... | collective-permute-start | bytes 3145736 | tf_op jit(solution)/shard_map/ppermute | solution.py:20
  72.7 1.9 %fusion.10 = bf16[128,2048]{0,1:T(8,128)(2,1)} fusion(f32[16,128,128]{2,1,0:T(8,128)S(1)} %convolution_multiply_fusion.3, f32[16,128,128]{2,1,0:T(8,128)S(1)} %convolution_multiply_fusion.4, f32[128,16,128]{0,2,1:T(8,128)S(1)} %copy-done.1, bf16[1,128,2048]{1,2,0:T(8,128)(2,1)S(1)} %copy-done.2, f32[2048]{0:T(1024)S(1)} %bitcast.136, f32[2048]{0:T(1024)S(1)} %bitcast.130, ...), kind=kLoop, calls=%fused_computation.23 | loop fusion | flops 2097152 | bytes 4218880 | tf_op jit(solution)/shard_map/convert_element_type | solution.py:137
  75.1 1.8 %add_select_fusion.1 = f32[16,128,128]{2,1,0:T(8,128)S(1)} fusion(f32[16,128,128]{2,1,0:T(8,128)} %collective-permute-done.5, f32[16,128,128]{2,1,0:T(8,128)} %copy-done, f32[16,128,128]{2,1,0:T(8,128)S(1)} %multiply_add_fusion.2, f32[16]{0:T(128)S(1)} %get-tuple-element.30, pred[]{:T(512)S(6)} %eq.33), kind=kLoop, calls=%fused_computation.39 | loop fusion | flops 786432 | bytes 4194369 | tf_op jit(solution)/shard_map/jit(_where)/select_n | solution.py:65
  76.9 1.7 %add_select_fusion = f32[16,128,128]{2,1,0:T(8,128)S(1)} fusion(f32[16,128,128]{2,1,0:T(8,128)} %collective-permute-done.10, f32[16,128,128]{2,1,0:T(8,128)} %collective-permute-done.6, f32[16,128,128]{2,1,0:T(8,128)} %multiply_add_fusion, f32[16]{0:T(128)S(1)} %get-tuple-element.28, pred[]{:T(512)S(6)} %eq.34), kind=kLoop, calls=%fused_computation.34 | loop fusion | flops 786432 | bytes 4194369 | tf_op jit(solution)/shard_map/jit(_where)/select_n | solution.py:65
  78.7 8.3 %collective-permute-done = bf16[128,2048]{0,1:T(8,128)(2,1)S(1)} collective-permute-done((bf16[128,2048]{0,1:T(8,128)(2,1)}, bf16[128,2048]{0,1:T(8,128)(2,1)S(1)}, u32[]{:S(2)}, u32[]{:S(2)}) %collective-permute-start) | collective-permute-done | bytes 524320 | tf_op jit(solution)/shard_map/ppermute | solution.py:71
  86.9 1.0 fusion.2
  88.6 1.2 %fusion.4 = f32[128,16,128]{0,2,1:T(8,128)S(1)} fusion(f32[16,128,128]{2,1,0:T(8,128)S(1)} %add_select_fusion.1, f32[128,16]{0,1:T(8,128)S(1)} %copy.98, bf16[128,16,128]{2,1,0:T(8,128)(2,1)S(1)} %bitcast.116), kind=kOutput, calls=%fused_computation.16 | convolution fusion | flops 402915328 | bytes 2629632 | tf_op jit(solution)/shard_map/the,hde->thd/dot_general | solution.py:143
  89.8 1.2 %fusion.13 = bf16[128,2048]{0,1:T(8,128)(2,1)S(1)} fusion(f32[128,16,128]{0,2,1:T(8,128)S(1)} %fusion.2, f32[128,16,128]{0,2,1:T(8,128)S(1)} %fusion.3, f32[128,16,128]{0,2,1:T(8,128)S(1)} %fusion.4, f32[2048]{0:T(1024)S(1)} %bitcast.137, f32[2048]{0:T(1024)S(1)} %bitcast.131, f32[2048]{0:T(1024)S(1)} %bitcast.134), kind=kLoop, calls=%fused_computation.28 | loop fusion | flops 1572864 | bytes 3694592 | tf_op jit(solution)/shard_map/convert_element_type | solution.py:150
  91.1 11.0 %collective-permute-done.11 = bf16[128,2048]{0,1:T(8,128)(2,1)S(1)} collective-permute-done((bf16[128,2048]{0,1:T(8,128)(2,1)S(1)}, bf16[128,2048]{0,1:T(8,128)(2,1)S(1)}, u32[]{:S(2)}, u32[]{:S(2)}) %collective-permute-start.11) | collective-permute-done | bytes 524320 | tf_op jit(solution)/shard_map/ppermute | solution.py:71
  102.2 1.0 copy.103
  (63 shorter events, 7.3 us)
Async XLA Ops:
  0.0 0.7 copy-start.4
  0.0 2.7 %copy-start.3 = (bf16[1,128,2048]{2,1,0:T(8,128)(2,1)S(1)}, bf16[1,128,2048]{2,1,0:T(8,128)(2,1)}, u32[]{:S(2)}) copy-start(bf16[1,128,2048]{2,1,0:T(8,128)(2,1)} %param.5) | copy-start | bytes 1572868
  6.2 15.5 %collective-permute-start.1 = (f32[16,128,128]{2,1,0:T(8,128)}, f32[16,128,128]{2,1,0:T(8,128)S(1)}, u32[]{:S(2)}, u32[]{:S(2)}) collective-permute-start(f32[16,128,128]{2,1,0:T(8,128)} %fusion.17), channel_id=1, source_target_pairs={{0,1},{2,3},{4,5},{6,7},{8,9},{10,11},{12,13},{14,15},{16,17},{18,... | collective-permute-start | bytes 3145736 | tf_op jit(solution)/shard_map/ppermute | solution.py:20
  10.9 21.5 %collective-permute-start.6 = (f32[16,128,128]{2,1,0:T(8,128)}, f32[16,128,128]{2,1,0:T(8,128)}, u32[]{:S(2)}, u32[]{:S(2)}) collective-permute-start(f32[16,128,128]{2,1,0:T(8,128)} %convolution_multiply_fusion), channel_id=1, source_target_pairs={{7,6},{5,4},{3,2},{1,0},{15,14},{13,12},{11,10},{9,8},{23,22},{21,... | collective-permute-start | bytes 3145736 | tf_op jit(solution)/shard_map/ppermute | solution.py:20
  21.7 2.8 %copy-start = (f32[16,128,128]{2,1,0:T(8,128)}, f32[16,128,128]{2,1,0:T(8,128)S(1)}, u32[]{:S(2)}) copy-start(f32[16,128,128]{2,1,0:T(8,128)S(1)} %collective-permute-done.1) | copy-start | bytes 3145732
  24.4 13.6 %collective-permute-start.4 = (f32[16,128,128]{2,1,0:T(8,128)}, f32[16,128,128]{2,1,0:T(8,128)}, u32[]{:S(2)}, u32[]{:S(2)}) collective-permute-start(f32[16,128,128]{2,1,0:T(8,128)} %multiply_add_fusion.3), channel_id=1, source_target_pairs={{1,7},{9,15},{17,23},{25,31}} | collective-permute-start | bytes 3145736 | tf_op jit(solution)/shard_map/ppermute | solution.py:20
  29.0 15.9 %collective-permute-start.3 = (f32[16,128,128]{2,1,0:T(8,128)}, f32[16,128,128]{2,1,0:T(8,128)}, u32[]{:S(2)}, u32[]{:S(2)}) collective-permute-start(f32[16,128,128]{2,1,0:T(8,128)} %multiply_add_fusion.3), channel_id=1, source_target_pairs={{1,5},{3,7},{9,13},{11,15},{17,21},{19,23},{25,29},{27,31}} | collective-permute-start | bytes 3145736 | tf_op jit(solution)/shard_map/ppermute | solution.py:20
  30.7 14.3 %collective-permute-start.2 = (f32[16,128,128]{2,1,0:T(8,128)}, f32[16,128,128]{2,1,0:T(8,128)}, u32[]{:S(2)}, u32[]{:S(2)}) collective-permute-start(f32[16,128,128]{2,1,0:T(8,128)} %multiply_add_fusion.3), channel_id=1, source_target_pairs={{1,3},{3,5},{5,7},{9,11},{11,13},{13,15},{17,19},{19,21},{21,23},{... | collective-permute-start | bytes 3145736 | tf_op jit(solution)/shard_map/ppermute | solution.py:20
  35.1 13.3 %collective-permute-start.9 = (f32[16,128,128]{2,1,0:T(8,128)}, f32[16,128,128]{2,1,0:T(8,128)}, u32[]{:S(2)}, u32[]{:S(2)}) collective-permute-start(f32[16,128,128]{2,1,0:T(8,128)} %multiply_add_fusion.1), channel_id=1, source_target_pairs={{6,0},{14,8},{22,16},{30,24}} | collective-permute-start | bytes 3145736 | tf_op jit(solution)/shard_map/ppermute | solution.py:20
  36.7 29.8 %collective-permute-start.8 = (f32[16,128,128]{2,1,0:T(8,128)}, f32[16,128,128]{2,1,0:T(8,128)}, u32[]{:S(2)}, u32[]{:S(2)}) collective-permute-start(f32[16,128,128]{2,1,0:T(8,128)} %multiply_add_fusion.1), channel_id=1, source_target_pairs={{6,2},{4,0},{14,10},{12,8},{22,18},{20,16},{30,26},{28,24}} | collective-permute-start | bytes 3145736 | tf_op jit(solution)/shard_map/ppermute | solution.py:20
  38.0 28.5 %collective-permute-start.7 = (f32[16,128,128]{2,1,0:T(8,128)}, f32[16,128,128]{2,1,0:T(8,128)}, u32[]{:S(2)}, u32[]{:S(2)}) collective-permute-start(f32[16,128,128]{2,1,0:T(8,128)} %multiply_add_fusion.1), channel_id=1, source_target_pairs={{6,4},{4,2},{2,0},{14,12},{12,10},{10,8},{22,20},{20,18},{18,16},{... | collective-permute-start | bytes 3145736 | tf_op jit(solution)/shard_map/ppermute | solution.py:20
  47.1 28.1 %collective-permute-start.5 = (f32[16,128,128]{2,1,0:T(8,128)S(1)}, f32[16,128,128]{2,1,0:T(8,128)}, u32[]{:S(2)}, u32[]{:S(2)}) collective-permute-start(f32[16,128,128]{2,1,0:T(8,128)S(1)} %multiply_add_fusion.2), channel_id=1, source_target_pairs={{1,0},{3,2},{5,4},{7,6},{9,8},{11,10},{13,12},{15,14},{17,16},{19,... | collective-permute-start | bytes 3145736 | tf_op jit(solution)/shard_map/ppermute | solution.py:20
  69.6 3.1 %copy-start.1 = (f32[128,16,128]{0,2,1:T(8,128)S(1)}, f32[128,16,128]{0,2,1:T(8,128)}, u32[]{:S(2)}) copy-start(f32[128,16,128]{0,2,1:T(8,128)} %copy.93) | copy-start | bytes 3145732
  69.6 3.1 %copy-start.2 = (bf16[1,128,2048]{1,2,0:T(8,128)(2,1)S(1)}, bf16[1,128,2048]{1,2,0:T(8,128)(2,1)}, u32[]{:S(2)}) copy-start(bf16[1,128,2048]{1,2,0:T(8,128)(2,1)} %copy.79) | copy-start | bytes 1572868
  69.6 7.3 %collective-permute-start.10 = (f32[16,128,128]{2,1,0:T(8,128)}, f32[16,128,128]{2,1,0:T(8,128)}, u32[]{:S(2)}, u32[]{:S(2)}) collective-permute-start(f32[16,128,128]{2,1,0:T(8,128)} %multiply_add_fusion), channel_id=1, source_target_pairs={{6,7},{4,5},{2,3},{0,1},{14,15},{12,13},{10,11},{8,9},{22,23},{20,... | collective-permute-start | bytes 3145736 | tf_op jit(solution)/shard_map/ppermute | solution.py:20
  74.6 12.3 %collective-permute-start = (bf16[128,2048]{0,1:T(8,128)(2,1)}, bf16[128,2048]{0,1:T(8,128)(2,1)S(1)}, u32[]{:S(2)}, u32[]{:S(2)}) collective-permute-start(bf16[128,2048]{0,1:T(8,128)(2,1)} %fusion.10), channel_id=1, source_target_pairs={{0,24},{8,0},{16,8},{24,16},{1,25},{9,1},{17,9},{25,17},{2,26},{10... | collective-permute-start | bytes 1572872 | tf_op jit(solution)/shard_map/ppermute | solution.py:71
  91.0 11.0 %collective-permute-start.11 = (bf16[128,2048]{0,1:T(8,128)(2,1)S(1)}, bf16[128,2048]{0,1:T(8,128)(2,1)S(1)}, u32[]{:S(2)}, u32[]{:S(2)}) collective-permute-start(bf16[128,2048]{0,1:T(8,128)(2,1)S(1)} %fusion.13), channel_id=1, source_target_pairs={{0,24},{8,0},{16,8},{24,16},{1,25},{9,1},{17,9},{25,17},{2,26},{10... | collective-permute-start | bytes 1572872 | tf_op jit(solution)/shard_map/ppermute | solution.py:71

commit v3 on v2

--- a/solution.py
+++ b/solution.py
@@ -20,48 +20,55 @@
     return lax.ppermute(value, axis, pairs)
 
 
-def span_decay(logs, low, high):
-    spots = jnp.arange(logs.shape[0])[:, None]
-    inside = (spots > low) & (spots < high)
-    return jnp.exp(jnp.sum(jnp.where(inside, logs, 0.0), axis=0))[:, None, None]
+def packed(state, rate):
+    tile = jnp.broadcast_to(rate[:, None, None], (state.shape[0], 8, state.shape[2]))
+    return jnp.concatenate([state, tile], axis=1)
 
 
-def scan_in(part, block_logs, axis, forward):
+def unpacked(message):
+    width = message.shape[1] - 8
+    return message[:, :width], message[:, width, 0]
+
+
+def merged(farther, nearer):
+    far_state, far_rate = unpacked(farther)
+    near_state, near_rate = unpacked(nearer)
+    return packed(near_rate[:, None, None] * far_state + near_state, far_rate * near_rate)
+
+
+def scan_in(part, rate, axis, forward):
     count = lax.axis_size(axis)
     if count == 1:
         return jnp.zeros_like(part)
     assert count % 2 == 0
     here = lax.axis_index(axis)
     rank = here if forward else count - 1 - here
-    ordered = block_logs if forward else block_logs[::-1]
     couples = count // 2
-    group = rank // 2
-    lower = ranked(part, axis, forward, [(2 * p, 2 * p + 1) for p in range(couples)])
-    own = jnp.exp(lax.dynamic_index_in_dim(ordered, rank, keepdims=False))[:, None, None]
-    window = own * lower + part
-    group_logs = ordered.reshape(couples, 2, -1).sum(axis=1)
+    moves = [(2 * p, 2 * p + 1) for p in range(couples)]
+    lower, lower_rate = unpacked(ranked(packed(part, rate), axis, forward, moves))
+    window = packed(rate[:, None, None] * lower + part, rate * lower_rate)
     if couples <= 4:
         incoming = jnp.zeros_like(part)
+        weight = jnp.ones_like(rate)
         for step in range(1, couples):
             moves = [(2 * p + 1, 2 * (p + step) + 1) for p in range(couples - step)]
-            got = ranked(window, axis, forward, moves)
-            incoming = incoming + span_decay(group_logs, group - step, group) * got
+            got, got_rate = unpacked(ranked(window, axis, forward, moves))
+            incoming = incoming + weight[:, None, None] * got
+            weight = weight * got_rate
     else:
         covered = 1
         while 2 * covered < couples:
             moves = [(2 * p + 1, 2 * (p + covered) + 1) for p in range(couples - covered)]
-            got = ranked(window, axis, forward, moves)
-            window = span_decay(group_logs, group - covered, group + 1) * got + window
+            window = merged(ranked(window, axis, forward, moves), window)
             covered *= 2
         moves = [(2 * p + 1, 2 * p + 3) for p in range(couples - 1)]
-        incoming = ranked(window, axis, forward, moves)
+        nearer = ranked(window, axis, forward, moves)
         if 1 + covered < couples:
             moves = [(2 * p + 1, 2 * (p + 1 + covered) + 1) for p in range(couples - 1 - covered)]
-            got = ranked(window, axis, forward, moves)
-            incoming = incoming + span_decay(group_logs, group - covered - 1, group) * got
+            nearer = merged(ranked(window, axis, forward, moves), nearer)
+        incoming = unpacked(nearer)[0]
     down = ranked(incoming, axis, forward, [(2 * p + 1, 2 * p) for p in range(couples)])
-    previous = jnp.exp(lax.dynamic_index_in_dim(ordered, jnp.maximum(rank - 1, 0), keepdims=False))
-    odd_value = previous[:, None, None] * incoming + lower
+    odd_value = lower_rate[:, None, None] * incoming + lower
     return jnp.where(rank % 2 == 0, down, odd_value)
 
 
@@ -113,9 +120,9 @@
     adjoint_part = scale * jnp.einsum(
         "shd,she->hde", queries * growth[:, :, None], grad_rows, precision=HIGH
     )
-    block_logs = lax.all_gather(cumul[-1], "ctx")
-    state_in = scan_in(forward_part, block_logs, "ctx", True)
-    adjoint_in = scan_in(adjoint_part, block_logs, "ctx", False)
+    whole_decay = jnp.exp(cumul[-1])
+    state_in = scan_in(forward_part, whole_decay, "ctx", True)
+    adjoint_in = scan_in(adjoint_part, whole_decay, "ctx", False)
     cum_heads = cumul.T
     gap = cum_heads[:, :, None] - cum_heads[:, None, :]
     lower = jnp.arange(rows)[:, None] >= jnp.arange(rows)[None, :]

time: 104 us -> 104 us (level)
  the two profiles are of different devices: /device:TPU:26 before, /device:TPU:30 now
where the time goes in v3:
time: 104 us; the launch traced here: 103 us
  waiting for transfers between devices  37.3 us (36%)
  starting transfers between devices  25.1 us (24%)
  other arithmetic  25 us (24%)
  matrix products  9.57 us (9%)
  local copies, waits for them, and re-layouts  5.6 us (5%)
    ppermute x10, starting transfers between devices, ranked(): return lax.ppermute(value, axis, pairs)  24.6 us
    ppermute x2, waiting for transfers between devices, passed_along(): return lax.ppermute(value, axis, pairs)  23.3 us
    ppermute x10, waiting for transfers between devices, ranked(): return lax.ppermute(value, axis, pairs)  14 us
    add x2, other arithmetic, scan_in(): incoming = incoming + weight[:, None, None] * got  4.92 us
    concatenate x3, other arithmetic, packed(): return jnp.concatenate([state, tile], axis=1)  3.8 us
    select_n x2, other arithmetic, scan_in(): return jnp.where(rank % 2 == 0, down, odd_value)  3.52 us
    slice x3, other arithmetic, unpacked(): return (message[:, :width], message[:, width, 0])  3.24 us
    add x1, other arithmetic, scan_in(): window = packed(rate[:, None, None] * lower + part, rate * lower_rate)  3 us
  transfers between devices with their start and end apart: 12, of which 5 were waited for; matrix products, arithmetic and copies ran while one was open for 19% of the time, Pallas kernels for 0%

profile of v3, /device:TPU:30, one launch (start us, length us, event | category | flops | bytes accessed | tf_op | source)
XLA Modules:
  0.0 102.9 jit_solution(1117244102213590715)
XLA Ops:
  1.9 1.3 %copy.35 = bf16[1,128,2048]{1,2,0:T(8,128)(2,1)S(1)} copy(bf16[1,128,2048]{2,1,0:T(8,128)(2,1)} %param.5) | data formatting | bytes 1048576 | tf_op args[0]
  3.3 1.7 %fusion.5 = (bf16[128,2048]{0,1:T(8,128)(2,1)S(1)}, bf16[128,2048]{0,1:T(8,128)(2,1)S(1)}, bf16[128,2048]{0,1:T(8,128)(2,1)}) fusion(bf16[1,128,2048]{1,2,0:T(8,128)(2,1)S(1)} %copy.35, f32[2048]{0:T(1024)S(1)} %bitcast.120, f32[2048]{0:T(1024)S(1)} %bitcast.123, f32[2048]{0:T(1024)S(1)} %bitcast.126), kind=kLoop, calls=%fused_computation.21 | loop fusion | flops 1835008 | bytes 2121728 | tf_op jit(solution)/shard_map/convert_element_type | solution.py:94
  6.0 2.3 %fusion.21 = f32[16,128,128]{2,1,0:T(8,128)S(1)} fusion(bf16[128,16,128]{0,2,1:T(8,128)(2,1)} %bitcast.112, bf16[128,16,128]{0,2,1:T(8,128)(2,1)S(1)} %bitcast.108, f32[128,16]{0,1:T(8,128)S(1)} %copy.46), kind=kOutput, calls=%fused_computation.52 | convolution fusion | flops 403177472 | bytes 2105344 | tf_op jit(solution)/shard_map/shd,she->hde/dot_general | solution.py:117
  8.3 1.5 %pad_maximum_fusion = (f32[16,136,128]{2,1,0:T(8,128)}, f32[16,136,128]{2,1,0:T(8,128)}) fusion(f32[16,8,128]{2,1,0:T(8,128)S(1)} %broadcast_in_dim.35, f32[16,128,128]{2,1,0:T(8,128)S(1)} %convolution_multiply_fusion, f32[16,128,128]{2,1,0:T(8,128)S(1)} %fusion.21), kind=kLoop, calls=%fused_computation | loop fusion | flops 557056 | bytes 4390912 | tf_op jit(solution)/shard_map/concatenate | solution.py:25
  9.8 1.3 %collective-permute-start.6 = (f32[16,136,128]{2,1,0:T(8,128)}, f32[16,136,128]{2,1,0:T(8,128)}, u32[]{:S(2)}, u32[]{:S(2)}) collective-permute-start(f32[16,136,128]{2,1,0:T(8,128)} %get-tuple-element.25), channel_id=1, source_target_pairs={{7,6},{5,4},{3,2},{1,0},{15,14},{13,12},{11,10},{9,8},{23,22},{21,... | collective-permute-start | bytes 3342344 | tf_op jit(solution)/shard_map/ppermute | solution.py:20
  11.1 5.0 %collective-permute-start.1 = (f32[16,136,128]{2,1,0:T(8,128)}, f32[16,136,128]{2,1,0:T(8,128)}, u32[]{:S(2)}, u32[]{:S(2)}) collective-permute-start(f32[16,136,128]{2,1,0:T(8,128)} %get-tuple-element.26), channel_id=1, source_target_pairs={{0,1},{2,3},{4,5},{6,7},{8,9},{10,11},{12,13},{14,15},{16,17},{18,... | collective-permute-start | bytes 3342344 | tf_op jit(solution)/shard_map/ppermute | solution.py:20
  16.2 1.6 %collective-permute-done.1 = f32[16,136,128]{2,1,0:T(8,128)} collective-permute-done((f32[16,136,128]{2,1,0:T(8,128)}, f32[16,136,128]{2,1,0:T(8,128)}, u32[]{:S(2)}, u32[]{:S(2)}) %collective-permute-start.1) | collective-permute-done | bytes 1114144 | tf_op jit(solution)/shard_map/ppermute | solution.py:20
  17.8 3.0 %multiply_add_fusion = (f32[16,128,128]{2,1,0:T(8,128)}, f32[16,128,128]{2,1,0:T(8,128)S(1)}) fusion(f32[16,128,128]{2,1,0:T(8,128)S(1)} %convolution_multiply_fusion, f32[16,136,128]{2,1,0:T(8,128)} %collective-permute-done.6, f32[16]{0:T(128)S(1)} %fusion.33, f32[16,128,128]{2,1,0:T(8,128)S(1)} %fusion.21, f32[16,136,128]{2,1,0:T(8,128)} %collective-permute-done.1), kind=kLoop, calls=%fused_computation.47 | loop fusion | flops 1048576 | bytes 6291520 | tf_op jit(solution)/shard_map/add | solution.py:49
  22.0 1.1 %pad_maximum_fusion.2 = f32[16,136,128]{2,1,0:T(8,128)} fusion(f32[16,8,128]{2,1,0:T(8,128)S(1)} %broadcast_in_dim.37, f32[16,128,128]{2,1,0:T(8,128)S(1)} %get-tuple-element.35), kind=kLoop, calls=%fused_computation.19 | loop fusion | flops 278528 | bytes 2228224 | tf_op jit(solution)/shard_map/concatenate | solution.py:25
  23.1 1.7 %collective-permute-start.3 = (f32[16,136,128]{2,1,0:T(8,128)}, f32[16,136,128]{2,1,0:T(8,128)}, u32[]{:S(2)}, u32[]{:S(2)}) collective-permute-start(f32[16,136,128]{2,1,0:T(8,128)} %pad_maximum_fusion.2), channel_id=1, source_target_pairs={{1,5},{3,7},{9,13},{11,15},{17,21},{19,23},{25,29},{27,31}} | collective-permute-start | bytes 3342344 | tf_op jit(solution)/shard_map/ppermute | solution.py:20
  24.8 1.8 %collective-permute-start.2 = (f32[16,136,128]{2,1,0:T(8,128)}, f32[16,136,128]{2,1,0:T(8,128)}, u32[]{:S(2)}, u32[]{:S(2)}) collective-permute-start(f32[16,136,128]{2,1,0:T(8,128)} %pad_maximum_fusion.2), channel_id=1, source_target_pairs={{1,3},{3,5},{5,7},{9,11},{11,13},{13,15},{17,19},{19,21},{21,23},{... | collective-permute-start | bytes 3342344 | tf_op jit(solution)/shard_map/ppermute | solution.py:20
  27.2 1.7 %collective-permute-start.4 = (f32[16,136,128]{2,1,0:T(8,128)}, f32[16,136,128]{2,1,0:T(8,128)}, u32[]{:S(2)}, u32[]{:S(2)}) collective-permute-start(f32[16,136,128]{2,1,0:T(8,128)} %pad_maximum_fusion.2), channel_id=1, source_target_pairs={{1,7},{9,15},{17,23},{25,31}} | collective-permute-start | bytes 3342344 | tf_op jit(solution)/shard_map/ppermute | solution.py:20
  29.0 1.2 %pad_maximum_fusion.3 = f32[16,136,128]{2,1,0:T(8,128)} fusion(f32[16,8,128]{2,1,0:T(8,128)S(1)} %broadcast_in_dim.39, f32[16,128,128]{2,1,0:T(8,128)S(1)} %copy-done.3), kind=kLoop, calls=%fused_computation.20 | loop fusion | flops 278528 | bytes 2228224 | tf_op jit(solution)/shard_map/concatenate | solution.py:25
  30.1 3.5 %collective-permute-start.8 = (f32[16,136,128]{2,1,0:T(8,128)}, f32[16,136,128]{2,1,0:T(8,128)}, u32[]{:S(2)}, u32[]{:S(2)}) collective-permute-start(f32[16,136,128]{2,1,0:T(8,128)} %pad_maximum_fusion.3), channel_id=1, source_target_pairs={{6,2},{4,0},{14,10},{12,8},{22,18},{20,16},{30,26},{28,24}} | collective-permute-start | bytes 3342344 | tf_op jit(solution)/shard_map/ppermute | solution.py:20
  33.7 3.4 %collective-permute-start.7 = (f32[16,136,128]{2,1,0:T(8,128)}, f32[16,136,128]{2,1,0:T(8,128)}, u32[]{:S(2)}, u32[]{:S(2)}) collective-permute-start(f32[16,136,128]{2,1,0:T(8,128)} %pad_maximum_fusion.3), channel_id=1, source_target_pairs={{6,4},{4,2},{2,0},{14,12},{12,10},{10,8},{22,20},{20,18},{18,16},{... | collective-permute-start | bytes 3342344 | tf_op jit(solution)/shard_map/ppermute | solution.py:20
  38.8 1.3 %copy.45 = f32[128,16,128]{0,2,1:T(8,128)} copy(f32[128,16,128]{2,0,1:T(8,128)S(1)} %fusion) | data formatting | bytes 2097152 | tf_op jit(solution)/shard_map/mul | solution.py:139
  40.1 1.3 %collective-permute-start.9 = (f32[16,136,128]{2,1,0:T(8,128)}, f32[16,136,128]{2,1,0:T(8,128)S(1)}, u32[]{:S(2)}, u32[]{:S(2)}) collective-permute-start(f32[16,136,128]{2,1,0:T(8,128)} %pad_maximum_fusion.3), channel_id=1, source_target_pairs={{6,0},{14,8},{22,16},{30,24}} | collective-permute-start | bytes 3342344 | tf_op jit(solution)/shard_map/ppermute | solution.py:20
  42.1 1.2 %convolution_multiply_fusion.3 = f32[16,128,128]{2,1,0:T(8,128)S(1)} fusion(bf16[128,16,128]{0,2,1:T(8,128)(2,1)S(1)} %bitcast.117, f32[16,128,128]{1,2,0:T(8,128)S(1)} %fusion.1), kind=kOutput, calls=%fused_computation.9 | convolution fusion | flops 402915328 | bytes 2621440 | tf_op jit(solution)/shard_map/hts,thd->shd/dot_general | solution.py:135
  43.3 1.1 %slice_reduce_fusion.2 = (f32[16]{0:T(128)S(1)}, f32[16]{0:T(128)S(1)}) fusion(f32[16,136,128]{2,1,0:T(8,128)} %collective-permute-done.2, f32[16,136,128]{2,1,0:T(8,128)} %collective-permute-done.3), kind=kLoop, calls=%fused_computation.75 | loop fusion | flops 16 | bytes 256 | tf_op jit(solution)/shard_map/slice | solution.py:30
  44.4 2.1 %fusion.10 = f32[16,128,128]{2,1,0:T(8,128)S(1)} fusion(f32[16,136,128]{2,1,0:T(8,128)} %collective-permute-done.4, f32[16,136,128]{2,1,0:T(8,128)} %collective-permute-done.3, f32[16,136,128]{2,1,0:T(8,128)} %collective-permute-done.2, f32[16]{0:T(128)S(1)} %get-tuple-element.18, f32[16]{0:T(128)S(1)} %get-tuple-element.17), kind=kLoop, calls=%fused_computation.29 | loop fusion | flops 1048576 | bytes 4194432 | tf_op jit(solution)/shard_map/add | solution.py:56
  46.6 1.3 %collective-permute-start.5 = (f32[16,128,128]{2,1,0:T(8,128)S(1)}, f32[16,128,128]{2,1,0:T(8,128)}, u32[]{:S(2)}, u32[]{:S(2)}) collective-permute-start(f32[16,128,128]{2,1,0:T(8,128)S(1)} %fusion.10), channel_id=1, source_target_pairs={{1,0},{3,2},{5,4},{7,6},{9,8},{11,10},{13,12},{15,14},{17,16},{19,... | collective-permute-start | bytes 3145736 | tf_op jit(solution)/shard_map/ppermute | solution.py:20
  47.9 10.1 %collective-permute-done.8 = f32[16,136,128]{2,1,0:T(8,128)} collective-permute-done((f32[16,136,128]{2,1,0:T(8,128)}, f32[16,136,128]{2,1,0:T(8,128)}, u32[]{:S(2)}, u32[]{:S(2)}) %collective-permute-start.8) | collective-permute-done | bytes 1114144 | tf_op jit(solution)/shard_map/ppermute | solution.py:20
  59.0 2.3 %collective-permute-done.9 = f32[16,136,128]{2,1,0:T(8,128)S(1)} collective-permute-done((f32[16,136,128]{2,1,0:T(8,128)}, f32[16,136,128]{2,1,0:T(8,128)S(1)}, u32[]{:S(2)}, u32[]{:S(2)}) %collective-permute-start.9) | collective-permute-done | bytes 1114144 | tf_op jit(solution)/shard_map/ppermute | solution.py:20
  61.4 2.8 %fusion.8 = f32[16,128,128]{2,1,0:T(8,128)} fusion(f32[16,136,128]{2,1,0:T(8,128)S(1)} %collective-permute-done.9, f32[16,136,128]{2,1,0:T(8,128)} %collective-permute-done.8, f32[16,136,128]{2,1,0:T(8,128)} %collective-permute-done.7, f32[16]{0:T(128)S(1)} %get-tuple-element.14, f32[16]{0:T(128)S(1)} %get-tuple-element.13), kind=kLoop, calls=%fused_computation.25 | loop fusion | flops 1048576 | bytes 4194432 | tf_op jit(solution)/shard_map/add | solution.py:56
  64.1 3.5 %collective-permute-start.10 = (f32[16,128,128]{2,1,0:T(8,128)}, f32[16,128,128]{2,1,0:T(8,128)}, u32[]{:S(2)}, u32[]{:S(2)}) collective-permute-start(f32[16,128,128]{2,1,0:T(8,128)} %fusion.8), channel_id=1, source_target_pairs={{6,7},{4,5},{2,3},{0,1},{14,15},{12,13},{10,11},{8,9},{22,23},{20,... | collective-permute-start | bytes 3145736 | tf_op jit(solution)/shard_map/ppermute | solution.py:20
  68.4 1.9 %fusion.14 = bf16[128,2048]{0,1:T(8,128)(2,1)} fusion(f32[16,128,128]{2,1,0:T(8,128)S(1)} %convolution_multiply_fusion.3, f32[16,128,128]{2,1,0:T(8,128)S(1)} %convolution_multiply_fusion.4, f32[128,16,128]{0,2,1:T(8,128)S(1)} %copy-done.4, bf16[1,128,2048]{1,2,0:T(8,128)(2,1)S(1)} %copy-done.7, f32[2048]{0:T(1024)S(1)} %bitcast.127, f32[2048]{0:T(1024)S(1)} %bitcast.121, ...), kind=kLoop, calls=%fused_computation.35 | loop fusion | flops 2097152 | bytes 4218880 | tf_op jit(solution)/shard_map/convert_element_type | solution.py:144
  70.8 1.8 %add_select_fusion.1 = f32[16,128,128]{2,1,0:T(8,128)S(1)} fusion(f32[16,128,128]{2,1,0:T(8,128)} %collective-permute-done.5, f32[16,128,128]{2,1,0:T(8,128)S(1)} %fusion.10, f32[16,136,128]{2,1,0:T(8,128)} %collective-permute-done.1, f32[16]{0:T(128)S(1)} %get-tuple-element.33, pred[]{:T(512)S(6)} %eq.33), kind=kLoop, calls=%fused_computation.50 | loop fusion | flops 786432 | bytes 4194369 | tf_op jit(solution)/shard_map/jit(_where)/select_n | solution.py:72
  72.5 1.8 %add_select_fusion = f32[16,128,128]{2,1,0:T(8,128)S(1)} fusion(f32[16,128,128]{2,1,0:T(8,128)} %collective-permute-done.10, f32[16,128,128]{2,1,0:T(8,128)} %fusion.8, f32[16,136,128]{2,1,0:T(8,128)} %collective-permute-done.6, f32[16]{0:T(128)S(1)} %get-tuple-element.11, pred[]{:T(512)S(6)} %eq.34), kind=kLoop, calls=%fused_computation.46 | loop fusion | flops 786432 | bytes 4194369 | tf_op jit(solution)/shard_map/jit(_where)/select_n | solution.py:72
  74.3 10.2 %collective-permute-done = bf16[128,2048]{0,1:T(8,128)(2,1)S(1)} collective-permute-done((bf16[128,2048]{0,1:T(8,128)(2,1)}, bf16[128,2048]{0,1:T(8,128)(2,1)S(1)}, u32[]{:S(2)}, u32[]{:S(2)}) %collective-permute-start) | collective-permute-done | bytes 524320 | tf_op jit(solution)/shard_map/ppermute | solution.py:78
  86.2 1.2 %fusion.4 = f32[128,16,128]{0,2,1:T(8,128)S(1)} fusion(f32[16,128,128]{2,1,0:T(8,128)S(1)} %add_select_fusion.1, f32[128,16]{0,1:T(8,128)S(1)} %copy.52, bf16[128,16,128]{2,1,0:T(8,128)(2,1)S(1)} %bitcast.107), kind=kOutput, calls=%fused_computation.18 | convolution fusion | flops 402915328 | bytes 2629632 | tf_op jit(solution)/shard_map/the,hde->thd/dot_general | solution.py:150
  87.4 1.2 %fusion.17 = bf16[128,2048]{0,1:T(8,128)(2,1)S(1)} fusion(f32[128,16,128]{0,2,1:T(8,128)S(1)} %fusion.2, f32[128,16,128]{0,2,1:T(8,128)S(1)} %fusion.3, f32[128,16,128]{0,2,1:T(8,128)S(1)} %fusion.4, f32[2048]{0:T(1024)S(1)} %bitcast.128, f32[2048]{0:T(1024)S(1)} %bitcast.122, f32[2048]{0:T(1024)S(1)} %bitcast.125), kind=kLoop, calls=%fused_computation.40 | loop fusion | flops 1572864 | bytes 3694592 | tf_op jit(solution)/shard_map/convert_element_type | solution.py:157
  88.7 13.1 %collective-permute-done.11 = bf16[128,2048]{0,1:T(8,128)(2,1)S(1)} collective-permute-done((bf16[128,2048]{0,1:T(8,128)(2,1)S(1)}, bf16[128,2048]{0,1:T(8,128)(2,1)S(1)}, u32[]{:S(2)}, u32[]{:S(2)}) %collective-permute-start.11) | collective-permute-done | bytes 524320 | tf_op jit(solution)/shard_map/ppermute | solution.py:78
  (63 shorter events, 12.3 us)
Async XLA Ops:
  0.0 3.2 %copy-start.8 = (f32[1,3,2048]{2,0,1:T(1,128)S(1)}, f32[1,3,2048]{2,0,1:T(1,128)}, u32[]{:S(2)}) copy-start(f32[1,3,2048]{2,0,1:T(1,128)} %param.7) | copy-start | bytes 73732
  3.2 1.7 %copy-start.5 = (bf16[1,128,2048]{2,1,0:T(8,128)(2,1)S(1)}, bf16[1,128,2048]{2,1,0:T(8,128)(2,1)}, u32[]{:S(2)}) copy-start(bf16[1,128,2048]{2,1,0:T(8,128)(2,1)} %param.6) | copy-start | bytes 1572868
  4.9 1.0 copy-start.1
  9.8 6.4 %collective-permute-start.6 = (f32[16,136,128]{2,1,0:T(8,128)}, f32[16,136,128]{2,1,0:T(8,128)}, u32[]{:S(2)}, u32[]{:S(2)}) collective-permute-start(f32[16,136,128]{2,1,0:T(8,128)} %get-tuple-element.25), channel_id=1, source_target_pairs={{7,6},{5,4},{3,2},{1,0},{15,14},{13,12},{11,10},{9,8},{23,22},{21,... | collective-permute-start | bytes 3342344 | tf_op jit(solution)/shard_map/ppermute | solution.py:20
  11.1 6.7 %collective-permute-start.1 = (f32[16,136,128]{2,1,0:T(8,128)}, f32[16,136,128]{2,1,0:T(8,128)}, u32[]{:S(2)}, u32[]{:S(2)}) collective-permute-start(f32[16,136,128]{2,1,0:T(8,128)} %get-tuple-element.26), channel_id=1, source_target_pairs={{0,1},{2,3},{4,5},{6,7},{8,9},{10,11},{12,13},{14,15},{16,17},{18,... | collective-permute-start | bytes 3342344 | tf_op jit(solution)/shard_map/ppermute | solution.py:20
  22.0 4.7 %copy-start.2 = (bf16[128,2048]{0,1:T(8,128)(2,1)S(1)}, bf16[128,2048]{0,1:T(8,128)(2,1)}, u32[]{:S(2)}) copy-start(bf16[128,2048]{0,1:T(8,128)(2,1)} %copy-done.1) | copy-start | bytes 1572868
  23.1 17.1 %collective-permute-start.3 = (f32[16,136,128]{2,1,0:T(8,128)}, f32[16,136,128]{2,1,0:T(8,128)}, u32[]{:S(2)}, u32[]{:S(2)}) collective-permute-start(f32[16,136,128]{2,1,0:T(8,128)} %pad_maximum_fusion.2), channel_id=1, source_target_pairs={{1,5},{3,7},{9,13},{11,15},{17,21},{19,23},{25,29},{27,31}} | collective-permute-start | bytes 3342344 | tf_op jit(solution)/shard_map/ppermute | solution.py:20
  24.8 4.1 %copy-start.3 = (f32[16,128,128]{2,1,0:T(8,128)S(1)}, f32[16,128,128]{2,1,0:T(8,128)}, u32[]{:S(2)}) copy-start(f32[16,128,128]{2,1,0:T(8,128)} %get-tuple-element.34) | copy-start | bytes 3145732
  24.8 18.5 %collective-permute-start.2 = (f32[16,136,128]{2,1,0:T(8,128)}, f32[16,136,128]{2,1,0:T(8,128)}, u32[]{:S(2)}, u32[]{:S(2)}) collective-permute-start(f32[16,136,128]{2,1,0:T(8,128)} %pad_maximum_fusion.2), channel_id=1, source_target_pairs={{1,3},{3,5},{5,7},{9,11},{11,13},{13,15},{17,19},{19,21},{21,23},{... | collective-permute-start | bytes 3342344 | tf_op jit(solution)/shard_map/ppermute | solution.py:20
  27.2 17.2 %collective-permute-start.4 = (f32[16,136,128]{2,1,0:T(8,128)}, f32[16,136,128]{2,1,0:T(8,128)}, u32[]{:S(2)}, u32[]{:S(2)}) collective-permute-start(f32[16,136,128]{2,1,0:T(8,128)} %pad_maximum_fusion.2), channel_id=1, source_target_pairs={{1,7},{9,15},{17,23},{25,31}} | collective-permute-start | bytes 3342344 | tf_op jit(solution)/shard_map/ppermute | solution.py:20
  30.1 7.7 %copy-start.6 = (bf16[1,128,2048]{2,1,0:T(8,128)(2,1)S(1)}, bf16[1,128,2048]{2,1,0:T(8,128)(2,1)}, u32[]{:S(2)}) copy-start(bf16[1,128,2048]{2,1,0:T(8,128)(2,1)} %param.6) | copy-start | bytes 1572868
  30.1 27.8 %collective-permute-start.8 = (f32[16,136,128]{2,1,0:T(8,128)}, f32[16,136,128]{2,1,0:T(8,128)}, u32[]{:S(2)}, u32[]{:S(2)}) collective-permute-start(f32[16,136,128]{2,1,0:T(8,128)} %pad_maximum_fusion.3), channel_id=1, source_target_pairs={{6,2},{4,0},{14,10},{12,8},{22,18},{20,16},{30,26},{28,24}} | collective-permute-start | bytes 3342344 | tf_op jit(solution)/shard_map/ppermute | solution.py:20
  33.7 24.3 %collective-permute-start.7 = (f32[16,136,128]{2,1,0:T(8,128)}, f32[16,136,128]{2,1,0:T(8,128)}, u32[]{:S(2)}, u32[]{:S(2)}) collective-permute-start(f32[16,136,128]{2,1,0:T(8,128)} %pad_maximum_fusion.3), channel_id=1, source_target_pairs={{6,4},{4,2},{2,0},{14,12},{12,10},{10,8},{22,20},{20,18},{18,16},{... | collective-permute-start | bytes 3342344 | tf_op jit(solution)/shard_map/ppermute | solution.py:20
  38.8 2.7 %copy-start = (bf16[128,2048]{0,1:T(8,128)(2,1)S(1)}, bf16[128,2048]{0,1:T(8,128)(2,1)}, u32[]{:S(2)}) copy-start(bf16[128,2048]{0,1:T(8,128)(2,1)} %get-tuple-element.21) | copy-start | bytes 1572868
  40.1 21.2 %collective-permute-start.9 = (f32[16,136,128]{2,1,0:T(8,128)}, f32[16,136,128]{2,1,0:T(8,128)S(1)}, u32[]{:S(2)}, u32[]{:S(2)}) collective-permute-start(f32[16,136,128]{2,1,0:T(8,128)} %pad_maximum_fusion.3), channel_id=1, source_target_pairs={{6,0},{14,8},{22,16},{30,24}} | collective-permute-start | bytes 3342344 | tf_op jit(solution)/shard_map/ppermute | solution.py:20
  46.6 24.2 %collective-permute-start.5 = (f32[16,128,128]{2,1,0:T(8,128)S(1)}, f32[16,128,128]{2,1,0:T(8,128)}, u32[]{:S(2)}, u32[]{:S(2)}) collective-permute-start(f32[16,128,128]{2,1,0:T(8,128)S(1)} %fusion.10), channel_id=1, source_target_pairs={{1,0},{3,2},{5,4},{7,6},{9,8},{11,10},{13,12},{15,14},{17,16},{19,... | collective-permute-start | bytes 3145736 | tf_op jit(solution)/shard_map/ppermute | solution.py:20
  64.1 4.2 %copy-start.4 = (f32[128,16,128]{0,2,1:T(8,128)S(1)}, f32[128,16,128]{0,2,1:T(8,128)}, u32[]{:S(2)}) copy-start(f32[128,16,128]{0,2,1:T(8,128)} %copy.45) | copy-start | bytes 3145732
  64.1 4.2 %copy-start.7 = (bf16[1,128,2048]{1,2,0:T(8,128)(2,1)S(1)}, bf16[1,128,2048]{1,2,0:T(8,128)(2,1)}, u32[]{:S(2)}) copy-start(bf16[1,128,2048]{1,2,0:T(8,128)(2,1)} %copy.34) | copy-start | bytes 1572868
  64.1 8.4 %collective-permute-start.10 = (f32[16,128,128]{2,1,0:T(8,128)}, f32[16,128,128]{2,1,0:T(8,128)}, u32[]{:S(2)}, u32[]{:S(2)}) collective-permute-start(f32[16,128,128]{2,1,0:T(8,128)} %fusion.8), channel_id=1, source_target_pairs={{6,7},{4,5},{2,3},{0,1},{14,15},{12,13},{10,11},{8,9},{22,23},{20,... | collective-permute-start | bytes 3145736 | tf_op jit(solution)/shard_map/ppermute | solution.py:20
  70.3 14.2 %collective-permute-start = (bf16[128,2048]{0,1:T(8,128)(2,1)}, bf16[128,2048]{0,1:T(8,128)(2,1)S(1)}, u32[]{:S(2)}, u32[]{:S(2)}) collective-permute-start(bf16[128,2048]{0,1:T(8,128)(2,1)} %fusion.14), channel_id=1, source_target_pairs={{0,24},{8,0},{16,8},{24,16},{1,25},{9,1},{17,9},{25,17},{2,26},{10... | collective-permute-start | bytes 1572872 | tf_op jit(solution)/shard_map/ppermute | solution.py:78
  88.6 13.1 %collective-permute-start.11 = (bf16[128,2048]{0,1:T(8,128)(2,1)S(1)}, bf16[128,2048]{0,1:T(8,128)(2,1)S(1)}, u32[]{:S(2)}, u32[]{:S(2)}) collective-permute-start(bf16[128,2048]{0,1:T(8,128)(2,1)S(1)} %fusion.17), channel_id=1, source_target_pairs={{0,24},{8,0},{16,8},{24,16},{1,25},{9,1},{17,9},{25,17},{2,26},{10... | collective-permute-start | bytes 1572872 | tf_op jit(solution)/shard_map/ppermute | solution.py:78

commit v4 on v3

--- a/solution.py
+++ b/solution.py
@@ -9,15 +9,6 @@
 
 
 HIGH = lax.Precision.HIGHEST
-
-
-def ranked(value, axis, forward, moves):
-    count = lax.axis_size(axis)
-    if forward:
-        pairs = list(moves)
-    else:
-        pairs = [(count - 1 - source, count - 1 - target) for source, target in moves]
-    return lax.ppermute(value, axis, pairs)
 
 
 def packed(state, rate):
@@ -36,40 +27,46 @@
     return packed(near_rate[:, None, None] * far_state + near_state, far_rate * near_rate)
 
 
-def scan_in(part, rate, axis, forward):
+def both_ways(count, moves):
+    return list(moves) + [(count - 1 - source, count - 1 - target) for source, target in moves]
+
+
+def scans_in(forward_part, backward_part, rate, axis, held):
     count = lax.axis_size(axis)
     if count == 1:
-        return jnp.zeros_like(part)
+        return jnp.zeros_like(forward_part), jnp.zeros_like(backward_part), held
     assert count % 2 == 0
-    here = lax.axis_index(axis)
-    rank = here if forward else count - 1 - here
+    odd = lax.axis_index(axis) % 2 == 1
     couples = count // 2
-    moves = [(2 * p, 2 * p + 1) for p in range(couples)]
-    lower, lower_rate = unpacked(ranked(packed(part, rate), axis, forward, moves))
-    window = packed(rate[:, None, None] * lower + part, rate * lower_rate)
+    swap = [(2 * p, 2 * p + 1) for p in range(couples)] + [(2 * p + 1, 2 * p) for p in range(couples)]
+    mine = jnp.where(odd, forward_part, backward_part)
+    sent = packed(jnp.where(odd, backward_part, forward_part), rate)
+    lower, lower_rate = unpacked(lax.ppermute(sent, axis, swap))
+    window = packed(rate[:, None, None] * lower + mine, rate * lower_rate)
     if couples <= 4:
-        incoming = jnp.zeros_like(part)
+        incoming = jnp.zeros_like(mine)
         weight = jnp.ones_like(rate)
         for step in range(1, couples):
             moves = [(2 * p + 1, 2 * (p + step) + 1) for p in range(couples - step)]
-            got, got_rate = unpacked(ranked(window, axis, forward, moves))
+            got, got_rate = unpacked(lax.ppermute(window, axis, both_ways(count, moves)))
             incoming = incoming + weight[:, None, None] * got
             weight = weight * got_rate
     else:
         covered = 1
         while 2 * covered < couples:
             moves = [(2 * p + 1, 2 * (p + covered) + 1) for p in range(couples - covered)]
-            window = merged(ranked(window, axis, forward, moves), window)
+            window = merged(lax.ppermute(window, axis, both_ways(count, moves)), window)
             covered *= 2
         moves = [(2 * p + 1, 2 * p + 3) for p in range(couples - 1)]
-        nearer = ranked(window, axis, forward, moves)
+        nearer = lax.ppermute(window, axis, both_ways(count, moves))
         if 1 + covered < couples:
             moves = [(2 * p + 1, 2 * (p + 1 + covered) + 1) for p in range(couples - 1 - covered)]
-            nearer = merged(ranked(window, axis, forward, moves), nearer)
+            nearer = merged(lax.ppermute(window, axis, both_ways(count, moves)), nearer)
         incoming = unpacked(nearer)[0]
-    down = ranked(incoming, axis, forward, [(2 * p + 1, 2 * p) for p in range(couples)])
-    odd_value = lower_rate[:, None, None] * incoming + lower
-    return jnp.where(rank % 2 == 0, down, odd_value)
+    incoming, held = lax.optimization_barrier((incoming, held))
+    other = lax.ppermute(incoming, axis, swap)
+    own = lower_rate[:, None, None] * incoming + lower
+    return jnp.where(odd, own, other), jnp.where(odd, other, own), held
 
 
 def passed_along(value, axis, steps):
@@ -121,8 +118,6 @@
         "shd,she->hde", queries * growth[:, :, None], grad_rows, precision=HIGH
     )
     whole_decay = jnp.exp(cumul[-1])
-    state_in = scan_in(forward_part, whole_decay, "ctx", True)
-    adjoint_in = scan_in(adjoint_part, whole_decay, "ctx", False)
     cum_heads = cumul.T
     gap = cum_heads[:, :, None] - cum_heads[:, None, :]
     lower = jnp.arange(rows)[:, None] >= jnp.arange(rows)[None, :]
@@ -143,8 +138,8 @@
     near_total = near_total + gain[2] * value_near.reshape(rows, width)
     near_round = near_total.astype(jnp.bfloat16)
     near_received = passed_along(near_round, "section", -1)
-    near_received, state_in, adjoint_in = lax.optimization_barrier(
-        (near_received, state_in, adjoint_in)
+    state_in, adjoint_in, near_received = scans_in(
+        forward_part, adjoint_part, whole_decay, "ctx", near_received
     )
     query_far = (
         scale * growth[:, :, None] * jnp.einsum("the,hde->thd", grad_rows, state_in, precision=HIGH)

time: 104 us -> 78.1 us (0.75)
  the two profiles are of different devices: /device:TPU:30 before, /device:TPU:0 now
where the time goes in v4:
time: 78.1 us; the launch traced here: 77.5 us
  waiting for transfers between devices  28.6 us (37%)
  other arithmetic  15.8 us (20%)
  starting transfers between devices  12.7 us (16%)
  matrix products  11.7 us (15%)
  local copies, waits for them, and re-layouts  8.53 us (11%)
    ppermute x3, waiting for transfers between devices, scans_in(): lax.ppermute(window, axis, both_ways(count, moves))  16 us
    ppermute x2, waiting for transfers between devices, passed_along(): return lax.ppermute(value, axis, pairs)  11.5 us
    ppermute x2, starting transfers between devices, passed_along(): return lax.ppermute(value, axis, pairs)  8.29 us
    ppermute x3, starting transfers between devices, scans_in(): lax.ppermute(window, axis, both_ways(count, moves))  4 us
    unnamed x19, local copies, waits for them, and re-layouts  3.33 us
    add x1, other arithmetic, scans_in(): incoming = incoming + weight[:, None, None] * got  3.11 us
    mul x1, local copies, waits for them, and re-layouts, local(): scale * jnp.einsum('hts,the->she', attention, grad_rows, precision=HIGH)  2.72 us
    concatenate x2, other arithmetic, packed(): return jnp.concatenate([state, tile], axis=1)  2.21 us
  transfers between devices with their start and end apart: 7, of which 4 were waited for; matrix products, arithmetic and copies ran while one was open for 22% of the time, Pallas kernels for 0%

profile of v4, /device:TPU:0, one launch (start us, length us, event | category | flops | bytes accessed | tf_op | source)
XLA Modules:
  0.0 77.5 jit_solution(12271300868689663060)
XLA Ops:
  0.9 0.7 log_bitcast_fusion
  1.9 0.7 fusion.33
  2.6 1.3 %copy.33 = bf16[1,128,2048]{1,2,0:T(8,128)(2,1)S(1)} copy(bf16[1,128,2048]{2,1,0:T(8,128)(2,1)} %param.5) | data formatting | bytes 1048576 | tf_op args[0]
  4.0 1.0 %fusion.7 = (bf16[128,2048]{0,1:T(8,128)(2,1)S(1)}, bf16[128,2048]{0,1:T(8,128)(2,1)S(1)}, bf16[128,2048]{0,1:T(8,128)(2,1)S(1)}) fusion(bf16[1,128,2048]{1,2,0:T(8,128)(2,1)S(1)} %copy.33, f32[2048]{0:T(1024)S(1)} %bitcast.117, f32[2048]{0:T(1024)S(1)} %bitcast.123, f32[2048]{0:T(1024)S(1)} %bitcast.120), kind=kLoop, calls=%fused_computation.21 | loop fusion | flops 1835008 | bytes 2121728 | tf_op jit(solution)/shard_map/convert_element_type | solution.py:91
  5.3 1.2 %fusion.18 = f32[16,128,128]{2,1,0:T(8,128)S(1)} fusion(bf16[128,16,128]{0,2,1:T(8,128)(2,1)S(1)} %bitcast.112, bf16[128,16,128]{0,2,1:T(8,128)(2,1)S(1)} %bitcast.105, f32[128,16]{0,1:T(8,128)S(1)} %copy.36), kind=kOutput, calls=%fused_computation.44 | convolution fusion | flops 403177472 | bytes 2105344 | tf_op jit(solution)/shard_map/shd,she->hde/dot_general | solution.py:114
  6.5 1.8 %broadcast_select_fusion.1 = (f32[16,128,128]{2,1,0:T(8,128)S(1)}, f32[16,128,128]{2,1,0:T(8,128)}) fusion(f32[16,128,128]{2,1,0:T(8,128)S(1)} %fusion.18, pred[]{:T(512)S(6)} %eq.29, bf16[128,16,128]{2,1,0:T(8,128)(2,1)S(1)} %bitcast.101, bf16[128,16,128]{0,2,1:T(8,128)(2,1)S(1)} %bitcast.109, f32[128,16]{0,1:T(8,128)S(1)} %copy.34), kind=kOutput, calls=%fused_computation.54 | convolution fusion | flops 403701760 | bytes 4202497 | tf_op jit(solution)/shard_map/shd,she->hde/dot_general | solution.py:117
  8.4 1.1 %pad_maximum_fusion = f32[16,136,128]{2,1,0:T(8,128)} fusion(f32[16,8,128]{2,1,0:T(8,128)S(1)} %broadcast_in_dim.34, f32[16,128,128]{2,1,0:T(8,128)S(1)} %get-tuple-element.24), kind=kLoop, calls=%fused_computation.17 | loop fusion | flops 278528 | bytes 2228224 | tf_op jit(solution)/shard_map/concatenate | solution.py:16
  11.7 1.6 %convolution_multiply_fusion.3 = f32[16,128,128]{2,1,0:T(8,128)} fusion(bf16[128,16,128]{0,2,1:T(8,128)(2,1)S(1)} %bitcast.107, f32[16,128,128]{1,2,0:T(8,128)S(1)} %fusion.1), kind=kOutput, calls=%fused_computation.7 | convolution fusion | flops 402915328 | bytes 2621440 | tf_op jit(solution)/shard_map/hts,shd->thd/dot_general | solution.py:129
  13.3 1.4 %select_add_fusion = f32[16,128,128]{2,1,0:T(8,128)S(1)} fusion(f32[16,128,128]{2,1,0:T(8,128)S(1)} %fusion.18, f32[16,128,128]{2,1,0:T(8,128)S(1)} %copy-done, f32[16,136,128]{2,1,0:T(8,128)} %collective-permute-done, f32[16]{0:T(128)S(1)} %fusion.32, pred[]{:T(512)S(6)} %eq.29), kind=kLoop, calls=%fused_computation.43 | loop fusion | flops 786432 | bytes 4194369 | tf_op jit(solution)/shard_map/add | solution.py:45
  14.7 1.0 %slice_reduce_fusion.1 = (f32[16]{0:T(128)S(1)}, f32[16]{0:T(128)S(1)}) fusion(f32[16,136,128]{2,1,0:T(8,128)} %collective-permute-done, f32[16,1,1]{2,1,0:T(1,128)S(1)} %copy.38), kind=kLoop, calls=%fused_computation.67 | loop fusion | flops 16 | bytes 256 | tf_op jit(solution)/shard_map/slice | solution.py:21
  15.8 1.1 %pad_maximum_fusion.1 = f32[16,136,128]{2,1,0:T(8,128)} fusion(f32[16,8,128]{2,1,0:T(8,128)S(1)} %broadcast_in_dim.36, f32[16,128,128]{2,1,0:T(8,128)S(1)} %select_add_fusion), kind=kLoop, calls=%fused_computation.18 | loop fusion | flops 278528 | bytes 2228224 | tf_op jit(solution)/shard_map/concatenate | solution.py:16
  17.0 1.4 %collective-permute-start.1 = (f32[16,136,128]{2,1,0:T(8,128)}, f32[16,136,128]{2,1,0:T(8,128)}, u32[]{:S(2)}, u32[]{:S(2)}) collective-permute-start(f32[16,136,128]{2,1,0:T(8,128)} %pad_maximum_fusion.1), channel_id=1, source_target_pairs={{1,3},{3,5},{5,7},{6,4},{4,2},{2,0},{9,11},{11,13},{13,15},{14,12}... | collective-permute-start | bytes 3342344 | tf_op jit(solution)/shard_map/ppermute | solution.py:51
  18.4 1.3 %collective-permute-start.2 = (f32[16,136,128]{2,1,0:T(8,128)}, f32[16,136,128]{2,1,0:T(8,128)}, u32[]{:S(2)}, u32[]{:S(2)}) collective-permute-start(f32[16,136,128]{2,1,0:T(8,128)} %pad_maximum_fusion.1), channel_id=1, source_target_pairs={{1,5},{3,7},{6,2},{4,0},{9,13},{11,15},{14,10},{12,8},{17,21},{19,... | collective-permute-start | bytes 3342344 | tf_op jit(solution)/shard_map/ppermute | solution.py:51
  19.7 1.3 %collective-permute-start.3 = (f32[16,136,128]{2,1,0:T(8,128)}, f32[16,136,128]{2,1,0:T(8,128)}, u32[]{:S(2)}, u32[]{:S(2)}) collective-permute-start(f32[16,136,128]{2,1,0:T(8,128)} %pad_maximum_fusion.1), channel_id=1, source_target_pairs={{1,7},{6,0},{9,15},{14,8},{17,23},{22,16},{25,31},{30,24}} | collective-permute-start | bytes 3342344 | tf_op jit(solution)/shard_map/ppermute | solution.py:51
  21.0 1.7 %fusion = f32[128,16,128]{2,0,1:T(8,128)} fusion(f32[16,128,128]{1,2,0:T(8,128)S(1)} %convolution_multiply_fusion.1, bf16[128,16,128]{2,1,0:T(8,128)(2,1)S(1)} %bitcast.103), kind=kOutput, calls=%fused_computation.4 | convolution fusion | flops 402915328 | bytes 2621440 | tf_op jit(solution)/shard_map/hts,the->she/dot_general | solution.py:134
  22.7 1.0 %copy.39 = bf16[1,128,2048]{1,2,0:T(8,128)(2,1)} copy(bf16[1,128,2048]{2,1,0:T(8,128)(2,1)S(1)} %copy-done.6) | data formatting | bytes 1048576 | tf_op args[1]
  23.7 2.7 %copy.49 = f32[128,16,128]{0,2,1:T(8,128)} copy(f32[128,16,128]{2,0,1:T(8,128)} %fusion) | data formatting | bytes 2097152 | tf_op jit(solution)/shard_map/mul | solution.py:134
  26.5 1.2 %convolution_multiply_fusion.2 = f32[16,128,128]{2,1,0:T(8,128)S(1)} fusion(bf16[128,16,128]{0,2,1:T(8,128)(2,1)S(1)} %bitcast.111, f32[16,128,128]{1,2,0:T(8,128)S(1)} %copy-done.2), kind=kOutput, calls=%fused_computation.6 | convolution fusion | flops 402915328 | bytes 2621440 | tf_op jit(solution)/shard_map/hts,thd->shd/dot_general | solution.py:130
  28.1 1.2 %fusion.12 = bf16[128,2048]{0,1:T(8,128)(2,1)S(1)} fusion(f32[16,128,128]{2,1,0:T(8,128)S(1)} %convolution_multiply_fusion.2, f32[16,128,128]{2,1,0:T(8,128)S(1)} %copy-done.3, f32[128,16,128]{0,2,1:T(8,128)S(1)} %copy-done.4, bf16[1,128,2048]{1,2,0:T(8,128)(2,1)S(1)} %copy-done.7, f32[2048]{0:T(1024)S(1)} %bitcast.118, f32[2048]{0:T(1024)S(1)} %bitcast.124, ...), kind=kLoop, calls=%fused_computation.29 | loop fusion | flops 2097152 | bytes 4218880 | tf_op jit(solution)/shard_map/convert_element_type | solution.py:139
  29.3 4.7 %collective-permute-start.4 = (bf16[128,2048]{0,1:T(8,128)(2,1)S(1)}, bf16[128,2048]{0,1:T(8,128)(2,1)S(1)}, u32[]{:S(2)}, u32[]{:S(2)}) collective-permute-start(bf16[128,2048]{0,1:T(8,128)(2,1)S(1)} %fusion.12), channel_id=1, source_target_pairs={{0,24},{8,0},{16,8},{24,16},{1,25},{9,1},{17,9},{25,17},{2,26},{10... | collective-permute-start | bytes 1572872 | tf_op jit(solution)/shard_map/ppermute | solution.py:75
  34.0 12.2 %collective-permute-done.1 = f32[16,136,128]{2,1,0:T(8,128)} collective-permute-done((f32[16,136,128]{2,1,0:T(8,128)}, f32[16,136,128]{2,1,0:T(8,128)}, u32[]{:S(2)}, u32[]{:S(2)}) %collective-permute-start.1) | collective-permute-done | bytes 1114144 | tf_op jit(solution)/shard_map/ppermute | solution.py:51
  46.2 3.8 %collective-permute-done.2 = f32[16,136,128]{2,1,0:T(8,128)} collective-permute-done((f32[16,136,128]{2,1,0:T(8,128)}, f32[16,136,128]{2,1,0:T(8,128)}, u32[]{:S(2)}, u32[]{:S(2)}) %collective-permute-start.2) | collective-permute-done | bytes 1114144 | tf_op jit(solution)/shard_map/ppermute | solution.py:51
  49.9 1.1 %slice_reduce_fusion = (f32[16]{0:T(128)S(1)}, f32[16]{0:T(128)S(1)}) fusion(f32[16,136,128]{2,1,0:T(8,128)} %collective-permute-done.1, f32[16,136,128]{2,1,0:T(8,128)} %collective-permute-done.2), kind=kLoop, calls=%fused_computation.66 | loop fusion | flops 16 | bytes 256 | tf_op jit(solution)/shard_map/slice | solution.py:21
  51.0 3.1 %fusion.8 = f32[16,128,128]{2,1,0:T(8,128)} fusion(f32[16,136,128]{2,1,0:T(8,128)} %collective-permute-done.3, f32[16,136,128]{2,1,0:T(8,128)} %collective-permute-done.2, f32[16,136,128]{2,1,0:T(8,128)} %collective-permute-done.1, f32[16]{0:T(128)S(1)} %get-tuple-element.12, f32[16]{0:T(128)S(1)} %get-tuple-element.11), kind=kLoop, calls=%fused_computation.23 | loop fusion | flops 1048576 | bytes 4194432 | tf_op jit(solution)/shard_map/add | solution.py:52
  54.2 1.7 %multiply_add_fusion = f32[16,128,128]{2,1,0:T(8,128)S(1)} fusion(f32[16,128,128]{2,1,0:T(8,128)} %fusion.8, f32[16,136,128]{2,1,0:T(8,128)} %collective-permute-done, f32[16]{0:T(128)S(1)} %get-tuple-element.9), kind=kLoop, calls=%fused_computation.41 | loop fusion | flops 524288 | bytes 3145792 | tf_op jit(solution)/shard_map/add | solution.py:68
  55.9 1.1 %collective-permute-done.5 = f32[16,128,128]{2,1,0:T(8,128)S(1)} collective-permute-done((f32[16,128,128]{2,1,0:T(8,128)}, f32[16,128,128]{2,1,0:T(8,128)S(1)}, u32[]{:S(2)}, u32[]{:S(2)}) %collective-permute-start.5) | collective-permute-done | bytes 1048608 | tf_op jit(solution)/shard_map/ppermute | solution.py:67
  57.7 1.0 %fusion.2 = f32[128,16,128]{0,2,1:T(8,128)S(1)} fusion(bf16[128,16,128]{0,2,1:T(8,128)(2,1)S(1)} %bitcast.108, f32[128,16]{0,1:T(8,128)S(1)} %copy.36, f32[16,128,128]{2,1,0:T(8,128)S(1)} %collective-permute-done.5, f32[16,128,128]{2,1,0:T(8,128)S(1)} %multiply_add_fusion, pred[]{:T(512)S(6)} %eq.29), kind=kOutput, calls=%fused_computation.12 | convolution fusion | flops 403177472 | bytes 3678209 | tf_op jit(solution)/shard_map/shd,hde->she/dot_general | solution.py:148
  58.7 1.3 %fusion.4 = f32[128,16,128]{0,2,1:T(8,128)S(1)} fusion(f32[16,128,128]{2,1,0:T(8,128)S(1)} %multiply_add_fusion, f32[16,128,128]{2,1,0:T(8,128)S(1)} %collective-permute-done.5, f32[128,16]{0,1:T(8,128)S(1)} %copy.50, pred[]{:T(512)S(6)} %eq.29, bf16[128,16,128]{2,1,0:T(8,128)(2,1)S(1)} %bitcast.104), kind=kOutput, calls=%fused_computation.16 | convolution fusion | flops 403177472 | bytes 3678209 | tf_op jit(solution)/shard_map/the,hde->thd/dot_general | solution.py:145
  60.0 1.2 %fusion.15 = bf16[128,2048]{0,1:T(8,128)(2,1)S(1)} fusion(f32[128,16,128]{0,2,1:T(8,128)S(1)} %fusion.2, f32[128,16,128]{0,2,1:T(8,128)S(1)} %fusion.3, f32[128,16,128]{0,2,1:T(8,128)S(1)} %fusion.4, f32[2048]{0:T(1024)S(1)} %bitcast.119, f32[2048]{0:T(1024)S(1)} %bitcast.125, f32[2048]{0:T(1024)S(1)} %bitcast.122), kind=kLoop, calls=%fused_computation.34 | loop fusion | flops 1572864 | bytes 3694592 | tf_op jit(solution)/shard_map/convert_element_type | solution.py:152
  61.2 3.6 %collective-permute-start.6 = (bf16[128,2048]{0,1:T(8,128)(2,1)S(1)}, bf16[128,2048]{0,1:T(8,128)(2,1)S(1)}, u32[]{:S(2)}, u32[]{:S(2)}) collective-permute-start(bf16[128,2048]{0,1:T(8,128)(2,1)S(1)} %fusion.15), channel_id=1, source_target_pairs={{0,24},{8,0},{16,8},{24,16},{1,25},{9,1},{17,9},{25,17},{2,26},{10... | collective-permute-start | bytes 1572872 | tf_op jit(solution)/shard_map/ppermute | solution.py:75
  64.8 11.5 %collective-permute-done.6 = bf16[128,2048]{0,1:T(8,128)(2,1)S(1)} collective-permute-done((bf16[128,2048]{0,1:T(8,128)(2,1)S(1)}, bf16[128,2048]{0,1:T(8,128)(2,1)S(1)}, u32[]{:S(2)}, u32[]{:S(2)}) %collective-permute-start.6) | collective-permute-done | bytes 524320 | tf_op jit(solution)/shard_map/ppermute | solution.py:75
  76.5 1.0 %copy.55 = bf16[1,128,2048]{2,1,0:T(8,128)(2,1)} copy(bf16[1,128,2048]{1,2,0:T(8,128)(2,1)S(1)} %fusion.23) | data formatting | bytes 1048576 | tf_op jit(solution)/shard_map/broadcast_in_dim | solution.py:157
  (46 shorter events, 5.1 us)
Async XLA Ops:
  4.0 1.0 %copy-start.5 = (bf16[1,128,2048]{2,1,0:T(8,128)(2,1)S(1)}, bf16[1,128,2048]{2,1,0:T(8,128)(2,1)}, u32[]{:S(2)}) copy-start(bf16[1,128,2048]{2,1,0:T(8,128)(2,1)} %param.6) | copy-start | bytes 1572868
  9.5 3.8 %collective-permute-start = (f32[16,136,128]{2,1,0:T(8,128)}, f32[16,136,128]{2,1,0:T(8,128)}, u32[]{:S(2)}, u32[]{:S(2)}) collective-permute-start(f32[16,136,128]{2,1,0:T(8,128)} %pad_maximum_fusion), channel_id=1, source_target_pairs={{0,1},{2,3},{4,5},{6,7},{1,0},{3,2},{5,4},{7,6},{8,9},{10,11},{12,... | collective-permute-start | bytes 3342344 | tf_op jit(solution)/shard_map/ppermute | solution.py:44
  10.7 1.0 %copy-start.1 = (f32[16,128,128]{1,2,0:T(8,128)}, f32[16,128,128]{1,2,0:T(8,128)S(1)}, u32[]{:S(2)}) copy-start(f32[16,128,128]{1,2,0:T(8,128)S(1)} %fusion.1) | copy-start | bytes 3145732
  11.7 1.6 %copy-start = (f32[16,128,128]{2,1,0:T(8,128)S(1)}, f32[16,128,128]{2,1,0:T(8,128)}, u32[]{:S(2)}) copy-start(f32[16,128,128]{2,1,0:T(8,128)} %get-tuple-element.25) | copy-start | bytes 3145732
  16.9 5.8 %copy-start.6 = (bf16[1,128,2048]{2,1,0:T(8,128)(2,1)S(1)}, bf16[1,128,2048]{2,1,0:T(8,128)(2,1)}, u32[]{:S(2)}) copy-start(bf16[1,128,2048]{2,1,0:T(8,128)(2,1)} %param.6) | copy-start | bytes 1572868
  17.0 29.2 %collective-permute-start.1 = (f32[16,136,128]{2,1,0:T(8,128)}, f32[16,136,128]{2,1,0:T(8,128)}, u32[]{:S(2)}, u32[]{:S(2)}) collective-permute-start(f32[16,136,128]{2,1,0:T(8,128)} %pad_maximum_fusion.1), channel_id=1, source_target_pairs={{1,3},{3,5},{5,7},{6,4},{4,2},{2,0},{9,11},{11,13},{13,15},{14,12}... | collective-permute-start | bytes 3342344 | tf_op jit(solution)/shard_map/ppermute | solution.py:51
  18.4 31.6 %collective-permute-start.2 = (f32[16,136,128]{2,1,0:T(8,128)}, f32[16,136,128]{2,1,0:T(8,128)}, u32[]{:S(2)}, u32[]{:S(2)}) collective-permute-start(f32[16,136,128]{2,1,0:T(8,128)} %pad_maximum_fusion.1), channel_id=1, source_target_pairs={{1,5},{3,7},{6,2},{4,0},{9,13},{11,15},{14,10},{12,8},{17,21},{19,... | collective-permute-start | bytes 3342344 | tf_op jit(solution)/shard_map/ppermute | solution.py:51
  19.7 31.4 %collective-permute-start.3 = (f32[16,136,128]{2,1,0:T(8,128)}, f32[16,136,128]{2,1,0:T(8,128)}, u32[]{:S(2)}, u32[]{:S(2)}) collective-permute-start(f32[16,136,128]{2,1,0:T(8,128)} %pad_maximum_fusion.1), channel_id=1, source_target_pairs={{1,7},{6,0},{9,15},{14,8},{17,23},{22,16},{25,31},{30,24}} | collective-permute-start | bytes 3342344 | tf_op jit(solution)/shard_map/ppermute | solution.py:51
  23.7 2.7 %copy-start.2 = (f32[16,128,128]{1,2,0:T(8,128)S(1)}, f32[16,128,128]{1,2,0:T(8,128)}, u32[]{:S(2)}) copy-start(f32[16,128,128]{1,2,0:T(8,128)} %copy-done.1) | copy-start | bytes 3145732
  26.4 1.2 %copy-start.3 = (f32[16,128,128]{2,1,0:T(8,128)S(1)}, f32[16,128,128]{2,1,0:T(8,128)}, u32[]{:S(2)}) copy-start(f32[16,128,128]{2,1,0:T(8,128)} %convolution_multiply_fusion.3) | copy-start | bytes 3145732
  26.4 1.5 %copy-start.4 = (f32[128,16,128]{0,2,1:T(8,128)S(1)}, f32[128,16,128]{0,2,1:T(8,128)}, u32[]{:S(2)}) copy-start(f32[128,16,128]{0,2,1:T(8,128)} %copy.49) | copy-start | bytes 3145732
  26.5 1.7 %copy-start.7 = (bf16[1,128,2048]{1,2,0:T(8,128)(2,1)S(1)}, bf16[1,128,2048]{1,2,0:T(8,128)(2,1)}, u32[]{:S(2)}) copy-start(bf16[1,128,2048]{1,2,0:T(8,128)(2,1)} %copy.39) | copy-start | bytes 1572868
  29.3 24.8 %collective-permute-start.4 = (bf16[128,2048]{0,1:T(8,128)(2,1)S(1)}, bf16[128,2048]{0,1:T(8,128)(2,1)S(1)}, u32[]{:S(2)}, u32[]{:S(2)}) collective-permute-start(bf16[128,2048]{0,1:T(8,128)(2,1)S(1)} %fusion.12), channel_id=1, source_target_pairs={{0,24},{8,0},{16,8},{24,16},{1,25},{9,1},{17,9},{25,17},{2,26},{10... | collective-permute-start | bytes 1572872 | tf_op jit(solution)/shard_map/ppermute | solution.py:75
  54.1 2.9 %collective-permute-start.5 = (f32[16,128,128]{2,1,0:T(8,128)}, f32[16,128,128]{2,1,0:T(8,128)S(1)}, u32[]{:S(2)}, u32[]{:S(2)}) collective-permute-start(f32[16,128,128]{2,1,0:T(8,128)} %fusion.8), channel_id=1, source_target_pairs={{0,1},{2,3},{4,5},{6,7},{1,0},{3,2},{5,4},{7,6},{8,9},{10,11},{12,... | collective-permute-start | bytes 3145736 | tf_op jit(solution)/shard_map/ppermute | solution.py:67
  61.2 15.1 %collective-permute-start.6 = (bf16[128,2048]{0,1:T(8,128)(2,1)S(1)}, bf16[128,2048]{0,1:T(8,128)(2,1)S(1)}, u32[]{:S(2)}, u32[]{:S(2)}) collective-permute-start(bf16[128,2048]{0,1:T(8,128)(2,1)S(1)} %fusion.15), channel_id=1, source_target_pairs={{0,24},{8,0},{16,8},{24,16},{1,25},{9,1},{17,9},{25,17},{2,26},{10... | collective-permute-start | bytes 1572872 | tf_op jit(solution)/shard_map/ppermute | solution.py:75

commit v5 on v4

--- a/solution.py
+++ b/solution.py
@@ -19,6 +19,25 @@
 def unpacked(message):
     width = message.shape[1] - 8
     return message[:, :width], message[:, width, 0]
+
+
+def narrow(message):
+    state, rate = unpacked(message)
+    high = rate.astype(jnp.bfloat16)
+    low = (rate - high.astype(jnp.float32)).astype(jnp.bfloat16)
+    rows = jnp.stack([high, low] + [jnp.zeros_like(high)] * 6, axis=1)
+    tile = jnp.broadcast_to(rows[:, :, None], (state.shape[0], 8, state.shape[2]))
+    return jnp.concatenate([state.astype(jnp.bfloat16), tile], axis=1)
+
+
+def widen(message):
+    width = message.shape[1] - 8
+    rate = message[:, width, 0].astype(jnp.float32) + message[:, width + 1, 0].astype(jnp.float32)
+    return packed(message[:, :width].astype(jnp.float32), rate)
+
+
+def sent_narrow(message, axis, pairs):
+    return widen(lax.ppermute(narrow(message), axis, pairs))
 
 
 def merged(farther, nearer):
@@ -48,20 +67,20 @@
         weight = jnp.ones_like(rate)
         for step in range(1, couples):
             moves = [(2 * p + 1, 2 * (p + step) + 1) for p in range(couples - step)]
-            got, got_rate = unpacked(lax.ppermute(window, axis, both_ways(count, moves)))
+            got, got_rate = unpacked(sent_narrow(window, axis, both_ways(count, moves)))
             incoming = incoming + weight[:, None, None] * got
             weight = weight * got_rate
     else:
         covered = 1
         while 2 * covered < couples:
             moves = [(2 * p + 1, 2 * (p + covered) + 1) for p in range(couples - covered)]
-            window = merged(lax.ppermute(window, axis, both_ways(count, moves)), window)
+            window = merged(sent_narrow(window, axis, both_ways(count, moves)), window)
             covered *= 2
         moves = [(2 * p + 1, 2 * p + 3) for p in range(couples - 1)]
-        nearer = lax.ppermute(window, axis, both_ways(count, moves))
+        nearer = sent_narrow(window, axis, both_ways(count, moves))
         if 1 + covered < couples:
             moves = [(2 * p + 1, 2 * (p + 1 + covered) + 1) for p in range(couples - 1 - covered)]
-            nearer = merged(lax.ppermute(window, axis, both_ways(count, moves)), nearer)
+            nearer = merged(sent_narrow(window, axis, both_ways(count, moves)), nearer)
         incoming = unpacked(nearer)[0]
     incoming, held = lax.optimization_barrier((incoming, held))
     other = lax.ppermute(incoming, axis, swap)

time: 78.1 us -> 71.6 us (0.917)
  waiting for transfers between devices: 28.6 us -> 23.3 us
  other arithmetic: 15.8 us -> 12.8 us
  matrix products: 11.7 us -> 12.5 us
    ppermute x3, waiting for transfers between devices: 16 us -> 10.6 us  [sent_narrow(): return widen(lax.ppermute(narrow(message), axis, pairs))]
    convert_element_type x0 -> x3, other arithmetic: none -> 1.92 us  [the longest x1 1.91 us: narrow(): return jnp.concatenate([state.astype(jnp.bfloat16), tile], axis=1)]
    add x1, other arithmetic: 3.11 us -> 1.43 us  [scans_in(): incoming = incoming + weight[:, None, None] * got]
    add x1, other arithmetic: 1.42 us -> 0.21 us  [widen(): message[:, width, 0].astype(jnp.float32)]
    concatenate x2 -> x1, other arithmetic: 2.21 us -> 1.13 us  [packed(): return jnp.concatenate([state, tile], axis=1)]
    slice x2 -> x1, other arithmetic: 2.13 us -> 1.05 us  [unpacked(): return (message[:, :width], message[:, width, 0])]
    dot_general x1, matrix products: 1.21 us -> 2.18 us  [local(): jnp.einsum('hts,thd->shd', mixing, queries, precision=HIGH)]
    unnamed x19 -> x13, local copies, waits for them, and re-layouts: 3.33 us -> 3.52 us
  transfers between devices with their start and end apart: 7 -> 7, of which waited for: 4 -> 4; matrix products, arithmetic and copies ran while one was open for 22% -> 23% of each run, Pallas kernels for 0% -> 0%
where the time goes in v5:
time: 71.6 us; the launch traced here: 71 us
  waiting for transfers between devices  23.3 us (33%)
  starting transfers between devices  13.3 us (19%)
  other arithmetic  12.8 us (18%)
  matrix products  12.5 us (17%)
  local copies, waits for them, and re-layouts  8.91 us (12%)
    ppermute x2, waiting for transfers between devices, passed_along(): return lax.ppermute(value, axis, pairs)  11.7 us
    ppermute x3, waiting for transfers between devices, sent_narrow(): return widen(lax.ppermute(narrow(message), axis, pairs))  10.6 us
    ppermute x2, starting transfers between devices, passed_along(): return lax.ppermute(value, axis, pairs)  8.66 us
    ppermute x3, starting transfers between devices, sent_narrow(): return widen(lax.ppermute(narrow(message), axis, pairs))  4.01 us
    unnamed x13, local copies, waits for them, and re-layouts  3.52 us
    mul x1, local copies, waits for them, and re-layouts, local(): scale * jnp.einsum('hts,the->she', attention, grad_rows, precision=HIGH)  2.56 us
    dot_general x1, matrix products, local(): jnp.einsum('hts,thd->shd', mixing, queries, precision=HIGH)  2.18 us
    convert_element_type x1, other arithmetic, narrow(): return jnp.concatenate([state.astype(jnp.bfloat16), tile], axis=1)  1.91 us
  transfers between devices with their start and end apart: 7, of which 4 were waited for; matrix products, arithmetic and copies ran while one was open for 23% of the time, Pallas kernels for 0%

profile of v5, /device:TPU:0, one launch (start us, length us, event | category | flops | bytes accessed | tf_op | source)
XLA Modules:
  0.0 71.0 jit_solution(425200694410331850)
XLA Ops:
  0.1 0.7 compare_bitcast_fusion
  0.9 0.7 log_bitcast_fusion
  1.9 0.7 %fusion.36 = (f32[1,1,2048]{2,0,1:T(1,128)S(1)}, f32[1,1,2048]{2,0,1:T(1,128)S(1)}, f32[1,1,2048]{2,0,1:T(1,128)S(1)}) fusion(f32[1,3,2048]{2,0,1:T(1,128)} %param.7), kind=kLoop, calls=%fused_computation.82 | loop fusion | bytes 49152 | tf_op jit(solution)/shard_map/slice | solution.py:110
  2.6 1.3 %copy.35 = bf16[1,128,2048]{1,2,0:T(8,128)(2,1)S(1)} copy(bf16[1,128,2048]{2,1,0:T(8,128)(2,1)} %param.5) | data formatting | bytes 1048576 | tf_op args[0]
  4.0 1.0 %fusion.7 = (bf16[128,2048]{0,1:T(8,128)(2,1)S(1)}, bf16[128,2048]{0,1:T(8,128)(2,1)S(1)}, bf16[128,2048]{0,1:T(8,128)(2,1)S(1)}) fusion(bf16[1,128,2048]{1,2,0:T(8,128)(2,1)S(1)} %copy.35, f32[2048]{0:T(1024)S(1)} %bitcast.124, f32[2048]{0:T(1024)S(1)} %bitcast.130, f32[2048]{0:T(1024)S(1)} %bitcast.127), kind=kLoop, calls=%fused_computation.20 | loop fusion | flops 1835008 | bytes 2121728 | tf_op jit(solution)/shard_map/convert_element_type | solution.py:110
  5.3 1.2 %fusion.16 = f32[16,128,128]{2,1,0:T(8,128)S(1)} fusion(bf16[128,16,128]{0,2,1:T(8,128)(2,1)S(1)} %bitcast.119, bf16[128,16,128]{0,2,1:T(8,128)(2,1)S(1)} %bitcast.112, f32[128,16]{0,1:T(8,128)S(1)} %copy.38), kind=kOutput, calls=%fused_computation.40 | convolution fusion | flops 403177472 | bytes 2105344 | tf_op jit(solution)/shard_map/shd,she->hde/dot_general | solution.py:133
  6.5 1.8 %broadcast_select_fusion.1 = (f32[16,128,128]{2,1,0:T(8,128)S(1)}, f32[16,128,128]{2,1,0:T(8,128)}) fusion(f32[16,128,128]{2,1,0:T(8,128)S(1)} %fusion.16, pred[]{:T(512)S(6)} %eq.29, bf16[128,16,128]{2,1,0:T(8,128)(2,1)S(1)} %bitcast.108, bf16[128,16,128]{0,2,1:T(8,128)(2,1)S(1)} %bitcast.116, f32[128,16]{0,1:T(8,128)S(1)} %copy.36), kind=kOutput, calls=%fused_computation.51 | convolution fusion | flops 403701760 | bytes 4202497 | tf_op jit(solution)/shard_map/shd,she->hde/dot_general | solution.py:136
  8.4 1.1 %pad_maximum_fusion = f32[16,136,128]{2,1,0:T(8,128)} fusion(f32[16,8,128]{2,1,0:T(8,128)S(1)} %broadcast_in_dim.34, f32[16,128,128]{2,1,0:T(8,128)S(1)} %get-tuple-element.24), kind=kLoop, calls=%fused_computation.17 | loop fusion | flops 278528 | bytes 2228224 | tf_op jit(solution)/shard_map/concatenate | solution.py:16
  10.0 2.0 %copy.43 = bf16[1,128,2048]{1,2,0:T(8,128)(2,1)} copy(bf16[1,128,2048]{2,1,0:T(8,128)(2,1)} %param.6) | data formatting | bytes 1048576 | tf_op args[1]
  12.6 1.6 %fusion = f32[128,16,128]{2,0,1:T(8,128)} fusion(f32[16,128,128]{1,2,0:T(8,128)S(1)} %convolution_multiply_fusion.1, bf16[128,16,128]{2,1,0:T(8,128)(2,1)S(1)} %bitcast.109), kind=kOutput, calls=%fused_computation.4 | convolution fusion | flops 402915328 | bytes 2621440 | tf_op jit(solution)/shard_map/hts,the->she/dot_general | solution.py:153
  14.3 2.6 %copy.53 = f32[128,16,128]{0,2,1:T(8,128)} copy(f32[128,16,128]{2,0,1:T(8,128)} %fusion) | data formatting | bytes 2097152 | tf_op jit(solution)/shard_map/mul | solution.py:153
  17.7 1.7 %convolution_multiply_fusion.3 = f32[16,128,128]{2,1,0:T(8,128)} fusion(bf16[128,16,128]{0,2,1:T(8,128)(2,1)S(1)} %bitcast.114, f32[16,128,128]{1,2,0:T(8,128)S(1)} %fusion.1), kind=kOutput, calls=%fused_computation.7 | convolution fusion | flops 402915328 | bytes 2621440 | tf_op jit(solution)/shard_map/hts,shd->thd/dot_general | solution.py:148
  19.3 2.2 %convolution_multiply_fusion.2 = f32[16,128,128]{2,1,0:T(8,128)} fusion(bf16[128,16,128]{0,2,1:T(8,128)(2,1)S(1)} %bitcast.118, f32[16,128,128]{1,2,0:T(8,128)S(1)} %fusion.1), kind=kOutput, calls=%fused_computation.6 | convolution fusion | flops 402915328 | bytes 2621440 | tf_op jit(solution)/shard_map/hts,thd->shd/dot_general | solution.py:149
  21.5 1.0 %slice_reduce_fusion = (f32[16]{0:T(128)S(1)}, f32[16]{0:T(128)S(1)}) fusion(f32[16,136,128]{2,1,0:T(8,128)} %collective-permute-done, f32[16,1,1]{2,1,0:T(1,128)S(1)} %copy.40), kind=kLoop, calls=%fused_computation.69 | loop fusion | flops 16 | bytes 256 | tf_op jit(solution)/shard_map/slice | solution.py:21
  22.8 1.9 %add_convert_fusion.1 = bf16[16,128,128]{2,1,0:T(8,128)(2,1)S(1)} fusion(f32[16,128,128]{2,1,0:T(8,128)S(1)} %fusion.16, f32[16,128,128]{2,1,0:T(8,128)} %get-tuple-element.25, f32[16,136,128]{2,1,0:T(8,128)} %collective-permute-done, f32[16]{0:T(128)S(1)} %fusion.34, pred[]{:T(512)S(6)} %eq.29), kind=kLoop, calls=%fused_computation.39 | loop fusion | flops 1048576 | bytes 3670081 | tf_op jit(solution)/shard_map/convert_element_type | solution.py:30
  24.9 1.4 %collective-permute-start.1 = (bf16[16,136,128]{2,1,0:T(8,128)(2,1)S(1)}, bf16[16,136,128]{2,1,0:T(8,128)(2,1)S(1)}, u32[]{:S(2)}, u32[]{:S(2)}) collective-permute-start(bf16[16,136,128]{2,1,0:T(8,128)(2,1)S(1)} %pad_maximum_fusion.1), channel_id=1, source_target_pairs={{1,3},{3,5},{5,7},{6,4},{4,2},{2,0},{9,11},{11,13},{13,15},{14,12}... | collective-permute-start | bytes 1671176 | tf_op jit(solution)/shard_map/ppermute | solution.py:40
  26.3 1.3 %collective-permute-start.2 = (bf16[16,136,128]{2,1,0:T(8,128)(2,1)S(1)}, bf16[16,136,128]{2,1,0:T(8,128)(2,1)S(1)}, u32[]{:S(2)}, u32[]{:S(2)}) collective-permute-start(bf16[16,136,128]{2,1,0:T(8,128)(2,1)S(1)} %pad_maximum_fusion.1), channel_id=1, source_target_pairs={{1,5},{3,7},{6,2},{4,0},{9,13},{11,15},{14,10},{12,8},{17,21},{19,... | collective-permute-start | bytes 1671176 | tf_op jit(solution)/shard_map/ppermute | solution.py:40
  27.6 1.3 %collective-permute-start.3 = (bf16[16,136,128]{2,1,0:T(8,128)(2,1)S(1)}, bf16[16,136,128]{2,1,0:T(8,128)(2,1)S(1)}, u32[]{:S(2)}, u32[]{:S(2)}) collective-permute-start(bf16[16,136,128]{2,1,0:T(8,128)(2,1)S(1)} %pad_maximum_fusion.1), channel_id=1, source_target_pairs={{1,7},{6,0},{9,15},{14,8},{17,23},{22,16},{25,31},{30,24}} | collective-permute-start | bytes 1671176 | tf_op jit(solution)/shard_map/ppermute | solution.py:40
  29.0 1.2 %fusion.10 = bf16[128,2048]{0,1:T(8,128)(2,1)S(1)} fusion(f32[16,128,128]{2,1,0:T(8,128)S(1)} %copy-done.2, f32[16,128,128]{2,1,0:T(8,128)S(1)} %copy-done.1, f32[128,16,128]{0,2,1:T(8,128)S(1)} %copy-done, bf16[1,128,2048]{1,2,0:T(8,128)(2,1)S(1)} %copy-done.4, f32[2048]{0:T(1024)S(1)} %bitcast.125, f32[2048]{0:T(1024)S(1)} %bitcast.131, f32[2048]{0:T(1024)S(1)} %bitcast.128), kind=kLoop, calls=%fused_computation.24 | loop fusion | flops 2097152 | bytes 4218880 | tf_op jit(solution)/shard_map/convert_element_type | solution.py:158
  30.2 4.8 %collective-permute-start.4 = (bf16[128,2048]{0,1:T(8,128)(2,1)S(1)}, bf16[128,2048]{0,1:T(8,128)(2,1)S(1)}, u32[]{:S(2)}, u32[]{:S(2)}) collective-permute-start(bf16[128,2048]{0,1:T(8,128)(2,1)S(1)} %fusion.10), channel_id=1, source_target_pairs={{0,24},{8,0},{16,8},{24,16},{1,25},{9,1},{17,9},{25,17},{2,26},{10... | collective-permute-start | bytes 1572872 | tf_op jit(solution)/shard_map/ppermute | solution.py:94
  35.0 7.2 %collective-permute-done.1 = bf16[16,136,128]{2,1,0:T(8,128)(2,1)S(1)} collective-permute-done((bf16[16,136,128]{2,1,0:T(8,128)(2,1)S(1)}, bf16[16,136,128]{2,1,0:T(8,128)(2,1)S(1)}, u32[]{:S(2)}, u32[]{:S(2)}) %collective-permute-start.1) | collective-permute-done | bytes 557088 | tf_op jit(solution)/shard_map/ppermute | solution.py:40
  42.2 3.4 %collective-permute-done.2 = bf16[16,136,128]{2,1,0:T(8,128)(2,1)S(1)} collective-permute-done((bf16[16,136,128]{2,1,0:T(8,128)(2,1)S(1)}, bf16[16,136,128]{2,1,0:T(8,128)(2,1)S(1)}, u32[]{:S(2)}, u32[]{:S(2)}) %collective-permute-start.2) | collective-permute-done | bytes 557088 | tf_op jit(solution)/shard_map/ppermute | solution.py:40
  45.9 1.4 %multiply_add_fusion.1 = f32[16,128,128]{2,1,0:T(8,128)} fusion(bf16[16,136,128]{2,1,0:T(8,128)(2,1)S(1)} %collective-permute-done.3, bf16[16,136,128]{2,1,0:T(8,128)(2,1)S(1)} %collective-permute-done.2, bf16[16,136,128]{2,1,0:T(8,128)(2,1)S(1)} %collective-permute-done.1, f32[16]{0:T(128)S(1)} %get-tuple-element.12, f32[16]{0:T(128)S(1)} %get-tuple-element.11), kind=kLoop, calls=%fused_computation.38 | loop fusion | flops 1835008 | bytes 2621568 | tf_op jit(solution)/shard_map/add | solution.py:71
  47.5 1.7 %multiply_add_fusion = f32[16,128,128]{2,1,0:T(8,128)S(1)} fusion(f32[16,128,128]{2,1,0:T(8,128)} %multiply_add_fusion.1, f32[16,136,128]{2,1,0:T(8,128)} %collective-permute-done, f32[16]{0:T(128)S(1)} %get-tuple-element.9), kind=kLoop, calls=%fused_computation.36 | loop fusion | flops 524288 | bytes 3145792 | tf_op jit(solution)/shard_map/add | solution.py:87
  49.2 0.9 %collective-permute-done.5 = f32[16,128,128]{2,1,0:T(8,128)S(1)} collective-permute-done((f32[16,128,128]{2,1,0:T(8,128)}, f32[16,128,128]{2,1,0:T(8,128)S(1)}, u32[]{:S(2)}, u32[]{:S(2)}) %collective-permute-start.5) | collective-permute-done | bytes 1048608 | tf_op jit(solution)/shard_map/ppermute | solution.py:86
  50.2 0.7 fusion.3
  50.8 1.0 %fusion.2 = f32[128,16,128]{0,2,1:T(8,128)S(1)} fusion(bf16[128,16,128]{0,2,1:T(8,128)(2,1)S(1)} %bitcast.115, f32[128,16]{0,1:T(8,128)S(1)} %copy.38, f32[16,128,128]{2,1,0:T(8,128)S(1)} %collective-permute-done.5, f32[16,128,128]{2,1,0:T(8,128)S(1)} %multiply_add_fusion, pred[]{:T(512)S(6)} %eq.29), kind=kOutput, calls=%fused_computation.12 | convolution fusion | flops 403177472 | bytes 3678209 | tf_op jit(solution)/shard_map/shd,hde->she/dot_general | solution.py:167
  51.9 1.3 %fusion.4 = f32[128,16,128]{0,2,1:T(8,128)S(1)} fusion(f32[16,128,128]{2,1,0:T(8,128)S(1)} %multiply_add_fusion, f32[16,128,128]{2,1,0:T(8,128)S(1)} %collective-permute-done.5, f32[128,16]{0,1:T(8,128)S(1)} %copy.54, pred[]{:T(512)S(6)} %eq.29, bf16[128,16,128]{2,1,0:T(8,128)(2,1)S(1)} %bitcast.111), kind=kOutput, calls=%fused_computation.16 | convolution fusion | flops 403177472 | bytes 3678209 | tf_op jit(solution)/shard_map/the,hde->thd/dot_general | solution.py:164
  53.1 1.2 %fusion.13 = bf16[128,2048]{0,1:T(8,128)(2,1)S(1)} fusion(f32[128,16,128]{0,2,1:T(8,128)S(1)} %fusion.2, f32[128,16,128]{0,2,1:T(8,128)S(1)} %fusion.3, f32[128,16,128]{0,2,1:T(8,128)S(1)} %fusion.4, f32[2048]{0:T(1024)S(1)} %bitcast.126, f32[2048]{0:T(1024)S(1)} %bitcast.132, f32[2048]{0:T(1024)S(1)} %bitcast.129), kind=kLoop, calls=%fused_computation.29 | loop fusion | flops 1572864 | bytes 3694592 | tf_op jit(solution)/shard_map/convert_element_type | solution.py:171
  54.4 3.8 %collective-permute-start.6 = (bf16[128,2048]{0,1:T(8,128)(2,1)S(1)}, bf16[128,2048]{0,1:T(8,128)(2,1)S(1)}, u32[]{:S(2)}, u32[]{:S(2)}) collective-permute-start(bf16[128,2048]{0,1:T(8,128)(2,1)S(1)} %fusion.13), channel_id=1, source_target_pairs={{0,24},{8,0},{16,8},{24,16},{1,25},{9,1},{17,9},{25,17},{2,26},{10... | collective-permute-start | bytes 1572872 | tf_op jit(solution)/shard_map/ppermute | solution.py:94
  58.2 11.7 %collective-permute-done.6 = bf16[128,2048]{0,1:T(8,128)(2,1)S(1)} collective-permute-done((bf16[128,2048]{0,1:T(8,128)(2,1)S(1)}, bf16[128,2048]{0,1:T(8,128)(2,1)S(1)}, u32[]{:S(2)}, u32[]{:S(2)}) %collective-permute-start.6) | collective-permute-done | bytes 524320 | tf_op jit(solution)/shard_map/ppermute | solution.py:94
  70.0 1.0 %copy.59 = bf16[1,128,2048]{2,1,0:T(8,128)(2,1)} copy(bf16[1,128,2048]{1,2,0:T(8,128)(2,1)S(1)} %fusion.21) | data formatting | bytes 1048576 | tf_op jit(solution)/shard_map/broadcast_in_dim | solution.py:176
  (49 shorter events, 3.8 us)
Async XLA Ops:
  4.0 1.0 %copy-start.3 = (bf16[1,128,2048]{2,1,0:T(8,128)(2,1)S(1)}, bf16[1,128,2048]{2,1,0:T(8,128)(2,1)}, u32[]{:S(2)}) copy-start(bf16[1,128,2048]{2,1,0:T(8,128)(2,1)} %param.6) | copy-start | bytes 1572868
  9.5 12.0 %collective-permute-start = (f32[16,136,128]{2,1,0:T(8,128)}, f32[16,136,128]{2,1,0:T(8,128)}, u32[]{:S(2)}, u32[]{:S(2)}) collective-permute-start(f32[16,136,128]{2,1,0:T(8,128)} %pad_maximum_fusion), channel_id=1, source_target_pairs={{0,1},{2,3},{4,5},{6,7},{1,0},{3,2},{5,4},{7,6},{8,9},{10,11},{12,... | collective-permute-start | bytes 3342344 | tf_op jit(solution)/shard_map/ppermute | solution.py:63
  22.8 6.1 %copy-start.1 = (f32[16,128,128]{2,1,0:T(8,128)S(1)}, f32[16,128,128]{2,1,0:T(8,128)}, u32[]{:S(2)}) copy-start(f32[16,128,128]{2,1,0:T(8,128)} %convolution_multiply_fusion.3) | copy-start | bytes 3145732
  22.8 6.1 %copy-start.2 = (f32[16,128,128]{2,1,0:T(8,128)S(1)}, f32[16,128,128]{2,1,0:T(8,128)}, u32[]{:S(2)}) copy-start(f32[16,128,128]{2,1,0:T(8,128)} %convolution_multiply_fusion.2) | copy-start | bytes 3145732
  22.8 6.1 %copy-start.4 = (bf16[1,128,2048]{1,2,0:T(8,128)(2,1)S(1)}, bf16[1,128,2048]{1,2,0:T(8,128)(2,1)}, u32[]{:S(2)}) copy-start(bf16[1,128,2048]{1,2,0:T(8,128)(2,1)} %copy.43) | copy-start | bytes 1572868
  24.7 4.2 %copy-start = (f32[128,16,128]{0,2,1:T(8,128)S(1)}, f32[128,16,128]{0,2,1:T(8,128)}, u32[]{:S(2)}) copy-start(f32[128,16,128]{0,2,1:T(8,128)} %copy.53) | copy-start | bytes 3145732
  24.9 17.3 %collective-permute-start.1 = (bf16[16,136,128]{2,1,0:T(8,128)(2,1)S(1)}, bf16[16,136,128]{2,1,0:T(8,128)(2,1)S(1)}, u32[]{:S(2)}, u32[]{:S(2)}) collective-permute-start(bf16[16,136,128]{2,1,0:T(8,128)(2,1)S(1)} %pad_maximum_fusion.1), channel_id=1, source_target_pairs={{1,3},{3,5},{5,7},{6,4},{4,2},{2,0},{9,11},{11,13},{13,15},{14,12}... | collective-permute-start | bytes 1671176 | tf_op jit(solution)/shard_map/ppermute | solution.py:40
  26.3 19.3 %collective-permute-start.2 = (bf16[16,136,128]{2,1,0:T(8,128)(2,1)S(1)}, bf16[16,136,128]{2,1,0:T(8,128)(2,1)S(1)}, u32[]{:S(2)}, u32[]{:S(2)}) collective-permute-start(bf16[16,136,128]{2,1,0:T(8,128)(2,1)S(1)} %pad_maximum_fusion.1), channel_id=1, source_target_pairs={{1,5},{3,7},{6,2},{4,0},{9,13},{11,15},{14,10},{12,8},{17,21},{19,... | collective-permute-start | bytes 1671176 | tf_op jit(solution)/shard_map/ppermute | solution.py:40
  27.6 18.2 %collective-permute-start.3 = (bf16[16,136,128]{2,1,0:T(8,128)(2,1)S(1)}, bf16[16,136,128]{2,1,0:T(8,128)(2,1)S(1)}, u32[]{:S(2)}, u32[]{:S(2)}) collective-permute-start(bf16[16,136,128]{2,1,0:T(8,128)(2,1)S(1)} %pad_maximum_fusion.1), channel_id=1, source_target_pairs={{1,7},{6,0},{9,15},{14,8},{17,23},{22,16},{25,31},{30,24}} | collective-permute-start | bytes 1671176 | tf_op jit(solution)/shard_map/ppermute | solution.py:40
  30.2 17.1 %collective-permute-start.4 = (bf16[128,2048]{0,1:T(8,128)(2,1)S(1)}, bf16[128,2048]{0,1:T(8,128)(2,1)S(1)}, u32[]{:S(2)}, u32[]{:S(2)}) collective-permute-start(bf16[128,2048]{0,1:T(8,128)(2,1)S(1)} %fusion.10), channel_id=1, source_target_pairs={{0,24},{8,0},{16,8},{24,16},{1,25},{9,1},{17,9},{25,17},{2,26},{10... | collective-permute-start | bytes 1572872 | tf_op jit(solution)/shard_map/ppermute | solution.py:94
  47.3 2.9 %collective-permute-start.5 = (f32[16,128,128]{2,1,0:T(8,128)}, f32[16,128,128]{2,1,0:T(8,128)S(1)}, u32[]{:S(2)}, u32[]{:S(2)}) collective-permute-start(f32[16,128,128]{2,1,0:T(8,128)} %multiply_add_fusion.1), channel_id=1, source_target_pairs={{0,1},{2,3},{4,5},{6,7},{1,0},{3,2},{5,4},{7,6},{8,9},{10,11},{12,... | collective-permute-start | bytes 3145736 | tf_op jit(solution)/shard_map/ppermute | solution.py:86
  54.4 15.5 %collective-permute-start.6 = (bf16[128,2048]{0,1:T(8,128)(2,1)S(1)}, bf16[128,2048]{0,1:T(8,128)(2,1)S(1)}, u32[]{:S(2)}, u32[]{:S(2)}) collective-permute-start(bf16[128,2048]{0,1:T(8,128)(2,1)S(1)} %fusion.13), channel_id=1, source_target_pairs={{0,24},{8,0},{16,8},{24,16},{1,25},{9,1},{17,9},{25,17},{2,26},{10... | collective-permute-start | bytes 1572872 | tf_op jit(solution)/shard_map/ppermute | solution.py:94

commit v6 on v5

--- a/solution.py
+++ b/solution.py
@@ -46,14 +46,21 @@
     return packed(near_rate[:, None, None] * far_state + near_state, far_rate * near_rate)
 
 
+def split_dot(spec, wide, exact):
+    high = wide.astype(jnp.bfloat16)
+    low = (wide - high.astype(jnp.float32)).astype(jnp.bfloat16)
+    first = jnp.einsum(spec, high, exact, preferred_element_type=jnp.float32)
+    return first + jnp.einsum(spec, low, exact, preferred_element_type=jnp.float32)
+
+
 def both_ways(count, moves):
     return list(moves) + [(count - 1 - source, count - 1 - target) for source, target in moves]
 
 
-def scans_in(forward_part, backward_part, rate, axis, held):
+def scans_in(forward_part, backward_part, rate, axis, middle, inputs):
     count = lax.axis_size(axis)
     if count == 1:
-        return jnp.zeros_like(forward_part), jnp.zeros_like(backward_part), held
+        return jnp.zeros_like(forward_part), jnp.zeros_like(backward_part), middle(*inputs)
     assert count % 2 == 0
     odd = lax.axis_index(axis) % 2 == 1
     couples = count // 2
@@ -62,6 +69,8 @@
     sent = packed(jnp.where(odd, backward_part, forward_part), rate)
     lower, lower_rate = unpacked(lax.ppermute(sent, axis, swap))
     window = packed(rate[:, None, None] * lower + mine, rate * lower_rate)
+    window, inputs = lax.optimization_barrier((window, inputs))
+    held = middle(*inputs)
     if couples <= 4:
         incoming = jnp.zeros_like(mine)
         weight = jnp.ones_like(rate)
@@ -112,6 +121,31 @@
     return result
 
 
+def near_terms(query_half, key_half, value_half, grad_half, cumul, grad_block, gain):
+    rows, heads, head_dim = query_half.shape
+    width = heads * head_dim
+    scale = 1.0 / head_dim
+    cum_heads = cumul.T
+    gap = cum_heads[:, :, None] - cum_heads[:, None, :]
+    lower = jnp.arange(rows)[:, None] >= jnp.arange(rows)[None, :]
+    decay = jnp.where(lower[None], jnp.exp(jnp.minimum(gap, 0.0)), 0.0)
+    mixing = (
+        jnp.einsum("thd,shd->hts", grad_half, value_half, preferred_element_type=jnp.float32)
+        * decay
+    )
+    query_near = scale * split_dot("hts,shd->thd", mixing, key_half)
+    key_near = scale * split_dot("hts,thd->shd", mixing, query_half)
+    attention = (
+        jnp.einsum("thd,shd->hts", query_half, key_half, preferred_element_type=jnp.float32) * decay
+    )
+    value_near = scale * split_dot("hts,the->she", attention, grad_half)
+    near_total = grad_block.astype(jnp.float32)
+    near_total = near_total + gain[0] * query_near.reshape(rows, width)
+    near_total = near_total + gain[1] * key_near.reshape(rows, width)
+    near_total = near_total + gain[2] * value_near.reshape(rows, width)
+    return passed_along(near_total.astype(jnp.bfloat16), "section", -1)
+
+
 def local(inputs, out_grad, gains, exponent, boundary):
     block = inputs[0]
     grad_block = out_grad[0]
@@ -122,54 +156,30 @@
     scale = 1.0 / head_dim
     query_half, key_half, value_half = projections(block, gain, heads)
     grad_half = grad_block.reshape(rows, heads, head_dim)
-    queries = query_half.astype(jnp.float32)
-    key_rows = key_half.astype(jnp.float32)
-    value_rows = value_half.astype(jnp.float32)
-    grad_rows = grad_half.astype(jnp.float32)
     logs = decay_logs(exponent[0], boundary[0], CH).reshape(rows, heads)
     cumul = jnp.cumsum(logs, axis=0)
     growth = jnp.exp(cumul)
     tail = jnp.exp(cumul[-1][None, :] - cumul)
-    forward_part = jnp.einsum(
-        "shd,she->hde", key_rows * tail[:, :, None], value_rows, precision=HIGH
-    )
-    adjoint_part = scale * jnp.einsum(
-        "shd,she->hde", queries * growth[:, :, None], grad_rows, precision=HIGH
+    forward_part = split_dot("shd,she->hde", key_half.astype(jnp.float32) * tail[:, :, None], value_half)
+    adjoint_part = scale * split_dot(
+        "shd,she->hde", query_half.astype(jnp.float32) * growth[:, :, None], grad_half
     )
     whole_decay = jnp.exp(cumul[-1])
-    cum_heads = cumul.T
-    gap = cum_heads[:, :, None] - cum_heads[:, None, :]
-    lower = jnp.arange(rows)[:, None] >= jnp.arange(rows)[None, :]
-    decay = jnp.where(lower[None], jnp.exp(jnp.minimum(gap, 0.0)), 0.0)
-    mixing = (
-        jnp.einsum("thd,shd->hts", grad_half, value_half, preferred_element_type=jnp.float32)
-        * decay
+    state_in, adjoint_in, near_received = scans_in(
+        forward_part,
+        adjoint_part,
+        whole_decay,
+        "ctx",
+        near_terms,
+        (query_half, key_half, value_half, grad_half, cumul, grad_block, gain),
     )
-    query_near = scale * jnp.einsum("hts,shd->thd", mixing, key_rows, precision=HIGH)
-    key_near = scale * jnp.einsum("hts,thd->shd", mixing, queries, precision=HIGH)
-    attention = (
-        jnp.einsum("thd,shd->hts", query_half, key_half, preferred_element_type=jnp.float32) * decay
-    )
-    value_near = scale * jnp.einsum("hts,the->she", attention, grad_rows, precision=HIGH)
-    near_total = grad_block.astype(jnp.float32)
-    near_total = near_total + gain[0] * query_near.reshape(rows, width)
-    near_total = near_total + gain[1] * key_near.reshape(rows, width)
-    near_total = near_total + gain[2] * value_near.reshape(rows, width)
-    near_round = near_total.astype(jnp.bfloat16)
-    near_received = passed_along(near_round, "section", -1)
-    state_in, adjoint_in, near_received = scans_in(
-        forward_part, adjoint_part, whole_decay, "ctx", near_received
-    )
-    query_far = (
-        scale * growth[:, :, None] * jnp.einsum("the,hde->thd", grad_rows, state_in, precision=HIGH)
-    )
-    key_far = tail[:, :, None] * jnp.einsum("she,hde->shd", value_rows, adjoint_in, precision=HIGH)
-    value_far = tail[:, :, None] * jnp.einsum("shd,hde->she", key_rows, adjoint_in, precision=HIGH)
+    query_far = scale * growth[:, :, None] * split_dot("hde,the->thd", state_in, grad_half)
+    key_far = tail[:, :, None] * split_dot("hde,she->shd", adjoint_in, value_half)
+    value_far = tail[:, :, None] * split_dot("hde,shd->she", adjoint_in, key_half)
     far_total = gain[0] * query_far.reshape(rows, width)
     far_total = far_total + gain[1] * key_far.reshape(rows, width)
     far_total = far_total + gain[2] * value_far.reshape(rows, width)
-    far_round = far_total.astype(jnp.bfloat16)
-    far_received = passed_along(far_round, "section", -1)
+    far_received = passed_along(far_total.astype(jnp.bfloat16), "section", -1)
     received = (near_received.astype(jnp.float32) + far_received.astype(jnp.float32)).astype(
         jnp.bfloat16
     )

time: 71.6 us -> 104 us (1.45); the launches traced: 71 us -> 102 us
  local copies, waits for them, and re-layouts: 8.91 us -> 23.6 us
  matrix products: 12.5 us -> 21.9 us
  other arithmetic: 12.8 us -> 18.8 us
  starting transfers between devices: 13.3 us -> 18.3 us
  waiting for transfers between devices: 23.3 us -> 19.5 us
    reshape x0 -> x7, local copies, waits for them, and re-layouts: none -> 16.9 us  [the longest x1 2.69 us: local(): far_total = gain[0] * query_far.reshape(rows, width)]
    ppermute x3, waiting for transfers between devices: 10.6 us -> 0.01 us  [sent_narrow(): return widen(lax.ppermute(narrow(message), axis, pairs))]
    dot_general x10 -> x18, matrix products: 12.5 us -> 21.9 us  [the longest x8 10.5 us: split_dot(): jnp.einsum(spec, low, exact, preferred_element_type=jnp.float32)]
    ppermute x1, starting transfers between devices: 0.16 us -> 4.65 us  [scans_in(): other = lax.ppermute(incoming, axis, swap)]
    ppermute x2, waiting for transfers between devices: 11.7 us -> 15.5 us  [passed_along(): return lax.ppermute(value, axis, pairs)]
    mul x2 -> x1, local copies, waits for them, and re-layouts: 2.61 us -> 0.05 us  [local(): scale * growth[:, :, None] * split_dot('hde,the->thd', state_in, grad_half)]
    convert_element_type x3, other arithmetic: 4.33 us -> 6.27 us  [the longest x1 2.9 us: split_dot(): low = (wide - high.astype(jnp.float32)).astype(jnp.bfloat16)]
    broadcast_in_dim x1, other arithmetic: 0.14 us -> 1.96 us  [local(): return received[None]]
  transfers between devices with their start and end apart: 7 -> 7, of which waited for: 4 -> 4; matrix products, arithmetic and copies ran while one was open for 23% -> 27% of each run, Pallas kernels for 0% -> 0%
where the time goes in v6:
time: 104 us; the launch traced here: 102 us
  local copies, waits for them, and re-layouts  23.6 us (23%)
  matrix products  21.9 us (21%)
  waiting for transfers between devices  19.5 us (19%)
  other arithmetic  18.8 us (18%)
  starting transfers between devices  18.3 us (18%)
    ppermute x2, waiting for transfers between devices, passed_along(): return lax.ppermute(value, axis, pairs)  15.5 us
    dot_general x8, matrix products, split_dot(): jnp.einsum(spec, low, exact, preferred_element_type=jnp.float32)  10.5 us
    ppermute x2, starting transfers between devices, passed_along(): return lax.ppermute(value, axis, pairs)  9.38 us
    dot_general x8, matrix products, split_dot(): first = jnp.einsum(spec, high, exact, preferred_element_type=jnp.float32)  9.22 us
    ppermute x1, starting transfers between devices, scans_in(): other = lax.ppermute(incoming, axis, swap)  4.65 us
    ppermute x3, starting transfers between devices, sent_narrow(): return widen(lax.ppermute(narrow(message), axis, pairs))  3.86 us
    unnamed x24, local copies, waits for them, and re-layouts  2.97 us
    convert_element_type x1, other arithmetic, split_dot(): low = (wide - high.astype(jnp.float32)).astype(jnp.bfloat16)  2.9 us
  transfers between devices with their start and end apart: 7, of which 4 were waited for; matrix products, arithmetic and copies ran while one was open for 27% of the time, Pallas kernels for 0%

profile of v6, /device:TPU:0, one launch (start us, length us, event | category | flops | bytes accessed | tf_op | source)
XLA Modules:
  0.0 102.4 jit_solution(18363817602650567869)
XLA Ops:
  7.6 1.4 %broadcast_select_fusion.2 = (f32[16,128,128]{2,1,0:T(8,128)S(1)}, f32[16,128,128]{2,1,0:T(8,128)}) fusion(f32[16,128,128]{2,1,0:T(8,128)S(1)} %convolution_add_fusion.6, pred[]{:T(512)S(6)} %eq.29, f32[16,128,128]{2,1,0:T(8,128)S(1)} %fusion.15, bf16[128,16,128]{2,1,0:T(8,128)(2,1)S(1)} %bitcast.113, bf16[128,16,128]{0,2,1:T(8,128)(2,1)S(1)} %copy-done.2, ...), kind=kOutput, calls=%fused_computation.63 | convolution fusion | flops 69468160 | bytes 5251073 | tf_op jit(solution)/shard_map/shd,she->hde/dot_general | solution.py:53
  11.8 1.5 %collective-permute-done = f32[16,136,128]{2,1,0:T(8,128)} collective-permute-done((f32[16,136,128]{2,1,0:T(8,128)}, f32[16,136,128]{2,1,0:T(8,128)}, u32[]{:S(2)}, u32[]{:S(2)}) %collective-permute-start) | collective-permute-done | bytes 1114144 | tf_op jit(solution)/shard_map/ppermute | solution.py:70
  13.4 1.4 %select_add_fusion = f32[16,128,128]{2,1,0:T(8,128)S(1)} fusion(f32[16,128,128]{2,1,0:T(8,128)S(1)} %convolution_add_fusion.6, f32[16,128,128]{2,1,0:T(8,128)S(1)} %copy-done.5, f32[16,136,128]{2,1,0:T(8,128)} %collective-permute-done, f32[16]{0:T(128)S(1)} %fusion.58, pred[]{:T(512)S(6)} %eq.29), kind=kLoop, calls=%fused_computation.39 | loop fusion | flops 786432 | bytes 4194369 | tf_op jit(solution)/shard_map/add | solution.py:71
  18.8 1.3 %collective-permute-start.2 = (bf16[16,136,128]{2,1,0:T(8,128)(2,1)}, bf16[16,136,128]{2,1,0:T(8,128)(2,1)}, u32[]{:S(2)}, u32[]{:S(2)}) collective-permute-start(bf16[16,136,128]{2,1,0:T(8,128)(2,1)} %pad_maximum_fusion.2), channel_id=1, source_target_pairs={{1,5},{3,7},{6,2},{4,0},{9,13},{11,15},{14,10},{12,8},{17,21},{19,... | collective-permute-start | bytes 1671176 | tf_op jit(solution)/shard_map/ppermute | solution.py:40
  20.1 1.3 %collective-permute-start.1 = (bf16[16,136,128]{2,1,0:T(8,128)(2,1)}, bf16[16,136,128]{2,1,0:T(8,128)(2,1)}, u32[]{:S(2)}, u32[]{:S(2)}) collective-permute-start(bf16[16,136,128]{2,1,0:T(8,128)(2,1)} %pad_maximum_fusion.2), channel_id=1, source_target_pairs={{1,3},{3,5},{5,7},{6,4},{4,2},{2,0},{9,11},{11,13},{13,15},{14,12}... | collective-permute-start | bytes 1671176 | tf_op jit(solution)/shard_map/ppermute | solution.py:40
  22.7 1.8 %convolution_multiply_fusion.1 = f32[16,128,128]{2,1,0:T(8,128)S(1)} fusion(bf16[128,16,128]{0,2,1:T(8,128)(2,1)} %copy.63, bf16[128,16,128]{2,1,0:T(8,128)(2,1)} %bitcast.132, f32[16,128]{1,0:T(8,128)S(1)} %copy.55, pred[128,128]{1,0:T(8,128)(4,1)S(1)} %iota_compare_fusion), kind=kOutput, calls=%fused_computation.19 | convolution fusion | flops 68157440 | bytes 2121728 | tf_op jit(solution)/shard_map/thd,shd->hts/dot_general | solution.py:133
  24.9 1.3 %fusion.36 = f32[16,128,128]{2,1,0:T(8,128)} fusion(bf16[128,16,128]{2,1,0:T(8,128)(2,1)S(1)} %bitcast.120, f32[16,128,128]{2,1,0:T(8,128)S(1)} %convolution_multiply_fusion.1), kind=kOutput, calls=%fused_computation.67 | convolution fusion | flops 67371008 | bytes 2621440 | tf_op jit(solution)/shard_map/hts,thd->shd/dot_general | solution.py:52
  26.2 1.5 %fusion.56 = f32[16,128,128]{2,1,0:T(8,128)} fusion(bf16[128,16,128]{0,2,1:T(8,128)(2,1)S(1)} %bitcast.108, f32[16,128,128]{2,1,0:T(8,128)S(1)} %convolution_multiply_fusion.1), kind=kOutput, calls=%fused_computation.108 | convolution fusion | flops 67371008 | bytes 2621440 | tf_op jit(solution)/shard_map/hts,shd->thd/dot_general | solution.py:52
  28.0 1.3 %fusion.6 = f32[16,128,128]{2,1,0:T(8,128)} fusion(f32[16,128,128]{2,1,0:T(8,128)S(1)} %fusion.48, bf16[128,16,128]{0,2,1:T(8,128)(2,1)S(1)} %copy-done.1, f32[16,128,128]{2,1,0:T(8,128)S(1)} %convolution_multiply_fusion), kind=kOutput, calls=%fused_computation.13 | convolution fusion | flops 68681728 | bytes 3670016 | tf_op jit(solution)/shard_map/hts,the->she/dot_general | solution.py:53
  29.3 2.6 %copy.65 = f32[128,2048]{1,0:T(8,128)} copy(f32[128,2048]{0,1:T(8,128)} %bitcast.124) | data formatting | bytes 2097152 | tf_op jit(solution)/shard_map/reshape | solution.py:145
  31.9 2.5 %fusion.7 = f32[16,128,128]{2,1,0:T(8,128)} fusion(f32[16,128,128]{2,1,0:T(8,128)} %fusion.36, bf16[128,16,128]{2,1,0:T(8,128)(2,1)S(1)} %bitcast.121, f32[16,128,128]{2,1,0:T(8,128)S(1)} %convolution_multiply_fusion.1), kind=kOutput, calls=%fused_computation.16 | convolution fusion | flops 68681728 | bytes 3670016 | tf_op jit(solution)/shard_map/hts,thd->shd/dot_general | solution.py:53
  34.4 2.6 %copy.60 = f32[128,2048]{1,0:T(8,128)} copy(f32[128,2048]{0,1:T(8,128)} %bitcast.125) | data formatting | bytes 2097152 | tf_op jit(solution)/shard_map/reshape | solution.py:144
  37.0 2.7 %fusion.8 = f32[16,128,128]{2,1,0:T(8,128)} fusion(f32[16,128,128]{2,1,0:T(8,128)} %fusion.56, bf16[128,16,128]{0,2,1:T(8,128)(2,1)S(1)} %bitcast.109, f32[16,128,128]{2,1,0:T(8,128)S(1)} %convolution_multiply_fusion.1), kind=kOutput, calls=%fused_computation.18 | convolution fusion | flops 68681728 | bytes 3670016 | tf_op jit(solution)/shard_map/hts,shd->thd/dot_general | solution.py:53
  39.7 2.6 %copy.57 = f32[128,2048]{1,0:T(8,128)} copy(f32[128,2048]{0,1:T(8,128)} %bitcast.126) | data formatting | bytes 2097152 | tf_op jit(solution)/shard_map/reshape | solution.py:143
  42.3 1.9 %add_convert_fusion.2 = bf16[128,2048]{1,0:T(8,128)(2,1)S(1)} fusion(f32[128,2048]{1,0:T(8,128)S(1)} %copy-done.6, f32[128,2048]{1,0:T(8,128)} %copy.60, f32[128,2048]{1,0:T(8,128)} %copy.57, bf16[128,2048]{1,0:T(8,128)(2,1)S(1)} %bitcast.130, f32[2048]{0:T(1024)S(1)} %bitcast.141, f32[2048]{0:T(1024)S(1)} %bitcast.142, f32[2048]{0:T(1024)S(1)} %bitcast.140), kind=kLoop, calls=%fused_computation.34 | loop fusion | flops 2097152 | bytes 4218880 | tf_op jit(solution)/shard_map/convert_element_type | solution.py:146
  44.2 5.2 %collective-permute-start.4 = (bf16[128,2048]{1,0:T(8,128)(2,1)S(1)}, bf16[128,2048]{1,0:T(8,128)(2,1)}, u32[]{:S(2)}, u32[]{:S(2)}) collective-permute-start(bf16[128,2048]{1,0:T(8,128)(2,1)S(1)} %add_convert_fusion.2), channel_id=1, source_target_pairs={{0,24},{8,0},{16,8},{24,16},{1,25},{9,1},{17,9},{25,17},{2,26},{10... | collective-permute-start | bytes 1572872 | tf_op jit(solution)/shard_map/ppermute | solution.py:103
  50.6 2.8 %multiply_add_fusion.1 = f32[16,128,128]{2,1,0:T(8,128)} fusion(bf16[16,136,128]{2,1,0:T(8,128)(2,1)} %collective-permute-done.3, bf16[16,136,128]{2,1,0:T(8,128)(2,1)} %collective-permute-done.2, bf16[16,136,128]{2,1,0:T(8,128)(2,1)} %collective-permute-done.1, f32[16]{0:T(128)S(1)} %get-tuple-element.28, f32[16]{0:T(128)S(1)} %get-tuple-element.27), kind=kLoop, calls=%fused_computation.38 | loop fusion | flops 1835008 | bytes 2621568 | tf_op jit(solution)/shard_map/add | solution.py:80
  53.4 3.8 %collective-permute-done.4 = bf16[128,2048]{1,0:T(8,128)(2,1)} collective-permute-done((bf16[128,2048]{1,0:T(8,128)(2,1)S(1)}, bf16[128,2048]{1,0:T(8,128)(2,1)}, u32[]{:S(2)}, u32[]{:S(2)}) %collective-permute-start.4) | collective-permute-done | bytes 524320 | tf_op jit(solution)/shard_map/ppermute | solution.py:103
  57.2 4.6 %collective-permute-start.5 = (f32[16,128,128]{2,1,0:T(8,128)}, f32[16,128,128]{2,1,0:T(8,128)S(1)}, u32[]{:S(2)}, u32[]{:S(2)}) collective-permute-start(f32[16,128,128]{2,1,0:T(8,128)} %multiply_add_fusion.1), channel_id=1, source_target_pairs={{0,1},{2,3},{4,5},{6,7},{1,0},{3,2},{5,4},{7,6},{8,9},{10,11},{12,... | collective-permute-start | bytes 3145736 | tf_op jit(solution)/shard_map/ppermute | solution.py:95
  61.9 2.4 %collective-permute-done.5 = f32[16,128,128]{2,1,0:T(8,128)S(1)} collective-permute-done((f32[16,128,128]{2,1,0:T(8,128)}, f32[16,128,128]{2,1,0:T(8,128)S(1)}, u32[]{:S(2)}, u32[]{:S(2)}) %collective-permute-start.5) | collective-permute-done | bytes 1048608 | tf_op jit(solution)/shard_map/ppermute | solution.py:95
  64.3 2.9 %subtract_convert_fusion = (bf16[16,128,128]{2,1,0:T(8,128)(2,1)S(1)}, bf16[16,128,128]{2,1,0:T(8,128)(2,1)S(1)}, f32[16,128,128]{2,1,0:T(8,128)}) fusion(f32[16,128,128]{2,1,0:T(8,128)S(1)} %collective-permute-done.5, pred[]{:T(512)S(6)} %eq.29, f32[16,136,128]{2,1,0:T(8,128)} %collective-permute-done, f32[16,128,128]{2,1,0:T(8,128)} %multiply_add_fusion.1, ...), kind=kLoop, calls=%fused_computation.31 | loop fusion | flops 1835008 | bytes 5242945 | tf_op jit(solution)/shard_map/convert_element_type | solution.py:51
  67.6 1.5 %fusion.21 = f32[16,128,128]{1,2,0:T(8,128)} fusion(bf16[16,128,128]{2,1,0:T(8,128)(2,1)S(1)} %get-tuple-element.29, bf16[128,2048]{1,0:T(8,128)(2,1)S(1)} %get-tuple-element.32), kind=kOutput, calls=%fused_computation.51 | convolution fusion | flops 67108864 | bytes 2097152 | tf_op jit(solution)/shard_map/hde,she->shd/dot_general | solution.py:53
  69.1 1.4 %fusion.1 = f32[128,16,128]{0,2,1:T(8,128)} fusion(f32[16,128,128]{1,2,0:T(8,128)S(1)} %fusion.63, bf16[128,16,128]{0,2,1:T(8,128)(2,1)S(1)} %bitcast.111, bf16[16,128,128]{2,1,0:T(8,128)(2,1)S(1)} %get-tuple-element.30, f32[128,16]{0,1:T(8,128)S(1)} %copy.47), kind=kOutput, calls=%fused_computation.5 | convolution fusion | flops 67633152 | bytes 3153920 | tf_op jit(solution)/shard_map/hde,shd->she/dot_general | solution.py:52
  70.5 2.5 %copy.77 = f32[128,2048]{1,0:T(8,128)} copy(f32[128,2048]{0,1:T(8,128)} %bitcast.127) | data formatting | bytes 2097152 | tf_op jit(solution)/shard_map/reshape | solution.py:181
  73.0 2.7 %fusion.3 = f32[128,16,128]{0,2,1:T(8,128)} fusion(f32[16,128,128]{1,2,0:T(8,128)} %fusion.21, bf16[16,128,128]{2,1,0:T(8,128)(2,1)S(1)} %get-tuple-element.30, f32[128,16]{0,1:T(8,128)S(1)} %copy.47, bf16[128,2048]{1,0:T(8,128)(2,1)S(1)} %get-tuple-element.32), kind=kOutput, calls=%fused_computation.8 | convolution fusion | flops 67633152 | bytes 3153920 | tf_op jit(solution)/shard_map/hde,she->shd/dot_general | solution.py:52
  75.7 2.7 %copy.72 = f32[128,2048]{1,0:T(8,128)} copy(f32[128,2048]{0,1:T(8,128)} %bitcast.123) | data formatting | bytes 2097152 | tf_op jit(solution)/shard_map/reshape | solution.py:180
  78.8 1.5 %fusion.5 = f32[128,16,128]{0,2,1:T(8,128)} fusion(f32[16,128,128]{2,1,0:T(8,128)S(1)} %fusion.19, f32[128,16]{0,1:T(8,128)S(1)} %copy.66, f32[16,128,128]{2,1,0:T(8,128)S(1)} %copy-done, f32[16,128,128]{2,1,0:T(8,128)S(1)} %collective-permute-done.5, pred[]{:T(512)S(6)} %eq.29, bf16[128,16,128]{2,1,0:T(8,128)(2,1)S(1)} %bitcast.116), kind=kOutput, calls=%fused_computation.11 | convolution fusion | flops 67895296 | bytes 4726785 | tf_op jit(solution)/shard_map/hde,the->thd/dot_general | solution.py:52
  80.3 2.7 %copy.69 = f32[128,2048]{1,0:T(8,128)} copy(f32[128,2048]{0,1:T(8,128)} %bitcast.122) | data formatting | bytes 2097152 | tf_op jit(solution)/shard_map/reshape | solution.py:179
  83.0 1.5 %add_convert_fusion.1 = bf16[128,2048]{1,0:T(8,128)(2,1)S(1)} fusion(f32[128,2048]{1,0:T(8,128)S(1)} %copy-done.3, f32[128,2048]{1,0:T(8,128)S(1)} %copy-done.4, f32[128,2048]{1,0:T(8,128)} %copy.69, f32[2048]{0:T(1024)S(1)} %bitcast.135, f32[2048]{0:T(1024)S(1)} %bitcast.137, f32[2048]{0:T(1024)S(1)} %bitcast.139), kind=kLoop, calls=%fused_computation.30 | loop fusion | flops 1572864 | bytes 3694592 | tf_op jit(solution)/shard_map/convert_element_type | solution.py:182
  84.5 4.2 %collective-permute-start.6 = (bf16[128,2048]{1,0:T(8,128)(2,1)S(1)}, bf16[128,2048]{1,0:T(8,128)(2,1)S(1)}, u32[]{:S(2)}, u32[]{:S(2)}) collective-permute-start(bf16[128,2048]{1,0:T(8,128)(2,1)S(1)} %add_convert_fusion.1), channel_id=1, source_target_pairs={{0,24},{8,0},{16,8},{24,16},{1,25},{9,1},{17,9},{25,17},{2,26},{10... | collective-permute-start | bytes 1572872 | tf_op jit(solution)/shard_map/ppermute | solution.py:103
  88.7 11.7 %collective-permute-done.6 = bf16[128,2048]{1,0:T(8,128)(2,1)S(1)} collective-permute-done((bf16[128,2048]{1,0:T(8,128)(2,1)S(1)}, bf16[128,2048]{1,0:T(8,128)(2,1)S(1)}, u32[]{:S(2)}, u32[]{:S(2)}) %collective-permute-start.6) | collective-permute-done | bytes 524320 | tf_op jit(solution)/shard_map/ppermute | solution.py:103
  100.4 2.0 %fusion.20 = bf16[1,128,2048]{2,1,0:T(8,128)(2,1)} fusion(bf16[128,2048]{1,0:T(8,128)(2,1)S(1)} %collective-permute-done.6, bf16[128,2048]{1,0:T(8,128)(2,1)} %collective-permute-done.4), kind=kLoop, calls=%fused_computation.50 | loop fusion | flops 1048576 | bytes 1572864 | tf_op jit(solution)/shard_map/broadcast_in_dim | solution.py:186
  (80 shorter events, 18.5 us)
Async XLA Ops:
  0.0 4.0 %copy-start.8 = (bf16[1,128,2048]{2,1,0:T(8,128)(2,1)S(1)}, bf16[1,128,2048]{2,1,0:T(8,128)(2,1)}, u32[]{:S(2)}) copy-start(bf16[1,128,2048]{2,1,0:T(8,128)(2,1)} %param.5) | copy-start | bytes 1572868
  6.3 1.0 %copy-start.2 = (bf16[128,16,128]{0,2,1:T(8,128)(2,1)S(1)}, bf16[128,16,128]{0,2,1:T(8,128)(2,1)}, u32[]{:S(2)}) copy-start(bf16[128,16,128]{0,2,1:T(8,128)(2,1)} %copy.42) | copy-start | bytes 1572868
  9.1 1.6 %copy-start.9 = (f32[1,3,2048]{2,0,1:T(1,128)S(1)}, f32[1,3,2048]{2,0,1:T(1,128)}, u32[]{:S(2)}) copy-start(f32[1,3,2048]{2,0,1:T(1,128)} %param.7) | copy-start | bytes 73732
  10.2 3.2 %collective-permute-start = (f32[16,136,128]{2,1,0:T(8,128)}, f32[16,136,128]{2,1,0:T(8,128)}, u32[]{:S(2)}, u32[]{:S(2)}) collective-permute-start(f32[16,136,128]{2,1,0:T(8,128)} %pad_maximum_fusion), channel_id=1, source_target_pairs={{0,1},{2,3},{4,5},{6,7},{1,0},{3,2},{5,4},{7,6},{8,9},{10,11},{12,... | collective-permute-start | bytes 3342344 | tf_op jit(solution)/shard_map/ppermute | solution.py:70
  10.9 2.5 %copy-start.5 = (f32[16,128,128]{2,1,0:T(8,128)S(1)}, f32[16,128,128]{2,1,0:T(8,128)}, u32[]{:S(2)}) copy-start(f32[16,128,128]{2,1,0:T(8,128)} %get-tuple-element.47) | copy-start | bytes 3145732
  17.6 33.1 %collective-permute-start.3 = (bf16[16,136,128]{2,1,0:T(8,128)(2,1)}, bf16[16,136,128]{2,1,0:T(8,128)(2,1)}, u32[]{:S(2)}, u32[]{:S(2)}) collective-permute-start(bf16[16,136,128]{2,1,0:T(8,128)(2,1)} %pad_maximum_fusion.2), channel_id=1, source_target_pairs={{1,7},{6,0},{9,15},{14,8},{17,23},{22,16},{25,31},{30,24}} | collective-permute-start | bytes 1671176 | tf_op jit(solution)/shard_map/ppermute | solution.py:40
  18.8 30.6 %collective-permute-start.2 = (bf16[16,136,128]{2,1,0:T(8,128)(2,1)}, bf16[16,136,128]{2,1,0:T(8,128)(2,1)}, u32[]{:S(2)}, u32[]{:S(2)}) collective-permute-start(bf16[16,136,128]{2,1,0:T(8,128)(2,1)} %pad_maximum_fusion.2), channel_id=1, source_target_pairs={{1,5},{3,7},{6,2},{4,0},{9,13},{11,15},{14,10},{12,8},{17,21},{19,... | collective-permute-start | bytes 1671176 | tf_op jit(solution)/shard_map/ppermute | solution.py:40
  20.1 29.3 %collective-permute-start.1 = (bf16[16,136,128]{2,1,0:T(8,128)(2,1)}, bf16[16,136,128]{2,1,0:T(8,128)(2,1)}, u32[]{:S(2)}, u32[]{:S(2)}) collective-permute-start(bf16[16,136,128]{2,1,0:T(8,128)(2,1)} %pad_maximum_fusion.2), channel_id=1, source_target_pairs={{1,3},{3,5},{5,7},{6,4},{4,2},{2,0},{9,11},{11,13},{13,15},{14,12}... | collective-permute-start | bytes 1671176 | tf_op jit(solution)/shard_map/ppermute | solution.py:40
  26.2 1.5 %copy-start.1 = (bf16[128,16,128]{0,2,1:T(8,128)(2,1)S(1)}, bf16[128,16,128]{0,2,1:T(8,128)(2,1)}, u32[]{:S(2)}) copy-start(bf16[128,16,128]{0,2,1:T(8,128)(2,1)} %copy.63) | copy-start | bytes 1572868
  39.7 2.7 %copy-start.6 = (f32[128,2048]{1,0:T(8,128)S(1)}, f32[128,2048]{1,0:T(8,128)}, u32[]{:S(2)}) copy-start(f32[128,2048]{1,0:T(8,128)} %copy.65) | copy-start | bytes 3145732
  39.7 2.7 %copy-start.7 = (bf16[1,128,2048]{2,1,0:T(8,128)(2,1)S(1)}, bf16[1,128,2048]{2,1,0:T(8,128)(2,1)}, u32[]{:S(2)}) copy-start(bf16[1,128,2048]{2,1,0:T(8,128)(2,1)} %param.6) | copy-start | bytes 1572868
  44.2 13.0 %collective-permute-start.4 = (bf16[128,2048]{1,0:T(8,128)(2,1)S(1)}, bf16[128,2048]{1,0:T(8,128)(2,1)}, u32[]{:S(2)}, u32[]{:S(2)}) collective-permute-start(bf16[128,2048]{1,0:T(8,128)(2,1)S(1)} %add_convert_fusion.2), channel_id=1, source_target_pairs={{0,24},{8,0},{16,8},{24,16},{1,25},{9,1},{17,9},{25,17},{2,26},{10... | collective-permute-start | bytes 1572872 | tf_op jit(solution)/shard_map/ppermute | solution.py:103
  57.2 7.1 %collective-permute-start.5 = (f32[16,128,128]{2,1,0:T(8,128)}, f32[16,128,128]{2,1,0:T(8,128)S(1)}, u32[]{:S(2)}, u32[]{:S(2)}) collective-permute-start(f32[16,128,128]{2,1,0:T(8,128)} %multiply_add_fusion.1), channel_id=1, source_target_pairs={{0,1},{2,3},{4,5},{6,7},{1,0},{3,2},{5,4},{7,6},{8,9},{10,11},{12,... | collective-permute-start | bytes 3145736 | tf_op jit(solution)/shard_map/ppermute | solution.py:95
  75.7 2.7 %copy-start = (f32[16,128,128]{2,1,0:T(8,128)S(1)}, f32[16,128,128]{2,1,0:T(8,128)}, u32[]{:S(2)}) copy-start(f32[16,128,128]{2,1,0:T(8,128)} %get-tuple-element.31) | copy-start | bytes 3145732
  80.3 2.7 %copy-start.3 = (f32[128,2048]{1,0:T(8,128)S(1)}, f32[128,2048]{1,0:T(8,128)}, u32[]{:S(2)}) copy-start(f32[128,2048]{1,0:T(8,128)} %copy.77) | copy-start | bytes 3145732
  80.3 2.7 %copy-start.4 = (f32[128,2048]{1,0:T(8,128)S(1)}, f32[128,2048]{1,0:T(8,128)}, u32[]{:S(2)}) copy-start(f32[128,2048]{1,0:T(8,128)} %copy.72) | copy-start | bytes 3145732
  84.5 15.9 %collective-permute-start.6 = (bf16[128,2048]{1,0:T(8,128)(2,1)S(1)}, bf16[128,2048]{1,0:T(8,128)(2,1)S(1)}, u32[]{:S(2)}, u32[]{:S(2)}) collective-permute-start(bf16[128,2048]{1,0:T(8,128)(2,1)S(1)} %add_convert_fusion.1), channel_id=1, source_target_pairs={{0,24},{8,0},{16,8},{24,16},{1,25},{9,1},{17,9},{25,17},{2,26},{10... | collective-permute-start | bytes 1572872 | tf_op jit(solution)/shard_map/ppermute | solution.py:103

commit v7 on v6

--- a/solution.py
+++ b/solution.py
@@ -44,13 +44,6 @@
     far_state, far_rate = unpacked(farther)
     near_state, near_rate = unpacked(nearer)
     return packed(near_rate[:, None, None] * far_state + near_state, far_rate * near_rate)
-
-
-def split_dot(spec, wide, exact):
-    high = wide.astype(jnp.bfloat16)
-    low = (wide - high.astype(jnp.float32)).astype(jnp.bfloat16)
-    first = jnp.einsum(spec, high, exact, preferred_element_type=jnp.float32)
-    return first + jnp.einsum(spec, low, exact, preferred_element_type=jnp.float32)
 
 
 def both_ways(count, moves):
@@ -133,12 +126,12 @@
         jnp.einsum("thd,shd->hts", grad_half, value_half, preferred_element_type=jnp.float32)
         * decay
     )
-    query_near = scale * split_dot("hts,shd->thd", mixing, key_half)
-    key_near = scale * split_dot("hts,thd->shd", mixing, query_half)
+    query_near = scale * jnp.einsum("hts,shd->thd", mixing, key_half.astype(jnp.float32), precision=HIGH)
+    key_near = scale * jnp.einsum("hts,thd->shd", mixing, query_half.astype(jnp.float32), precision=HIGH)
     attention = (
         jnp.einsum("thd,shd->hts", query_half, key_half, preferred_element_type=jnp.float32) * decay
     )
-    value_near = scale * split_dot("hts,the->she", attention, grad_half)
+    value_near = scale * jnp.einsum("hts,the->she", attention, grad_half.astype(jnp.float32), precision=HIGH)
     near_total = grad_block.astype(jnp.float32)
     near_total = near_total + gain[0] * query_near.reshape(rows, width)
     near_total = near_total + gain[1] * key_near.reshape(rows, width)
@@ -160,9 +153,15 @@
     cumul = jnp.cumsum(logs, axis=0)
     growth = jnp.exp(cumul)
     tail = jnp.exp(cumul[-1][None, :] - cumul)
-    forward_part = split_dot("shd,she->hde", key_half.astype(jnp.float32) * tail[:, :, None], value_half)
-    adjoint_part = scale * split_dot(
-        "shd,she->hde", query_half.astype(jnp.float32) * growth[:, :, None], grad_half
+    queries = query_half.astype(jnp.float32)
+    key_rows = key_half.astype(jnp.float32)
+    value_rows = value_half.astype(jnp.float32)
+    grad_rows = grad_half.astype(jnp.float32)
+    forward_part = jnp.einsum(
+        "shd,she->hde", key_rows * tail[:, :, None], value_rows, precision=HIGH
+    )
+    adjoint_part = scale * jnp.einsum(
+        "shd,she->hde", queries * growth[:, :, None], grad_rows, precision=HIGH
     )
     whole_decay = jnp.exp(cumul[-1])
     state_in, adjoint_in, near_received = scans_in(
@@ -173,9 +172,11 @@
         near_terms,
         (query_half, key_half, value_half, grad_half, cumul, grad_block, gain),
     )
-    query_far = scale * growth[:, :, None] * split_dot("hde,the->thd", state_in, grad_half)
-    key_far = tail[:, :, None] * split_dot("hde,she->shd", adjoint_in, value_half)
-    value_far = tail[:, :, None] * split_dot("hde,shd->she", adjoint_in, key_half)
+    query_far = (
+        scale * growth[:, :, None] * jnp.einsum("the,hde->thd", grad_rows, state_in, precision=HIGH)
+    )
+    key_far = tail[:, :, None] * jnp.einsum("she,hde->shd", value_rows, adjoint_in, precision=HIGH)
+    value_far = tail[:, :, None] * jnp.einsum("shd,hde->she", key_rows, adjoint_in, precision=HIGH)
     far_total = gain[0] * query_far.reshape(rows, width)
     far_total = far_total + gain[1] * key_far.reshape(rows, width)
     far_total = far_total + gain[2] * value_far.reshape(rows, width)

time: 104 us -> 86.9 us (0.84)
  matrix products: 21.9 us -> 13.4 us
  local copies, waits for them, and re-layouts: 23.6 us -> 19.2 us
  other arithmetic: 18.8 us -> 16.4 us
  waiting for transfers between devices: 19.5 us -> 17.8 us
    dot_general x16 -> x8, matrix products: 19.7 us -> 12.5 us  [the longest x1 2.25 us: local(): jnp.einsum('the,hde->thd', grad_rows, state_in, precision=HIGH)]
    convert_element_type x1 -> x0, other arithmetic: 2.9 us -> none  [split_dot(): low = (wide - high.astype(jnp.float32)).astype(jnp.bfloat16)]
    ppermute x1, waiting for transfers between devices: 2.45 us -> 0.71 us  [scans_in(): other = lax.ppermute(incoming, axis, swap)]
    add x0 -> x1, other arithmetic: none -> 1.73 us  [scans_in(): own = lower_rate[:, None, None] * incoming + lower]
    reshape x1, local copies, waits for them, and re-layouts: 2.64 us -> 1.33 us  [near_terms(): near_total = near_total + gain[0] * query_near.reshape(rows, width)]
    reshape x1, local copies, waits for them, and re-layouts: 2.56 us -> 1.31 us  [near_terms(): near_total = near_total + gain[1] * key_near.reshape(rows, width)]
    convert_element_type x1, other arithmetic: 1.49 us -> 0.27 us  [local(): far_received = passed_along(far_total.astype(jnp.bfloat16), 'section', -1)]
    dot_general x1, matrix products: 1.78 us -> 0.59 us  [near_terms(): jnp.einsum('thd,shd->hts', grad_half, value_half, preferred_element_type=...]
  transfers between devices with their start and end apart: 7 -> 7, of which waited for: 4 -> 4; matrix products, arithmetic and copies ran while one was open for 27% -> 22% of each run, Pallas kernels for 0% -> 0%
where the time goes in v7:
time: 86.9 us; the launch traced here: 85.6 us
  local copies, waits for them, and re-layouts  19.2 us (22%)
  starting transfers between devices  18.4 us (21%)
  waiting for transfers between devices  17.8 us (20%)
  other arithmetic  16.4 us (19%)
  matrix products  13.4 us (15%)
    ppermute x2, waiting for transfers between devices, passed_along(): return lax.ppermute(value, axis, pairs)  15.6 us
    ppermute x2, starting transfers between devices, passed_along(): return lax.ppermute(value, axis, pairs)  9.36 us
    ppermute x1, starting transfers between devices, scans_in(): other = lax.ppermute(incoming, axis, swap)  4.69 us
    ppermute x3, starting transfers between devices, sent_narrow(): return widen(lax.ppermute(narrow(message), axis, pairs))  3.86 us
    unnamed x28, local copies, waits for them, and re-layouts  2.93 us
    add x1, other arithmetic, scans_in(): incoming = incoming + weight[:, None, None] * got  2.77 us
    reshape x1, local copies, waits for them, and re-layouts, local(): far_total = far_total + gain[1] * key_far.reshape(rows, width)  2.58 us
    reshape x1, local copies, waits for them, and re-layouts, local(): far_total = gain[0] * query_far.reshape(rows, width)  2.58 us
  transfers between devices with their start and end apart: 7, of which 4 were waited for; matrix products, arithmetic and copies ran while one was open for 22% of the time, Pallas kernels for 0%

profile of v7, /device:TPU:0, one launch (start us, length us, event | category | flops | bytes accessed | tf_op | source)
XLA Modules:
  0.0 85.6 jit_solution(2841517066684113759)
XLA Ops:
  2.9 1.2 %copy.64 = bf16[16,8,16,128]{3,2,1,0:T(8,128)(2,1)S(1)} copy(bf16[16,8,16,128]{3,1,2,0:T(8,128)(2,1)} %bitcast.109) | data formatting | bytes 1048576
  4.7 1.2 %copy.32 = bf16[128,16,128]{0,2,1:T(8,128)(2,1)} copy(bf16[128,16,128]{2,1,0:T(8,128)(2,1)S(1)} %bitcast.99) | data formatting | bytes 1048576 | tf_op jit(solution)/shard_map/reshape | solution.py:113
  7.0 1.7 %broadcast_select_fusion.1 = (f32[16,128,128]{2,1,0:T(8,128)S(1)}, f32[16,128,128]{2,1,0:T(8,128)}) fusion(f32[16,128,128]{2,1,0:T(8,128)S(1)} %fusion.7, pred[]{:T(512)S(6)} %eq.29, bf16[128,16,128]{2,1,0:T(8,128)(2,1)S(1)} %bitcast.95, bf16[128,16,128]{0,2,1:T(8,128)(2,1)S(1)} %copy-done.8, f32[128,16]{0,1:T(8,128)S(1)} %copy.33), kind=kOutput, calls=%fused_computation.43 | convolution fusion | flops 403701760 | bytes 4202497 | tf_op jit(solution)/shard_map/shd,she->hde/dot_general | solution.py:163
  8.8 1.1 %pad_maximum_fusion = f32[16,136,128]{2,1,0:T(8,128)} fusion(f32[16,8,128]{2,1,0:T(8,128)S(1)} %broadcast_in_dim.36, f32[16,128,128]{2,1,0:T(8,128)S(1)} %get-tuple-element.43), kind=kLoop, calls=%fused_computation.15 | loop fusion | flops 278528 | bytes 2228224 | tf_op jit(solution)/shard_map/concatenate | solution.py:16
  10.7 0.9 %copy.65 = bf16[16,8,16,128]{3,2,1,0:T(8,128)(2,1)} copy(bf16[16,8,16,128]{3,1,2,0:T(8,128)(2,1)S(1)} %bitcast.98) | data formatting | bytes 1048576
  11.6 1.5 %collective-permute-done = f32[16,136,128]{2,1,0:T(8,128)} collective-permute-done((f32[16,136,128]{2,1,0:T(8,128)}, f32[16,136,128]{2,1,0:T(8,128)}, u32[]{:S(2)}, u32[]{:S(2)}) %collective-permute-start) | collective-permute-done | bytes 1114144 | tf_op jit(solution)/shard_map/ppermute | solution.py:63
  13.1 1.4 %select_add_fusion = f32[16,128,128]{2,1,0:T(8,128)S(1)} fusion(f32[16,128,128]{2,1,0:T(8,128)S(1)} %fusion.7, f32[16,128,128]{2,1,0:T(8,128)S(1)} %copy-done.2, f32[16,136,128]{2,1,0:T(8,128)} %collective-permute-done, f32[16]{0:T(128)S(1)} %fusion.30, pred[]{:T(512)S(6)} %eq.29), kind=kLoop, calls=%fused_computation.28 | loop fusion | flops 786432 | bytes 4194369 | tf_op jit(solution)/shard_map/add | solution.py:64
  14.6 1.0 %slice_reduce_fusion.1 = (f32[16]{0:T(128)S(1)}, f32[16]{0:T(128)S(1)}) fusion(f32[16,136,128]{2,1,0:T(8,128)} %collective-permute-done, f32[16,1,1]{2,1,0:T(1,128)S(1)} %copy.38), kind=kLoop, calls=%fused_computation.65 | loop fusion | flops 16 | bytes 256 | tf_op jit(solution)/shard_map/slice | solution.py:21
  17.3 1.3 %collective-permute-start.3 = (bf16[16,136,128]{2,1,0:T(8,128)(2,1)}, bf16[16,136,128]{2,1,0:T(8,128)(2,1)}, u32[]{:S(2)}, u32[]{:S(2)}) collective-permute-start(bf16[16,136,128]{2,1,0:T(8,128)(2,1)} %pad_maximum_fusion.2), channel_id=1, source_target_pairs={{1,7},{6,0},{9,15},{14,8},{17,23},{22,16},{25,31},{30,24}} | collective-permute-start | bytes 1671176 | tf_op jit(solution)/shard_map/ppermute | solution.py:40
  18.6 1.3 %collective-permute-start.2 = (bf16[16,136,128]{2,1,0:T(8,128)(2,1)}, bf16[16,136,128]{2,1,0:T(8,128)(2,1)}, u32[]{:S(2)}, u32[]{:S(2)}) collective-permute-start(bf16[16,136,128]{2,1,0:T(8,128)(2,1)} %pad_maximum_fusion.2), channel_id=1, source_target_pairs={{1,5},{3,7},{6,2},{4,0},{9,13},{11,15},{14,10},{12,8},{17,21},{19,... | collective-permute-start | bytes 1671176 | tf_op jit(solution)/shard_map/ppermute | solution.py:40
  19.9 1.3 %collective-permute-start.1 = (bf16[16,136,128]{2,1,0:T(8,128)(2,1)}, bf16[16,136,128]{2,1,0:T(8,128)(2,1)}, u32[]{:S(2)}, u32[]{:S(2)}) collective-permute-start(bf16[16,136,128]{2,1,0:T(8,128)(2,1)} %pad_maximum_fusion.2), channel_id=1, source_target_pairs={{1,3},{3,5},{5,7},{6,4},{4,2},{2,0},{9,11},{11,13},{13,15},{14,12}... | collective-permute-start | bytes 1671176 | tf_op jit(solution)/shard_map/ppermute | solution.py:40
  23.8 1.2 %convolution_multiply_fusion.3 = f32[16,128,128]{2,1,0:T(8,128)S(1)} fusion(bf16[128,16,128]{0,2,1:T(8,128)(2,1)S(1)} %bitcast.93, f32[16,128,128]{2,1,0:T(8,128)S(1)} %convolution_multiply_fusion.4), kind=kOutput, calls=%fused_computation.6 | convolution fusion | flops 402915328 | bytes 2621440 | tf_op jit(solution)/shard_map/hts,shd->thd/dot_general | solution.py:129
  25.0 1.6 %convolution_multiply_fusion = f32[16,128,128]{2,1,0:T(8,128)} fusion(bf16[128,16,128]{0,2,1:T(8,128)(2,1)S(1)} %copy-done.7, f32[16,128,128]{2,1,0:T(8,128)S(1)} %convolution_multiply_fusion.1), kind=kOutput, calls=%fused_computation.3 | convolution fusion | flops 402915328 | bytes 2621440 | tf_op jit(solution)/shard_map/hts,the->she/dot_general | solution.py:134
  26.7 2.6 %copy.49 = f32[128,2048]{1,0:T(8,128)} copy(f32[128,2048]{0,1:T(8,128)} %bitcast.104) | data formatting | bytes 2097152 | tf_op jit(solution)/shard_map/reshape | solution.py:138
  29.2 1.3 %copy.45 = f32[128,2048]{1,0:T(8,128)} copy(f32[128,2048]{0,1:T(8,128)S(1)} %bitcast.103) | data formatting | bytes 2097152 | tf_op jit(solution)/shard_map/reshape | solution.py:136
  30.6 1.3 %copy.47 = f32[128,2048]{1,0:T(8,128)} copy(f32[128,2048]{0,1:T(8,128)S(1)} %bitcast.102) | data formatting | bytes 2097152 | tf_op jit(solution)/shard_map/reshape | solution.py:137
  31.9 2.0 %add_convert_fusion.2 = bf16[128,2048]{1,0:T(8,128)(2,1)S(1)} fusion(f32[128,2048]{1,0:T(8,128)S(1)} %copy-done.5, f32[128,2048]{1,0:T(8,128)} %copy.47, f32[128,2048]{1,0:T(8,128)} %copy.45, bf16[128,2048]{1,0:T(8,128)(2,1)} %bitcast.110, f32[2048]{0:T(1024)S(1)} %bitcast.121, f32[2048]{0:T(1024)S(1)} %bitcast.122, f32[2048]{0:T(1024)S(1)} %bitcast.120), kind=kLoop, calls=%fused_computation.25 | loop fusion | flops 2097152 | bytes 4218880 | tf_op jit(solution)/shard_map/convert_element_type | solution.py:139
  33.9 5.2 %collective-permute-start.4 = (bf16[128,2048]{1,0:T(8,128)(2,1)S(1)}, bf16[128,2048]{1,0:T(8,128)(2,1)}, u32[]{:S(2)}, u32[]{:S(2)}) collective-permute-start(bf16[128,2048]{1,0:T(8,128)(2,1)S(1)} %add_convert_fusion.2), channel_id=1, source_target_pairs={{0,24},{8,0},{16,8},{24,16},{1,25},{9,1},{17,9},{25,17},{2,26},{10... | collective-permute-start | bytes 1572872 | tf_op jit(solution)/shard_map/ppermute | solution.py:96
  39.1 1.1 %fusion.31 = (f32[16]{0:T(128)S(1)}, f32[16]{0:T(128)S(1)}) fusion(bf16[16,136,128]{2,1,0:T(8,128)(2,1)} %collective-permute-done.2, bf16[16,136,128]{2,1,0:T(8,128)(2,1)} %collective-permute-done.1), kind=kLoop, calls=%fused_computation.77 | loop fusion | flops 112 | bytes 256 | tf_op jit(solution)/shard_map/add | solution.py:35
  40.2 2.8 %multiply_add_fusion.1 = f32[16,128,128]{2,1,0:T(8,128)} fusion(bf16[16,136,128]{2,1,0:T(8,128)(2,1)} %collective-permute-done.3, bf16[16,136,128]{2,1,0:T(8,128)(2,1)} %collective-permute-done.2, bf16[16,136,128]{2,1,0:T(8,128)(2,1)} %collective-permute-done.1, f32[16]{0:T(128)S(1)} %get-tuple-element.28, f32[16]{0:T(128)S(1)} %get-tuple-element.27), kind=kLoop, calls=%fused_computation.27 | loop fusion | flops 1835008 | bytes 2621568 | tf_op jit(solution)/shard_map/add | solution.py:73
  42.9 3.9 %collective-permute-done.4 = bf16[128,2048]{1,0:T(8,128)(2,1)} collective-permute-done((bf16[128,2048]{1,0:T(8,128)(2,1)S(1)}, bf16[128,2048]{1,0:T(8,128)(2,1)}, u32[]{:S(2)}, u32[]{:S(2)}) %collective-permute-start.4) | collective-permute-done | bytes 524320 | tf_op jit(solution)/shard_map/ppermute | solution.py:96
  46.8 4.7 %collective-permute-start.5 = (f32[16,128,128]{2,1,0:T(8,128)}, f32[16,128,128]{2,1,0:T(8,128)S(1)}, u32[]{:S(2)}, u32[]{:S(2)}) collective-permute-start(f32[16,128,128]{2,1,0:T(8,128)} %multiply_add_fusion.1), channel_id=1, source_target_pairs={{0,1},{2,3},{4,5},{6,7},{1,0},{3,2},{5,4},{7,6},{8,9},{10,11},{12,... | collective-permute-start | bytes 3145736 | tf_op jit(solution)/shard_map/ppermute | solution.py:88
  51.6 1.7 %multiply_add_fusion = f32[16,128,128]{2,1,0:T(8,128)S(1)} fusion(f32[16,128,128]{2,1,0:T(8,128)} %multiply_add_fusion.1, f32[16,136,128]{2,1,0:T(8,128)} %collective-permute-done, f32[16]{0:T(128)S(1)} %get-tuple-element.25), kind=kLoop, calls=%fused_computation.24 | loop fusion | flops 524288 | bytes 3145792 | tf_op jit(solution)/shard_map/add | solution.py:89
  54.0 2.3 %fusion.2 = f32[128,16,128]{0,2,1:T(8,128)} fusion(f32[16,128,128]{2,1,0:T(8,128)S(1)} %multiply_add_fusion, f32[16,128,128]{2,1,0:T(8,128)S(1)} %collective-permute-done.5, f32[128,16]{0,1:T(8,128)S(1)} %copy.50, pred[]{:T(512)S(6)} %eq.29, bf16[128,16,128]{2,1,0:T(8,128)(2,1)S(1)} %bitcast.97), kind=kOutput, calls=%fused_computation.14 | convolution fusion | flops 403177472 | bytes 3678209 | tf_op jit(solution)/shard_map/the,hde->thd/dot_general | solution.py:176
  56.3 2.6 %copy.52 = f32[128,2048]{1,0:T(8,128)} copy(f32[128,2048]{0,1:T(8,128)} %bitcast.106) | data formatting | bytes 2097152 | tf_op jit(solution)/shard_map/reshape | solution.py:180
  58.8 2.2 %fusion.1 = f32[128,16,128]{0,2,1:T(8,128)} fusion(f32[128,16]{0,1:T(8,128)S(1)} %copy.36, f32[16,128,128]{2,1,0:T(8,128)S(1)} %collective-permute-done.5, f32[16,128,128]{2,1,0:T(8,128)S(1)} %multiply_add_fusion, pred[]{:T(512)S(6)} %eq.29, bf16[128,2048]{1,0:T(8,128)(2,1)S(1)} %copy-done.1), kind=kOutput, calls=%fused_computation.12 | convolution fusion | flops 403177472 | bytes 3678209 | tf_op jit(solution)/shard_map/she,hde->shd/dot_general | solution.py:178
  61.0 2.6 %copy.54 = f32[128,2048]{1,0:T(8,128)} copy(f32[128,2048]{0,1:T(8,128)} %bitcast.107) | data formatting | bytes 2097152 | tf_op jit(solution)/shard_map/reshape | solution.py:181
  63.6 2.0 %fusion = f32[128,16,128]{0,2,1:T(8,128)} fusion(bf16[128,16,128]{0,2,1:T(8,128)(2,1)S(1)} %bitcast.94, f32[128,16]{0,1:T(8,128)S(1)} %copy.36, f32[16,128,128]{2,1,0:T(8,128)S(1)} %collective-permute-done.5, f32[16,128,128]{2,1,0:T(8,128)S(1)} %multiply_add_fusion, pred[]{:T(512)S(6)} %eq.29), kind=kOutput, calls=%fused_computation.10 | convolution fusion | flops 403177472 | bytes 3678209 | tf_op jit(solution)/shard_map/shd,hde->she/dot_general | solution.py:179
  65.6 1.7 %copy.57 = f32[128,2048]{1,0:T(8,128)S(1)} copy(f32[128,2048]{0,1:T(8,128)} %bitcast.105) | data formatting | bytes 2097152 | tf_op jit(solution)/shard_map/reshape | solution.py:182
  67.7 4.2 %collective-permute-start.6 = (bf16[128,2048]{1,0:T(8,128)(2,1)S(1)}, bf16[128,2048]{1,0:T(8,128)(2,1)S(1)}, u32[]{:S(2)}, u32[]{:S(2)}) collective-permute-start(bf16[128,2048]{1,0:T(8,128)(2,1)S(1)} %add_convert_fusion.1), channel_id=1, source_target_pairs={{0,24},{8,0},{16,8},{24,16},{1,25},{9,1},{17,9},{25,17},{2,26},{10... | collective-permute-start | bytes 1572872 | tf_op jit(solution)/shard_map/ppermute | solution.py:96
  71.9 11.7 %collective-permute-done.6 = bf16[128,2048]{1,0:T(8,128)(2,1)S(1)} collective-permute-done((bf16[128,2048]{1,0:T(8,128)(2,1)S(1)}, bf16[128,2048]{1,0:T(8,128)(2,1)S(1)}, u32[]{:S(2)}, u32[]{:S(2)}) %collective-permute-start.6) | collective-permute-done | bytes 524320 | tf_op jit(solution)/shard_map/ppermute | solution.py:96
  83.6 2.0 %fusion.12 = bf16[1,128,2048]{2,1,0:T(8,128)(2,1)} fusion(bf16[128,2048]{1,0:T(8,128)(2,1)S(1)} %collective-permute-done.6, bf16[128,2048]{1,0:T(8,128)(2,1)} %collective-permute-done.4), kind=kLoop, calls=%fused_computation.35 | loop fusion | flops 1048576 | bytes 1572864 | tf_op jit(solution)/shard_map/broadcast_in_dim | solution.py:187
  (76 shorter events, 10.7 us)
Async XLA Ops:
  0.0 4.0 %copy-start.10 = (bf16[1,128,2048]{2,1,0:T(8,128)(2,1)S(1)}, bf16[1,128,2048]{2,1,0:T(8,128)(2,1)}, u32[]{:S(2)}) copy-start(bf16[1,128,2048]{2,1,0:T(8,128)(2,1)} %param.5) | copy-start | bytes 1572868
  4.3 6.4 %copy-start = (bf16[128,2048]{1,0:T(8,128)(2,1)}, bf16[128,2048]{1,0:T(8,128)(2,1)S(1)}, u32[]{:S(2)}) copy-start(bf16[128,2048]{1,0:T(8,128)(2,1)S(1)} %get-tuple-element.29) | copy-start | bytes 1572868
  6.0 1.0 %copy-start.8 = (bf16[128,16,128]{0,2,1:T(8,128)(2,1)S(1)}, bf16[128,16,128]{0,2,1:T(8,128)(2,1)}, u32[]{:S(2)}) copy-start(bf16[128,16,128]{0,2,1:T(8,128)(2,1)} %copy.32) | copy-start | bytes 1572868
  8.8 1.6 %copy-start.11 = (f32[1,3,2048]{2,0,1:T(1,128)S(1)}, f32[1,3,2048]{2,0,1:T(1,128)}, u32[]{:S(2)}) copy-start(f32[1,3,2048]{2,0,1:T(1,128)} %param.7) | copy-start | bytes 73732
  9.9 3.2 %collective-permute-start = (f32[16,136,128]{2,1,0:T(8,128)}, f32[16,136,128]{2,1,0:T(8,128)}, u32[]{:S(2)}, u32[]{:S(2)}) collective-permute-start(f32[16,136,128]{2,1,0:T(8,128)} %pad_maximum_fusion), channel_id=1, source_target_pairs={{0,1},{2,3},{4,5},{6,7},{1,0},{3,2},{5,4},{7,6},{8,9},{10,11},{12,... | collective-permute-start | bytes 3342344 | tf_op jit(solution)/shard_map/ppermute | solution.py:63
  10.7 2.5 %copy-start.2 = (f32[16,128,128]{2,1,0:T(8,128)S(1)}, f32[16,128,128]{2,1,0:T(8,128)}, u32[]{:S(2)}) copy-start(f32[16,128,128]{2,1,0:T(8,128)} %get-tuple-element.44) | copy-start | bytes 3145732
  16.5 5.3 %copy-start.9 = (bf16[16,8,16,128]{3,2,1,0:T(8,128)(2,1)S(1)}, bf16[16,8,16,128]{3,2,1,0:T(8,128)(2,1)}, u32[]{:S(2)}) copy-start(bf16[16,8,16,128]{3,2,1,0:T(8,128)(2,1)} %copy.65) | copy-start | bytes 1572868
  17.3 22.8 %collective-permute-start.3 = (bf16[16,136,128]{2,1,0:T(8,128)(2,1)}, bf16[16,136,128]{2,1,0:T(8,128)(2,1)}, u32[]{:S(2)}, u32[]{:S(2)}) collective-permute-start(bf16[16,136,128]{2,1,0:T(8,128)(2,1)} %pad_maximum_fusion.2), channel_id=1, source_target_pairs={{1,7},{6,0},{9,15},{14,8},{17,23},{22,16},{25,31},{30,24}} | collective-permute-start | bytes 1671176 | tf_op jit(solution)/shard_map/ppermute | solution.py:40
  18.6 20.4 %collective-permute-start.2 = (bf16[16,136,128]{2,1,0:T(8,128)(2,1)}, bf16[16,136,128]{2,1,0:T(8,128)(2,1)}, u32[]{:S(2)}, u32[]{:S(2)}) collective-permute-start(bf16[16,136,128]{2,1,0:T(8,128)(2,1)} %pad_maximum_fusion.2), channel_id=1, source_target_pairs={{1,5},{3,7},{6,2},{4,0},{9,13},{11,15},{14,10},{12,8},{17,21},{19,... | collective-permute-start | bytes 1671176 | tf_op jit(solution)/shard_map/ppermute | solution.py:40
  19.9 19.1 %collective-permute-start.1 = (bf16[16,136,128]{2,1,0:T(8,128)(2,1)}, bf16[16,136,128]{2,1,0:T(8,128)(2,1)}, u32[]{:S(2)}, u32[]{:S(2)}) collective-permute-start(bf16[16,136,128]{2,1,0:T(8,128)(2,1)} %pad_maximum_fusion.2), channel_id=1, source_target_pairs={{1,3},{3,5},{5,7},{6,4},{4,2},{2,0},{9,11},{11,13},{13,15},{14,12}... | collective-permute-start | bytes 1671176 | tf_op jit(solution)/shard_map/ppermute | solution.py:40
  21.8 0.8 copy-start.6
  23.8 1.3 %copy-start.7 = (bf16[128,16,128]{0,2,1:T(8,128)(2,1)S(1)}, bf16[128,16,128]{0,2,1:T(8,128)(2,1)}, u32[]{:S(2)}) copy-start(bf16[128,16,128]{0,2,1:T(8,128)(2,1)} %copy-done.6) | copy-start | bytes 1572868
  30.6 1.3 %copy-start.5 = (f32[128,2048]{1,0:T(8,128)S(1)}, f32[128,2048]{1,0:T(8,128)}, u32[]{:S(2)}) copy-start(f32[128,2048]{1,0:T(8,128)} %copy.49) | copy-start | bytes 3145732
  33.9 12.9 %collective-permute-start.4 = (bf16[128,2048]{1,0:T(8,128)(2,1)S(1)}, bf16[128,2048]{1,0:T(8,128)(2,1)}, u32[]{:S(2)}, u32[]{:S(2)}) collective-permute-start(bf16[128,2048]{1,0:T(8,128)(2,1)S(1)} %add_convert_fusion.2), channel_id=1, source_target_pairs={{0,24},{8,0},{16,8},{24,16},{1,25},{9,1},{17,9},{25,17},{2,26},{10... | collective-permute-start | bytes 1572872 | tf_op jit(solution)/shard_map/ppermute | solution.py:96
  46.8 7.2 %collective-permute-start.5 = (f32[16,128,128]{2,1,0:T(8,128)}, f32[16,128,128]{2,1,0:T(8,128)S(1)}, u32[]{:S(2)}, u32[]{:S(2)}) collective-permute-start(f32[16,128,128]{2,1,0:T(8,128)} %multiply_add_fusion.1), channel_id=1, source_target_pairs={{0,1},{2,3},{4,5},{6,7},{1,0},{3,2},{5,4},{7,6},{8,9},{10,11},{12,... | collective-permute-start | bytes 3145736 | tf_op jit(solution)/shard_map/ppermute | solution.py:88
  56.3 2.6 %copy-start.1 = (bf16[128,2048]{1,0:T(8,128)(2,1)S(1)}, bf16[128,2048]{1,0:T(8,128)(2,1)}, u32[]{:S(2)}) copy-start(bf16[128,2048]{1,0:T(8,128)(2,1)} %copy-done) | copy-start | bytes 1572868
  65.6 1.7 %copy-start.3 = (f32[128,2048]{1,0:T(8,128)S(1)}, f32[128,2048]{1,0:T(8,128)}, u32[]{:S(2)}) copy-start(f32[128,2048]{1,0:T(8,128)} %copy.52) | copy-start | bytes 3145732
  65.6 1.9 %copy-start.4 = (f32[128,2048]{1,0:T(8,128)S(1)}, f32[128,2048]{1,0:T(8,128)}, u32[]{:S(2)}) copy-start(f32[128,2048]{1,0:T(8,128)} %copy.54) | copy-start | bytes 3145732
  67.7 15.9 %collective-permute-start.6 = (bf16[128,2048]{1,0:T(8,128)(2,1)S(1)}, bf16[128,2048]{1,0:T(8,128)(2,1)S(1)}, u32[]{:S(2)}, u32[]{:S(2)}) collective-permute-start(bf16[128,2048]{1,0:T(8,128)(2,1)S(1)} %add_convert_fusion.1), channel_id=1, source_target_pairs={{0,24},{8,0},{16,8},{24,16},{1,25},{9,1},{17,9},{25,17},{2,26},{10... | collective-permute-start | bytes 1572872 | tf_op jit(solution)/shard_map/ppermute | solution.py:96

commit v8 on v7

--- a/solution.py
+++ b/solution.py
@@ -84,7 +84,6 @@
             moves = [(2 * p + 1, 2 * (p + 1 + covered) + 1) for p in range(couples - 1 - covered)]
             nearer = merged(sent_narrow(window, axis, both_ways(count, moves)), nearer)
         incoming = unpacked(nearer)[0]
-    incoming, held = lax.optimization_barrier((incoming, held))
     other = lax.ppermute(incoming, axis, swap)
     own = lower_rate[:, None, None] * incoming + lower
     return jnp.where(odd, own, other), jnp.where(odd, other, own), held
@@ -136,7 +135,9 @@
     near_total = near_total + gain[0] * query_near.reshape(rows, width)
     near_total = near_total + gain[1] * key_near.reshape(rows, width)
     near_total = near_total + gain[2] * value_near.reshape(rows, width)
-    return passed_along(near_total.astype(jnp.bfloat16), "section", -1)
+    near_received = passed_along(near_total.astype(jnp.bfloat16), "section", -1)
+    widened = [part.astype(jnp.float32) for part in (key_half, value_half, grad_half)]
+    return near_received, widened
 
 
 def local(inputs, out_grad, gains, exponent, boundary):
@@ -164,7 +165,7 @@
         "shd,she->hde", queries * growth[:, :, None], grad_rows, precision=HIGH
     )
     whole_decay = jnp.exp(cumul[-1])
-    state_in, adjoint_in, near_received = scans_in(
+    state_in, adjoint_in, (near_received, widened) = scans_in(
         forward_part,
         adjoint_part,
         whole_decay,
@@ -172,6 +173,7 @@
         near_terms,
         (query_half, key_half, value_half, grad_half, cumul, grad_block, gain),
     )
+    key_rows, value_rows, grad_rows = widened
     query_far = (
         scale * growth[:, :, None] * jnp.einsum("the,hde->thd", grad_rows, state_in, precision=HIGH)
     )

time: 86.9 us -> 89.8 us (1.033)
  starting transfers between devices: 18.4 us -> 9.16 us
  waiting for transfers between devices: 17.8 us -> 25.9 us
  matrix products: 13.4 us -> 15.5 us
  other arithmetic: 16.4 us -> 17.7 us
  local copies, waits for them, and re-layouts: 19.2 us -> 20.5 us
    ppermute x3, waiting for transfers between devices: 0.01 us -> 10.8 us  [sent_narrow(): return widen(lax.ppermute(narrow(message), axis, pairs))]
    ppermute x1, starting transfers between devices: 4.69 us -> 0.01 us  [scans_in(): other = lax.ppermute(incoming, axis, swap)]
    ppermute x2, starting transfers between devices: 9.36 us -> 4.84 us  [passed_along(): return lax.ppermute(value, axis, pairs)]
    add x1 -> x0, other arithmetic: 2.77 us -> none  [scans_in(): incoming = incoming + weight[:, None, None] * got]
    ppermute x2, waiting for transfers between devices: 15.6 us -> 13.6 us  [passed_along(): return lax.ppermute(value, axis, pairs)]
    add x1, other arithmetic: 1.73 us -> 3.13 us  [scans_in(): own = lower_rate[:, None, None] * incoming + lower]
    reshape x1, local copies, waits for them, and re-layouts: 1.33 us -> 2.55 us  [near_terms(): near_total = near_total + gain[0] * query_near.reshape(rows, width)]
    reshape x1, local copies, waits for them, and re-layouts: 1.31 us -> 2.52 us  [near_terms(): near_total = near_total + gain[1] * key_near.reshape(rows, width)]
  transfers between devices with their start and end apart: 7 -> 7, of which waited for: 4 -> 4; matrix products, arithmetic and copies ran while one was open for 22% -> 38% of each run, Pallas kernels for 0% -> 0%
where the time goes in v8:
time: 89.8 us; the launch traced here: 89 us
  waiting for transfers between devices  25.9 us (29%)
  local copies, waits for them, and re-layouts  20.5 us (23%)
  other arithmetic  17.7 us (20%)
  matrix products  15.5 us (17%)
  starting transfers between devices  9.16 us (10%)
    ppermute x2, waiting for transfers between devices, passed_along(): return lax.ppermute(value, axis, pairs)  13.6 us
    ppermute x3, waiting for transfers between devices, sent_narrow(): return widen(lax.ppermute(narrow(message), axis, pairs))  10.8 us
    ppermute x2, starting transfers between devices, passed_along(): return lax.ppermute(value, axis, pairs)  4.84 us
    ppermute x3, starting transfers between devices, sent_narrow(): return widen(lax.ppermute(narrow(message), axis, pairs))  3.86 us
    convert_element_type x1, other arithmetic, near_terms(): near_received = passed_along(near_total.astype(jnp.bfloat16), 'section', -1)  3.15 us
    add x1, other arithmetic, scans_in(): own = lower_rate[:, None, None] * incoming + lower  3.13 us
    reshape x1, local copies, waits for them, and re-layouts, local(): far_total = far_total + gain[2] * value_far.reshape(rows, width)  2.59 us
    reshape x1, local copies, waits for them, and re-layouts, local(): far_total = far_total + gain[1] * key_far.reshape(rows, width)  2.58 us
  transfers between devices with their start and end apart: 7, of which 4 were waited for; matrix products, arithmetic and copies ran while one was open for 38% of the time, Pallas kernels for 0%

profile of v8, /device:TPU:0, one launch (start us, length us, event | category | flops | bytes accessed | tf_op | source)
XLA Modules:
  0.0 89.0 jit_solution(12954227683112216783)
XLA Ops:
  2.6 1.3 %fusion.5 = (bf16[128,2048]{1,0:T(8,128)(2,1)S(1)}, bf16[128,2048]{1,0:T(8,128)(2,1)S(1)}, bf16[128,2048]{1,0:T(8,128)(2,1)S(1)}) fusion(bf16[1,128,2048]{2,1,0:T(8,128)(2,1)} %param.5, f32[2048]{0:T(1024)S(1)} %bitcast.109, f32[2048]{0:T(1024)S(1)} %bitcast.111, f32[2048]{0:T(1024)S(1)} %bitcast.113), kind=kLoop, calls=%fused_computation.19 | loop fusion | flops 1835008 | bytes 2121728 | tf_op jit(solution)/shard_map/convert_element_type | solution.py:111
  5.3 1.2 %copy.32 = bf16[128,16,128]{0,2,1:T(8,128)(2,1)} copy(bf16[128,16,128]{2,1,0:T(8,128)(2,1)S(1)} %bitcast.92) | data formatting | bytes 1048576 | tf_op jit(solution)/shard_map/reshape | solution.py:112
  7.6 1.7 %broadcast_select_fusion.1 = (f32[16,128,128]{2,1,0:T(8,128)S(1)}, f32[16,128,128]{2,1,0:T(8,128)}) fusion(f32[16,128,128]{2,1,0:T(8,128)S(1)} %fusion.7, pred[]{:T(512)S(6)} %eq.29, bf16[128,16,128]{2,1,0:T(8,128)(2,1)S(1)} %bitcast.84, bf16[128,16,128]{0,2,1:T(8,128)(2,1)S(1)} %copy-done.2, f32[128,16]{0,1:T(8,128)S(1)} %copy.33), kind=kOutput, calls=%fused_computation.43 | convolution fusion | flops 403701760 | bytes 4202497 | tf_op jit(solution)/shard_map/shd,she->hde/dot_general | solution.py:164
  9.4 1.1 %pad_maximum_fusion = f32[16,136,128]{2,1,0:T(8,128)} fusion(f32[16,8,128]{2,1,0:T(8,128)S(1)} %broadcast_in_dim.36, f32[16,128,128]{2,1,0:T(8,128)S(1)} %get-tuple-element.41), kind=kLoop, calls=%fused_computation.15 | loop fusion | flops 278528 | bytes 2228224 | tf_op jit(solution)/shard_map/concatenate | solution.py:16
  11.1 0.9 %copy.65 = bf16[16,8,16,128]{3,2,1,0:T(8,128)(2,1)} copy(bf16[16,8,16,128]{3,1,2,0:T(8,128)(2,1)S(1)} %bitcast.95) | data formatting | bytes 1048576
  12.3 1.5 %collective-permute-done = f32[16,136,128]{2,1,0:T(8,128)} collective-permute-done((f32[16,136,128]{2,1,0:T(8,128)}, f32[16,136,128]{2,1,0:T(8,128)}, u32[]{:S(2)}, u32[]{:S(2)}) %collective-permute-start) | collective-permute-done | bytes 1114144 | tf_op jit(solution)/shard_map/ppermute | solution.py:63
  13.7 1.0 %slice_reduce_fusion.1 = (f32[16]{0:T(128)S(1)}, f32[16]{0:T(128)S(1)}) fusion(f32[16,136,128]{2,1,0:T(8,128)} %collective-permute-done, f32[16,1,1]{2,1,0:T(1,128)S(1)} %copy.38), kind=kLoop, calls=%fused_computation.66 | loop fusion | flops 16 | bytes 256 | tf_op jit(solution)/shard_map/slice | solution.py:21
  14.8 1.7 %select_add_fusion = f32[16,128,128]{2,1,0:T(8,128)S(1)} fusion(f32[16,128,128]{2,1,0:T(8,128)S(1)} %fusion.7, f32[16,128,128]{2,1,0:T(8,128)} %get-tuple-element.42, f32[16,136,128]{2,1,0:T(8,128)} %collective-permute-done, f32[16]{0:T(128)S(1)} %fusion.31, pred[]{:T(512)S(6)} %eq.29), kind=kLoop, calls=%fused_computation.28 | loop fusion | flops 786432 | bytes 4194369 | tf_op jit(solution)/shard_map/add | solution.py:64
  17.4 0.9 pad_maximum_fusion.2
  18.3 1.3 %collective-permute-start.4 = (bf16[16,136,128]{2,1,0:T(8,128)(2,1)}, bf16[16,136,128]{2,1,0:T(8,128)(2,1)}, u32[]{:S(2)}, u32[]{:S(2)}) collective-permute-start(bf16[16,136,128]{2,1,0:T(8,128)(2,1)} %pad_maximum_fusion.2), channel_id=1, source_target_pairs={{1,7},{6,0},{9,15},{14,8},{17,23},{22,16},{25,31},{30,24}} | collective-permute-start | bytes 1671176 | tf_op jit(solution)/shard_map/ppermute | solution.py:40
  19.5 1.3 %collective-permute-start.3 = (bf16[16,136,128]{2,1,0:T(8,128)(2,1)}, bf16[16,136,128]{2,1,0:T(8,128)(2,1)}, u32[]{:S(2)}, u32[]{:S(2)}) collective-permute-start(bf16[16,136,128]{2,1,0:T(8,128)(2,1)} %pad_maximum_fusion.2), channel_id=1, source_target_pairs={{1,5},{3,7},{6,2},{4,0},{9,13},{11,15},{14,10},{12,8},{17,21},{19,... | collective-permute-start | bytes 1671176 | tf_op jit(solution)/shard_map/ppermute | solution.py:40
  20.8 1.3 %collective-permute-start.2 = (bf16[16,136,128]{2,1,0:T(8,128)(2,1)}, bf16[16,136,128]{2,1,0:T(8,128)(2,1)}, u32[]{:S(2)}, u32[]{:S(2)}) collective-permute-start(bf16[16,136,128]{2,1,0:T(8,128)(2,1)} %pad_maximum_fusion.2), channel_id=1, source_target_pairs={{1,3},{3,5},{5,7},{6,4},{4,2},{2,0},{9,11},{11,13},{13,15},{14,12}... | collective-permute-start | bytes 1671176 | tf_op jit(solution)/shard_map/ppermute | solution.py:40
  22.7 1.8 %convolution_multiply_fusion.2 = f32[16,128,128]{2,1,0:T(8,128)} fusion(f32[16,128,128]{2,1,0:T(8,128)S(1)} %convolution_multiply_fusion.4, bf16[128,16,128]{2,1,0:T(8,128)(2,1)S(1)} %bitcast.93), kind=kOutput, calls=%fused_computation.5 | convolution fusion | flops 402915328 | bytes 2621440 | tf_op jit(solution)/shard_map/hts,thd->shd/dot_general | solution.py:129
  24.9 2.2 %convolution_multiply_fusion.3 = f32[16,128,128]{2,1,0:T(8,128)} fusion(bf16[128,16,128]{0,2,1:T(8,128)(2,1)S(1)} %bitcast.90, f32[16,128,128]{2,1,0:T(8,128)S(1)} %convolution_multiply_fusion.4), kind=kOutput, calls=%fused_computation.6 | convolution fusion | flops 402915328 | bytes 2621440 | tf_op jit(solution)/shard_map/hts,shd->thd/dot_general | solution.py:128
  27.1 10.0 %collective-permute-done.3 = bf16[16,136,128]{2,1,0:T(8,128)(2,1)} collective-permute-done((bf16[16,136,128]{2,1,0:T(8,128)(2,1)}, bf16[16,136,128]{2,1,0:T(8,128)(2,1)}, u32[]{:S(2)}, u32[]{:S(2)}) %collective-permute-start.3) | collective-permute-done | bytes 557088 | tf_op jit(solution)/shard_map/ppermute | solution.py:40
  37.1 0.8 collective-permute-done.2
  37.9 1.2 %fusion.32 = (f32[16]{0:T(128)S(1)}, f32[16]{0:T(128)S(1)}) fusion(bf16[16,136,128]{2,1,0:T(8,128)(2,1)} %collective-permute-done.3, bf16[16,136,128]{2,1,0:T(8,128)(2,1)} %collective-permute-done.2), kind=kLoop, calls=%fused_computation.78 | loop fusion | flops 112 | bytes 256 | tf_op jit(solution)/shard_map/add | solution.py:35
  39.1 3.1 %multiply_add_fusion = (f32[16,128,128]{2,1,0:T(8,128)S(1)}, f32[16,128,128]{2,1,0:T(8,128)}) fusion(f32[16,136,128]{2,1,0:T(8,128)} %collective-permute-done, f32[16]{0:T(128)S(1)} %get-tuple-element.21, bf16[16,136,128]{2,1,0:T(8,128)(2,1)} %collective-permute-done.4, f32[16]{0:T(128)S(1)} %get-tuple-element.24, ...), kind=kLoop, calls=%fused_computation.24 | loop fusion | flops 2359296 | bytes 4718784 | tf_op jit(solution)/shard_map/add | solution.py:88
  42.2 1.7 %convolution_multiply_fusion = f32[16,128,128]{2,1,0:T(8,128)} fusion(f32[16,128,128]{2,1,0:T(8,128)S(1)} %convolution_multiply_fusion.1, bf16[128,16,128]{2,1,0:T(8,128)(2,1)S(1)} %bitcast.86), kind=kOutput, calls=%fused_computation.3 | convolution fusion | flops 402915328 | bytes 2621440 | tf_op jit(solution)/shard_map/hts,the->she/dot_general | solution.py:133
  44.0 2.5 %copy.47 = f32[128,2048]{1,0:T(8,128)} copy(f32[128,2048]{0,1:T(8,128)} %bitcast.98) | data formatting | bytes 2097152 | tf_op jit(solution)/shard_map/reshape | solution.py:137
  46.5 2.5 %copy.45 = f32[128,2048]{1,0:T(8,128)} copy(f32[128,2048]{0,1:T(8,128)} %bitcast.96) | data formatting | bytes 2097152 | tf_op jit(solution)/shard_map/reshape | solution.py:136
  49.0 2.6 %copy.43 = f32[128,2048]{1,0:T(8,128)} copy(f32[128,2048]{0,1:T(8,128)} %bitcast.97) | data formatting | bytes 2097152 | tf_op jit(solution)/shard_map/reshape | solution.py:135
  51.6 3.1 %add_convert_fusion.2 = bf16[128,2048]{1,0:T(8,128)(2,1)} fusion(f32[128,2048]{1,0:T(8,128)} %copy.47, f32[128,2048]{1,0:T(8,128)} %copy.45, f32[128,2048]{1,0:T(8,128)} %copy.43, bf16[128,2048]{1,0:T(8,128)(2,1)} %bitcast.105, f32[2048]{0:T(1024)S(1)} %bitcast.116, f32[2048]{0:T(1024)S(1)} %bitcast.117, f32[2048]{0:T(1024)S(1)} %bitcast.115), kind=kLoop, calls=%fused_computation.26 | loop fusion | flops 2097152 | bytes 4218880 | tf_op jit(solution)/shard_map/convert_element_type | solution.py:138
  54.8 4.3 %collective-permute-start.1 = (bf16[128,2048]{1,0:T(8,128)(2,1)}, bf16[128,2048]{1,0:T(8,128)(2,1)}, u32[]{:S(2)}, u32[]{:S(2)}) collective-permute-start(bf16[128,2048]{1,0:T(8,128)(2,1)} %add_convert_fusion.2), channel_id=1, source_target_pairs={{0,24},{8,0},{16,8},{24,16},{1,25},{9,1},{17,9},{25,17},{2,26},{10... | collective-permute-start | bytes 1572872 | tf_op jit(solution)/shard_map/ppermute | solution.py:95
  59.1 2.0 %fusion = f32[128,16,128]{0,2,1:T(8,128)} fusion(bf16[128,16,128]{0,2,1:T(8,128)(2,1)S(1)} %bitcast.91, f32[128,16]{0,1:T(8,128)S(1)} %copy.36, f32[16,128,128]{2,1,0:T(8,128)S(1)} %collective-permute-done.5, f32[16,128,128]{2,1,0:T(8,128)S(1)} %get-tuple-element.25, pred[]{:T(512)S(6)} %eq.29), kind=kOutput, calls=%fused_computation.10 | convolution fusion | flops 403177472 | bytes 3678209 | tf_op jit(solution)/shard_map/shd,hde->she/dot_general | solution.py:181
  61.1 2.6 %copy.57 = f32[128,2048]{1,0:T(8,128)} copy(f32[128,2048]{0,1:T(8,128)} %bitcast.101) | data formatting | bytes 2097152 | tf_op jit(solution)/shard_map/reshape | solution.py:184
  63.7 2.2 %fusion.1 = f32[128,16,128]{0,2,1:T(8,128)} fusion(f32[128,16]{0,1:T(8,128)S(1)} %copy.36, bf16[128,16,128]{2,1,0:T(8,128)(2,1)S(1)} %bitcast.103, f32[16,128,128]{2,1,0:T(8,128)S(1)} %collective-permute-done.5, f32[16,128,128]{2,1,0:T(8,128)S(1)} %get-tuple-element.25, pred[]{:T(512)S(6)} %eq.29), kind=kOutput, calls=%fused_computation.12 | convolution fusion | flops 403177472 | bytes 3678209 | tf_op jit(solution)/shard_map/she,hde->shd/dot_general | solution.py:180
  66.0 2.6 %copy.54 = f32[128,2048]{1,0:T(8,128)} copy(f32[128,2048]{0,1:T(8,128)} %bitcast.100) | data formatting | bytes 2097152 | tf_op jit(solution)/shard_map/reshape | solution.py:183
  68.5 2.2 %fusion.2 = f32[128,16,128]{0,2,1:T(8,128)} fusion(f32[16,128,128]{2,1,0:T(8,128)S(1)} %get-tuple-element.25, f32[16,128,128]{2,1,0:T(8,128)S(1)} %collective-permute-done.5, f32[128,16]{0,1:T(8,128)S(1)} %copy.48, pred[]{:T(512)S(6)} %eq.29, bf16[128,16,128]{2,1,0:T(8,128)(2,1)S(1)} %bitcast.87), kind=kOutput, calls=%fused_computation.14 | convolution fusion | flops 403177472 | bytes 3678209 | tf_op jit(solution)/shard_map/the,hde->thd/dot_general | solution.py:178
  70.8 1.7 %copy.52 = f32[128,2048]{1,0:T(8,128)S(1)} copy(f32[128,2048]{0,1:T(8,128)} %bitcast.99) | data formatting | bytes 2097152 | tf_op jit(solution)/shard_map/reshape | solution.py:182
  73.4 13.6 %collective-permute-done.6 = bf16[128,2048]{1,0:T(8,128)(2,1)S(1)} collective-permute-done((bf16[128,2048]{1,0:T(8,128)(2,1)S(1)}, bf16[128,2048]{1,0:T(8,128)(2,1)S(1)}, u32[]{:S(2)}, u32[]{:S(2)}) %collective-permute-start.6) | collective-permute-done | bytes 524320 | tf_op jit(solution)/shard_map/ppermute | solution.py:95
  87.0 2.0 %fusion.12 = bf16[1,128,2048]{2,1,0:T(8,128)(2,1)} fusion(bf16[128,2048]{1,0:T(8,128)(2,1)S(1)} %collective-permute-done.6, bf16[128,2048]{1,0:T(8,128)(2,1)} %collective-permute-done.1), kind=kLoop, calls=%fused_computation.35 | loop fusion | flops 1048576 | bytes 1572864 | tf_op jit(solution)/shard_map/broadcast_in_dim | solution.py:189
  (64 shorter events, 8.6 us)
Async XLA Ops:
  4.0 1.0 %copy-start.5 = (bf16[1,128,2048]{2,1,0:T(8,128)(2,1)S(1)}, bf16[1,128,2048]{2,1,0:T(8,128)(2,1)}, u32[]{:S(2)}) copy-start(bf16[1,128,2048]{2,1,0:T(8,128)(2,1)} %param.6) | copy-start | bytes 1572868
  6.5 1.1 %copy-start.2 = (bf16[128,16,128]{0,2,1:T(8,128)(2,1)S(1)}, bf16[128,16,128]{0,2,1:T(8,128)(2,1)}, u32[]{:S(2)}) copy-start(bf16[128,16,128]{0,2,1:T(8,128)(2,1)} %copy.32) | copy-start | bytes 1572868
  9.4 1.6 %copy-start.6 = (f32[1,3,2048]{2,0,1:T(1,128)S(1)}, f32[1,3,2048]{2,0,1:T(1,128)}, u32[]{:S(2)}) copy-start(f32[1,3,2048]{2,0,1:T(1,128)} %param.7) | copy-start | bytes 73732
  10.5 3.2 %collective-permute-start = (f32[16,136,128]{2,1,0:T(8,128)}, f32[16,136,128]{2,1,0:T(8,128)}, u32[]{:S(2)}, u32[]{:S(2)}) collective-permute-start(f32[16,136,128]{2,1,0:T(8,128)} %pad_maximum_fusion), channel_id=1, source_target_pairs={{0,1},{2,3},{4,5},{6,7},{1,0},{3,2},{5,4},{7,6},{8,9},{10,11},{12,... | collective-permute-start | bytes 3342344 | tf_op jit(solution)/shard_map/ppermute | solution.py:63
  16.9 5.3 %copy-start.3 = (bf16[16,8,16,128]{3,2,1,0:T(8,128)(2,1)S(1)}, bf16[16,8,16,128]{3,2,1,0:T(8,128)(2,1)}, u32[]{:S(2)}) copy-start(bf16[16,8,16,128]{3,2,1,0:T(8,128)(2,1)} %copy.65) | copy-start | bytes 1572868
  18.3 20.8 %collective-permute-start.4 = (bf16[16,136,128]{2,1,0:T(8,128)(2,1)}, bf16[16,136,128]{2,1,0:T(8,128)(2,1)}, u32[]{:S(2)}, u32[]{:S(2)}) collective-permute-start(bf16[16,136,128]{2,1,0:T(8,128)(2,1)} %pad_maximum_fusion.2), channel_id=1, source_target_pairs={{1,7},{6,0},{9,15},{14,8},{17,23},{22,16},{25,31},{30,24}} | collective-permute-start | bytes 1671176 | tf_op jit(solution)/shard_map/ppermute | solution.py:40
  19.5 17.6 %collective-permute-start.3 = (bf16[16,136,128]{2,1,0:T(8,128)(2,1)}, bf16[16,136,128]{2,1,0:T(8,128)(2,1)}, u32[]{:S(2)}, u32[]{:S(2)}) collective-permute-start(bf16[16,136,128]{2,1,0:T(8,128)(2,1)} %pad_maximum_fusion.2), channel_id=1, source_target_pairs={{1,5},{3,7},{6,2},{4,0},{9,13},{11,15},{14,10},{12,8},{17,21},{19,... | collective-permute-start | bytes 1671176 | tf_op jit(solution)/shard_map/ppermute | solution.py:40
  20.8 17.0 %collective-permute-start.2 = (bf16[16,136,128]{2,1,0:T(8,128)(2,1)}, bf16[16,136,128]{2,1,0:T(8,128)(2,1)}, u32[]{:S(2)}, u32[]{:S(2)}) collective-permute-start(bf16[16,136,128]{2,1,0:T(8,128)(2,1)} %pad_maximum_fusion.2), channel_id=1, source_target_pairs={{1,3},{3,5},{5,7},{6,4},{4,2},{2,0},{9,11},{11,13},{13,15},{14,12}... | collective-permute-start | bytes 1671176 | tf_op jit(solution)/shard_map/ppermute | solution.py:40
  42.2 16.9 %collective-permute-start.5 = (f32[16,128,128]{2,1,0:T(8,128)}, f32[16,128,128]{2,1,0:T(8,128)S(1)}, u32[]{:S(2)}, u32[]{:S(2)}) collective-permute-start(f32[16,128,128]{2,1,0:T(8,128)} %get-tuple-element.26), channel_id=1, source_target_pairs={{0,1},{2,3},{4,5},{6,7},{1,0},{3,2},{5,4},{7,6},{8,9},{10,11},{12,... | collective-permute-start | bytes 3145736 | tf_op jit(solution)/shard_map/ppermute | solution.py:87
  54.8 18.6 %collective-permute-start.1 = (bf16[128,2048]{1,0:T(8,128)(2,1)}, bf16[128,2048]{1,0:T(8,128)(2,1)}, u32[]{:S(2)}, u32[]{:S(2)}) collective-permute-start(bf16[128,2048]{1,0:T(8,128)(2,1)} %add_convert_fusion.2), channel_id=1, source_target_pairs={{0,24},{8,0},{16,8},{24,16},{1,25},{9,1},{17,9},{25,17},{2,26},{10... | collective-permute-start | bytes 1572872 | tf_op jit(solution)/shard_map/ppermute | solution.py:95
  61.1 2.6 %copy-start.4 = (bf16[16,8,16,128]{3,2,1,0:T(8,128)(2,1)S(1)}, bf16[16,8,16,128]{3,2,1,0:T(8,128)(2,1)}, u32[]{:S(2)}) copy-start(bf16[16,8,16,128]{3,2,1,0:T(8,128)(2,1)} %copy.65) | copy-start | bytes 1572868
  70.8 1.7 %copy-start = (f32[128,2048]{1,0:T(8,128)S(1)}, f32[128,2048]{1,0:T(8,128)}, u32[]{:S(2)}) copy-start(f32[128,2048]{1,0:T(8,128)} %copy.57) | copy-start | bytes 3145732
  70.8 1.9 %copy-start.1 = (f32[128,2048]{1,0:T(8,128)S(1)}, f32[128,2048]{1,0:T(8,128)}, u32[]{:S(2)}) copy-start(f32[128,2048]{1,0:T(8,128)} %copy.54) | copy-start | bytes 3145732
  72.9 14.1 %collective-permute-start.6 = (bf16[128,2048]{1,0:T(8,128)(2,1)S(1)}, bf16[128,2048]{1,0:T(8,128)(2,1)S(1)}, u32[]{:S(2)}, u32[]{:S(2)}) collective-permute-start(bf16[128,2048]{1,0:T(8,128)(2,1)S(1)} %add_convert_fusion.1), channel_id=1, source_target_pairs={{0,24},{8,0},{16,8},{24,16},{1,25},{9,1},{17,9},{25,17},{2,26},{10... | collective-permute-start | bytes 1572872 | tf_op jit(solution)/shard_map/ppermute | solution.py:95

commit v9 on v5

--- a/solution.py
+++ b/solution.py
@@ -50,10 +50,10 @@
     return list(moves) + [(count - 1 - source, count - 1 - target) for source, target in moves]
 
 
-def scans_in(forward_part, backward_part, rate, axis, held):
+def scans_in(forward_part, backward_part, rate, axis):
     count = lax.axis_size(axis)
     if count == 1:
-        return jnp.zeros_like(forward_part), jnp.zeros_like(backward_part), held
+        return jnp.zeros_like(forward_part), jnp.zeros_like(backward_part)
     assert count % 2 == 0
     odd = lax.axis_index(axis) % 2 == 1
     couples = count // 2
@@ -82,10 +82,9 @@
             moves = [(2 * p + 1, 2 * (p + 1 + covered) + 1) for p in range(couples - 1 - covered)]
             nearer = merged(sent_narrow(window, axis, both_ways(count, moves)), nearer)
         incoming = unpacked(nearer)[0]
-    incoming, held = lax.optimization_barrier((incoming, held))
     other = lax.ppermute(incoming, axis, swap)
     own = lower_rate[:, None, None] * incoming + lower
-    return jnp.where(odd, own, other), jnp.where(odd, other, own), held
+    return jnp.where(odd, own, other), jnp.where(odd, other, own)
 
 
 def passed_along(value, axis, steps):
@@ -112,12 +111,42 @@
     return result
 
 
-def local(inputs, out_grad, gains, exponent, boundary):
-    block = inputs[0]
-    grad_block = out_grad[0]
-    gain = gains[0]
+def near_terms(block, grad_block, gain, exponent, boundary):
     rows, width = block.shape
-    heads = exponent.shape[2]
+    heads = exponent.shape[1]
+    head_dim = width // heads
+    scale = 1.0 / head_dim
+    query_half, key_half, value_half = projections(block, gain, heads)
+    grad_half = grad_block.reshape(rows, heads, head_dim)
+    queries = query_half.astype(jnp.float32)
+    key_rows = key_half.astype(jnp.float32)
+    grad_rows = grad_half.astype(jnp.float32)
+    logs = decay_logs(exponent, boundary, CH).reshape(rows, heads)
+    cumul = jnp.cumsum(logs, axis=0)
+    cum_heads = cumul.T
+    gap = cum_heads[:, :, None] - cum_heads[:, None, :]
+    lower = jnp.arange(rows)[:, None] >= jnp.arange(rows)[None, :]
+    decay = jnp.where(lower[None], jnp.exp(jnp.minimum(gap, 0.0)), 0.0)
+    mixing = (
+        jnp.einsum("thd,shd->hts", grad_half, value_half, preferred_element_type=jnp.float32)
+        * decay
+    )
+    query_near = scale * jnp.einsum("hts,shd->thd", mixing, key_rows, precision=HIGH)
+    key_near = scale * jnp.einsum("hts,thd->shd", mixing, queries, precision=HIGH)
+    attention = (
+        jnp.einsum("thd,shd->hts", query_half, key_half, preferred_element_type=jnp.float32) * decay
+    )
+    value_near = scale * jnp.einsum("hts,the->she", attention, grad_rows, precision=HIGH)
+    near_total = grad_block.astype(jnp.float32)
+    near_total = near_total + gain[0] * query_near.reshape(rows, width)
+    near_total = near_total + gain[1] * key_near.reshape(rows, width)
+    near_total = near_total + gain[2] * value_near.reshape(rows, width)
+    return near_total.astype(jnp.bfloat16)
+
+
+def far_terms(block, grad_block, gain, exponent, boundary):
+    rows, width = block.shape
+    heads = exponent.shape[1]
     head_dim = width // heads
     scale = 1.0 / head_dim
     query_half, key_half, value_half = projections(block, gain, heads)
@@ -126,7 +155,7 @@
     key_rows = key_half.astype(jnp.float32)
     value_rows = value_half.astype(jnp.float32)
     grad_rows = grad_half.astype(jnp.float32)
-    logs = decay_logs(exponent[0], boundary[0], CH).reshape(rows, heads)
+    logs = decay_logs(exponent, boundary, CH).reshape(rows, heads)
     cumul = jnp.cumsum(logs, axis=0)
     growth = jnp.exp(cumul)
     tail = jnp.exp(cumul[-1][None, :] - cumul)
@@ -136,30 +165,7 @@
     adjoint_part = scale * jnp.einsum(
         "shd,she->hde", queries * growth[:, :, None], grad_rows, precision=HIGH
     )
-    whole_decay = jnp.exp(cumul[-1])
-    cum_heads = cumul.T
-    gap = cum_heads[:, :, None] - cum_heads[:, None, :]
-    lower = jnp.arange(rows)[:, None] >= jnp.arange(rows)[None, :]
-    decay = jnp.where(lower[None], jnp.exp(jnp.minimum(gap, 0.0)), 0.0)
-    mixing = (
-        jnp.einsum("thd,shd->hts", grad_half, value_half, preferred_element_type=jnp.float32)
-        * decay
-    )
-    query_near = scale * jnp.einsum("hts,shd->thd", mixing, key_rows, precision=HIGH)
-    key_near = scale * jnp.einsum("hts,thd->shd", mixing, queries, precision=HIGH)
-    attention = (
-        jnp.einsum("thd,shd->hts", query_half, key_half, preferred_element_type=jnp.float32) * decay
-    )
-    value_near = scale * jnp.einsum("hts,the->she", attention, grad_rows, precision=HIGH)
-    near_total = grad_block.astype(jnp.float32)
-    near_total = near_total + gain[0] * query_near.reshape(rows, width)
-    near_total = near_total + gain[1] * key_near.reshape(rows, width)
-    near_total = near_total + gain[2] * value_near.reshape(rows, width)
-    near_round = near_total.astype(jnp.bfloat16)
-    near_received = passed_along(near_round, "section", -1)
-    state_in, adjoint_in, near_received = scans_in(
-        forward_part, adjoint_part, whole_decay, "ctx", near_received
-    )
+    state_in, adjoint_in = scans_in(forward_part, adjoint_part, jnp.exp(cumul[-1]), "ctx")
     query_far = (
         scale * growth[:, :, None] * jnp.einsum("the,hde->thd", grad_rows, state_in, precision=HIGH)
     )
@@ -168,9 +174,26 @@
     far_total = gain[0] * query_far.reshape(rows, width)
     far_total = far_total + gain[1] * key_far.reshape(rows, width)
     far_total = far_total + gain[2] * value_far.reshape(rows, width)
-    far_round = far_total.astype(jnp.bfloat16)
-    far_received = passed_along(far_round, "section", -1)
-    received = (near_received.astype(jnp.float32) + far_received.astype(jnp.float32)).astype(
+    return far_total.astype(jnp.bfloat16)
+
+
+def local(inputs, out_grad, gains, exponent, boundary):
+    own = (inputs[0], out_grad[0], gains[0], exponent[0], boundary[0])
+    small = jnp.concatenate(
+        [gains[0].reshape(-1), exponent[0].reshape(-1).astype(jnp.float32), boundary[0].astype(jnp.float32)]
+    )
+    rows_in, small_in = passed_along((jnp.stack([inputs[0], out_grad[0]]), small), "section", -1)
+    sizes = (gains[0].size, exponent[0].size)
+    fetched = (
+        rows_in[0],
+        rows_in[1],
+        small_in[: sizes[0]].reshape(gains[0].shape),
+        jnp.round(small_in[sizes[0] : sizes[0] + sizes[1]]).astype(jnp.int32).reshape(exponent[0].shape),
+        jnp.round(small_in[sizes[0] + sizes[1] :]).astype(jnp.int32),
+    )
+    near_received = passed_along(near_terms(*own), "section", -1)
+    far_round = far_terms(*fetched)
+    received = (near_received.astype(jnp.float32) + far_round.astype(jnp.float32)).astype(
         jnp.bfloat16
     )
     return received[None]

time: 71.6 us -> 94.9 us (1.33); the launches traced: 71 us -> 93.3 us
  waiting for transfers between devices: 23.3 us -> 44.1 us
  other arithmetic: 12.8 us -> 16.3 us
  starting transfers between devices: 13.3 us -> 12 us
    ppermute x2 -> x3, waiting for transfers between devices: 11.7 us -> 32.5 us  [passed_along(): return lax.ppermute(value, axis, pairs)]
    convert_element_type x1 -> x2, other arithmetic: 0.99 us -> 3.75 us  [projections(): (widened * gain[index]).astype(jnp.bfloat16)]
    add x1 -> x0, other arithmetic: 1.43 us -> none  [scans_in(): incoming = incoming + weight[:, None, None] * got]
    mul x2, local copies, waits for them, and re-layouts: 2.61 us -> 1.37 us  [the longest x1 1.31 us: near_terms(): scale * jnp.einsum('hts,the->she', attention, grad_rows, precision=HIGH)]
    slice x0 -> x1, local copies, waits for them, and re-layouts: none -> 1.08 us  [local(): rows_in[1]]
    broadcast_in_dim x1, other arithmetic: 0.14 us -> 1.22 us  [local(): return received[None]]
    ppermute x3, waiting for transfers between devices: 10.6 us -> 11.6 us  [sent_narrow(): return widen(lax.ppermute(narrow(message), axis, pairs))]
    unnamed x13 -> x24, local copies, waits for them, and re-layouts: 3.52 us -> 2.74 us
  transfers between devices with their start and end apart: 7 -> 8, of which waited for: 4 -> 3; matrix products, arithmetic and copies ran while one was open for 23% -> 19% of each run, Pallas kernels for 0% -> 0%
where the time goes in v9:
time: 94.9 us; the launch traced here: 93.3 us
  waiting for transfers between devices  44.1 us (46%)
  other arithmetic  16.3 us (17%)
  matrix products  12.2 us (13%)
  starting transfers between devices  12 us (13%)
  local copies, waits for them, and re-layouts  8.38 us (9%)
    ppermute x3, waiting for transfers between devices, passed_along(): return lax.ppermute(value, axis, pairs)  32.5 us
    ppermute x3, waiting for transfers between devices, sent_narrow(): return widen(lax.ppermute(narrow(message), axis, pairs))  11.6 us
    ppermute x3, starting transfers between devices, passed_along(): return lax.ppermute(value, axis, pairs)  8.04 us
    ppermute x3, starting transfers between devices, sent_narrow(): return widen(lax.ppermute(narrow(message), axis, pairs))  3.86 us
    convert_element_type x2, other arithmetic, projections(): (widened * gain[index]).astype(jnp.bfloat16)  3.75 us
    dot_general x1, matrix products, near_terms(): jnp.einsum('thd,shd->hts', query_half, key_half, preferred_element_type=j...  2.74 us
    unnamed x24, local copies, waits for them, and re-layouts  2.74 us
    dot_general x1, matrix products, far_terms(): jnp.einsum('shd,she->hde', queries * growth[:, :, None], grad_rows, preci...  2.21 us
  transfers between devices with their start and end apart: 8, of which 3 were waited for; matrix products, arithmetic and copies ran while one was open for 19% of the time, Pallas kernels for 0%

profile of v9, /device:TPU:0, one launch (start us, length us, event | category | flops | bytes accessed | tf_op | source)
XLA Modules:
  0.0 93.3 jit_solution(878600534250611243)
XLA Ops:
  0.0 0.7 convert_bitcast_fusion
  1.5 0.8 concatenate.11
  2.3 5.0 %collective-permute-start.1 = (f32[6178]{0:T(1024)S(1)}, f32[6178]{0:T(1024)S(1)}, u32[]{:S(2)}, u32[]{:S(2)}) collective-permute-start(f32[6178]{0:T(1024)S(1)} %concatenate.11), channel_id=1, source_target_pairs={{0,24},{8,0},{16,8},{24,16},{1,25},{9,1},{17,9},{25,17},{2,26},{10... | collective-permute-start | bytes 74144 | tf_op jit(solution)/shard_map/ppermute | solution.py:93
  7.3 1.3 %copy.34 = bf16[1,128,2048]{1,2,0:T(8,128)(2,1)S(1)} copy(bf16[1,128,2048]{2,1,0:T(8,128)(2,1)} %param.6) | data formatting | bytes 1048576 | tf_op args[1]
  10.8 23.1 %collective-permute-done.2 = bf16[2,128,2048]{1,2,0:T(8,128)(2,1)} collective-permute-done((bf16[2,128,2048]{1,2,0:T(8,128)(2,1)S(1)}, bf16[2,128,2048]{1,2,0:T(8,128)(2,1)}, u32[]{:S(2)}, u32[]{:S(2)}) %collective-permute-start.2) | collective-permute-done | bytes 1048608 | tf_op jit(solution)/shard_map/ppermute | solution.py:93
  33.9 1.9 %fusion.10 = (bf16[128,2048]{0,1:T(8,128)(2,1)S(1)}, bf16[128,2048]{0,1:T(8,128)(2,1)S(1)}, bf16[128,2048]{0,1:T(8,128)(2,1)S(1)}) fusion(f32[2048]{0:T(1024)S(1)} %get-tuple-element.22, bf16[2,128,2048]{1,2,0:T(8,128)(2,1)} %collective-permute-done.2, f32[2048]{0:T(1024)S(1)} %get-tuple-element.23, f32[2048]{0:T(1024)S(1)} %get-tuple-element.24), kind=kLoop, calls=%fused_computation.26 | loop fusion | flops 1835008 | bytes 2121728 | tf_op jit(solution)/shard_map/convert_element_type | solution.py:109
  35.8 0.8 copy-done
  36.6 1.2 %fusion.19 = f32[16,128,128]{2,1,0:T(8,128)S(1)} fusion(bf16[128,16,128]{0,2,1:T(8,128)(2,1)S(1)} %bitcast.139, bf16[128,16,128]{0,2,1:T(8,128)(2,1)S(1)} %bitcast.141, f32[128,16]{0,1:T(8,128)S(1)} %copy.51), kind=kOutput, calls=%fused_computation.47 | convolution fusion | flops 403177472 | bytes 2105344 | tf_op jit(solution)/shard_map/shd,she->hde/dot_general | solution.py:162
  37.8 1.1 %slice.106 = bf16[1,128,2048]{1,2,0:T(8,128)(2,1)S(1)} slice(bf16[2,128,2048]{1,2,0:T(8,128)(2,1)} %collective-permute-done.2), slice={[1:2], [0:128], [0:2048]} | slice | bytes 1048576 | tf_op jit(solution)/shard_map/slice | solution.py:189
  38.9 2.2 %broadcast_select_fusion.1 = (f32[16,128,128]{2,1,0:T(8,128)S(1)}, f32[16,128,128]{2,1,0:T(8,128)}) fusion(f32[16,128,128]{2,1,0:T(8,128)S(1)} %fusion.19, pred[]{:T(512)S(6)} %eq.32, bf16[128,16,128]{0,2,1:T(8,128)(2,1)S(1)} %bitcast.137, bf16[128,16,128]{0,2,1:T(8,128)(2,1)S(1)} %bitcast.147, f32[128,16]{0,1:T(8,128)S(1)} %copy.49), kind=kOutput, calls=%fused_computation.58 | convolution fusion | flops 403701760 | bytes 4202497 | tf_op jit(solution)/shard_map/shd,she->hde/dot_general | solution.py:165
  41.2 1.1 %pad_maximum_fusion = f32[16,136,128]{2,1,0:T(8,128)} fusion(f32[16,8,128]{2,1,0:T(8,128)S(1)} %broadcast_in_dim.43, f32[16,128,128]{2,1,0:T(8,128)S(1)} %get-tuple-element.30), kind=kLoop, calls=%fused_computation.20 | loop fusion | flops 278528 | bytes 2228224 | tf_op jit(solution)/shard_map/concatenate | solution.py:16
  42.4 1.8 %fusion.5 = (bf16[128,2048]{0,1:T(8,128)(2,1)}, bf16[128,2048]{0,1:T(8,128)(2,1)}, bf16[128,2048]{0,1:T(8,128)(2,1)}) fusion(bf16[1,128,2048]{1,2,0:T(8,128)(2,1)S(1)} %copy.35, f32[2048]{0:T(1024)S(1)} %bitcast.151, f32[2048]{0:T(1024)S(1)} %bitcast.153, f32[2048]{0:T(1024)S(1)} %bitcast.155), kind=kLoop, calls=%fused_computation.21 | loop fusion | flops 1835008 | bytes 2121728 | tf_op jit(solution)/shard_map/convert_element_type | solution.py:109
  44.7 2.7 %convolution_multiply_fusion.2 = f32[16,128,128]{1,2,0:T(8,128)} fusion(bf16[128,16,128]{0,2,1:T(8,128)(2,1)} %bitcast.143, bf16[128,16,128]{0,2,1:T(8,128)(2,1)} %bitcast.145, f32[16,128]{1,0:T(8,128)S(1)} %copy.38, pred[128,128]{0,1:T(8,128)(4,1)S(1)} %iota_compare_fusion), kind=kOutput, calls=%fused_computation.9 | convolution fusion | flops 68157440 | bytes 2121728 | tf_op jit(solution)/shard_map/thd,shd->hts/dot_general | solution.py:137
  47.4 1.0 %slice_reduce_fusion = (f32[16]{0:T(128)S(1)}, f32[16]{0:T(128)S(1)}) fusion(f32[16,136,128]{2,1,0:T(8,128)} %collective-permute-done.3, f32[16,1,1]{2,1,0:T(1,128)S(1)} %copy.53), kind=kLoop, calls=%fused_computation.73 | loop fusion | flops 16 | bytes 256 | tf_op jit(solution)/shard_map/slice | solution.py:21
  48.7 1.8 %add_convert_fusion.1 = bf16[16,128,128]{2,1,0:T(8,128)(2,1)S(1)} fusion(f32[16,128,128]{2,1,0:T(8,128)S(1)} %fusion.19, f32[16,128,128]{2,1,0:T(8,128)} %get-tuple-element.31, f32[16,136,128]{2,1,0:T(8,128)} %collective-permute-done.3, f32[16]{0:T(128)S(1)} %fusion.38, pred[]{:T(512)S(6)} %eq.32), kind=kLoop, calls=%fused_computation.46 | loop fusion | flops 1048576 | bytes 3670081 | tf_op jit(solution)/shard_map/convert_element_type | solution.py:30
  50.6 0.8 pad_maximum_fusion.2
  51.4 1.3 %collective-permute-start.6 = (bf16[16,136,128]{2,1,0:T(8,128)(2,1)}, bf16[16,136,128]{2,1,0:T(8,128)(2,1)}, u32[]{:S(2)}, u32[]{:S(2)}) collective-permute-start(bf16[16,136,128]{2,1,0:T(8,128)(2,1)} %pad_maximum_fusion.2), channel_id=1, source_target_pairs={{1,7},{6,0},{9,15},{14,8},{17,23},{22,16},{25,31},{30,24}} | collective-permute-start | bytes 1671176 | tf_op jit(solution)/shard_map/ppermute | solution.py:40
  52.7 1.3 %collective-permute-start.5 = (bf16[16,136,128]{2,1,0:T(8,128)(2,1)}, bf16[16,136,128]{2,1,0:T(8,128)(2,1)}, u32[]{:S(2)}, u32[]{:S(2)}) collective-permute-start(bf16[16,136,128]{2,1,0:T(8,128)(2,1)} %pad_maximum_fusion.2), channel_id=1, source_target_pairs={{1,5},{3,7},{6,2},{4,0},{9,13},{11,15},{14,10},{12,8},{17,21},{19,... | collective-permute-start | bytes 1671176 | tf_op jit(solution)/shard_map/ppermute | solution.py:40
  54.0 1.3 %collective-permute-start.4 = (bf16[16,136,128]{2,1,0:T(8,128)(2,1)}, bf16[16,136,128]{2,1,0:T(8,128)(2,1)}, u32[]{:S(2)}, u32[]{:S(2)}) collective-permute-start(bf16[16,136,128]{2,1,0:T(8,128)(2,1)} %pad_maximum_fusion.2), channel_id=1, source_target_pairs={{1,3},{3,5},{5,7},{6,4},{4,2},{2,0},{9,11},{11,13},{13,15},{14,12}... | collective-permute-start | bytes 1671176 | tf_op jit(solution)/shard_map/ppermute | solution.py:40
  55.3 1.2 %fusion = f32[128,16,128]{2,0,1:T(8,128)S(1)} fusion(f32[16,128,128]{1,2,0:T(8,128)S(1)} %copy-done.5, bf16[128,16,128]{0,2,1:T(8,128)(2,1)S(1)} %bitcast.135), kind=kOutput, calls=%fused_computation.8 | convolution fusion | flops 402915328 | bytes 2621440 | tf_op jit(solution)/shard_map/hts,the->she/dot_general | solution.py:139
  56.6 1.3 %copy.45 = f32[128,16,128]{0,2,1:T(8,128)} copy(f32[128,16,128]{2,0,1:T(8,128)S(1)} %fusion) | data formatting | bytes 2097152 | tf_op jit(solution)/shard_map/mul | solution.py:139
  58.4 11.6 %collective-permute-done.5 = bf16[16,136,128]{2,1,0:T(8,128)(2,1)} collective-permute-done((bf16[16,136,128]{2,1,0:T(8,128)(2,1)}, bf16[16,136,128]{2,1,0:T(8,128)(2,1)}, u32[]{:S(2)}, u32[]{:S(2)}) %collective-permute-start.5) | collective-permute-done | bytes 557088 | tf_op jit(solution)/shard_map/ppermute | solution.py:40
  70.0 1.1 %fusion.39 = (f32[16]{0:T(128)S(1)}, f32[16]{0:T(128)S(1)}) fusion(bf16[16,136,128]{2,1,0:T(8,128)(2,1)} %collective-permute-done.5, bf16[16,136,128]{2,1,0:T(8,128)(2,1)} %collective-permute-done.4), kind=kLoop, calls=%fused_computation.96 | loop fusion | flops 112 | bytes 256 | tf_op jit(solution)/shard_map/add | solution.py:35
  71.1 2.2 %multiply_add_fusion = (f32[16,128,128]{2,1,0:T(8,128)S(1)}, f32[16,128,128]{2,1,0:T(8,128)S(1)}) fusion(f32[16,136,128]{2,1,0:T(8,128)} %collective-permute-done.3, f32[16]{0:T(128)S(1)} %get-tuple-element.5, bf16[16,136,128]{2,1,0:T(8,128)(2,1)} %collective-permute-done.6, f32[16]{0:T(128)S(1)} %get-tuple-element.8, ...), kind=kLoop, calls=%fused_computation.44 | loop fusion | flops 2359296 | bytes 4718784 | tf_op jit(solution)/shard_map/add | solution.py:86
  74.4 1.2 %convolution_multiply_fusion.3 = f32[16,128,128]{2,1,0:T(8,128)S(1)} fusion(bf16[128,16,128]{0,2,1:T(8,128)(2,1)S(1)} %bitcast.144, f32[16,128,128]{1,2,0:T(8,128)S(1)} %fusion.1), kind=kOutput, calls=%fused_computation.10 | convolution fusion | flops 402915328 | bytes 2621440 | tf_op jit(solution)/shard_map/hts,thd->shd/dot_general | solution.py:135
  75.6 1.2 %fusion.13 = bf16[128,2048]{0,1:T(8,128)(2,1)S(1)} fusion(f32[16,128,128]{2,1,0:T(8,128)S(1)} %convolution_multiply_fusion.3, f32[16,128,128]{2,1,0:T(8,128)S(1)} %convolution_multiply_fusion.4, f32[128,16,128]{0,2,1:T(8,128)S(1)} %copy-done.2, bf16[1,128,2048]{1,2,0:T(8,128)(2,1)S(1)} %copy.34, f32[2048]{0:T(1024)S(1)} %bitcast.156, f32[2048]{0:T(1024)S(1)} %bitcast.152, ...), kind=kLoop, calls=%fused_computation.32 | loop fusion | flops 2097152 | bytes 4218880 | tf_op jit(solution)/shard_map/convert_element_type | solution.py:144
  76.8 2.5 %collective-permute-start = (bf16[128,2048]{0,1:T(8,128)(2,1)S(1)}, bf16[128,2048]{0,1:T(8,128)(2,1)S(1)}, u32[]{:S(2)}, u32[]{:S(2)}) collective-permute-start(bf16[128,2048]{0,1:T(8,128)(2,1)S(1)} %fusion.13), channel_id=1, source_target_pairs={{0,24},{8,0},{16,8},{24,16},{1,25},{9,1},{17,9},{25,17},{2,26},{10... | collective-permute-start | bytes 1572872 | tf_op jit(solution)/shard_map/ppermute | solution.py:93
  79.3 1.0 %fusion.2 = f32[128,16,128]{0,2,1:T(8,128)S(1)} fusion(bf16[128,16,128]{0,2,1:T(8,128)(2,1)S(1)} %bitcast.142, f32[128,16]{0,1:T(8,128)S(1)} %copy.51, f32[16,128,128]{2,1,0:T(8,128)S(1)} %collective-permute-done.7, f32[16,128,128]{2,1,0:T(8,128)S(1)} %get-tuple-element.9, pred[]{:T(512)S(6)} %eq.32), kind=kOutput, calls=%fused_computation.15 | convolution fusion | flops 403177472 | bytes 3678209 | tf_op jit(solution)/shard_map/shd,hde->she/dot_general | solution.py:173
  80.3 0.7 fusion.3
  81.7 9.4 %collective-permute-done = bf16[128,2048]{0,1:T(8,128)(2,1)S(1)} collective-permute-done((bf16[128,2048]{0,1:T(8,128)(2,1)S(1)}, bf16[128,2048]{0,1:T(8,128)(2,1)S(1)}, u32[]{:S(2)}, u32[]{:S(2)}) %collective-permute-start) | collective-permute-done | bytes 524320 | tf_op jit(solution)/shard_map/ppermute | solution.py:93
  91.1 1.2 %fusion.22 = bf16[1,128,2048]{1,2,0:T(8,128)(2,1)S(1)} fusion(bf16[128,2048]{0,1:T(8,128)(2,1)S(1)} %collective-permute-done, f32[128,16,128]{0,2,1:T(8,128)S(1)} %fusion.2, f32[128,16,128]{0,2,1:T(8,128)S(1)} %fusion.3, f32[128,16,128]{0,2,1:T(8,128)S(1)} %fusion.4, f32[2048]{0:T(1024)S(1)} %get-tuple-element.22, f32[2048]{0:T(1024)S(1)} %get-tuple-element.23, ...), kind=kLoop, calls=%fused_computation.52 | loop fusion | flops 2621440 | bytes 4218880 | tf_op jit(solution)/shard_map/broadcast_in_dim | solution.py:199
  92.3 1.0 %copy.60 = bf16[1,128,2048]{2,1,0:T(8,128)(2,1)} copy(bf16[1,128,2048]{1,2,0:T(8,128)(2,1)S(1)} %fusion.22) | data formatting | bytes 1048576 | tf_op jit(solution)/shard_map/broadcast_in_dim | solution.py:199
  (74 shorter events, 6.0 us)
Async XLA Ops:
  0.0 8.7 %copy-start.6 = (bf16[1,128,2048]{2,1,0:T(8,128)(2,1)S(1)}, bf16[1,128,2048]{2,1,0:T(8,128)(2,1)}, u32[]{:S(2)}) copy-start(bf16[1,128,2048]{2,1,0:T(8,128)(2,1)} %param.5) | copy-start | bytes 1572868
  2.3 7.6 %collective-permute-start.1 = (f32[6178]{0:T(1024)S(1)}, f32[6178]{0:T(1024)S(1)}, u32[]{:S(2)}, u32[]{:S(2)}) collective-permute-start(f32[6178]{0:T(1024)S(1)} %concatenate.11), channel_id=1, source_target_pairs={{0,24},{8,0},{16,8},{24,16},{1,25},{9,1},{17,9},{25,17},{2,26},{10... | collective-permute-start | bytes 74144 | tf_op jit(solution)/shard_map/ppermute | solution.py:93
  8.9 0.7 copy-start.10
  9.0 0.7 copy-start.9
  9.1 24.8 %collective-permute-start.2 = (bf16[2,128,2048]{1,2,0:T(8,128)(2,1)S(1)}, bf16[2,128,2048]{1,2,0:T(8,128)(2,1)}, u32[]{:S(2)}, u32[]{:S(2)}) collective-permute-start(bf16[2,128,2048]{1,2,0:T(8,128)(2,1)S(1)} %pad_maximum_fusion.1), channel_id=1, source_target_pairs={{0,24},{8,0},{16,8},{24,16},{1,25},{9,1},{17,9},{25,17},{2,26},{10... | collective-permute-start | bytes 3145736 | tf_op jit(solution)/shard_map/ppermute | solution.py:93
  35.8 0.8 copy-start
  41.2 1.1 %copy-start.8 = (f32[1,3,2048]{2,0,1:T(1,128)S(1)}, f32[1,3,2048]{2,0,1:T(1,128)}, u32[]{:S(2)}) copy-start(f32[1,3,2048]{2,0,1:T(1,128)} %param.7) | copy-start | bytes 73732
  42.3 5.1 %collective-permute-start.3 = (f32[16,136,128]{2,1,0:T(8,128)}, f32[16,136,128]{2,1,0:T(8,128)}, u32[]{:S(2)}, u32[]{:S(2)}) collective-permute-start(f32[16,136,128]{2,1,0:T(8,128)} %pad_maximum_fusion), channel_id=1, source_target_pairs={{0,1},{2,3},{4,5},{6,7},{1,0},{3,2},{5,4},{7,6},{8,9},{10,11},{12,... | collective-permute-start | bytes 3342344 | tf_op jit(solution)/shard_map/ppermute | solution.py:63
  50.5 4.8 %copy-start.5 = (f32[16,128,128]{1,2,0:T(8,128)S(1)}, f32[16,128,128]{1,2,0:T(8,128)}, u32[]{:S(2)}) copy-start(f32[16,128,128]{1,2,0:T(8,128)} %convolution_multiply_fusion.2) | copy-start | bytes 3145732
  51.4 19.7 %collective-permute-start.6 = (bf16[16,136,128]{2,1,0:T(8,128)(2,1)}, bf16[16,136,128]{2,1,0:T(8,128)(2,1)}, u32[]{:S(2)}, u32[]{:S(2)}) collective-permute-start(bf16[16,136,128]{2,1,0:T(8,128)(2,1)} %pad_maximum_fusion.2), channel_id=1, source_target_pairs={{1,7},{6,0},{9,15},{14,8},{17,23},{22,16},{25,31},{30,24}} | collective-permute-start | bytes 1671176 | tf_op jit(solution)/shard_map/ppermute | solution.py:40
  52.7 17.3 %collective-permute-start.5 = (bf16[16,136,128]{2,1,0:T(8,128)(2,1)}, bf16[16,136,128]{2,1,0:T(8,128)(2,1)}, u32[]{:S(2)}, u32[]{:S(2)}) collective-permute-start(bf16[16,136,128]{2,1,0:T(8,128)(2,1)} %pad_maximum_fusion.2), channel_id=1, source_target_pairs={{1,5},{3,7},{6,2},{4,0},{9,13},{11,15},{14,10},{12,8},{17,21},{19,... | collective-permute-start | bytes 1671176 | tf_op jit(solution)/shard_map/ppermute | solution.py:40
  54.0 16.0 %collective-permute-start.4 = (bf16[16,136,128]{2,1,0:T(8,128)(2,1)}, bf16[16,136,128]{2,1,0:T(8,128)(2,1)}, u32[]{:S(2)}, u32[]{:S(2)}) collective-permute-start(bf16[16,136,128]{2,1,0:T(8,128)(2,1)} %pad_maximum_fusion.2), channel_id=1, source_target_pairs={{1,3},{3,5},{5,7},{6,4},{4,2},{2,0},{9,11},{11,13},{13,15},{14,12}... | collective-permute-start | bytes 1671176 | tf_op jit(solution)/shard_map/ppermute | solution.py:40
  56.6 1.3 %copy-start.7 = (bf16[128,2048]{0,1:T(8,128)(2,1)S(1)}, bf16[128,2048]{0,1:T(8,128)(2,1)}, u32[]{:S(2)}) copy-start(bf16[128,2048]{0,1:T(8,128)(2,1)} %get-tuple-element.16) | copy-start | bytes 1572868
  71.1 2.3 %copy-start.4 = (bf16[128,2048]{0,1:T(8,128)(2,1)S(1)}, bf16[128,2048]{0,1:T(8,128)(2,1)}, u32[]{:S(2)}) copy-start(bf16[128,2048]{0,1:T(8,128)(2,1)} %get-tuple-element.14) | copy-start | bytes 1572868
  73.3 1.0 %copy-start.3 = (bf16[128,2048]{0,1:T(8,128)(2,1)S(1)}, bf16[128,2048]{0,1:T(8,128)(2,1)}, u32[]{:S(2)}) copy-start(bf16[128,2048]{0,1:T(8,128)(2,1)} %get-tuple-element.15) | copy-start | bytes 1572868
  73.3 6.0 %collective-permute-start.7 = (f32[16,128,128]{2,1,0:T(8,128)S(1)}, f32[16,128,128]{2,1,0:T(8,128)S(1)}, u32[]{:S(2)}, u32[]{:S(2)}) collective-permute-start(f32[16,128,128]{2,1,0:T(8,128)S(1)} %get-tuple-element.10), channel_id=1, source_target_pairs={{0,1},{2,3},{4,5},{6,7},{1,0},{3,2},{5,4},{7,6},{8,9},{10,11},{12,... | collective-permute-start | bytes 3145736 | tf_op jit(solution)/shard_map/ppermute | solution.py:85
  74.3 1.2 %copy-start.2 = (f32[128,16,128]{0,2,1:T(8,128)S(1)}, f32[128,16,128]{0,2,1:T(8,128)}, u32[]{:S(2)}) copy-start(f32[128,16,128]{0,2,1:T(8,128)} %copy.45) | copy-start | bytes 3145732
  75.6 3.7 %copy-start.1 = (bf16[128,2048]{0,1:T(8,128)(2,1)S(1)}, bf16[128,2048]{0,1:T(8,128)(2,1)}, u32[]{:S(2)}) copy-start(bf16[128,2048]{0,1:T(8,128)(2,1)} %copy-done) | copy-start | bytes 1572868
  76.8 14.3 %collective-permute-start = (bf16[128,2048]{0,1:T(8,128)(2,1)S(1)}, bf16[128,2048]{0,1:T(8,128)(2,1)S(1)}, u32[]{:S(2)}, u32[]{:S(2)}) collective-permute-start(bf16[128,2048]{0,1:T(8,128)(2,1)S(1)} %fusion.13), channel_id=1, source_target_pairs={{0,24},{8,0},{16,8},{24,16},{1,25},{9,1},{17,9},{25,17},{2,26},{10... | collective-permute-start | bytes 1572872 | tf_op jit(solution)/shard_map/ppermute | solution.py:93

commit v10 on v5

--- a/solution.py
+++ b/solution.py
@@ -3,6 +3,7 @@
 import jax
 import jax.numpy as jnp
 from jax import lax
+from jax.experimental.layout import Layout, with_layout_constraint
 from jax.sharding import PartitionSpec as P
 
 CH = 64
@@ -62,6 +63,7 @@
     sent = packed(jnp.where(odd, backward_part, forward_part), rate)
     lower, lower_rate = unpacked(lax.ppermute(sent, axis, swap))
     window = packed(rate[:, None, None] * lower + mine, rate * lower_rate)
+    window, held = lax.optimization_barrier((window, held))
     if couples <= 4:
         incoming = jnp.zeros_like(mine)
         weight = jnp.ones_like(rate)
@@ -82,7 +84,6 @@
             moves = [(2 * p + 1, 2 * (p + 1 + covered) + 1) for p in range(couples - 1 - covered)]
             nearer = merged(sent_narrow(window, axis, both_ways(count, moves)), nearer)
         incoming = unpacked(nearer)[0]
-    incoming, held = lax.optimization_barrier((incoming, held))
     other = lax.ppermute(incoming, axis, swap)
     own = lower_rate[:, None, None] * incoming + lower
     return jnp.where(odd, own, other), jnp.where(odd, other, own), held
@@ -137,6 +138,14 @@
         "shd,she->hde", queries * growth[:, :, None], grad_rows, precision=HIGH
     )
     whole_decay = jnp.exp(cumul[-1])
+    state_in, adjoint_in, held = scans_in(
+        forward_part, adjoint_part, whole_decay, "ctx", (query_half, key_half, value_half, grad_half)
+    )
+    query_half, key_half, value_half, grad_half = held
+    queries = query_half.astype(jnp.float32)
+    key_rows = key_half.astype(jnp.float32)
+    value_rows = value_half.astype(jnp.float32)
+    grad_rows = grad_half.astype(jnp.float32)
     cum_heads = cumul.T
     gap = cum_heads[:, :, None] - cum_heads[:, None, :]
     lower = jnp.arange(rows)[:, None] >= jnp.arange(rows)[None, :]
@@ -155,10 +164,10 @@
     near_total = near_total + gain[0] * query_near.reshape(rows, width)
     near_total = near_total + gain[1] * key_near.reshape(rows, width)
     near_total = near_total + gain[2] * value_near.reshape(rows, width)
-    near_round = near_total.astype(jnp.bfloat16)
+    near_round = with_layout_constraint(near_total.astype(jnp.bfloat16), Layout((1, 0)))
     near_received = passed_along(near_round, "section", -1)
-    state_in, adjoint_in, near_received = scans_in(
-        forward_part, adjoint_part, whole_decay, "ctx", near_received
+    near_received, state_in, adjoint_in = lax.optimization_barrier(
+        (near_received, state_in, adjoint_in)
     )
     query_far = (
         scale * growth[:, :, None] * jnp.einsum("the,hde->thd", grad_rows, state_in, precision=HIGH)
@@ -168,7 +177,7 @@
     far_total = gain[0] * query_far.reshape(rows, width)
     far_total = far_total + gain[1] * key_far.reshape(rows, width)
     far_total = far_total + gain[2] * value_far.reshape(rows, width)
-    far_round = far_total.astype(jnp.bfloat16)
+    far_round = with_layout_constraint(far_total.astype(jnp.bfloat16), Layout((1, 0)))
     far_received = passed_along(far_round, "section", -1)
     received = (near_received.astype(jnp.float32) + far_received.astype(jnp.float32)).astype(
         jnp.bfloat16

time: 71.6 us -> 78.3 us (1.094)
  waiting for transfers between devices: 23.3 us -> 36.4 us
  matrix products: 12.5 us -> 9.43 us
  local copies, waits for them, and re-layouts: 8.91 us -> 6.95 us
  starting transfers between devices: 13.3 us -> 12.2 us
    ppermute x2, waiting for transfers between devices: 11.7 us -> 21.3 us  [passed_along(): return lax.ppermute(value, axis, pairs)]
    ppermute x3, waiting for transfers between devices: 10.6 us -> 14.8 us  [sent_narrow(): return widen(lax.ppermute(narrow(message), axis, pairs))]
    mul x1 -> x0, local copies, waits for them, and re-layouts: 2.56 us -> none  [local(): scale * jnp.einsum('hts,the->she', attention, grad_rows, precision=HIGH)]
    select_n x0 -> x1, other arithmetic: none -> 1.89 us  [scans_in(): return (jnp.where(odd, own, other), jnp.where(odd, other, own), held)]
    dot_general x1, matrix products: 2.18 us -> 0.66 us  [local(): jnp.einsum('hts,thd->shd', mixing, queries, precision=HIGH)]
    convert_element_type x3 -> x2, other arithmetic: 4.33 us -> 3.09 us  [the longest x1 1.89 us: local(): near_total.astype(jnp.bfloat16)]
    add x1, other arithmetic: 1.43 us -> 0.4 us  [scans_in(): incoming = incoming + weight[:, None, None] * got]
    ppermute x1, waiting for transfers between devices: 0.93 us -> 0.01 us  [scans_in(): other = lax.ppermute(incoming, axis, swap)]
  transfers between devices with their start and end apart: 7 -> 7, of which waited for: 4 -> 5; matrix products, arithmetic and copies ran while one was open for 23% -> 13% of each run, Pallas kernels for 0% -> 0%
where the time goes in v10:
time: 78.3 us; the launch traced here: 77.8 us
  waiting for transfers between devices  36.4 us (46%)
  other arithmetic  12.5 us (16%)
  starting transfers between devices  12.2 us (16%)
  matrix products  9.43 us (12%)
  local copies, waits for them, and re-layouts  6.95 us (9%)
    ppermute x2, waiting for transfers between devices, passed_along(): return lax.ppermute(value, axis, pairs)  21.3 us
    ppermute x3, waiting for transfers between devices, sent_narrow(): return widen(lax.ppermute(narrow(message), axis, pairs))  14.8 us
    ppermute x2, starting transfers between devices, passed_along(): return lax.ppermute(value, axis, pairs)  7.83 us
    ppermute x3, starting transfers between devices, sent_narrow(): return widen(lax.ppermute(narrow(message), axis, pairs))  3.88 us
    unnamed x7, local copies, waits for them, and re-layouts  3.75 us
    select_n x1, other arithmetic, scans_in(): return (jnp.where(odd, own, other), jnp.where(odd, other, own), held)  1.89 us
    convert_element_type x1, other arithmetic, local(): near_total.astype(jnp.bfloat16)  1.89 us
    dot_general x1, matrix products, local(): jnp.einsum('shd,she->hde', queries * growth[:, :, None], grad_rows, preci...  1.77 us
  transfers between devices with their start and end apart: 7, of which 5 were waited for; matrix products, arithmetic and copies ran while one was open for 13% of the time, Pallas kernels for 0%

profile of v10, /device:TPU:0, one launch (start us, length us, event | category | flops | bytes accessed | tf_op | source)
XLA Modules:
  0.0 77.8 jit_solution(10391504477497614979)
XLA Ops:
  0.1 0.7 compare_bitcast_fusion
  0.9 0.7 log_bitcast_fusion
  1.9 0.7 fusion.32
  2.6 1.3 %copy.27 = bf16[1,128,2048]{1,2,0:T(8,128)(2,1)S(1)} copy(bf16[1,128,2048]{2,1,0:T(8,128)(2,1)} %param.5) | data formatting | bytes 1048576 | tf_op args[0]
  4.0 1.0 %fusion.4 = (bf16[128,2048]{0,1:T(8,128)(2,1)S(1)}, bf16[128,2048]{0,1:T(8,128)(2,1)S(1)}, bf16[128,2048]{0,1:T(8,128)(2,1)S(1)}) fusion(bf16[1,128,2048]{1,2,0:T(8,128)(2,1)S(1)} %copy.27, f32[2048]{0:T(1024)S(1)} %bitcast.123, f32[2048]{0:T(1024)S(1)} %bitcast.129, f32[2048]{0:T(1024)S(1)} %bitcast.126), kind=kLoop, calls=%fused_computation.18 | loop fusion | flops 1835008 | bytes 2121728 | tf_op jit(solution)/shard_map/convert_element_type | solution.py:111
  5.3 1.2 %fusion.13 = f32[16,128,128]{2,1,0:T(8,128)S(1)} fusion(bf16[128,16,128]{0,2,1:T(8,128)(2,1)S(1)} %bitcast.118, bf16[128,16,128]{0,2,1:T(8,128)(2,1)S(1)} %bitcast.111, f32[128,16]{0,1:T(8,128)S(1)} %copy.30), kind=kOutput, calls=%fused_computation.39 | convolution fusion | flops 403177472 | bytes 2105344 | tf_op jit(solution)/shard_map/shd,she->hde/dot_general | solution.py:134
  6.5 1.8 %broadcast_select_fusion.2 = (f32[16,128,128]{2,1,0:T(8,128)S(1)}, f32[16,128,128]{2,1,0:T(8,128)}) fusion(f32[16,128,128]{2,1,0:T(8,128)S(1)} %fusion.13, pred[]{:T(512)S(6)} %eq.29, bf16[128,16,128]{2,1,0:T(8,128)(2,1)S(1)} %bitcast.107, bf16[128,16,128]{0,2,1:T(8,128)(2,1)S(1)} %bitcast.115, f32[128,16]{0,1:T(8,128)S(1)} %copy.28), kind=kOutput, calls=%fused_computation.51 | convolution fusion | flops 403701760 | bytes 4202497 | tf_op jit(solution)/shard_map/shd,she->hde/dot_general | solution.py:137
  8.3 1.1 %pad_maximum_fusion = f32[16,136,128]{2,1,0:T(8,128)} fusion(f32[16,8,128]{2,1,0:T(8,128)S(1)} %broadcast_in_dim.32, f32[16,128,128]{2,1,0:T(8,128)S(1)} %get-tuple-element.38), kind=kLoop, calls=%fused_computation.15 | loop fusion | flops 278528 | bytes 2228224 | tf_op jit(solution)/shard_map/concatenate | solution.py:17
  9.5 0.5 collective-permute-start
  9.9 2.0 %copy.26 = bf16[1,128,2048]{1,2,0:T(8,128)(2,1)} copy(bf16[1,128,2048]{2,1,0:T(8,128)(2,1)} %param.6) | data formatting | bytes 1048576 | tf_op args[1]
  12.6 1.7 %select_add_fusion = f32[16,128,128]{2,1,0:T(8,128)S(1)} fusion(f32[16,128,128]{2,1,0:T(8,128)S(1)} %fusion.13, f32[16,128,128]{2,1,0:T(8,128)} %get-tuple-element.39, f32[16,136,128]{2,1,0:T(8,128)} %collective-permute-done, f32[16]{0:T(128)S(1)} %fusion.30, pred[]{:T(512)S(6)} %eq.29), kind=kLoop, calls=%fused_computation.38 | loop fusion | flops 786432 | bytes 4194369 | tf_op jit(solution)/shard_map/add | solution.py:65
  14.4 1.0 %slice_reduce_fusion.1 = (f32[16]{0:T(128)S(1)}, f32[16]{0:T(128)S(1)}) fusion(f32[16,136,128]{2,1,0:T(8,128)} %collective-permute-done, f32[16,1,1]{2,1,0:T(1,128)S(1)} %copy.32), kind=kLoop, calls=%fused_computation.69 | loop fusion | flops 16 | bytes 256 | tf_op jit(solution)/shard_map/slice | solution.py:22
  16.3 1.3 %collective-permute-start.2 = (bf16[16,136,128]{2,1,0:T(8,128)(2,1)S(1)}, bf16[16,136,128]{2,1,0:T(8,128)(2,1)S(1)}, u32[]{:S(2)}, u32[]{:S(2)}) collective-permute-start(bf16[16,136,128]{2,1,0:T(8,128)(2,1)S(1)} %pad_maximum_fusion.2), channel_id=1, source_target_pairs={{1,3},{3,5},{5,7},{6,4},{4,2},{2,0},{9,11},{11,13},{13,15},{14,12}... | collective-permute-start | bytes 1671176 | tf_op jit(solution)/shard_map/ppermute | solution.py:41
  17.6 1.3 %collective-permute-start.3 = (bf16[16,136,128]{2,1,0:T(8,128)(2,1)S(1)}, bf16[16,136,128]{2,1,0:T(8,128)(2,1)S(1)}, u32[]{:S(2)}, u32[]{:S(2)}) collective-permute-start(bf16[16,136,128]{2,1,0:T(8,128)(2,1)S(1)} %pad_maximum_fusion.2), channel_id=1, source_target_pairs={{1,5},{3,7},{6,2},{4,0},{9,13},{11,15},{14,10},{12,8},{17,21},{19,... | collective-permute-start | bytes 1671176 | tf_op jit(solution)/shard_map/ppermute | solution.py:41
  18.9 1.3 %collective-permute-start.4 = (bf16[16,136,128]{2,1,0:T(8,128)(2,1)S(1)}, bf16[16,136,128]{2,1,0:T(8,128)(2,1)S(1)}, u32[]{:S(2)}, u32[]{:S(2)}) collective-permute-start(bf16[16,136,128]{2,1,0:T(8,128)(2,1)S(1)} %pad_maximum_fusion.2), channel_id=1, source_target_pairs={{1,7},{6,0},{9,15},{14,8},{17,23},{22,16},{25,31},{30,24}} | collective-permute-start | bytes 1671176 | tf_op jit(solution)/shard_map/ppermute | solution.py:41
  20.6 1.2 %convolution_multiply_fusion.3 = f32[16,128,128]{2,1,0:T(8,128)S(1)} fusion(bf16[128,16,128]{0,2,1:T(8,128)(2,1)S(1)} %bitcast.112, f32[16,128,128]{2,1,0:T(8,128)S(1)} %convolution_multiply_fusion.4), kind=kOutput, calls=%fused_computation.6 | convolution fusion | flops 402915328 | bytes 2621440 | tf_op jit(solution)/shard_map/hts,shd->thd/dot_general | solution.py:157
  21.9 0.7 convolution_multiply_fusion.2
  22.5 11.7 %collective-permute-done.2 = bf16[16,136,128]{2,1,0:T(8,128)(2,1)S(1)} collective-permute-done((bf16[16,136,128]{2,1,0:T(8,128)(2,1)S(1)}, bf16[16,136,128]{2,1,0:T(8,128)(2,1)S(1)}, u32[]{:S(2)}, u32[]{:S(2)}) %collective-permute-start.2) | collective-permute-done | bytes 557088 | tf_op jit(solution)/shard_map/ppermute | solution.py:41
  34.3 3.1 %collective-permute-done.3 = bf16[16,136,128]{2,1,0:T(8,128)(2,1)S(1)} collective-permute-done((bf16[16,136,128]{2,1,0:T(8,128)(2,1)S(1)}, bf16[16,136,128]{2,1,0:T(8,128)(2,1)S(1)}, u32[]{:S(2)}, u32[]{:S(2)}) %collective-permute-start.3) | collective-permute-done | bytes 557088 | tf_op jit(solution)/shard_map/ppermute | solution.py:41
  38.0 0.5 convolution_multiply_fusion.1
  38.6 0.8 convolution_multiply_fusion
  39.6 1.9 %fusion.7 = bf16[128,2048]{0,1:T(8,128)(2,1)} fusion(f32[16,128,128]{2,1,0:T(8,128)S(1)} %convolution_multiply_fusion, f32[16,128,128]{2,1,0:T(8,128)S(1)} %convolution_multiply_fusion.2, f32[16,128,128]{2,1,0:T(8,128)S(1)} %convolution_multiply_fusion.3, bf16[1,128,2048]{1,2,0:T(8,128)(2,1)S(1)} %copy-done.1, f32[2048]{0:T(1024)S(1)} %bitcast.130, ...), kind=kLoop, calls=%fused_computation.23 | loop fusion | flops 2097152 | bytes 4218880 | tf_op jit(solution)/shard_map/convert_element_type | solution.py:167
  41.5 3.6 %collective-permute-start.1 = (bf16[128,2048]{0,1:T(8,128)(2,1)}, bf16[128,2048]{0,1:T(8,128)(2,1)S(1)}, u32[]{:S(2)}, u32[]{:S(2)}) collective-permute-start(bf16[128,2048]{0,1:T(8,128)(2,1)} %fusion.7), channel_id=1, source_target_pairs={{0,24},{8,0},{16,8},{24,16},{1,25},{9,1},{17,9},{25,17},{2,26},{10... | collective-permute-start | bytes 1572872 | tf_op jit(solution)/shard_map/ppermute | solution.py:95
  45.2 1.9 %broadcast_select_fusion = (f32[16,128,128]{2,1,0:T(8,128)S(1)}, f32[16,128,128]{2,1,0:T(8,128)S(1)}) fusion(f32[16,128,128]{2,1,0:T(8,128)} %collective-permute-done.5, pred[]{:T(512)S(6)} %eq.29, f32[16,136,128]{2,1,0:T(8,128)} %collective-permute-done, f32[16,128,128]{2,1,0:T(8,128)S(1)} %multiply_add_fusion.1, f32[16]{0:T(128)S(1)} %get-tuple-element.21), kind=kLoop, calls=%fused_computation.49 | loop fusion | flops 1048576 | bytes 5242945 | tf_op jit(solution)/shard_map/jit(_where)/select_n | solution.py:89
  47.1 10.2 %collective-permute-done.1 = bf16[128,2048]{0,1:T(8,128)(2,1)S(1)} collective-permute-done((bf16[128,2048]{0,1:T(8,128)(2,1)}, bf16[128,2048]{0,1:T(8,128)(2,1)S(1)}, u32[]{:S(2)}, u32[]{:S(2)}) %collective-permute-start.1) | collective-permute-done | bytes 524320 | tf_op jit(solution)/shard_map/ppermute | solution.py:95
  57.3 0.6 fusion.1
  57.9 1.0 %fusion = f32[128,16,128]{0,2,1:T(8,128)S(1)} fusion(f32[16,128,128]{2,1,0:T(8,128)S(1)} %get-tuple-element.20, bf16[128,16,128]{0,2,1:T(8,128)(2,1)S(1)} %bitcast.114, f32[128,16]{0,1:T(8,128)S(1)} %copy.30), kind=kOutput, calls=%fused_computation.10 | convolution fusion | flops 402915328 | bytes 2629632 | tf_op jit(solution)/shard_map/shd,hde->she/dot_general | solution.py:176
  58.9 1.2 %fusion.2 = f32[128,16,128]{0,2,1:T(8,128)S(1)} fusion(f32[16,128,128]{2,1,0:T(8,128)S(1)} %get-tuple-element.19, f32[128,16]{0,1:T(8,128)S(1)} %copy.40, bf16[128,16,128]{2,1,0:T(8,128)(2,1)S(1)} %bitcast.110), kind=kOutput, calls=%fused_computation.14 | convolution fusion | flops 402915328 | bytes 2629632 | tf_op jit(solution)/shard_map/the,hde->thd/dot_general | solution.py:173
  60.2 1.2 %fusion.11 = bf16[128,2048]{0,1:T(8,128)(2,1)S(1)} fusion(f32[128,16,128]{0,2,1:T(8,128)S(1)} %fusion, f32[128,16,128]{0,2,1:T(8,128)S(1)} %fusion.1, f32[128,16,128]{0,2,1:T(8,128)S(1)} %fusion.2, f32[2048]{0:T(1024)S(1)} %bitcast.131, f32[2048]{0:T(1024)S(1)} %bitcast.125, f32[2048]{0:T(1024)S(1)} %bitcast.128), kind=kLoop, calls=%fused_computation.30 | loop fusion | flops 1572864 | bytes 3694592 | tf_op jit(solution)/shard_map/convert_element_type | solution.py:180
  61.4 4.2 %collective-permute-start.6 = (bf16[128,2048]{0,1:T(8,128)(2,1)S(1)}, bf16[128,2048]{0,1:T(8,128)(2,1)S(1)}, u32[]{:S(2)}, u32[]{:S(2)}) collective-permute-start(bf16[128,2048]{0,1:T(8,128)(2,1)S(1)} %fusion.11), channel_id=1, source_target_pairs={{0,24},{8,0},{16,8},{24,16},{1,25},{9,1},{17,9},{25,17},{2,26},{10... | collective-permute-start | bytes 1572872 | tf_op jit(solution)/shard_map/ppermute | solution.py:95
  65.6 11.1 %collective-permute-done.6 = bf16[128,2048]{0,1:T(8,128)(2,1)S(1)} collective-permute-done((bf16[128,2048]{0,1:T(8,128)(2,1)S(1)}, bf16[128,2048]{0,1:T(8,128)(2,1)S(1)}, u32[]{:S(2)}, u32[]{:S(2)}) %collective-permute-start.6) | collective-permute-done | bytes 524320 | tf_op jit(solution)/shard_map/ppermute | solution.py:95
  76.8 1.0 %copy.45 = bf16[1,128,2048]{2,1,0:T(8,128)(2,1)} copy(bf16[1,128,2048]{1,2,0:T(8,128)(2,1)S(1)} %fusion.18) | data formatting | bytes 1048576 | tf_op jit(solution)/shard_map/broadcast_in_dim | solution.py:185
  (46 shorter events, 4.0 us)
Async XLA Ops:
  4.0 1.2 %copy-start = (bf16[1,128,2048]{2,1,0:T(8,128)(2,1)S(1)}, bf16[1,128,2048]{2,1,0:T(8,128)(2,1)}, u32[]{:S(2)}) copy-start(bf16[1,128,2048]{2,1,0:T(8,128)(2,1)} %param.6) | copy-start | bytes 1572868
  9.5 3.2 %collective-permute-start = (f32[16,136,128]{2,1,0:T(8,128)}, f32[16,136,128]{2,1,0:T(8,128)}, u32[]{:S(2)}, u32[]{:S(2)}) collective-permute-start(f32[16,136,128]{2,1,0:T(8,128)} %pad_maximum_fusion), channel_id=1, source_target_pairs={{0,1},{2,3},{4,5},{6,7},{1,0},{3,2},{5,4},{7,6},{8,9},{10,11},{12,... | collective-permute-start | bytes 3342344 | tf_op jit(solution)/shard_map/ppermute | solution.py:64
  16.3 17.9 %collective-permute-start.2 = (bf16[16,136,128]{2,1,0:T(8,128)(2,1)S(1)}, bf16[16,136,128]{2,1,0:T(8,128)(2,1)S(1)}, u32[]{:S(2)}, u32[]{:S(2)}) collective-permute-start(bf16[16,136,128]{2,1,0:T(8,128)(2,1)S(1)} %pad_maximum_fusion.2), channel_id=1, source_target_pairs={{1,3},{3,5},{5,7},{6,4},{4,2},{2,0},{9,11},{11,13},{13,15},{14,12}... | collective-permute-start | bytes 1671176 | tf_op jit(solution)/shard_map/ppermute | solution.py:41
  17.6 19.7 %collective-permute-start.3 = (bf16[16,136,128]{2,1,0:T(8,128)(2,1)S(1)}, bf16[16,136,128]{2,1,0:T(8,128)(2,1)S(1)}, u32[]{:S(2)}, u32[]{:S(2)}) collective-permute-start(bf16[16,136,128]{2,1,0:T(8,128)(2,1)S(1)} %pad_maximum_fusion.2), channel_id=1, source_target_pairs={{1,5},{3,7},{6,2},{4,0},{9,13},{11,15},{14,10},{12,8},{17,21},{19,... | collective-permute-start | bytes 1671176 | tf_op jit(solution)/shard_map/ppermute | solution.py:41
  18.9 18.6 %collective-permute-start.4 = (bf16[16,136,128]{2,1,0:T(8,128)(2,1)S(1)}, bf16[16,136,128]{2,1,0:T(8,128)(2,1)S(1)}, u32[]{:S(2)}, u32[]{:S(2)}) collective-permute-start(bf16[16,136,128]{2,1,0:T(8,128)(2,1)S(1)} %pad_maximum_fusion.2), channel_id=1, source_target_pairs={{1,7},{6,0},{9,15},{14,8},{17,23},{22,16},{25,31},{30,24}} | collective-permute-start | bytes 1671176 | tf_op jit(solution)/shard_map/ppermute | solution.py:41
  37.9 7.2 %collective-permute-start.5 = (f32[16,128,128]{2,1,0:T(8,128)S(1)}, f32[16,128,128]{2,1,0:T(8,128)}, u32[]{:S(2)}, u32[]{:S(2)}) collective-permute-start(f32[16,128,128]{2,1,0:T(8,128)S(1)} %multiply_add_fusion.1), channel_id=1, source_target_pairs={{0,1},{2,3},{4,5},{6,7},{1,0},{3,2},{5,4},{7,6},{8,9},{10,11},{12,... | collective-permute-start | bytes 3145736 | tf_op jit(solution)/shard_map/ppermute | solution.py:87
  38.6 1.0 %copy-start.1 = (bf16[1,128,2048]{1,2,0:T(8,128)(2,1)S(1)}, bf16[1,128,2048]{1,2,0:T(8,128)(2,1)}, u32[]{:S(2)}) copy-start(bf16[1,128,2048]{1,2,0:T(8,128)(2,1)} %copy.26) | copy-start | bytes 1572868
  41.5 15.8 %collective-permute-start.1 = (bf16[128,2048]{0,1:T(8,128)(2,1)}, bf16[128,2048]{0,1:T(8,128)(2,1)S(1)}, u32[]{:S(2)}, u32[]{:S(2)}) collective-permute-start(bf16[128,2048]{0,1:T(8,128)(2,1)} %fusion.7), channel_id=1, source_target_pairs={{0,24},{8,0},{16,8},{24,16},{1,25},{9,1},{17,9},{25,17},{2,26},{10... | collective-permute-start | bytes 1572872 | tf_op jit(solution)/shard_map/ppermute | solution.py:95
  61.4 15.3 %collective-permute-start.6 = (bf16[128,2048]{0,1:T(8,128)(2,1)S(1)}, bf16[128,2048]{0,1:T(8,128)(2,1)S(1)}, u32[]{:S(2)}, u32[]{:S(2)}) collective-permute-start(bf16[128,2048]{0,1:T(8,128)(2,1)S(1)} %fusion.11), channel_id=1, source_target_pairs={{0,24},{8,0},{16,8},{24,16},{1,25},{9,1},{17,9},{25,17},{2,26},{10... | collective-permute-start | bytes 1572872 | tf_op jit(solution)/shard_map/ppermute | solution.py:95

commit v11 on v7

--- a/solution.py
+++ b/solution.py
@@ -3,6 +3,7 @@
 import jax
 import jax.numpy as jnp
 from jax import lax
+from jax.experimental.layout import Layout, with_layout_constraint
 from jax.sharding import PartitionSpec as P
 
 CH = 64
@@ -50,10 +51,10 @@
     return list(moves) + [(count - 1 - source, count - 1 - target) for source, target in moves]
 
 
-def scans_in(forward_part, backward_part, rate, axis, middle, inputs):
+def scans_in(forward_part, backward_part, rate, axis, held, middle):
     count = lax.axis_size(axis)
     if count == 1:
-        return jnp.zeros_like(forward_part), jnp.zeros_like(backward_part), middle(*inputs)
+        return jnp.zeros_like(forward_part), jnp.zeros_like(backward_part), middle(*held)
     assert count % 2 == 0
     odd = lax.axis_index(axis) % 2 == 1
     couples = count // 2
@@ -62,17 +63,22 @@
     sent = packed(jnp.where(odd, backward_part, forward_part), rate)
     lower, lower_rate = unpacked(lax.ppermute(sent, axis, swap))
     window = packed(rate[:, None, None] * lower + mine, rate * lower_rate)
-    window, inputs = lax.optimization_barrier((window, inputs))
-    held = middle(*inputs)
+    window, held = lax.optimization_barrier((window, held))
     if couples <= 4:
+        arrived = []
+        for step in range(1, couples):
+            moves = [(2 * p + 1, 2 * (p + step) + 1) for p in range(couples - step)]
+            arrived.append(lax.ppermute(narrow(window), axis, both_ways(count, moves)))
+        made = middle(*held)
+        arrived, made = lax.optimization_barrier((arrived, made))
         incoming = jnp.zeros_like(mine)
         weight = jnp.ones_like(rate)
-        for step in range(1, couples):
-            moves = [(2 * p + 1, 2 * (p + step) + 1) for p in range(couples - step)]
-            got, got_rate = unpacked(sent_narrow(window, axis, both_ways(count, moves)))
+        for message in arrived:
+            got, got_rate = unpacked(widen(message))
             incoming = incoming + weight[:, None, None] * got
             weight = weight * got_rate
     else:
+        made = middle(*held)
         covered = 1
         while 2 * covered < couples:
             moves = [(2 * p + 1, 2 * (p + covered) + 1) for p in range(couples - covered)]
@@ -84,10 +90,9 @@
             moves = [(2 * p + 1, 2 * (p + 1 + covered) + 1) for p in range(couples - 1 - covered)]
             nearer = merged(sent_narrow(window, axis, both_ways(count, moves)), nearer)
         incoming = unpacked(nearer)[0]
-    incoming, held = lax.optimization_barrier((incoming, held))
     other = lax.ppermute(incoming, axis, swap)
     own = lower_rate[:, None, None] * incoming + lower
-    return jnp.where(odd, own, other), jnp.where(odd, other, own), held
+    return jnp.where(odd, own, other), jnp.where(odd, other, own), made
 
 
 def passed_along(value, axis, steps):
@@ -118,6 +123,9 @@
     rows, heads, head_dim = query_half.shape
     width = heads * head_dim
     scale = 1.0 / head_dim
+    queries = query_half.astype(jnp.float32)
+    key_rows = key_half.astype(jnp.float32)
+    grad_rows = grad_half.astype(jnp.float32)
     cum_heads = cumul.T
     gap = cum_heads[:, :, None] - cum_heads[:, None, :]
     lower = jnp.arange(rows)[:, None] >= jnp.arange(rows)[None, :]
@@ -126,17 +134,18 @@
         jnp.einsum("thd,shd->hts", grad_half, value_half, preferred_element_type=jnp.float32)
         * decay
     )
-    query_near = scale * jnp.einsum("hts,shd->thd", mixing, key_half.astype(jnp.float32), precision=HIGH)
-    key_near = scale * jnp.einsum("hts,thd->shd", mixing, query_half.astype(jnp.float32), precision=HIGH)
+    query_near = scale * jnp.einsum("hts,shd->thd", mixing, key_rows, precision=HIGH)
+    key_near = scale * jnp.einsum("hts,thd->shd", mixing, queries, precision=HIGH)
     attention = (
         jnp.einsum("thd,shd->hts", query_half, key_half, preferred_element_type=jnp.float32) * decay
     )
-    value_near = scale * jnp.einsum("hts,the->she", attention, grad_half.astype(jnp.float32), precision=HIGH)
+    value_near = scale * jnp.einsum("hts,the->she", attention, grad_rows, precision=HIGH)
     near_total = grad_block.astype(jnp.float32)
     near_total = near_total + gain[0] * query_near.reshape(rows, width)
     near_total = near_total + gain[1] * key_near.reshape(rows, width)
     near_total = near_total + gain[2] * value_near.reshape(rows, width)
-    return passed_along(near_total.astype(jnp.bfloat16), "section", -1)
+    near_round = with_layout_constraint(near_total.astype(jnp.bfloat16), Layout((1, 0)))
+    return passed_along(near_round, "section", -1)
 
 
 def local(inputs, out_grad, gains, exponent, boundary):
@@ -149,14 +158,14 @@
     scale = 1.0 / head_dim
     query_half, key_half, value_half = projections(block, gain, heads)
     grad_half = grad_block.reshape(rows, heads, head_dim)
+    queries = query_half.astype(jnp.float32)
+    key_rows = key_half.astype(jnp.float32)
+    value_rows = value_half.astype(jnp.float32)
+    grad_rows = grad_half.astype(jnp.float32)
     logs = decay_logs(exponent[0], boundary[0], CH).reshape(rows, heads)
     cumul = jnp.cumsum(logs, axis=0)
     growth = jnp.exp(cumul)
     tail = jnp.exp(cumul[-1][None, :] - cumul)
-    queries = query_half.astype(jnp.float32)
-    key_rows = key_half.astype(jnp.float32)
-    value_rows = value_half.astype(jnp.float32)
-    grad_rows = grad_half.astype(jnp.float32)
     forward_part = jnp.einsum(
         "shd,she->hde", key_rows * tail[:, :, None], value_rows, precision=HIGH
     )
@@ -169,8 +178,8 @@
         adjoint_part,
         whole_decay,
         "ctx",
+        (query_half, key_half, value_half, grad_half, cumul, grad_block, gain),
         near_terms,
-        (query_half, key_half, value_half, grad_half, cumul, grad_block, gain),
     )
     query_far = (
         scale * growth[:, :, None] * jnp.einsum("the,hde->thd", grad_rows, state_in, precision=HIGH)
@@ -180,7 +189,8 @@
     far_total = gain[0] * query_far.reshape(rows, width)
     far_total = far_total + gain[1] * key_far.reshape(rows, width)
     far_total = far_total + gain[2] * value_far.reshape(rows, width)
-    far_received = passed_along(far_total.astype(jnp.bfloat16), "section", -1)
+    far_round = with_layout_constraint(far_total.astype(jnp.bfloat16), Layout((1, 0)))
+    far_received = passed_along(far_round, "section", -1)
     received = (near_received.astype(jnp.float32) + far_received.astype(jnp.float32)).astype(
         jnp.bfloat16
     )

time: 86.9 us -> 74.5 us (0.86)
  local copies, waits for them, and re-layouts: 19.2 us -> 7.62 us
  waiting for transfers between devices: 17.8 us -> 22.6 us
  matrix products: 13.4 us -> 9.54 us
  other arithmetic: 16.4 us -> 15.4 us
    reshape x7 -> x0, local copies, waits for them, and re-layouts: 13.3 us -> none  [the longest x1 2.58 us: local(): far_total = far_total + gain[1] * key_far.reshape(rows, width)]
    ppermute x2, waiting for transfers between devices: 15.6 us -> 19.8 us  [passed_along(): return lax.ppermute(value, axis, pairs)]
    add x1 -> x0, other arithmetic: 2.77 us -> none  [scans_in(): incoming = incoming + weight[:, None, None] * got]
    ppermute x1, waiting for transfers between devices: 0.71 us -> 2.45 us  [scans_in(): other = lax.ppermute(incoming, axis, swap)]
    dot_general x1, matrix products: 2.19 us -> 0.7 us  [local(): jnp.einsum('she,hde->shd', value_rows, adjoint_in, precision=HIGH)]
    add x1, other arithmetic: 1.73 us -> 3.14 us  [scans_in(): own = lower_rate[:, None, None] * incoming + lower]
    ppermute x1, waiting for transfers between devices: 1.53 us -> 0.4 us  [scans_in(): lower, lower_rate = unpacked(lax.ppermute(sent, axis, swap))]
    dot_general x3, matrix products: 3.62 us -> 2.53 us  [the longest x1 1.21 us: near_terms(): jnp.einsum('hts,shd->thd', mixing, key_rows, precision=HIGH)]
  transfers between devices with their start and end apart: 7 -> 7, of which waited for: 4 -> 4; matrix products, arithmetic and copies ran while one was open for 22% -> 11% of each run, Pallas kernels for 0% -> 0%
where the time goes in v11:
time: 74.5 us; the launch traced here: 73.5 us
  waiting for transfers between devices  22.6 us (30%)
  starting transfers between devices  18 us (24%)
  other arithmetic  15.4 us (21%)
  matrix products  9.54 us (13%)
  local copies, waits for them, and re-layouts  7.62 us (10%)
    ppermute x2, waiting for transfers between devices, passed_along(): return lax.ppermute(value, axis, pairs)  19.8 us
    ppermute x2, starting transfers between devices, passed_along(): return lax.ppermute(value, axis, pairs)  9.36 us
    ppermute x1, starting transfers between devices, scans_in(): other = lax.ppermute(incoming, axis, swap)  4.34 us
    unnamed x14, local copies, waits for them, and re-layouts  3.91 us
    ppermute x3, starting transfers between devices, scans_in(): arrived.append(lax.ppermute(narrow(window), axis, both_ways(count, moves)))  3.86 us
    add x1, other arithmetic, scans_in(): own = lower_rate[:, None, None] * incoming + lower  3.14 us
    ppermute x1, waiting for transfers between devices, scans_in(): other = lax.ppermute(incoming, axis, swap)  2.45 us
    dot_general x1, matrix products, local(): jnp.einsum('shd,she->hde', queries * growth[:, :, None], grad_rows, preci...  1.77 us
  transfers between devices with their start and end apart: 7, of which 4 were waited for; matrix products, arithmetic and copies ran while one was open for 11% of the time, Pallas kernels for 0%

profile of v11, /device:TPU:0, one launch (start us, length us, event | category | flops | bytes accessed | tf_op | source)
XLA Modules:
  0.0 73.5 jit_solution(16700902918493178111)
XLA Ops:
  0.0 0.7 compare_bitcast_fusion
  1.0 0.7 log_bitcast_fusion
  2.0 0.7 %fusion.29 = (f32[1,1,2048]{2,0,1:T(1,128)S(1)}, f32[1,1,2048]{2,0,1:T(1,128)S(1)}, f32[1,1,2048]{2,0,1:T(1,128)S(1)}) fusion(f32[1,3,2048]{2,0,1:T(1,128)} %param.7), kind=kLoop, calls=%fused_computation.77 | loop fusion | bytes 49152 | tf_op jit(solution)/shard_map/slice | solution.py:117
  2.9 1.3 %copy.26 = bf16[1,128,2048]{1,2,0:T(8,128)(2,1)S(1)} copy(bf16[1,128,2048]{2,1,0:T(8,128)(2,1)} %param.5) | data formatting | bytes 1048576 | tf_op args[0]
  4.3 1.0 %fusion.5 = (bf16[128,2048]{0,1:T(8,128)(2,1)S(1)}, bf16[128,2048]{0,1:T(8,128)(2,1)S(1)}, bf16[128,2048]{0,1:T(8,128)(2,1)S(1)}) fusion(bf16[1,128,2048]{1,2,0:T(8,128)(2,1)S(1)} %copy.26, f32[2048]{0:T(1024)S(1)} %bitcast.127, f32[2048]{0:T(1024)S(1)} %bitcast.129, f32[2048]{0:T(1024)S(1)} %bitcast.131), kind=kLoop, calls=%fused_computation.19 | loop fusion | flops 1835008 | bytes 2121728 | tf_op jit(solution)/shard_map/convert_element_type | solution.py:117
  5.3 1.2 %fusion.14 = f32[16,128,128]{2,1,0:T(8,128)S(1)} fusion(bf16[128,16,128]{0,2,1:T(8,128)(2,1)S(1)} %bitcast.120, bf16[128,16,128]{0,2,1:T(8,128)(2,1)S(1)} %bitcast.113, f32[128,16]{0,1:T(8,128)S(1)} %copy.29), kind=kOutput, calls=%fused_computation.40 | convolution fusion | flops 403177472 | bytes 2105344 | tf_op jit(solution)/shard_map/shd,she->hde/dot_general | solution.py:169
  6.5 1.8 %broadcast_select_fusion.1 = (f32[16,128,128]{2,1,0:T(8,128)S(1)}, f32[16,128,128]{2,1,0:T(8,128)}) fusion(f32[16,128,128]{2,1,0:T(8,128)S(1)} %fusion.14, pred[]{:T(512)S(6)} %eq.29, bf16[128,16,128]{2,1,0:T(8,128)(2,1)S(1)} %bitcast.110, bf16[128,16,128]{0,2,1:T(8,128)(2,1)S(1)} %bitcast.117, f32[128,16]{0,1:T(8,128)S(1)} %copy.27), kind=kOutput, calls=%fused_computation.51 | convolution fusion | flops 403701760 | bytes 4202497 | tf_op jit(solution)/shard_map/shd,she->hde/dot_general | solution.py:172
  8.4 1.1 %pad_maximum_fusion = f32[16,136,128]{2,1,0:T(8,128)} fusion(f32[16,8,128]{2,1,0:T(8,128)S(1)} %broadcast_in_dim.32, f32[16,128,128]{2,1,0:T(8,128)S(1)} %get-tuple-element.49), kind=kLoop, calls=%fused_computation.15 | loop fusion | flops 278528 | bytes 2228224 | tf_op jit(solution)/shard_map/concatenate | solution.py:17
  10.0 2.0 %copy.32 = bf16[1,128,2048]{1,2,0:T(8,128)(2,1)} copy(bf16[1,128,2048]{2,1,0:T(8,128)(2,1)} %param.6) | data formatting | bytes 1048576 | tf_op args[1]
  12.7 1.7 %select_add_fusion = f32[16,128,128]{2,1,0:T(8,128)S(1)} fusion(f32[16,128,128]{2,1,0:T(8,128)S(1)} %fusion.14, f32[16,128,128]{2,1,0:T(8,128)} %get-tuple-element.50, f32[16,136,128]{2,1,0:T(8,128)} %collective-permute-done, f32[16]{0:T(128)S(1)} %fusion.26, pred[]{:T(512)S(6)} %eq.29), kind=kLoop, calls=%fused_computation.39 | loop fusion | flops 786432 | bytes 4194369 | tf_op jit(solution)/shard_map/add | solution.py:65
  14.4 1.0 %slice_reduce_fusion.1 = (f32[16]{0:T(128)S(1)}, f32[16]{0:T(128)S(1)}) fusion(f32[16,136,128]{2,1,0:T(8,128)} %collective-permute-done, f32[16,1,1]{2,1,0:T(1,128)S(1)} %copy.31), kind=kLoop, calls=%fused_computation.63 | loop fusion | flops 16 | bytes 256 | tf_op jit(solution)/shard_map/slice | solution.py:22
  16.3 0.9 %pad_maximum_fusion.2 = bf16[16,136,128]{2,1,0:T(8,128)(2,1)} fusion(bf16[16,8,128]{2,1,0:T(8,128)(2,1)S(1)} %broadcast_in_dim.35, bf16[16,128,128]{2,1,0:T(8,128)(2,1)S(1)} %slice.107), kind=kLoop, calls=%fused_computation.45 | loop fusion | flops 1114112 | bytes 1114112 | tf_op jit(solution)/shard_map/concatenate | solution.py:31
  17.2 1.3 %collective-permute-start.3 = (bf16[16,136,128]{2,1,0:T(8,128)(2,1)}, bf16[16,136,128]{2,1,0:T(8,128)(2,1)}, u32[]{:S(2)}, u32[]{:S(2)}) collective-permute-start(bf16[16,136,128]{2,1,0:T(8,128)(2,1)} %pad_maximum_fusion.2), channel_id=1, source_target_pairs={{1,7},{6,0},{9,15},{14,8},{17,23},{22,16},{25,31},{30,24}} | collective-permute-start | bytes 1671176 | tf_op jit(solution)/shard_map/ppermute | solution.py:71
  18.5 1.3 %collective-permute-start.2 = (bf16[16,136,128]{2,1,0:T(8,128)(2,1)}, bf16[16,136,128]{2,1,0:T(8,128)(2,1)}, u32[]{:S(2)}, u32[]{:S(2)}) collective-permute-start(bf16[16,136,128]{2,1,0:T(8,128)(2,1)} %pad_maximum_fusion.2), channel_id=1, source_target_pairs={{1,5},{3,7},{6,2},{4,0},{9,13},{11,15},{14,10},{12,8},{17,21},{19,... | collective-permute-start | bytes 1671176 | tf_op jit(solution)/shard_map/ppermute | solution.py:71
  19.8 1.3 %collective-permute-start.1 = (bf16[16,136,128]{2,1,0:T(8,128)(2,1)}, bf16[16,136,128]{2,1,0:T(8,128)(2,1)}, u32[]{:S(2)}, u32[]{:S(2)}) collective-permute-start(bf16[16,136,128]{2,1,0:T(8,128)(2,1)} %pad_maximum_fusion.2), channel_id=1, source_target_pairs={{1,3},{3,5},{5,7},{6,4},{4,2},{2,0},{9,11},{11,13},{13,15},{14,12}... | collective-permute-start | bytes 1671176 | tf_op jit(solution)/shard_map/ppermute | solution.py:71
  22.7 0.7 convolution_multiply_fusion.2
  23.4 1.2 %convolution_multiply_fusion.3 = f32[16,128,128]{2,1,0:T(8,128)S(1)} fusion(bf16[128,16,128]{0,2,1:T(8,128)(2,1)S(1)} %bitcast.115, f32[16,128,128]{2,1,0:T(8,128)S(1)} %convolution_multiply_fusion.4), kind=kOutput, calls=%fused_computation.6 | convolution fusion | flops 402915328 | bytes 2621440 | tf_op jit(solution)/shard_map/hts,shd->thd/dot_general | solution.py:137
  25.7 1.2 %fusion.7 = bf16[128,2048]{0,1:T(8,128)(2,1)S(1)} fusion(f32[16,128,128]{2,1,0:T(8,128)S(1)} %convolution_multiply_fusion, f32[16,128,128]{2,1,0:T(8,128)S(1)} %convolution_multiply_fusion.2, f32[16,128,128]{2,1,0:T(8,128)S(1)} %convolution_multiply_fusion.3, bf16[128,2048]{0,1:T(8,128)(2,1)S(1)} %bitcast.124, f32[2048]{0:T(1024)S(1)} %bitcast.134, ...), kind=kLoop, calls=%fused_computation.23 | loop fusion | flops 2097152 | bytes 4218880 | tf_op jit(solution)/shard_map/convert_element_type | solution.py:147
  26.9 5.2 %collective-permute-start.4 = (bf16[128,2048]{0,1:T(8,128)(2,1)S(1)}, bf16[128,2048]{0,1:T(8,128)(2,1)}, u32[]{:S(2)}, u32[]{:S(2)}) collective-permute-start(bf16[128,2048]{0,1:T(8,128)(2,1)S(1)} %fusion.7), channel_id=1, source_target_pairs={{0,24},{8,0},{16,8},{24,16},{1,25},{9,1},{17,9},{25,17},{2,26},{10... | collective-permute-start | bytes 1572872 | tf_op jit(solution)/shard_map/ppermute | solution.py:101
  32.1 8.1 %collective-permute-done.4 = bf16[128,2048]{0,1:T(8,128)(2,1)} collective-permute-done((bf16[128,2048]{0,1:T(8,128)(2,1)S(1)}, bf16[128,2048]{0,1:T(8,128)(2,1)}, u32[]{:S(2)}, u32[]{:S(2)}) %collective-permute-start.4) | collective-permute-done | bytes 524320 | tf_op jit(solution)/shard_map/ppermute | solution.py:101
  40.2 1.1 %fusion.27 = (f32[16]{0:T(128)S(1)}, f32[16]{0:T(128)S(1)}) fusion(bf16[16,136,128]{2,1,0:T(8,128)(2,1)} %collective-permute-done.2, bf16[16,136,128]{2,1,0:T(8,128)(2,1)} %collective-permute-done.1), kind=kLoop, calls=%fused_computation.75 | loop fusion | flops 112 | bytes 256 | tf_op jit(solution)/shard_map/add | solution.py:36
  41.3 3.1 %multiply_add_fusion = (f32[16,128,128]{2,1,0:T(8,128)S(1)}, f32[16,128,128]{2,1,0:T(8,128)}) fusion(f32[16,136,128]{2,1,0:T(8,128)} %collective-permute-done, f32[16]{0:T(128)S(1)} %get-tuple-element.29, bf16[16,136,128]{2,1,0:T(8,128)(2,1)} %collective-permute-done.3, f32[16]{0:T(128)S(1)} %get-tuple-element.32, ...), kind=kLoop, calls=%fused_computation.36 | loop fusion | flops 2359296 | bytes 4718784 | tf_op jit(solution)/shard_map/add | solution.py:94
  44.4 4.3 %collective-permute-start.5 = (f32[16,128,128]{2,1,0:T(8,128)}, f32[16,128,128]{2,1,0:T(8,128)S(1)}, u32[]{:S(2)}, u32[]{:S(2)}) collective-permute-start(f32[16,128,128]{2,1,0:T(8,128)} %get-tuple-element.34), channel_id=1, source_target_pairs={{0,1},{2,3},{4,5},{6,7},{1,0},{3,2},{5,4},{7,6},{8,9},{10,11},{12,... | collective-permute-start | bytes 3145736 | tf_op jit(solution)/shard_map/ppermute | solution.py:93
  48.8 2.4 %collective-permute-done.5 = f32[16,128,128]{2,1,0:T(8,128)S(1)} collective-permute-done((f32[16,128,128]{2,1,0:T(8,128)}, f32[16,128,128]{2,1,0:T(8,128)S(1)}, u32[]{:S(2)}, u32[]{:S(2)}) %collective-permute-start.5) | collective-permute-done | bytes 1048608 | tf_op jit(solution)/shard_map/ppermute | solution.py:93
  51.3 1.0 %fusion = f32[128,16,128]{0,2,1:T(8,128)S(1)} fusion(bf16[128,16,128]{0,2,1:T(8,128)(2,1)S(1)} %bitcast.116, f32[128,16]{0,1:T(8,128)S(1)} %copy.29, f32[16,128,128]{2,1,0:T(8,128)S(1)} %collective-permute-done.5, f32[16,128,128]{2,1,0:T(8,128)S(1)} %get-tuple-element.33, pred[]{:T(512)S(6)} %eq.29), kind=kOutput, calls=%fused_computation.10 | convolution fusion | flops 403177472 | bytes 3678209 | tf_op jit(solution)/shard_map/shd,hde->she/dot_general | solution.py:188
  52.3 0.7 fusion.1
  53.0 1.2 %fusion.2 = f32[128,16,128]{0,2,1:T(8,128)S(1)} fusion(f32[16,128,128]{2,1,0:T(8,128)S(1)} %get-tuple-element.33, f32[16,128,128]{2,1,0:T(8,128)S(1)} %collective-permute-done.5, f32[128,16]{0,1:T(8,128)S(1)} %copy.40, pred[]{:T(512)S(6)} %eq.29, bf16[128,16,128]{2,1,0:T(8,128)(2,1)S(1)} %bitcast.112), kind=kOutput, calls=%fused_computation.14 | convolution fusion | flops 403177472 | bytes 3678209 | tf_op jit(solution)/shard_map/the,hde->thd/dot_general | solution.py:185
  54.2 1.2 %fusion.11 = bf16[128,2048]{0,1:T(8,128)(2,1)S(1)} fusion(f32[128,16,128]{0,2,1:T(8,128)S(1)} %fusion, f32[128,16,128]{0,2,1:T(8,128)S(1)} %fusion.1, f32[128,16,128]{0,2,1:T(8,128)S(1)} %fusion.2, f32[2048]{0:T(1024)S(1)} %bitcast.128, f32[2048]{0:T(1024)S(1)} %bitcast.130, f32[2048]{0:T(1024)S(1)} %bitcast.132), kind=kLoop, calls=%fused_computation.30 | loop fusion | flops 1572864 | bytes 3694592 | tf_op jit(solution)/shard_map/convert_element_type | solution.py:192
  55.5 4.2 %collective-permute-start.6 = (bf16[128,2048]{0,1:T(8,128)(2,1)S(1)}, bf16[128,2048]{0,1:T(8,128)(2,1)S(1)}, u32[]{:S(2)}, u32[]{:S(2)}) collective-permute-start(bf16[128,2048]{0,1:T(8,128)(2,1)S(1)} %fusion.11), channel_id=1, source_target_pairs={{0,24},{8,0},{16,8},{24,16},{1,25},{9,1},{17,9},{25,17},{2,26},{10... | collective-permute-start | bytes 1572872 | tf_op jit(solution)/shard_map/ppermute | solution.py:101
  59.6 11.7 %collective-permute-done.6 = bf16[128,2048]{0,1:T(8,128)(2,1)S(1)} collective-permute-done((bf16[128,2048]{0,1:T(8,128)(2,1)S(1)}, bf16[128,2048]{0,1:T(8,128)(2,1)S(1)}, u32[]{:S(2)}, u32[]{:S(2)}) %collective-permute-start.6) | collective-permute-done | bytes 524320 | tf_op jit(solution)/shard_map/ppermute | solution.py:101
  71.3 1.2 %fusion.19 = bf16[1,128,2048]{1,2,0:T(8,128)(2,1)S(1)} fusion(bf16[128,2048]{0,1:T(8,128)(2,1)S(1)} %collective-permute-done.6, bf16[128,2048]{0,1:T(8,128)(2,1)} %collective-permute-done.4), kind=kLoop, calls=%fused_computation.46 | loop fusion | flops 1048576 | bytes 1572864 | tf_op jit(solution)/shard_map/broadcast_in_dim | solution.py:197
  72.5 1.0 %copy.45 = bf16[1,128,2048]{2,1,0:T(8,128)(2,1)} copy(bf16[1,128,2048]{1,2,0:T(8,128)(2,1)S(1)} %fusion.19) | data formatting | bytes 1048576 | tf_op jit(solution)/shard_map/broadcast_in_dim | solution.py:197
  (54 shorter events, 5.6 us)
Async XLA Ops:
  0.0 4.2 %copy-start.2 = (bf16[1,128,2048]{2,1,0:T(8,128)(2,1)S(1)}, bf16[1,128,2048]{2,1,0:T(8,128)(2,1)}, u32[]{:S(2)}) copy-start(bf16[1,128,2048]{2,1,0:T(8,128)(2,1)} %param.6) | copy-start | bytes 1572868
  5.3 16.3 %copy-start = (bf16[128,2048]{0,1:T(8,128)(2,1)}, bf16[128,2048]{0,1:T(8,128)(2,1)S(1)}, u32[]{:S(2)}) copy-start(bf16[128,2048]{0,1:T(8,128)(2,1)S(1)} %get-tuple-element.35) | copy-start | bytes 1572868
  8.4 1.6 %copy-start.4 = (f32[1,3,2048]{2,0,1:T(1,128)S(1)}, f32[1,3,2048]{2,0,1:T(1,128)}, u32[]{:S(2)}) copy-start(f32[1,3,2048]{2,0,1:T(1,128)} %param.7) | copy-start | bytes 73732
  9.5 3.2 %collective-permute-start = (f32[16,136,128]{2,1,0:T(8,128)}, f32[16,136,128]{2,1,0:T(8,128)}, u32[]{:S(2)}, u32[]{:S(2)}) collective-permute-start(f32[16,136,128]{2,1,0:T(8,128)} %pad_maximum_fusion), channel_id=1, source_target_pairs={{0,1},{2,3},{4,5},{6,7},{1,0},{3,2},{5,4},{7,6},{8,9},{10,11},{12,... | collective-permute-start | bytes 3342344 | tf_op jit(solution)/shard_map/ppermute | solution.py:64
  17.2 23.0 %collective-permute-start.3 = (bf16[16,136,128]{2,1,0:T(8,128)(2,1)}, bf16[16,136,128]{2,1,0:T(8,128)(2,1)}, u32[]{:S(2)}, u32[]{:S(2)}) collective-permute-start(bf16[16,136,128]{2,1,0:T(8,128)(2,1)} %pad_maximum_fusion.2), channel_id=1, source_target_pairs={{1,7},{6,0},{9,15},{14,8},{17,23},{22,16},{25,31},{30,24}} | collective-permute-start | bytes 1671176 | tf_op jit(solution)/shard_map/ppermute | solution.py:71
  18.5 21.7 %collective-permute-start.2 = (bf16[16,136,128]{2,1,0:T(8,128)(2,1)}, bf16[16,136,128]{2,1,0:T(8,128)(2,1)}, u32[]{:S(2)}, u32[]{:S(2)}) collective-permute-start(bf16[16,136,128]{2,1,0:T(8,128)(2,1)} %pad_maximum_fusion.2), channel_id=1, source_target_pairs={{1,5},{3,7},{6,2},{4,0},{9,13},{11,15},{14,10},{12,8},{17,21},{19,... | collective-permute-start | bytes 1671176 | tf_op jit(solution)/shard_map/ppermute | solution.py:71
  19.8 20.4 %collective-permute-start.1 = (bf16[16,136,128]{2,1,0:T(8,128)(2,1)}, bf16[16,136,128]{2,1,0:T(8,128)(2,1)}, u32[]{:S(2)}, u32[]{:S(2)}) collective-permute-start(bf16[16,136,128]{2,1,0:T(8,128)(2,1)} %pad_maximum_fusion.2), channel_id=1, source_target_pairs={{1,3},{3,5},{5,7},{6,4},{4,2},{2,0},{9,11},{11,13},{13,15},{14,12}... | collective-permute-start | bytes 1671176 | tf_op jit(solution)/shard_map/ppermute | solution.py:71
  24.7 1.0 %copy-start.3 = (bf16[1,128,2048]{1,2,0:T(8,128)(2,1)S(1)}, bf16[1,128,2048]{1,2,0:T(8,128)(2,1)}, u32[]{:S(2)}) copy-start(bf16[1,128,2048]{1,2,0:T(8,128)(2,1)} %copy.32) | copy-start | bytes 1572868
  26.9 13.3 %collective-permute-start.4 = (bf16[128,2048]{0,1:T(8,128)(2,1)S(1)}, bf16[128,2048]{0,1:T(8,128)(2,1)}, u32[]{:S(2)}, u32[]{:S(2)}) collective-permute-start(bf16[128,2048]{0,1:T(8,128)(2,1)S(1)} %fusion.7), channel_id=1, source_target_pairs={{0,24},{8,0},{16,8},{24,16},{1,25},{9,1},{17,9},{25,17},{2,26},{10... | collective-permute-start | bytes 1572872 | tf_op jit(solution)/shard_map/ppermute | solution.py:101
  44.4 6.8 %collective-permute-start.5 = (f32[16,128,128]{2,1,0:T(8,128)}, f32[16,128,128]{2,1,0:T(8,128)S(1)}, u32[]{:S(2)}, u32[]{:S(2)}) collective-permute-start(f32[16,128,128]{2,1,0:T(8,128)} %get-tuple-element.34), channel_id=1, source_target_pairs={{0,1},{2,3},{4,5},{6,7},{1,0},{3,2},{5,4},{7,6},{8,9},{10,11},{12,... | collective-permute-start | bytes 3145736 | tf_op jit(solution)/shard_map/ppermute | solution.py:93
  51.3 1.0 %copy-start.1 = (bf16[128,2048]{0,1:T(8,128)(2,1)S(1)}, bf16[128,2048]{0,1:T(8,128)(2,1)}, u32[]{:S(2)}) copy-start(bf16[128,2048]{0,1:T(8,128)(2,1)} %copy-done) | copy-start | bytes 1572868
  55.5 15.9 %collective-permute-start.6 = (bf16[128,2048]{0,1:T(8,128)(2,1)S(1)}, bf16[128,2048]{0,1:T(8,128)(2,1)S(1)}, u32[]{:S(2)}, u32[]{:S(2)}) collective-permute-start(bf16[128,2048]{0,1:T(8,128)(2,1)S(1)} %fusion.11), channel_id=1, source_target_pairs={{0,24},{8,0},{16,8},{24,16},{1,25},{9,1},{17,9},{25,17},{2,26},{10... | collective-permute-start | bytes 1572872 | tf_op jit(solution)/shard_map/ppermute | solution.py:101

commit v12 on v5

--- a/solution.py
+++ b/solution.py
@@ -50,11 +50,72 @@
     return list(moves) + [(count - 1 - source, count - 1 - target) for source, target in moves]
 
 
+def table(values, index):
+    return jnp.asarray(values, jnp.float32)[index]
+
+
+def scans_four(forward_part, backward_part, rate, axis):
+    here = lax.axis_index(axis)
+    odd = here % 2 == 1
+    swap = [(2 * p, 2 * p + 1) for p in range(4)] + [(2 * p + 1, 2 * p) for p in range(4)]
+    mine = jnp.stack([packed(forward_part, rate), packed(backward_part, rate)])
+    theirs = lax.ppermute(mine, axis, swap)
+    even_forward, even_rate = unpacked(jnp.where(odd, theirs[0], mine[0]))
+    odd_forward, odd_rate = unpacked(jnp.where(odd, mine[0], theirs[0]))
+    even_backward = unpacked(jnp.where(odd, theirs[1], mine[1]))[0]
+    odd_backward = unpacked(jnp.where(odd, mine[1], theirs[1]))[0]
+    both_rate = even_rate * odd_rate
+    ahead = packed(odd_rate[:, None, None] * even_forward + odd_forward, both_rate)
+    behind = packed(even_rate[:, None, None] * odd_backward + even_backward, both_rate)
+    first_pairs = [(0, 2), (1, 5), (2, 0), (3, 7), (4, 3), (5, 6), (6, 4), (7, 1)]
+    second_pairs = [(0, 7), (2, 4), (4, 1), (6, 2)]
+    first_sent = jnp.where(table([1, 1, 0, 1, 0, 1, 0, 0], here) > 0, ahead, behind)
+    second_sent = jnp.where(table([1, 0, 1, 0, 0, 0, 0, 0], here) > 0, ahead, behind)
+    one, one_rate = unpacked(widen(lax.ppermute(narrow(first_sent), axis, first_pairs)))
+    two, two_rate = unpacked(widen(lax.ppermute(narrow(second_sent), axis, second_pairs)))
+
+    def partial(c_one, c_two, c_one_two, c_two_one, r_one, r_two):
+        value = (
+            table(c_one, here) * one
+            + table(c_two, here) * two
+            + (table(c_one_two, here) * one_rate)[:, None, None] * two
+            + (table(c_two_one, here) * two_rate)[:, None, None] * one
+        )
+        kept = table(r_one, here) * one_rate + table(r_two, here) * two_rate
+        kept = kept + (1.0 - table(r_one, here) - table(r_two, here))
+        return packed(value, kept)
+
+    forward_partial = partial(
+        [0, 0, 1, 0, 0, 1, 1, 1], [0, 0, 0, 0, 1, 0, 0, 0], [0, 0, 0, 0, 0, 0, 0, 1],
+        [0] * 8, [0, 0, 1, 0, 0, 0, 1, 0], [0, 0, 0, 0, 1, 0, 0, 0],
+    )
+    backward_partial = partial(
+        [1, 0, 0, 1, 1, 0, 0, 0], [0, 1, 1, 0, 0, 0, 0, 0], [0] * 8,
+        [0, 1, 0, 0, 0, 0, 0, 0], [1, 0, 0, 1, 1, 0, 0, 0], [0] * 8,
+    )
+    own = jnp.stack([forward_partial, backward_partial])
+    other = lax.ppermute(own, axis, swap)
+
+    def joined(position, near_flags):
+        near = table(near_flags, here) > 0
+        near_value, near_rate = unpacked(jnp.where(near, own[position], other[position]))
+        far_value = unpacked(jnp.where(near, other[position], own[position]))[0]
+        return near_value + near_rate[:, None, None] * far_value
+
+    forward_in = joined(0, [1, 0, 1, 0, 1, 0, 1, 0])
+    backward_in = joined(1, [1, 0, 0, 1, 1, 0, 1, 0])
+    state_in = jnp.where(odd, even_rate[:, None, None] * forward_in + even_forward, forward_in)
+    adjoint_in = jnp.where(odd, backward_in, odd_rate[:, None, None] * backward_in + odd_backward)
+    return state_in, adjoint_in
+
+
 def scans_in(forward_part, backward_part, rate, axis, held):
     count = lax.axis_size(axis)
     if count == 1:
         return jnp.zeros_like(forward_part), jnp.zeros_like(backward_part), held
     assert count % 2 == 0
+    if count == 8:
+        return scans_four(forward_part, backward_part, rate, axis) + (held,)
     odd = lax.axis_index(axis) % 2 == 1
     couples = count // 2
     swap = [(2 * p, 2 * p + 1) for p in range(couples)] + [(2 * p + 1, 2 * p) for p in range(couples)]

time: 71.6 us -> 101 us (1.41)
  local copies, waits for them, and re-layouts: 8.91 us -> 22.4 us
  waiting for transfers between devices: 23.3 us -> 31.1 us
  other arithmetic: 12.8 us -> 18.6 us
  between operations: 0.25 us -> 5.03 us
  starting transfers between devices: 13.3 us -> 11.1 us
    ppermute x2, waiting for transfers between devices: 11.7 us -> 22.6 us  [passed_along(): return lax.ppermute(value, axis, pairs)]
    dynamic_slice x0 -> x11, local copies, waits for them, and re-layouts: none -> 6.79 us  [table(): return jnp.asarray(values, jnp.float32)[index]]
    ppermute x2, starting transfers between devices: 8.66 us -> 4.1 us  [passed_along(): return lax.ppermute(value, axis, pairs)]
    select_n x0 -> x4, other arithmetic: none -> 3.82 us  [the longest x1 1.81 us: joined(): jnp.where(near, own[position], other[position])]
    mul x0 -> x1, other arithmetic: none -> 3.39 us  [partial(): table(c_one_two, here) * one_rate]
    another operation x0 -> x5, other arithmetic: none -> 3.35 us  [the longest x3 1.68 us: scans_four(): own = jnp.stack([forward_partial, backward_partial])]
    squeeze x0 -> x2, local copies, waits for them, and re-layouts: none -> 3.33 us  [the longest x1 1.82 us: joined(): other[position]]
    convert_element_type x2 -> x0, other arithmetic: 3.12 us -> none  [the longest x1 1.91 us: narrow(): return jnp.concatenate([state.astype(jnp.bfloat16), tile], axis=1)]
  transfers between devices with their start and end apart: 7 -> 6, of which waited for: 4 -> 4; matrix products, arithmetic and copies ran while one was open for 23% -> 19% of each run, Pallas kernels for 0% -> 0%
where the time goes in v12:
time: 101 us; the launch traced here: 100 us
  waiting for transfers between devices  31.1 us (31%)
  local copies, waits for them, and re-layouts  22.4 us (22%)
  other arithmetic  18.6 us (18%)
  matrix products  12.2 us (12%)
  starting transfers between devices  11.1 us (11%)
  between operations  5.03 us (5%)
    ppermute x2, waiting for transfers between devices, passed_along(): return lax.ppermute(value, axis, pairs)  22.6 us
    ppermute x1, waiting for transfers between devices, scans_four(): lax.ppermute(narrow(first_sent), axis, first_pairs)  6.91 us
    dynamic_slice x11, local copies, waits for them, and re-layouts, table(): return jnp.asarray(values, jnp.float32)[index]  6.79 us
    unnamed x57, local copies, waits for them, and re-layouts  5.51 us
    ppermute x1, starting transfers between devices, scans_four(): lax.ppermute(narrow(second_sent), axis, second_pairs)  5.49 us
    ppermute x2, starting transfers between devices, passed_along(): return lax.ppermute(value, axis, pairs)  4.1 us
    mul x1, other arithmetic, partial(): table(c_one_two, here) * one_rate  3.39 us
    add x1, other arithmetic, partial(): table(c_one, here) * one + table(c_two, here) * two  3.09 us
  transfers between devices with their start and end apart: 6, of which 4 were waited for; matrix products, arithmetic and copies ran while one was open for 19% of the time, Pallas kernels for 0%

profile of v12, /device:TPU:0, one launch (start us, length us, event | category | flops | bytes accessed | tf_op | source)
XLA Modules:
  0.0 100.5 jit_solution(18439850414751648071)
XLA Ops:
  0.9 0.7 log_bitcast_fusion
  1.9 0.7 fusion.67
  2.6 1.3 %copy.57 = bf16[1,128,2048]{1,2,0:T(8,128)(2,1)S(1)} copy(bf16[1,128,2048]{2,1,0:T(8,128)(2,1)} %param.25) | data formatting | bytes 1048576 | tf_op args[0]
  4.0 1.0 fusion.15
  5.3 1.2 %fusion.37 = f32[16,128,128]{2,1,0:T(8,128)S(1)} fusion(bf16[128,16,128]{0,2,1:T(8,128)(2,1)S(1)} %bitcast.160, bf16[128,16,128]{0,2,1:T(8,128)(2,1)S(1)} %bitcast.152, f32[128,16]{0,1:T(8,128)S(1)} %copy.69), kind=kOutput, calls=%fused_computation.86 | convolution fusion | flops 403177472 | bytes 2105344 | tf_op jit(solution)/shard_map/shd,she->hde/dot_general | solution.py:194
  6.5 0.7 convolution_multiply_fusion
  7.6 1.5 %pad_maximum_fusion = f32[2,16,136,128]{3,2,1,0:T(8,128)} fusion(f32[1,16,136,128]{3,2,1,0:T(8,128)S(1)} %get-tuple-element.33, f32[1,16,136,128]{3,2,1,0:T(8,128)S(1)} %get-tuple-element.32), kind=kLoop, calls=%fused_computation | loop fusion | flops 557056 | bytes 4456448 | tf_op jit(solution)/shard_map/stack | solution.py:61
  12.2 1.6 %collective-permute-done.1 = f32[2,16,136,128]{3,2,1,0:T(8,128)} collective-permute-done((f32[2,16,136,128]{3,2,1,0:T(8,128)}, f32[2,16,136,128]{3,2,1,0:T(8,128)}, u32[]{:S(2)}, u32[]{:S(2)}) %collective-permute-start.1) | collective-permute-done | bytes 2228256 | tf_op jit(solution)/shard_map/ppermute | solution.py:62
  13.8 1.4 %fusion.40 = (f32[16,136,128]{2,1,0:T(8,128)S(1)}, f32[16,136,128]{2,1,0:T(8,128)S(1)}) fusion(f32[2,16,136,128]{3,2,1,0:T(8,128)} %collective-permute-done.1, f32[16,8,128]{2,1,0:T(8,128)S(1)} %broadcast_in_dim.47, f32[16,128,128]{2,1,0:T(8,128)S(1)} %fusion.37, pred[]{:T(512)S(6)} %eq.29), kind=kLoop, calls=%fused_computation.90 | loop fusion | flops 835584 | bytes 4456449 | tf_op jit(solution)/shard_map/jit(_where)/select_n | solution.py:64
  15.4 1.5 %slice_bitcast_fusion.2 = f32[16,136,128]{2,1,0:T(8,128)S(1)} fusion(f32[2,16,136,128]{3,2,1,0:T(8,128)} %collective-permute-done.1), kind=kLoop, calls=%fused_computation.39 | loop fusion | bytes 2228224 | tf_op jit(solution)/shard_map/squeeze | solution.py:66
  19.6 5.5 %collective-permute-start.3 = (bf16[16,136,128]{2,1,0:T(8,128)(2,1)S(1)}, bf16[16,136,128]{2,1,0:T(8,128)(2,1)S(1)}, u32[]{:S(2)}, u32[]{:S(2)}) collective-permute-start(bf16[16,136,128]{2,1,0:T(8,128)(2,1)S(1)} %pad_maximum_fusion.9), channel_id=1, source_target_pairs={{0,7},{2,4},{4,1},{6,2},{8,15},{10,12},{12,9},{14,10},{16,23},{18,... | collective-permute-start | bytes 1671176 | tf_op jit(solution)/shard_map/ppermute | solution.py:75
  25.2 1.0 collective-permute-start.2
  32.4 6.9 %collective-permute-done.2 = bf16[16,136,128]{2,1,0:T(8,128)(2,1)S(1)} collective-permute-done((bf16[16,136,128]{2,1,0:T(8,128)(2,1)S(1)}, bf16[16,136,128]{2,1,0:T(8,128)(2,1)S(1)}, u32[]{:S(2)}, u32[]{:S(2)}) %collective-permute-start.2) | collective-permute-done | bytes 557088 | tf_op jit(solution)/shard_map/ppermute | solution.py:74
  39.3 3.4 %multiply_reduce_fusion.2 = (f32[16]{0:T(128)S(1)}, f32[16]{0:T(128)S(1)}, f32[16]{0:T(128)S(1)}, f32[16]{0:T(128)S(1)}, f32[16]{0:T(128)S(1)}, /*index=5*/f32[16]{0:T(128)S(1)}) fusion(f32[]{:T(128)} %bitcast.30, f32[]{:T(128)} %bitcast.37, f32[]{:T(128)} %bitcast.34, f32[]{:T(128)} %bitcast.32, f32[]{:T(128)} %bitcast.28, f32[]{:T(128)} %bitcast.31, ...), kind=kLoop, calls=%fused_computation.132 | loop fusion | flops 272 | bytes 540 | tf_op jit(solution)/shard_map/mul | solution.py:81
  42.7 3.1 %fusion.20 = (f32[16,128,128]{2,1,0:T(8,128)S(1)}, f32[16,128,128]{2,1,0:T(8,128)S(1)}) fusion(f32[16]{0:T(128)S(1)} %get-tuple-element.14, f32[16]{0:T(128)S(1)} %get-tuple-element.10, f32[]{:T(128)} %bitcast.28, f32[]{:T(128)} %bitcast.25, bf16[16,136,128]{2,1,0:T(8,128)(2,1)S(1)} %collective-permute-done.3, ...), kind=kLoop, calls=%fused_computation.58 | loop fusion | flops 4194304 | bytes 3146000 | tf_op jit(solution)/shard_map/add | solution.py:79
  46.2 1.5 %pad_maximum_fusion.1 = f32[2,16,136,128]{3,2,1,0:T(8,128)} fusion(f32[1,16,136,128]{3,2,1,0:T(8,128)S(1)} %fusion.44, f32[1,16,136,128]{3,2,1,0:T(8,128)S(1)} %fusion.46), kind=kLoop, calls=%fused_computation.1 | loop fusion | flops 557056 | bytes 4456448 | tf_op jit(solution)/shard_map/stack | solution.py:96
  47.7 2.1 %copy.56 = bf16[1,128,2048]{1,2,0:T(8,128)(2,1)} copy(bf16[1,128,2048]{2,1,0:T(8,128)(2,1)} %param.26) | data formatting | bytes 1048576 | tf_op args[1]
  52.5 1.8 %convolution_multiply_fusion.2 = f32[16,128,128]{1,2,0:T(8,128)S(1)} fusion(bf16[128,16,128]{0,2,1:T(8,128)(2,1)} %bitcast.164, bf16[128,16,128]{0,2,1:T(8,128)(2,1)} %bitcast.153, f32[16,128]{1,0:T(8,128)S(1)} %copy.60, pred[128,128]{0,1:T(8,128)(4,1)S(1)} %iota_compare_fusion), kind=kOutput, calls=%fused_computation.25 | convolution fusion | flops 68157440 | bytes 2121728 | tf_op jit(solution)/shard_map/thd,shd->hts/dot_general | solution.py:212
  54.3 1.8 %fusion = f32[128,16,128]{2,0,1:T(8,128)} fusion(f32[16,128,128]{1,2,0:T(8,128)S(1)} %convolution_multiply_fusion.2, bf16[128,16,128]{2,1,0:T(8,128)(2,1)S(1)} %bitcast.158), kind=kOutput, calls=%fused_computation.24 | convolution fusion | flops 402915328 | bytes 2621440 | tf_op jit(solution)/shard_map/hts,the->she/dot_general | solution.py:214
  56.0 2.5 %copy.67 = f32[128,16,128]{0,2,1:T(8,128)} copy(f32[128,16,128]{2,0,1:T(8,128)} %fusion) | data formatting | bytes 2097152 | tf_op jit(solution)/shard_map/mul | solution.py:214
  58.6 1.8 %fusion.1 = f32[16,128,128]{1,2,0:T(8,128)S(1)} fusion(bf16[128,16,128]{0,2,1:T(8,128)(2,1)} %bitcast.161, f32[16,128]{1,0:T(8,128)S(1)} %copy.60, pred[128,128]{0,1:T(8,128)(4,1)S(1)} %iota_compare_fusion, bf16[128,16,128]{2,1,0:T(8,128)(2,1)} %bitcast.157), kind=kOutput, calls=%fused_computation.29 | convolution fusion | flops 68157440 | bytes 2121728 | tf_op jit(solution)/shard_map/thd,shd->hts/dot_general | solution.py:206
  60.4 0.7 convolution_multiply_fusion.4
  61.5 1.2 %convolution_multiply_fusion.3 = f32[16,128,128]{2,1,0:T(8,128)S(1)} fusion(bf16[128,16,128]{0,2,1:T(8,128)(2,1)S(1)} %bitcast.165, f32[16,128,128]{1,2,0:T(8,128)S(1)} %fusion.1), kind=kOutput, calls=%fused_computation.26 | convolution fusion | flops 402915328 | bytes 2621440 | tf_op jit(solution)/shard_map/hts,thd->shd/dot_general | solution.py:210
  62.7 1.8 %fusion.45 = (f32[16,136,128]{2,1,0:T(8,128)S(1)}, f32[16,136,128]{2,1,0:T(8,128)S(1)}) fusion(f32[16,8,128]{2,1,0:T(8,128)S(1)} %broadcast_in_dim.53, f32[16,128,128]{2,1,0:T(8,128)S(1)} %get-tuple-element.24, pred[]{:T(512)} %bitcast.24, f32[2,16,136,128]{3,2,1,0:T(8,128)} %collective-permute-done.4, f32[16,8,128]{2,1,0:T(8,128)S(1)} %broadcast_in_dim.55, ...), kind=kLoop, calls=%fused_computation.96 | loop fusion | flops 1114112 | bytes 6684674 | tf_op jit(solution)/shard_map/jit(_where)/select_n | solution.py:101
  64.7 1.8 %slice_bitcast_fusion.1 = (f32[16,136,128]{2,1,0:T(8,128)S(1)}, f32[16,136,128]{2,1,0:T(8,128)S(1)}) fusion(f32[2,16,136,128]{3,2,1,0:T(8,128)} %collective-permute-done.4), kind=kLoop, calls=%fused_computation.38 | loop fusion | bytes 4456448 | tf_op jit(solution)/shard_map/squeeze | solution.py:101
  68.4 1.0 fusion.2
  69.7 1.4 %fusion.4 = f32[128,16,128]{0,2,1:T(8,128)S(1)} fusion(f32[16,128,128]{2,1,0:T(8,128)S(1)} %get-tuple-element.24, f32[16,8,128]{2,1,0:T(8,128)S(1)} %broadcast_in_dim.53, f32[16,136,128]{2,1,0:T(8,128)S(1)} %get-tuple-element.20, f32[16,136,128]{2,1,0:T(8,128)S(1)} %get-tuple-element.18, f32[16,136,128]{2,1,0:T(8,128)S(1)} %copy-done.1, ...), kind=kOutput, calls=%fused_computation.35 | convolution fusion | flops 404750336 | bytes 5841922 | tf_op jit(solution)/shard_map/the,hde->thd/dot_general | solution.py:225
  71.1 1.4 %fusion.26 = (bf16[128,2048]{0,1:T(8,128)(2,1)S(1)}, bf16[128,2048]{0,1:T(8,128)(2,1)S(1)}) fusion(f32[16,128,128]{2,1,0:T(8,128)S(1)} %convolution_multiply_fusion.3, f32[16,128,128]{2,1,0:T(8,128)S(1)} %convolution_multiply_fusion.4, f32[128,16,128]{0,2,1:T(8,128)S(1)} %copy-done.13, bf16[1,128,2048]{1,2,0:T(8,128)(2,1)S(1)} %copy-done.14, ...), kind=kLoop, calls=%fused_computation.68 | loop fusion | flops 3670016 | bytes 7888896 | tf_op jit(solution)/shard_map/convert_element_type | solution.py:219
  72.6 3.7 %collective-permute-start = (bf16[128,2048]{0,1:T(8,128)(2,1)S(1)}, bf16[128,2048]{0,1:T(8,128)(2,1)S(1)}, u32[]{:S(2)}, u32[]{:S(2)}) collective-permute-start(bf16[128,2048]{0,1:T(8,128)(2,1)S(1)} %get-tuple-element.34), channel_id=1, source_target_pairs={{0,24},{8,0},{16,8},{24,16},{1,25},{9,1},{17,9},{25,17},{2,26},{10... | collective-permute-start | bytes 1572872 | tf_op jit(solution)/shard_map/ppermute | solution.py:155
  76.7 11.8 %collective-permute-done = bf16[128,2048]{0,1:T(8,128)(2,1)S(1)} collective-permute-done((bf16[128,2048]{0,1:T(8,128)(2,1)S(1)}, bf16[128,2048]{0,1:T(8,128)(2,1)S(1)}, u32[]{:S(2)}, u32[]{:S(2)}) %collective-permute-start) | collective-permute-done | bytes 524320 | tf_op jit(solution)/shard_map/ppermute | solution.py:155
  88.5 10.8 %collective-permute-done.5 = bf16[128,2048]{0,1:T(8,128)(2,1)S(1)} collective-permute-done((bf16[128,2048]{0,1:T(8,128)(2,1)S(1)}, bf16[128,2048]{0,1:T(8,128)(2,1)S(1)}, u32[]{:S(2)}, u32[]{:S(2)}) %collective-permute-start.5) | collective-permute-done | bytes 524320 | tf_op jit(solution)/shard_map/ppermute | solution.py:155
  99.5 1.0 %copy.81 = bf16[1,128,2048]{2,1,0:T(8,128)(2,1)} copy(bf16[1,128,2048]{1,2,0:T(8,128)(2,1)S(1)} %fusion.50) | data formatting | bytes 1048576 | tf_op jit(solution)/shard_map/broadcast_in_dim | solution.py:237
  (124 shorter events, 15.8 us)
Async XLA Ops:
  4.0 1.2 %copy-start.15 = (bf16[1,128,2048]{2,1,0:T(8,128)(2,1)S(1)}, bf16[1,128,2048]{2,1,0:T(8,128)(2,1)}, u32[]{:S(2)}) copy-start(bf16[1,128,2048]{2,1,0:T(8,128)(2,1)} %param.26) | copy-start | bytes 1572868
  5.0 1.6 %copy-start.4 = (bf16[128,2048]{0,1:T(8,128)(2,1)}, bf16[128,2048]{0,1:T(8,128)(2,1)S(1)}, u32[]{:S(2)}) copy-start(bf16[128,2048]{0,1:T(8,128)(2,1)S(1)} %get-tuple-element.26) | copy-start | bytes 1572868
  5.0 1.6 %copy-start.9 = (bf16[128,2048]{0,1:T(8,128)(2,1)}, bf16[128,2048]{0,1:T(8,128)(2,1)S(1)}, u32[]{:S(2)}) copy-start(bf16[128,2048]{0,1:T(8,128)(2,1)S(1)} %get-tuple-element.28) | copy-start | bytes 1572868
  5.0 1.6 %copy-start.11 = (bf16[128,2048]{0,1:T(8,128)(2,1)}, bf16[128,2048]{0,1:T(8,128)(2,1)S(1)}, u32[]{:S(2)}) copy-start(bf16[128,2048]{0,1:T(8,128)(2,1)S(1)} %get-tuple-element.27) | copy-start | bytes 1572868
  5.3 2.0 %copy-start.6 = (bf16[16,8,16,128]{3,2,1,0:T(8,128)(2,1)}, bf16[16,8,16,128]{3,2,1,0:T(8,128)(2,1)S(1)}, u32[]{:S(2)}) copy-start(bf16[16,8,16,128]{3,2,1,0:T(8,128)(2,1)S(1)} %copy.91) | copy-start | bytes 1572868
  7.5 2.0 %copy-start.26 = (f32[8]{0:T(128)S(1)}, f32[8]{0:T(128)}, u32[]{:S(2)}) copy-start(f32[8]{0:T(128)} %constant.76.clone) | copy-start | bytes 100
  7.5 2.6 %copy-start.25 = (f32[8]{0:T(128)S(1)}, f32[8]{0:T(128)}, u32[]{:S(2)}) copy-start(f32[8]{0:T(128)} %constant.77.clone) | copy-start | bytes 100
  9.0 4.8 %collective-permute-start.1 = (f32[2,16,136,128]{3,2,1,0:T(8,128)}, f32[2,16,136,128]{3,2,1,0:T(8,128)}, u32[]{:S(2)}, u32[]{:S(2)}) collective-permute-start(f32[2,16,136,128]{3,2,1,0:T(8,128)} %pad_maximum_fusion), channel_id=1, source_target_pairs={{0,1},{2,3},{4,5},{6,7},{1,0},{3,2},{5,4},{7,6},{8,9},{10,11},{12,... | collective-permute-start | bytes 6684680 | tf_op jit(solution)/shard_map/ppermute | solution.py:62
  15.2 1.7 %copy-start = (f32[16,136,128]{2,1,0:T(8,128)}, f32[16,136,128]{2,1,0:T(8,128)S(1)}, u32[]{:S(2)}) copy-start(f32[16,136,128]{2,1,0:T(8,128)S(1)} %get-tuple-element.17) | copy-start | bytes 3342340
  19.4 6.8 %copy-start.24 = (f32[8]{0:T(128)S(1)}, f32[8]{0:T(128)}, u32[]{:S(2)}) copy-start(f32[8]{0:T(128)} %constant.82.clone) | copy-start | bytes 100
  19.4 7.4 %copy-start.23 = (f32[8]{0:T(128)S(1)}, f32[8]{0:T(128)}, u32[]{:S(2)}) copy-start(f32[8]{0:T(128)} %constant.79.clone) | copy-start | bytes 100
  19.5 8.0 %copy-start.22 = (f32[8]{0:T(128)S(1)}, f32[8]{0:T(128)}, u32[]{:S(2)}) copy-start(f32[8]{0:T(128)} %constant.83.clone) | copy-start | bytes 100
  19.5 9.9 %copy-start.21 = (f32[8]{0:T(128)S(1)}, f32[8]{0:T(128)}, u32[]{:S(2)}) copy-start(f32[8]{0:T(128)} %constant.80.clone) | copy-start | bytes 100
  19.5 10.5 %copy-start.20 = (f32[8]{0:T(128)S(1)}, f32[8]{0:T(128)}, u32[]{:S(2)}) copy-start(f32[8]{0:T(128)} %constant.85.clone) | copy-start | bytes 100
  19.5 11.0 %copy-start.19 = (f32[8]{0:T(128)S(1)}, f32[8]{0:T(128)}, u32[]{:S(2)}) copy-start(f32[8]{0:T(128)} %constant.78.clone) | copy-start | bytes 100
  19.5 11.7 %copy-start.18 = (f32[8]{0:T(128)S(1)}, f32[8]{0:T(128)}, u32[]{:S(2)}) copy-start(f32[8]{0:T(128)} %constant.84.clone) | copy-start | bytes 100
  19.6 12.8 %collective-permute-start.3 = (bf16[16,136,128]{2,1,0:T(8,128)(2,1)S(1)}, bf16[16,136,128]{2,1,0:T(8,128)(2,1)S(1)}, u32[]{:S(2)}, u32[]{:S(2)}) collective-permute-start(bf16[16,136,128]{2,1,0:T(8,128)(2,1)S(1)} %pad_maximum_fusion.9), channel_id=1, source_target_pairs={{0,7},{2,4},{4,1},{6,2},{8,15},{10,12},{12,9},{14,10},{16,23},{18,... | collective-permute-start | bytes 1671176 | tf_op jit(solution)/shard_map/ppermute | solution.py:75
  25.2 14.1 %collective-permute-start.2 = (bf16[16,136,128]{2,1,0:T(8,128)(2,1)S(1)}, bf16[16,136,128]{2,1,0:T(8,128)(2,1)S(1)}, u32[]{:S(2)}, u32[]{:S(2)}) collective-permute-start(bf16[16,136,128]{2,1,0:T(8,128)(2,1)S(1)} %pad_maximum_fusion.8), channel_id=1, source_target_pairs={{0,2},{1,5},{2,0},{3,7},{4,3},{5,6},{6,4},{7,1},{8,10},{9,13},{10,... | collective-permute-start | bytes 1671176 | tf_op jit(solution)/shard_map/ppermute | solution.py:74
  46.2 3.6 %copy-start.17 = (f32[8]{0:T(128)S(1)}, f32[8]{0:T(128)}, u32[]{:S(2)}) copy-start(f32[8]{0:T(128)} %constant.86.clone) | copy-start | bytes 100
  46.2 4.9 %copy-start.16 = (f32[8]{0:T(128)S(1)}, f32[8]{0:T(128)}, u32[]{:S(2)}) copy-start(f32[8]{0:T(128)} %constant.87.clone) | copy-start | bytes 100
  47.7 15.0 %collective-permute-start.4 = (f32[2,16,136,128]{3,2,1,0:T(8,128)}, f32[2,16,136,128]{3,2,1,0:T(8,128)}, u32[]{:S(2)}, u32[]{:S(2)}) collective-permute-start(f32[2,16,136,128]{3,2,1,0:T(8,128)} %pad_maximum_fusion.1), channel_id=1, source_target_pairs={{0,1},{2,3},{4,5},{6,7},{1,0},{3,2},{5,4},{7,6},{8,9},{10,11},{12,... | collective-permute-start | bytes 6684680 | tf_op jit(solution)/shard_map/ppermute | solution.py:97
  52.4 1.8 %copy-start.7 = (bf16[16,8,16,128]{3,2,1,0:T(8,128)(2,1)S(1)}, bf16[16,8,16,128]{3,2,1,0:T(8,128)(2,1)}, u32[]{:S(2)}) copy-start(bf16[16,8,16,128]{3,2,1,0:T(8,128)(2,1)} %copy-done.6) | copy-start | bytes 1572868
  58.6 1.9 %copy-start.5 = (bf16[128,2048]{0,1:T(8,128)(2,1)S(1)}, bf16[128,2048]{0,1:T(8,128)(2,1)}, u32[]{:S(2)}) copy-start(bf16[128,2048]{0,1:T(8,128)(2,1)} %copy-done.4) | copy-start | bytes 1572868
  60.4 1.0 %copy-start.12 = (bf16[128,2048]{0,1:T(8,128)(2,1)S(1)}, bf16[128,2048]{0,1:T(8,128)(2,1)}, u32[]{:S(2)}) copy-start(bf16[128,2048]{0,1:T(8,128)(2,1)} %copy-done.11) | copy-start | bytes 1572868
  64.7 1.9 %copy-start.3 = (f32[16,136,128]{2,1,0:T(8,128)S(1)}, f32[16,136,128]{2,1,0:T(8,128)}, u32[]{:S(2)}) copy-start(f32[16,136,128]{2,1,0:T(8,128)} %copy-done.2) | copy-start | bytes 3342340
  66.6 1.0 %copy-start.10 = (bf16[128,2048]{0,1:T(8,128)(2,1)S(1)}, bf16[128,2048]{0,1:T(8,128)(2,1)}, u32[]{:S(2)}) copy-start(bf16[128,2048]{0,1:T(8,128)(2,1)} %copy-done.9) | copy-start | bytes 1572868
  68.3 1.2 %copy-start.1 = (f32[16,136,128]{2,1,0:T(8,128)S(1)}, f32[16,136,128]{2,1,0:T(8,128)}, u32[]{:S(2)}) copy-start(f32[16,136,128]{2,1,0:T(8,128)} %copy-done) | copy-start | bytes 3342340
  68.4 1.4 %copy-start.8 = (bf16[16,8,16,128]{3,2,1,0:T(8,128)(2,1)S(1)}, bf16[16,8,16,128]{3,2,1,0:T(8,128)(2,1)}, u32[]{:S(2)}) copy-start(bf16[16,8,16,128]{3,2,1,0:T(8,128)(2,1)} %copy-done.6) | copy-start | bytes 1572868
  69.7 1.4 %copy-start.13 = (f32[128,16,128]{0,2,1:T(8,128)S(1)}, f32[128,16,128]{0,2,1:T(8,128)}, u32[]{:S(2)}) copy-start(f32[128,16,128]{0,2,1:T(8,128)} %copy.67) | copy-start | bytes 3145732
  69.7 1.4 %copy-start.14 = (bf16[1,128,2048]{1,2,0:T(8,128)(2,1)S(1)}, bf16[1,128,2048]{1,2,0:T(8,128)(2,1)}, u32[]{:S(2)}) copy-start(bf16[1,128,2048]{1,2,0:T(8,128)(2,1)} %copy.56) | copy-start | bytes 1572868
  72.6 15.9 %collective-permute-start = (bf16[128,2048]{0,1:T(8,128)(2,1)S(1)}, bf16[128,2048]{0,1:T(8,128)(2,1)S(1)}, u32[]{:S(2)}, u32[]{:S(2)}) collective-permute-start(bf16[128,2048]{0,1:T(8,128)(2,1)S(1)} %get-tuple-element.34), channel_id=1, source_target_pairs={{0,24},{8,0},{16,8},{24,16},{1,25},{9,1},{17,9},{25,17},{2,26},{10... | collective-permute-start | bytes 1572872 | tf_op jit(solution)/shard_map/ppermute | solution.py:155
  76.2 23.1 %collective-permute-start.5 = (bf16[128,2048]{0,1:T(8,128)(2,1)S(1)}, bf16[128,2048]{0,1:T(8,128)(2,1)S(1)}, u32[]{:S(2)}, u32[]{:S(2)}) collective-permute-start(bf16[128,2048]{0,1:T(8,128)(2,1)S(1)} %get-tuple-element.35), channel_id=1, source_target_pairs={{0,24},{8,0},{16,8},{24,16},{1,25},{9,1},{17,9},{25,17},{2,26},{10... | collective-permute-start | bytes 1572872 | tf_op jit(solution)/shard_map/ppermute | solution.py:155
  (1 other events, 1.0 us)

commit v13 on v5

--- a/solution.py
+++ b/solution.py
@@ -91,7 +91,15 @@
 def passed_along(value, axis, steps):
     count = lax.axis_size(axis)
     pairs = [(source, (source + steps) % count) for source in range(count)]
-    return lax.ppermute(value, axis, pairs)
+    straight = [pair for pair in pairs if abs(pair[1] - pair[0]) == abs(steps)]
+    wrapped = [pair for pair in pairs if abs(pair[1] - pair[0]) != abs(steps)]
+    if not straight or not wrapped:
+        return lax.ppermute(value, axis, pairs)
+    near = lax.ppermute(value, axis, straight)
+    far = lax.ppermute(value, axis, wrapped)
+    here = lax.axis_index(axis)
+    takes_wrapped = (here - steps < 0) | (here - steps >= count)
+    return jax.tree.map(lambda a, b: jnp.where(takes_wrapped, b, a), near, far)
 
 
 def decay_logs(exponent, boundary, length):

time: 71.6 us -> 88.4 us (1.23)
  waiting for transfers between devices: 23.3 us -> 29.9 us
  starting transfers between devices: 13.3 us -> 16.9 us
  other arithmetic: 12.8 us -> 16.3 us
  matrix products: 12.5 us -> 15.1 us
    ppermute x2 -> x4, waiting for transfers between devices: 11.7 us -> 21.7 us  [the longest x2 12.6 us: passed_along(): far = lax.ppermute(value, axis, wrapped)]
    ppermute x2 -> x4, starting transfers between devices: 8.66 us -> 12.4 us  [the longest x2 9.86 us: passed_along(): far = lax.ppermute(value, axis, wrapped)]
    ppermute x3, waiting for transfers between devices: 10.6 us -> 7.14 us  [sent_narrow(): return widen(lax.ppermute(narrow(message), axis, pairs))]
    dot_general x1, matrix products: 1.64 us -> 2.86 us  [local(): jnp.einsum('hts,the->she', attention, grad_rows, precision=HIGH)]
    select_n x0 -> x1, other arithmetic: none -> 1.1 us  [passed_along(): return jax.tree.map(lambda a, b: jnp.where(takes_wrapped, b, a), near, far)]
    add x1, other arithmetic: 1.43 us -> 2.47 us  [scans_in(): incoming = incoming + weight[:, None, None] * got]
    dot_general x1, matrix products: 0.58 us -> 1.61 us  [local(): jnp.einsum('thd,shd->hts', grad_half, value_half, preferred_element_type=...]
    dot_general x1, matrix products: 0.56 us -> 1.55 us  [local(): jnp.einsum('thd,shd->hts', query_half, key_half, preferred_element_type=j...]
  transfers between devices with their start and end apart: 7 -> 9, of which waited for: 4 -> 7; matrix products, arithmetic and copies ran while one was open for 23% -> 26% of each run, Pallas kernels for 0% -> 0%
where the time goes in v13:
time: 88.4 us; the launch traced here: 87.6 us
  waiting for transfers between devices  29.9 us (34%)
  starting transfers between devices  16.9 us (19%)
  other arithmetic  16.3 us (18%)
  matrix products  15.1 us (17%)
  local copies, waits for them, and re-layouts  9.01 us (10%)
    ppermute x2, waiting for transfers between devices, passed_along(): far = lax.ppermute(value, axis, wrapped)  12.6 us
    ppermute x2, starting transfers between devices, passed_along(): far = lax.ppermute(value, axis, wrapped)  9.86 us
    ppermute x2, waiting for transfers between devices, passed_along(): near = lax.ppermute(value, axis, straight)  9.06 us
    ppermute x3, waiting for transfers between devices, sent_narrow(): return widen(lax.ppermute(narrow(message), axis, pairs))  7.14 us
    ppermute x3, starting transfers between devices, sent_narrow(): return widen(lax.ppermute(narrow(message), axis, pairs))  4.06 us
    unnamed x11, local copies, waits for them, and re-layouts  3.62 us
    dot_general x1, matrix products, local(): jnp.einsum('hts,the->she', attention, grad_rows, precision=HIGH)  2.86 us
    ppermute x2, starting transfers between devices, passed_along(): near = lax.ppermute(value, axis, straight)  2.57 us
  transfers between devices with their start and end apart: 9, of which 7 were waited for; matrix products, arithmetic and copies ran while one was open for 26% of the time, Pallas kernels for 0%

profile of v13, /device:TPU:0, one launch (start us, length us, event | category | flops | bytes accessed | tf_op | source)
XLA Modules:
  0.0 87.6 jit_solution(18062952029185782571)
XLA Ops:
  2.6 1.3 %copy.35 = bf16[1,128,2048]{1,2,0:T(8,128)(2,1)S(1)} copy(bf16[1,128,2048]{2,1,0:T(8,128)(2,1)} %param.5) | data formatting | bytes 1048576 | tf_op args[0]
  5.3 1.2 %fusion.16 = f32[16,128,128]{2,1,0:T(8,128)S(1)} fusion(bf16[128,16,128]{0,2,1:T(8,128)(2,1)S(1)} %bitcast.119, bf16[128,16,128]{0,2,1:T(8,128)(2,1)S(1)} %bitcast.112, f32[128,16]{0,1:T(8,128)S(1)} %copy.38), kind=kOutput, calls=%fused_computation.40 | convolution fusion | flops 403177472 | bytes 2105344 | tf_op jit(solution)/shard_map/shd,she->hde/dot_general | solution.py:141
  6.5 1.8 %broadcast_select_fusion.2 = (f32[16,128,128]{2,1,0:T(8,128)S(1)}, f32[16,128,128]{2,1,0:T(8,128)}) fusion(f32[16,128,128]{2,1,0:T(8,128)S(1)} %fusion.16, pred[]{:T(512)S(6)} %eq.29, bf16[128,16,128]{2,1,0:T(8,128)(2,1)S(1)} %bitcast.108, bf16[128,16,128]{0,2,1:T(8,128)(2,1)S(1)} %bitcast.116, f32[128,16]{0,1:T(8,128)S(1)} %copy.36), kind=kOutput, calls=%fused_computation.52 | convolution fusion | flops 403701760 | bytes 4202497 | tf_op jit(solution)/shard_map/shd,she->hde/dot_general | solution.py:144
  8.4 1.1 %pad_maximum_fusion = f32[16,136,128]{2,1,0:T(8,128)} fusion(f32[16,8,128]{2,1,0:T(8,128)S(1)} %broadcast_in_dim.34, f32[16,128,128]{2,1,0:T(8,128)S(1)} %get-tuple-element.24), kind=kLoop, calls=%fused_computation.17 | loop fusion | flops 278528 | bytes 2228224 | tf_op jit(solution)/shard_map/concatenate | solution.py:16
  10.0 1.6 %fusion.1 = f32[16,128,128]{1,2,0:T(8,128)} fusion(bf16[128,16,128]{0,2,1:T(8,128)(2,1)S(1)} %bitcast.120, f32[16,128]{1,0:T(8,128)S(1)} %copy.46, pred[128,128]{0,1:T(8,128)(4,1)S(1)} %iota_compare_fusion, bf16[128,16,128]{2,1,0:T(8,128)(2,1)S(1)} %bitcast.109), kind=kOutput, calls=%fused_computation.9 | convolution fusion | flops 68157440 | bytes 2121728 | tf_op jit(solution)/shard_map/thd,shd->hts/dot_general | solution.py:153
  11.6 1.5 %convolution_multiply_fusion.1 = f32[16,128,128]{1,2,0:T(8,128)} fusion(bf16[128,16,128]{0,2,1:T(8,128)(2,1)S(1)} %bitcast.117, bf16[128,16,128]{0,2,1:T(8,128)(2,1)S(1)} %bitcast.113, f32[16,128]{1,0:T(8,128)S(1)} %copy.46, pred[128,128]{0,1:T(8,128)(4,1)S(1)} %iota_compare_fusion), kind=kOutput, calls=%fused_computation.5 | convolution fusion | flops 68157440 | bytes 2121728 | tf_op jit(solution)/shard_map/thd,shd->hts/dot_general | solution.py:159
  13.2 2.0 %copy.43 = bf16[1,128,2048]{1,2,0:T(8,128)(2,1)} copy(bf16[1,128,2048]{2,1,0:T(8,128)(2,1)} %param.6) | data formatting | bytes 1048576 | tf_op args[1]
  15.2 2.9 %fusion = f32[128,16,128]{2,0,1:T(8,128)} fusion(f32[16,128,128]{1,2,0:T(8,128)} %convolution_multiply_fusion.1, bf16[128,16,128]{2,1,0:T(8,128)(2,1)S(1)} %bitcast.110), kind=kOutput, calls=%fused_computation.4 | convolution fusion | flops 402915328 | bytes 2621440 | tf_op jit(solution)/shard_map/hts,the->she/dot_general | solution.py:161
  18.1 2.6 %copy.53 = f32[128,16,128]{0,2,1:T(8,128)} copy(f32[128,16,128]{2,0,1:T(8,128)} %fusion) | data formatting | bytes 2097152 | tf_op jit(solution)/shard_map/mul | solution.py:161
  20.6 2.0 %convolution_multiply_fusion.3 = f32[16,128,128]{2,1,0:T(8,128)S(1)} fusion(bf16[128,16,128]{0,2,1:T(8,128)(2,1)S(1)} %bitcast.114, f32[16,128,128]{1,2,0:T(8,128)} %fusion.1), kind=kOutput, calls=%fused_computation.7 | convolution fusion | flops 402915328 | bytes 2621440 | tf_op jit(solution)/shard_map/hts,shd->thd/dot_general | solution.py:156
  22.6 1.2 %convolution_multiply_fusion.2 = f32[16,128,128]{2,1,0:T(8,128)S(1)} fusion(bf16[128,16,128]{0,2,1:T(8,128)(2,1)S(1)} %bitcast.118, f32[16,128,128]{1,2,0:T(8,128)S(1)} %copy-done), kind=kOutput, calls=%fused_computation.6 | convolution fusion | flops 402915328 | bytes 2621440 | tf_op jit(solution)/shard_map/hts,thd->shd/dot_general | solution.py:157
  24.0 1.9 %fusion.10 = bf16[128,2048]{0,1:T(8,128)(2,1)} fusion(f32[16,128,128]{2,1,0:T(8,128)S(1)} %convolution_multiply_fusion.2, f32[16,128,128]{2,1,0:T(8,128)S(1)} %convolution_multiply_fusion.3, f32[128,16,128]{0,2,1:T(8,128)S(1)} %copy-done.1, bf16[1,128,2048]{1,2,0:T(8,128)(2,1)S(1)} %copy-done.3, f32[2048]{0:T(1024)S(1)} %bitcast.131, f32[2048]{0:T(1024)S(1)} %bitcast.125, ...), kind=kLoop, calls=%fused_computation.24 | loop fusion | flops 2097152 | bytes 4218880 | tf_op jit(solution)/shard_map/convert_element_type | solution.py:166
  25.9 7.3 %collective-permute-start.4 = (bf16[128,2048]{0,1:T(8,128)(2,1)}, bf16[128,2048]{0,1:T(8,128)(2,1)}, u32[]{:S(2)}, u32[]{:S(2)}) collective-permute-start(bf16[128,2048]{0,1:T(8,128)(2,1)} %fusion.10), channel_id=1, source_target_pairs={{0,24},{1,25},{2,26},{3,27},{4,28},{5,29},{6,30},{7,31}} | collective-permute-start | bytes 1572872 | tf_op jit(solution)/shard_map/ppermute | solution.py:99
  33.2 1.3 %collective-permute-start.5 = (bf16[128,2048]{0,1:T(8,128)(2,1)}, bf16[128,2048]{0,1:T(8,128)(2,1)}, u32[]{:S(2)}, u32[]{:S(2)}) collective-permute-start(bf16[128,2048]{0,1:T(8,128)(2,1)} %fusion.10), channel_id=1, source_target_pairs={{8,0},{16,8},{24,16},{9,1},{17,9},{25,17},{10,2},{18,10},{26,18},{... | collective-permute-start | bytes 1572872 | tf_op jit(solution)/shard_map/ppermute | solution.py:98
  36.0 1.8 %add_convert_fusion.1 = bf16[16,128,128]{2,1,0:T(8,128)(2,1)S(1)} fusion(f32[16,128,128]{2,1,0:T(8,128)S(1)} %fusion.16, f32[16,128,128]{2,1,0:T(8,128)} %get-tuple-element.25, f32[16,136,128]{2,1,0:T(8,128)} %collective-permute-done, f32[16]{0:T(128)S(1)} %fusion.34, pred[]{:T(512)S(6)} %eq.29), kind=kLoop, calls=%fused_computation.39 | loop fusion | flops 1048576 | bytes 3670081 | tf_op jit(solution)/shard_map/convert_element_type | solution.py:30
  37.9 1.3 %collective-permute-start.1 = (bf16[16,136,128]{2,1,0:T(8,128)(2,1)S(1)}, bf16[16,136,128]{2,1,0:T(8,128)(2,1)S(1)}, u32[]{:S(2)}, u32[]{:S(2)}) collective-permute-start(bf16[16,136,128]{2,1,0:T(8,128)(2,1)S(1)} %pad_maximum_fusion.1), channel_id=1, source_target_pairs={{1,3},{3,5},{5,7},{6,4},{4,2},{2,0},{9,11},{11,13},{13,15},{14,12}... | collective-permute-start | bytes 1671176 | tf_op jit(solution)/shard_map/ppermute | solution.py:40
  39.2 1.3 %collective-permute-start.2 = (bf16[16,136,128]{2,1,0:T(8,128)(2,1)S(1)}, bf16[16,136,128]{2,1,0:T(8,128)(2,1)}, u32[]{:S(2)}, u32[]{:S(2)}) collective-permute-start(bf16[16,136,128]{2,1,0:T(8,128)(2,1)S(1)} %pad_maximum_fusion.1), channel_id=1, source_target_pairs={{1,5},{3,7},{6,2},{4,0},{9,13},{11,15},{14,10},{12,8},{17,21},{19,... | collective-permute-start | bytes 1671176 | tf_op jit(solution)/shard_map/ppermute | solution.py:40
  40.5 1.5 %collective-permute-start.3 = (bf16[16,136,128]{2,1,0:T(8,128)(2,1)S(1)}, bf16[16,136,128]{2,1,0:T(8,128)(2,1)S(1)}, u32[]{:S(2)}, u32[]{:S(2)}) collective-permute-start(bf16[16,136,128]{2,1,0:T(8,128)(2,1)S(1)} %pad_maximum_fusion.1), channel_id=1, source_target_pairs={{1,7},{6,0},{9,15},{14,8},{17,23},{22,16},{25,31},{30,24}} | collective-permute-start | bytes 1671176 | tf_op jit(solution)/shard_map/ppermute | solution.py:40
  42.0 2.5 %collective-permute-done.4 = bf16[128,2048]{0,1:T(8,128)(2,1)} collective-permute-done((bf16[128,2048]{0,1:T(8,128)(2,1)}, bf16[128,2048]{0,1:T(8,128)(2,1)}, u32[]{:S(2)}, u32[]{:S(2)}) %collective-permute-start.4) | collective-permute-done | bytes 524320 | tf_op jit(solution)/shard_map/ppermute | solution.py:99
  44.5 4.9 %collective-permute-done.5 = bf16[128,2048]{0,1:T(8,128)(2,1)} collective-permute-done((bf16[128,2048]{0,1:T(8,128)(2,1)}, bf16[128,2048]{0,1:T(8,128)(2,1)}, u32[]{:S(2)}, u32[]{:S(2)}) %collective-permute-start.5) | collective-permute-done | bytes 524320 | tf_op jit(solution)/shard_map/ppermute | solution.py:98
  49.4 1.1 %broadcast_select_fusion = bf16[128,2048]{0,1:T(8,128)(2,1)S(1)} fusion(bf16[128,2048]{0,1:T(8,128)(2,1)} %collective-permute-done.4, bf16[128,2048]{0,1:T(8,128)(2,1)} %collective-permute-done.5, pred[]{:T(512)S(6)} %or.4), kind=kLoop, calls=%fused_computation.49 | loop fusion | flops 262144 | bytes 1572865 | tf_op jit(solution)/shard_map/jit(_where)/select_n | solution.py:102
  50.5 4.7 %collective-permute-done.1 = bf16[16,136,128]{2,1,0:T(8,128)(2,1)S(1)} collective-permute-done((bf16[16,136,128]{2,1,0:T(8,128)(2,1)S(1)}, bf16[16,136,128]{2,1,0:T(8,128)(2,1)S(1)}, u32[]{:S(2)}, u32[]{:S(2)}) %collective-permute-start.1) | collective-permute-done | bytes 557088 | tf_op jit(solution)/shard_map/ppermute | solution.py:40
  55.2 2.4 %collective-permute-done.2 = bf16[16,136,128]{2,1,0:T(8,128)(2,1)} collective-permute-done((bf16[16,136,128]{2,1,0:T(8,128)(2,1)S(1)}, bf16[16,136,128]{2,1,0:T(8,128)(2,1)}, u32[]{:S(2)}, u32[]{:S(2)}) %collective-permute-start.2) | collective-permute-done | bytes 557088 | tf_op jit(solution)/shard_map/ppermute | solution.py:40
  58.7 2.5 %multiply_add_fusion.1 = f32[16,128,128]{2,1,0:T(8,128)} fusion(bf16[16,136,128]{2,1,0:T(8,128)(2,1)S(1)} %collective-permute-done.3, bf16[16,136,128]{2,1,0:T(8,128)(2,1)} %collective-permute-done.2, bf16[16,136,128]{2,1,0:T(8,128)(2,1)S(1)} %collective-permute-done.1, f32[16]{0:T(128)S(1)} %get-tuple-element.12, f32[16]{0:T(128)S(1)} %get-tuple-element.11), kind=kLoop, calls=%fused_computation.38 | loop fusion | flops 1835008 | bytes 2621568 | tf_op jit(solution)/shard_map/add | solution.py:71
  61.2 1.7 %multiply_add_fusion = f32[16,128,128]{2,1,0:T(8,128)S(1)} fusion(f32[16,128,128]{2,1,0:T(8,128)} %multiply_add_fusion.1, f32[16,136,128]{2,1,0:T(8,128)} %collective-permute-done, f32[16]{0:T(128)S(1)} %get-tuple-element.9), kind=kLoop, calls=%fused_computation.36 | loop fusion | flops 524288 | bytes 3145792 | tf_op jit(solution)/shard_map/add | solution.py:87
  63.0 1.1 %collective-permute-done.6 = f32[16,128,128]{2,1,0:T(8,128)S(1)} collective-permute-done((f32[16,128,128]{2,1,0:T(8,128)}, f32[16,128,128]{2,1,0:T(8,128)S(1)}, u32[]{:S(2)}, u32[]{:S(2)}) %collective-permute-start.6) | collective-permute-done | bytes 1048608 | tf_op jit(solution)/shard_map/ppermute | solution.py:86
  65.8 1.3 %fusion.4 = f32[128,16,128]{0,2,1:T(8,128)S(1)} fusion(f32[16,128,128]{2,1,0:T(8,128)S(1)} %multiply_add_fusion, f32[16,128,128]{2,1,0:T(8,128)S(1)} %collective-permute-done.6, f32[128,16]{0,1:T(8,128)S(1)} %copy.54, pred[]{:T(512)S(6)} %eq.29, bf16[128,16,128]{2,1,0:T(8,128)(2,1)S(1)} %bitcast.111), kind=kOutput, calls=%fused_computation.16 | convolution fusion | flops 403177472 | bytes 3678209 | tf_op jit(solution)/shard_map/the,hde->thd/dot_general | solution.py:172
  67.0 1.2 %fusion.13 = bf16[128,2048]{0,1:T(8,128)(2,1)S(1)} fusion(f32[128,16,128]{0,2,1:T(8,128)S(1)} %fusion.2, f32[128,16,128]{0,2,1:T(8,128)S(1)} %fusion.3, f32[128,16,128]{0,2,1:T(8,128)S(1)} %fusion.4, f32[2048]{0:T(1024)S(1)} %bitcast.132, f32[2048]{0:T(1024)S(1)} %bitcast.126, f32[2048]{0:T(1024)S(1)} %bitcast.129), kind=kLoop, calls=%fused_computation.29 | loop fusion | flops 1572864 | bytes 3694592 | tf_op jit(solution)/shard_map/convert_element_type | solution.py:179
  68.2 2.5 %collective-permute-start.7 = (bf16[128,2048]{0,1:T(8,128)(2,1)S(1)}, bf16[128,2048]{0,1:T(8,128)(2,1)S(1)}, u32[]{:S(2)}, u32[]{:S(2)}) collective-permute-start(bf16[128,2048]{0,1:T(8,128)(2,1)S(1)} %fusion.13), channel_id=1, source_target_pairs={{0,24},{1,25},{2,26},{3,27},{4,28},{5,29},{6,30},{7,31}} | collective-permute-start | bytes 1572872 | tf_op jit(solution)/shard_map/ppermute | solution.py:99
  70.8 1.3 %collective-permute-start.8 = (bf16[128,2048]{0,1:T(8,128)(2,1)S(1)}, bf16[128,2048]{0,1:T(8,128)(2,1)S(1)}, u32[]{:S(2)}, u32[]{:S(2)}) collective-permute-start(bf16[128,2048]{0,1:T(8,128)(2,1)S(1)} %fusion.13), channel_id=1, source_target_pairs={{8,0},{16,8},{24,16},{9,1},{17,9},{25,17},{10,2},{18,10},{26,18},{... | collective-permute-start | bytes 1572872 | tf_op jit(solution)/shard_map/ppermute | solution.py:98
  72.1 10.1 %collective-permute-done.7 = bf16[128,2048]{0,1:T(8,128)(2,1)S(1)} collective-permute-done((bf16[128,2048]{0,1:T(8,128)(2,1)S(1)}, bf16[128,2048]{0,1:T(8,128)(2,1)S(1)}, u32[]{:S(2)}, u32[]{:S(2)}) %collective-permute-start.7) | collective-permute-done | bytes 524320 | tf_op jit(solution)/shard_map/ppermute | solution.py:99
  82.2 4.1 %collective-permute-done.8 = bf16[128,2048]{0,1:T(8,128)(2,1)S(1)} collective-permute-done((bf16[128,2048]{0,1:T(8,128)(2,1)S(1)}, bf16[128,2048]{0,1:T(8,128)(2,1)S(1)}, u32[]{:S(2)}, u32[]{:S(2)}) %collective-permute-start.8) | collective-permute-done | bytes 524320 | tf_op jit(solution)/shard_map/ppermute | solution.py:98
  (52 shorter events, 10.3 us)
Async XLA Ops:
  4.0 1.0 %copy-start.2 = (bf16[1,128,2048]{2,1,0:T(8,128)(2,1)S(1)}, bf16[1,128,2048]{2,1,0:T(8,128)(2,1)}, u32[]{:S(2)}) copy-start(bf16[1,128,2048]{2,1,0:T(8,128)(2,1)} %param.6) | copy-start | bytes 1572868
  9.5 25.2 %collective-permute-start = (f32[16,136,128]{2,1,0:T(8,128)}, f32[16,136,128]{2,1,0:T(8,128)}, u32[]{:S(2)}, u32[]{:S(2)}) collective-permute-start(f32[16,136,128]{2,1,0:T(8,128)} %pad_maximum_fusion), channel_id=1, source_target_pairs={{0,1},{2,3},{4,5},{6,7},{1,0},{3,2},{5,4},{7,6},{8,9},{10,11},{12,... | collective-permute-start | bytes 3342344 | tf_op jit(solution)/shard_map/ppermute | solution.py:63
  20.6 2.0 %copy-start = (f32[16,128,128]{1,2,0:T(8,128)S(1)}, f32[16,128,128]{1,2,0:T(8,128)}, u32[]{:S(2)}) copy-start(f32[16,128,128]{1,2,0:T(8,128)} %fusion.1) | copy-start | bytes 3145732
  22.6 1.2 %copy-start.1 = (f32[128,16,128]{0,2,1:T(8,128)S(1)}, f32[128,16,128]{0,2,1:T(8,128)}, u32[]{:S(2)}) copy-start(f32[128,16,128]{0,2,1:T(8,128)} %copy.53) | copy-start | bytes 3145732
  22.6 1.3 %copy-start.3 = (bf16[1,128,2048]{1,2,0:T(8,128)(2,1)S(1)}, bf16[1,128,2048]{1,2,0:T(8,128)(2,1)}, u32[]{:S(2)}) copy-start(bf16[1,128,2048]{1,2,0:T(8,128)(2,1)} %copy.43) | copy-start | bytes 1572868
  25.9 18.7 %collective-permute-start.4 = (bf16[128,2048]{0,1:T(8,128)(2,1)}, bf16[128,2048]{0,1:T(8,128)(2,1)}, u32[]{:S(2)}, u32[]{:S(2)}) collective-permute-start(bf16[128,2048]{0,1:T(8,128)(2,1)} %fusion.10), channel_id=1, source_target_pairs={{0,24},{1,25},{2,26},{3,27},{4,28},{5,29},{6,30},{7,31}} | collective-permute-start | bytes 1572872 | tf_op jit(solution)/shard_map/ppermute | solution.py:99
  33.2 16.3 %collective-permute-start.5 = (bf16[128,2048]{0,1:T(8,128)(2,1)}, bf16[128,2048]{0,1:T(8,128)(2,1)}, u32[]{:S(2)}, u32[]{:S(2)}) collective-permute-start(bf16[128,2048]{0,1:T(8,128)(2,1)} %fusion.10), channel_id=1, source_target_pairs={{8,0},{16,8},{24,16},{9,1},{17,9},{25,17},{10,2},{18,10},{26,18},{... | collective-permute-start | bytes 1572872 | tf_op jit(solution)/shard_map/ppermute | solution.py:98
  37.9 17.3 %collective-permute-start.1 = (bf16[16,136,128]{2,1,0:T(8,128)(2,1)S(1)}, bf16[16,136,128]{2,1,0:T(8,128)(2,1)S(1)}, u32[]{:S(2)}, u32[]{:S(2)}) collective-permute-start(bf16[16,136,128]{2,1,0:T(8,128)(2,1)S(1)} %pad_maximum_fusion.1), channel_id=1, source_target_pairs={{1,3},{3,5},{5,7},{6,4},{4,2},{2,0},{9,11},{11,13},{13,15},{14,12}... | collective-permute-start | bytes 1671176 | tf_op jit(solution)/shard_map/ppermute | solution.py:40
  39.2 18.4 %collective-permute-start.2 = (bf16[16,136,128]{2,1,0:T(8,128)(2,1)S(1)}, bf16[16,136,128]{2,1,0:T(8,128)(2,1)}, u32[]{:S(2)}, u32[]{:S(2)}) collective-permute-start(bf16[16,136,128]{2,1,0:T(8,128)(2,1)S(1)} %pad_maximum_fusion.1), channel_id=1, source_target_pairs={{1,5},{3,7},{6,2},{4,0},{9,13},{11,15},{14,10},{12,8},{17,21},{19,... | collective-permute-start | bytes 1671176 | tf_op jit(solution)/shard_map/ppermute | solution.py:40
  40.5 18.2 %collective-permute-start.3 = (bf16[16,136,128]{2,1,0:T(8,128)(2,1)S(1)}, bf16[16,136,128]{2,1,0:T(8,128)(2,1)S(1)}, u32[]{:S(2)}, u32[]{:S(2)}) collective-permute-start(bf16[16,136,128]{2,1,0:T(8,128)(2,1)S(1)} %pad_maximum_fusion.1), channel_id=1, source_target_pairs={{1,7},{6,0},{9,15},{14,8},{17,23},{22,16},{25,31},{30,24}} | collective-permute-start | bytes 1671176 | tf_op jit(solution)/shard_map/ppermute | solution.py:40
  61.2 2.9 %collective-permute-start.6 = (f32[16,128,128]{2,1,0:T(8,128)}, f32[16,128,128]{2,1,0:T(8,128)S(1)}, u32[]{:S(2)}, u32[]{:S(2)}) collective-permute-start(f32[16,128,128]{2,1,0:T(8,128)} %multiply_add_fusion.1), channel_id=1, source_target_pairs={{0,1},{2,3},{4,5},{6,7},{1,0},{3,2},{5,4},{7,6},{8,9},{10,11},{12,... | collective-permute-start | bytes 3145736 | tf_op jit(solution)/shard_map/ppermute | solution.py:86
  68.2 14.0 %collective-permute-start.7 = (bf16[128,2048]{0,1:T(8,128)(2,1)S(1)}, bf16[128,2048]{0,1:T(8,128)(2,1)S(1)}, u32[]{:S(2)}, u32[]{:S(2)}) collective-permute-start(bf16[128,2048]{0,1:T(8,128)(2,1)S(1)} %fusion.13), channel_id=1, source_target_pairs={{0,24},{1,25},{2,26},{3,27},{4,28},{5,29},{6,30},{7,31}} | collective-permute-start | bytes 1572872 | tf_op jit(solution)/shard_map/ppermute | solution.py:99
  70.8 15.6 %collective-permute-start.8 = (bf16[128,2048]{0,1:T(8,128)(2,1)S(1)}, bf16[128,2048]{0,1:T(8,128)(2,1)S(1)}, u32[]{:S(2)}, u32[]{:S(2)}) collective-permute-start(bf16[128,2048]{0,1:T(8,128)(2,1)S(1)} %fusion.13), channel_id=1, source_target_pairs={{8,0},{16,8},{24,16},{9,1},{17,9},{25,17},{10,2},{18,10},{26,18},{... | collective-permute-start | bytes 1572872 | tf_op jit(solution)/shard_map/ppermute | solution.py:98

commit v14 on v5

--- a/solution.py
+++ b/solution.py
@@ -8,7 +8,7 @@
 CH = 64
 
 
-HIGH = lax.Precision.HIGHEST
+HIGH = lax.Precision.HIGH
 
 
 def packed(state, rate):

time: 71.6 us -> 69.2 us (0.966)
  matrix products: 12.5 us -> 10.3 us
  transfers between devices with their start and end apart: 7 -> 7, of which waited for: 4 -> 4; matrix products, arithmetic and copies ran while one was open for 23% -> 22% of each run, Pallas kernels for 0% -> 0%
where the time goes in v14:
time: 69.2 us; the launch traced here: 68.6 us
  waiting for transfers between devices  23.6 us (34%)
  other arithmetic  12.8 us (18%)
  starting transfers between devices  12.8 us (18%)
  matrix products  10.3 us (15%)
  local copies, waits for them, and re-layouts  8.91 us (13%)
    ppermute x2, waiting for transfers between devices, passed_along(): return lax.ppermute(value, axis, pairs)  11.7 us
    ppermute x3, waiting for transfers between devices, sent_narrow(): return widen(lax.ppermute(narrow(message), axis, pairs))  10.8 us
    ppermute x2, starting transfers between devices, passed_along(): return lax.ppermute(value, axis, pairs)  8.33 us
    ppermute x3, starting transfers between devices, sent_narrow(): return widen(lax.ppermute(narrow(message), axis, pairs))  4.01 us
    unnamed x13, local copies, waits for them, and re-layouts  3.52 us
    mul x1, local copies, waits for them, and re-layouts, local(): scale * jnp.einsum('hts,the->she', attention, grad_rows, precision=HIGH)  2.56 us
    convert_element_type x1, other arithmetic, narrow(): return jnp.concatenate([state.astype(jnp.bfloat16), tile], axis=1)  1.91 us
    dot_general x1, matrix products, local(): jnp.einsum('hts,thd->shd', mixing, queries, precision=HIGH)  1.82 us
  transfers between devices with their start and end apart: 7, of which 4 were waited for; matrix products, arithmetic and copies ran while one was open for 22% of the time, Pallas kernels for 0%

profile of v14, /device:TPU:0, one launch (start us, length us, event | category | flops | bytes accessed | tf_op | source)
XLA Modules:
  0.0 68.6 jit_solution(14336866985412013692)
XLA Ops:
  0.1 0.7 compare_bitcast_fusion
  0.9 0.7 log_bitcast_fusion
  1.9 0.7 %fusion.36 = (f32[1,1,2048]{2,0,1:T(1,128)S(1)}, f32[1,1,2048]{2,0,1:T(1,128)S(1)}, f32[1,1,2048]{2,0,1:T(1,128)S(1)}) fusion(f32[1,3,2048]{2,0,1:T(1,128)} %param.7), kind=kLoop, calls=%fused_computation.82 | loop fusion | bytes 49152 | tf_op jit(solution)/shard_map/slice | solution.py:110
  2.6 1.3 %copy.35 = bf16[1,128,2048]{1,2,0:T(8,128)(2,1)S(1)} copy(bf16[1,128,2048]{2,1,0:T(8,128)(2,1)} %param.5) | data formatting | bytes 1048576 | tf_op args[0]
  4.0 1.0 %fusion.7 = (bf16[128,2048]{0,1:T(8,128)(2,1)S(1)}, bf16[128,2048]{0,1:T(8,128)(2,1)S(1)}, bf16[128,2048]{0,1:T(8,128)(2,1)S(1)}) fusion(bf16[1,128,2048]{1,2,0:T(8,128)(2,1)S(1)} %copy.35, f32[2048]{0:T(1024)S(1)} %bitcast.124, f32[2048]{0:T(1024)S(1)} %bitcast.130, f32[2048]{0:T(1024)S(1)} %bitcast.127), kind=kLoop, calls=%fused_computation.20 | loop fusion | flops 1835008 | bytes 2121728 | tf_op jit(solution)/shard_map/convert_element_type | solution.py:110
  5.3 0.9 %fusion.16 = f32[16,128,128]{2,1,0:T(8,128)S(1)} fusion(bf16[128,16,128]{0,2,1:T(8,128)(2,1)S(1)} %bitcast.119, bf16[128,16,128]{0,2,1:T(8,128)(2,1)S(1)} %bitcast.112, f32[128,16]{0,1:T(8,128)S(1)} %copy.38), kind=kOutput, calls=%fused_computation.40 | convolution fusion | flops 201850880 | bytes 2105344 | tf_op jit(solution)/shard_map/shd,she->hde/dot_general | solution.py:133
  6.2 1.5 %broadcast_select_fusion.1 = (f32[16,128,128]{2,1,0:T(8,128)S(1)}, f32[16,128,128]{2,1,0:T(8,128)}) fusion(f32[16,128,128]{2,1,0:T(8,128)S(1)} %fusion.16, pred[]{:T(512)S(6)} %eq.29, bf16[128,16,128]{2,1,0:T(8,128)(2,1)S(1)} %bitcast.108, bf16[128,16,128]{0,2,1:T(8,128)(2,1)S(1)} %bitcast.116, f32[128,16]{0,1:T(8,128)S(1)} %copy.36), kind=kOutput, calls=%fused_computation.51 | convolution fusion | flops 202375168 | bytes 4202497 | tf_op jit(solution)/shard_map/shd,she->hde/dot_general | solution.py:136
  7.8 1.1 %pad_maximum_fusion = f32[16,136,128]{2,1,0:T(8,128)} fusion(f32[16,8,128]{2,1,0:T(8,128)S(1)} %broadcast_in_dim.34, f32[16,128,128]{2,1,0:T(8,128)S(1)} %get-tuple-element.24), kind=kLoop, calls=%fused_computation.17 | loop fusion | flops 278528 | bytes 2228224 | tf_op jit(solution)/shard_map/concatenate | solution.py:16
  9.4 2.0 %copy.43 = bf16[1,128,2048]{1,2,0:T(8,128)(2,1)} copy(bf16[1,128,2048]{2,1,0:T(8,128)(2,1)} %param.6) | data formatting | bytes 1048576 | tf_op args[1]
  12.0 1.4 %fusion = f32[128,16,128]{2,0,1:T(8,128)} fusion(f32[16,128,128]{1,2,0:T(8,128)S(1)} %convolution_multiply_fusion.1, bf16[128,16,128]{2,1,0:T(8,128)(2,1)S(1)} %bitcast.109), kind=kOutput, calls=%fused_computation.4 | convolution fusion | flops 201588736 | bytes 2621440 | tf_op jit(solution)/shard_map/hts,the->she/dot_general | solution.py:153
  13.5 2.6 %copy.53 = f32[128,16,128]{0,2,1:T(8,128)} copy(f32[128,16,128]{2,0,1:T(8,128)} %fusion) | data formatting | bytes 2097152 | tf_op jit(solution)/shard_map/mul | solution.py:153
  16.3 0.6 fusion.1
  16.8 1.4 %convolution_multiply_fusion.3 = f32[16,128,128]{2,1,0:T(8,128)} fusion(bf16[128,16,128]{0,2,1:T(8,128)(2,1)S(1)} %bitcast.114, f32[16,128,128]{1,2,0:T(8,128)S(1)} %fusion.1), kind=kOutput, calls=%fused_computation.7 | convolution fusion | flops 201588736 | bytes 2621440 | tf_op jit(solution)/shard_map/hts,shd->thd/dot_general | solution.py:148
  18.3 1.8 %convolution_multiply_fusion.2 = f32[16,128,128]{2,1,0:T(8,128)} fusion(bf16[128,16,128]{0,2,1:T(8,128)(2,1)S(1)} %bitcast.118, f32[16,128,128]{1,2,0:T(8,128)S(1)} %fusion.1), kind=kOutput, calls=%fused_computation.6 | convolution fusion | flops 201588736 | bytes 2621440 | tf_op jit(solution)/shard_map/hts,thd->shd/dot_general | solution.py:149
  20.1 1.0 %slice_reduce_fusion = (f32[16]{0:T(128)S(1)}, f32[16]{0:T(128)S(1)}) fusion(f32[16,136,128]{2,1,0:T(8,128)} %collective-permute-done, f32[16,1,1]{2,1,0:T(1,128)S(1)} %copy.40), kind=kLoop, calls=%fused_computation.69 | loop fusion | flops 16 | bytes 256 | tf_op jit(solution)/shard_map/slice | solution.py:21
  21.5 1.9 %add_convert_fusion.1 = bf16[16,128,128]{2,1,0:T(8,128)(2,1)S(1)} fusion(f32[16,128,128]{2,1,0:T(8,128)S(1)} %fusion.16, f32[16,128,128]{2,1,0:T(8,128)} %get-tuple-element.25, f32[16,136,128]{2,1,0:T(8,128)} %collective-permute-done, f32[16]{0:T(128)S(1)} %fusion.34, pred[]{:T(512)S(6)} %eq.29), kind=kLoop, calls=%fused_computation.39 | loop fusion | flops 1048576 | bytes 3670081 | tf_op jit(solution)/shard_map/convert_element_type | solution.py:30
  23.5 1.4 %collective-permute-start.1 = (bf16[16,136,128]{2,1,0:T(8,128)(2,1)S(1)}, bf16[16,136,128]{2,1,0:T(8,128)(2,1)S(1)}, u32[]{:S(2)}, u32[]{:S(2)}) collective-permute-start(bf16[16,136,128]{2,1,0:T(8,128)(2,1)S(1)} %pad_maximum_fusion.1), channel_id=1, source_target_pairs={{1,3},{3,5},{5,7},{6,4},{4,2},{2,0},{9,11},{11,13},{13,15},{14,12}... | collective-permute-start | bytes 1671176 | tf_op jit(solution)/shard_map/ppermute | solution.py:40
  24.9 1.3 %collective-permute-start.2 = (bf16[16,136,128]{2,1,0:T(8,128)(2,1)S(1)}, bf16[16,136,128]{2,1,0:T(8,128)(2,1)S(1)}, u32[]{:S(2)}, u32[]{:S(2)}) collective-permute-start(bf16[16,136,128]{2,1,0:T(8,128)(2,1)S(1)} %pad_maximum_fusion.1), channel_id=1, source_target_pairs={{1,5},{3,7},{6,2},{4,0},{9,13},{11,15},{14,10},{12,8},{17,21},{19,... | collective-permute-start | bytes 1671176 | tf_op jit(solution)/shard_map/ppermute | solution.py:40
  26.2 1.3 %collective-permute-start.3 = (bf16[16,136,128]{2,1,0:T(8,128)(2,1)S(1)}, bf16[16,136,128]{2,1,0:T(8,128)(2,1)S(1)}, u32[]{:S(2)}, u32[]{:S(2)}) collective-permute-start(bf16[16,136,128]{2,1,0:T(8,128)(2,1)S(1)} %pad_maximum_fusion.1), channel_id=1, source_target_pairs={{1,7},{6,0},{9,15},{14,8},{17,23},{22,16},{25,31},{30,24}} | collective-permute-start | bytes 1671176 | tf_op jit(solution)/shard_map/ppermute | solution.py:40
  27.6 1.2 %fusion.10 = bf16[128,2048]{0,1:T(8,128)(2,1)S(1)} fusion(f32[16,128,128]{2,1,0:T(8,128)S(1)} %copy-done.2, f32[16,128,128]{2,1,0:T(8,128)S(1)} %copy-done.1, f32[128,16,128]{0,2,1:T(8,128)S(1)} %copy-done, bf16[1,128,2048]{1,2,0:T(8,128)(2,1)S(1)} %copy-done.4, f32[2048]{0:T(1024)S(1)} %bitcast.125, f32[2048]{0:T(1024)S(1)} %bitcast.131, f32[2048]{0:T(1024)S(1)} %bitcast.128), kind=kLoop, calls=%fused_computation.24 | loop fusion | flops 2097152 | bytes 4218880 | tf_op jit(solution)/shard_map/convert_element_type | solution.py:158
  28.8 4.7 %collective-permute-start.4 = (bf16[128,2048]{0,1:T(8,128)(2,1)S(1)}, bf16[128,2048]{0,1:T(8,128)(2,1)S(1)}, u32[]{:S(2)}, u32[]{:S(2)}) collective-permute-start(bf16[128,2048]{0,1:T(8,128)(2,1)S(1)} %fusion.10), channel_id=1, source_target_pairs={{0,24},{8,0},{16,8},{24,16},{1,25},{9,1},{17,9},{25,17},{2,26},{10... | collective-permute-start | bytes 1572872 | tf_op jit(solution)/shard_map/ppermute | solution.py:94
  33.5 7.4 %collective-permute-done.1 = bf16[16,136,128]{2,1,0:T(8,128)(2,1)S(1)} collective-permute-done((bf16[16,136,128]{2,1,0:T(8,128)(2,1)S(1)}, bf16[16,136,128]{2,1,0:T(8,128)(2,1)S(1)}, u32[]{:S(2)}, u32[]{:S(2)}) %collective-permute-start.1) | collective-permute-done | bytes 557088 | tf_op jit(solution)/shard_map/ppermute | solution.py:40
  40.8 3.4 %collective-permute-done.2 = bf16[16,136,128]{2,1,0:T(8,128)(2,1)S(1)} collective-permute-done((bf16[16,136,128]{2,1,0:T(8,128)(2,1)S(1)}, bf16[16,136,128]{2,1,0:T(8,128)(2,1)S(1)}, u32[]{:S(2)}, u32[]{:S(2)}) %collective-permute-start.2) | collective-permute-done | bytes 557088 | tf_op jit(solution)/shard_map/ppermute | solution.py:40
  44.5 1.4 %multiply_add_fusion.1 = f32[16,128,128]{2,1,0:T(8,128)} fusion(bf16[16,136,128]{2,1,0:T(8,128)(2,1)S(1)} %collective-permute-done.3, bf16[16,136,128]{2,1,0:T(8,128)(2,1)S(1)} %collective-permute-done.2, bf16[16,136,128]{2,1,0:T(8,128)(2,1)S(1)} %collective-permute-done.1, f32[16]{0:T(128)S(1)} %get-tuple-element.12, f32[16]{0:T(128)S(1)} %get-tuple-element.11), kind=kLoop, calls=%fused_computation.38 | loop fusion | flops 1835008 | bytes 2621568 | tf_op jit(solution)/shard_map/add | solution.py:71
  46.0 1.7 %multiply_add_fusion = f32[16,128,128]{2,1,0:T(8,128)S(1)} fusion(f32[16,128,128]{2,1,0:T(8,128)} %multiply_add_fusion.1, f32[16,136,128]{2,1,0:T(8,128)} %collective-permute-done, f32[16]{0:T(128)S(1)} %get-tuple-element.9), kind=kLoop, calls=%fused_computation.36 | loop fusion | flops 524288 | bytes 3145792 | tf_op jit(solution)/shard_map/add | solution.py:87
  47.7 1.1 %collective-permute-done.5 = f32[16,128,128]{2,1,0:T(8,128)S(1)} collective-permute-done((f32[16,128,128]{2,1,0:T(8,128)}, f32[16,128,128]{2,1,0:T(8,128)S(1)}, u32[]{:S(2)}, u32[]{:S(2)}) %collective-permute-start.5) | collective-permute-done | bytes 1048608 | tf_op jit(solution)/shard_map/ppermute | solution.py:86
  49.3 0.7 %fusion.2 = f32[128,16,128]{0,2,1:T(8,128)S(1)} fusion(bf16[128,16,128]{0,2,1:T(8,128)(2,1)S(1)} %bitcast.115, f32[128,16]{0,1:T(8,128)S(1)} %copy.38, f32[16,128,128]{2,1,0:T(8,128)S(1)} %collective-permute-done.5, f32[16,128,128]{2,1,0:T(8,128)S(1)} %multiply_add_fusion, pred[]{:T(512)S(6)} %eq.29), kind=kOutput, calls=%fused_computation.12 | convolution fusion | flops 201850880 | bytes 3678209 | tf_op jit(solution)/shard_map/shd,hde->she/dot_general | solution.py:167
  50.0 0.9 %fusion.4 = f32[128,16,128]{0,2,1:T(8,128)S(1)} fusion(f32[16,128,128]{2,1,0:T(8,128)S(1)} %multiply_add_fusion, f32[16,128,128]{2,1,0:T(8,128)S(1)} %collective-permute-done.5, f32[128,16]{0,1:T(8,128)S(1)} %copy.54, pred[]{:T(512)S(6)} %eq.29, bf16[128,16,128]{2,1,0:T(8,128)(2,1)S(1)} %bitcast.111), kind=kOutput, calls=%fused_computation.16 | convolution fusion | flops 201850880 | bytes 3678209 | tf_op jit(solution)/shard_map/the,hde->thd/dot_general | solution.py:164
  50.9 1.2 %fusion.13 = bf16[128,2048]{0,1:T(8,128)(2,1)S(1)} fusion(f32[128,16,128]{0,2,1:T(8,128)S(1)} %fusion.2, f32[128,16,128]{0,2,1:T(8,128)S(1)} %fusion.3, f32[128,16,128]{0,2,1:T(8,128)S(1)} %fusion.4, f32[2048]{0:T(1024)S(1)} %bitcast.126, f32[2048]{0:T(1024)S(1)} %bitcast.132, f32[2048]{0:T(1024)S(1)} %bitcast.129), kind=kLoop, calls=%fused_computation.29 | loop fusion | flops 1572864 | bytes 3694592 | tf_op jit(solution)/shard_map/convert_element_type | solution.py:171
  52.1 3.7 %collective-permute-start.6 = (bf16[128,2048]{0,1:T(8,128)(2,1)S(1)}, bf16[128,2048]{0,1:T(8,128)(2,1)S(1)}, u32[]{:S(2)}, u32[]{:S(2)}) collective-permute-start(bf16[128,2048]{0,1:T(8,128)(2,1)S(1)} %fusion.13), channel_id=1, source_target_pairs={{0,24},{8,0},{16,8},{24,16},{1,25},{9,1},{17,9},{25,17},{2,26},{10... | collective-permute-start | bytes 1572872 | tf_op jit(solution)/shard_map/ppermute | solution.py:94
  55.8 11.7 %collective-permute-done.6 = bf16[128,2048]{0,1:T(8,128)(2,1)S(1)} collective-permute-done((bf16[128,2048]{0,1:T(8,128)(2,1)S(1)}, bf16[128,2048]{0,1:T(8,128)(2,1)S(1)}, u32[]{:S(2)}, u32[]{:S(2)}) %collective-permute-start.6) | collective-permute-done | bytes 524320 | tf_op jit(solution)/shard_map/ppermute | solution.py:94
  67.6 1.0 %copy.59 = bf16[1,128,2048]{2,1,0:T(8,128)(2,1)} copy(bf16[1,128,2048]{1,2,0:T(8,128)(2,1)S(1)} %fusion.21) | data formatting | bytes 1048576 | tf_op jit(solution)/shard_map/broadcast_in_dim | solution.py:176
  (49 shorter events, 3.5 us)
Async XLA Ops:
  4.0 1.0 %copy-start.3 = (bf16[1,128,2048]{2,1,0:T(8,128)(2,1)S(1)}, bf16[1,128,2048]{2,1,0:T(8,128)(2,1)}, u32[]{:S(2)}) copy-start(bf16[1,128,2048]{2,1,0:T(8,128)(2,1)} %param.6) | copy-start | bytes 1572868
  8.9 11.2 %collective-permute-start = (f32[16,136,128]{2,1,0:T(8,128)}, f32[16,136,128]{2,1,0:T(8,128)}, u32[]{:S(2)}, u32[]{:S(2)}) collective-permute-start(f32[16,136,128]{2,1,0:T(8,128)} %pad_maximum_fusion), channel_id=1, source_target_pairs={{0,1},{2,3},{4,5},{6,7},{1,0},{3,2},{5,4},{7,6},{8,9},{10,11},{12,... | collective-permute-start | bytes 3342344 | tf_op jit(solution)/shard_map/ppermute | solution.py:63
  21.4 6.1 %copy-start.1 = (f32[16,128,128]{2,1,0:T(8,128)S(1)}, f32[16,128,128]{2,1,0:T(8,128)}, u32[]{:S(2)}) copy-start(f32[16,128,128]{2,1,0:T(8,128)} %convolution_multiply_fusion.3) | copy-start | bytes 3145732
  21.4 6.1 %copy-start.2 = (f32[16,128,128]{2,1,0:T(8,128)S(1)}, f32[16,128,128]{2,1,0:T(8,128)}, u32[]{:S(2)}) copy-start(f32[16,128,128]{2,1,0:T(8,128)} %convolution_multiply_fusion.2) | copy-start | bytes 3145732
  21.4 6.1 %copy-start.4 = (bf16[1,128,2048]{1,2,0:T(8,128)(2,1)S(1)}, bf16[1,128,2048]{1,2,0:T(8,128)(2,1)}, u32[]{:S(2)}) copy-start(bf16[1,128,2048]{1,2,0:T(8,128)(2,1)} %copy.43) | copy-start | bytes 1572868
  23.4 4.2 %copy-start = (f32[128,16,128]{0,2,1:T(8,128)S(1)}, f32[128,16,128]{0,2,1:T(8,128)}, u32[]{:S(2)}) copy-start(f32[128,16,128]{0,2,1:T(8,128)} %copy.53) | copy-start | bytes 3145732
  23.5 17.3 %collective-permute-start.1 = (bf16[16,136,128]{2,1,0:T(8,128)(2,1)S(1)}, bf16[16,136,128]{2,1,0:T(8,128)(2,1)S(1)}, u32[]{:S(2)}, u32[]{:S(2)}) collective-permute-start(bf16[16,136,128]{2,1,0:T(8,128)(2,1)S(1)} %pad_maximum_fusion.1), channel_id=1, source_target_pairs={{1,3},{3,5},{5,7},{6,4},{4,2},{2,0},{9,11},{11,13},{13,15},{14,12}... | collective-permute-start | bytes 1671176 | tf_op jit(solution)/shard_map/ppermute | solution.py:40
  24.9 19.3 %collective-permute-start.2 = (bf16[16,136,128]{2,1,0:T(8,128)(2,1)S(1)}, bf16[16,136,128]{2,1,0:T(8,128)(2,1)S(1)}, u32[]{:S(2)}, u32[]{:S(2)}) collective-permute-start(bf16[16,136,128]{2,1,0:T(8,128)(2,1)S(1)} %pad_maximum_fusion.1), channel_id=1, source_target_pairs={{1,5},{3,7},{6,2},{4,0},{9,13},{11,15},{14,10},{12,8},{17,21},{19,... | collective-permute-start | bytes 1671176 | tf_op jit(solution)/shard_map/ppermute | solution.py:40
  26.2 18.2 %collective-permute-start.3 = (bf16[16,136,128]{2,1,0:T(8,128)(2,1)S(1)}, bf16[16,136,128]{2,1,0:T(8,128)(2,1)S(1)}, u32[]{:S(2)}, u32[]{:S(2)}) collective-permute-start(bf16[16,136,128]{2,1,0:T(8,128)(2,1)S(1)} %pad_maximum_fusion.1), channel_id=1, source_target_pairs={{1,7},{6,0},{9,15},{14,8},{17,23},{22,16},{25,31},{30,24}} | collective-permute-start | bytes 1671176 | tf_op jit(solution)/shard_map/ppermute | solution.py:40
  28.8 17.1 %collective-permute-start.4 = (bf16[128,2048]{0,1:T(8,128)(2,1)S(1)}, bf16[128,2048]{0,1:T(8,128)(2,1)S(1)}, u32[]{:S(2)}, u32[]{:S(2)}) collective-permute-start(bf16[128,2048]{0,1:T(8,128)(2,1)S(1)} %fusion.10), channel_id=1, source_target_pairs={{0,24},{8,0},{16,8},{24,16},{1,25},{9,1},{17,9},{25,17},{2,26},{10... | collective-permute-start | bytes 1572872 | tf_op jit(solution)/shard_map/ppermute | solution.py:94
  45.9 2.9 %collective-permute-start.5 = (f32[16,128,128]{2,1,0:T(8,128)}, f32[16,128,128]{2,1,0:T(8,128)S(1)}, u32[]{:S(2)}, u32[]{:S(2)}) collective-permute-start(f32[16,128,128]{2,1,0:T(8,128)} %multiply_add_fusion.1), channel_id=1, source_target_pairs={{0,1},{2,3},{4,5},{6,7},{1,0},{3,2},{5,4},{7,6},{8,9},{10,11},{12,... | collective-permute-start | bytes 3145736 | tf_op jit(solution)/shard_map/ppermute | solution.py:86
  52.1 15.4 %collective-permute-start.6 = (bf16[128,2048]{0,1:T(8,128)(2,1)S(1)}, bf16[128,2048]{0,1:T(8,128)(2,1)S(1)}, u32[]{:S(2)}, u32[]{:S(2)}) collective-permute-start(bf16[128,2048]{0,1:T(8,128)(2,1)S(1)} %fusion.13), channel_id=1, source_target_pairs={{0,24},{8,0},{16,8},{24,16},{1,25},{9,1},{17,9},{25,17},{2,26},{10... | collective-permute-start | bytes 1572872 | tf_op jit(solution)/shard_map/ppermute | solution.py:94

commit v15 on v14

--- a/solution.py
+++ b/solution.py
@@ -60,8 +60,9 @@
     swap = [(2 * p, 2 * p + 1) for p in range(couples)] + [(2 * p + 1, 2 * p) for p in range(couples)]
     mine = jnp.where(odd, forward_part, backward_part)
     sent = packed(jnp.where(odd, backward_part, forward_part), rate)
-    lower, lower_rate = unpacked(lax.ppermute(sent, axis, swap))
-    window = packed(rate[:, None, None] * lower + mine, rate * lower_rate)
+    message = lax.ppermute(sent, axis, swap)
+    lower, lower_rate = unpacked(message)
+    window = rate[:, None, None] * message + packed(mine, jnp.zeros_like(rate))
     if couples <= 4:
         incoming = jnp.zeros_like(mine)
         weight = jnp.ones_like(rate)

time: 69.2 us -> 66.2 us (0.957)
  waiting for transfers between devices: 23.6 us -> 21.3 us
  starting transfers between devices: 12.8 us -> 14 us
  local copies, waits for them, and re-layouts: 8.91 us -> 7.92 us
  matrix products: 10.3 us -> 9.4 us
    convert_element_type x1 -> x0, other arithmetic: 1.91 us -> none  [narrow(): return jnp.concatenate([state.astype(jnp.bfloat16), tile], axis=1)]
    add x0 -> x1, other arithmetic: none -> 1.46 us  [scans_in(): window = rate[:, None, None] * message + packed(mine, jnp.zeros_like(rate))]
    slice x0 -> x3, local copies, waits for them, and re-layouts: none -> 1.36 us  [unpacked(): return (message[:, :width], message[:, width, 0])]
    mul x1, local copies, waits for them, and re-layouts: 2.56 us -> 1.34 us  [local(): scale * jnp.einsum('hts,the->she', attention, grad_rows, precision=HIGH)]
    ppermute x1, waiting for transfers between devices: 1.08 us -> 0.01 us  [scans_in(): other = lax.ppermute(incoming, axis, swap)]
    unnamed x13 -> x11, local copies, waits for them, and re-layouts: 3.52 us -> 2.48 us
    slice x1 -> x0, other arithmetic: 1.05 us -> none  [unpacked(): return (message[:, :width], message[:, width, 0])]
    dot_general x1, matrix products: 1.43 us -> 0.46 us  [local(): jnp.einsum('hts,the->she', attention, grad_rows, precision=HIGH)]
  transfers between devices with their start and end apart: 7 -> 7, of which waited for: 4 -> 3; matrix products, arithmetic and copies ran while one was open for 22% -> 21% of each run, Pallas kernels for 0% -> 0%
where the time goes in v15:
time: 66.2 us; the launch traced here: 65.1 us
  waiting for transfers between devices  21.3 us (32%)
  starting transfers between devices  14 us (21%)
  other arithmetic  12.2 us (18%)
  matrix products  9.4 us (14%)
  local copies, waits for them, and re-layouts  7.92 us (12%)
    ppermute x2, waiting for transfers between devices, passed_along(): return lax.ppermute(value, axis, pairs)  11.4 us
    ppermute x3, waiting for transfers between devices, sent_narrow(): return widen(lax.ppermute(narrow(message), axis, pairs))  9.91 us
    ppermute x2, starting transfers between devices, passed_along(): return lax.ppermute(value, axis, pairs)  8.7 us
    ppermute x3, starting transfers between devices, sent_narrow(): return widen(lax.ppermute(narrow(message), axis, pairs))  4.01 us
    unnamed x11, local copies, waits for them, and re-layouts  2.48 us
    convert_element_type x1, other arithmetic, local(): near_round = near_total.astype(jnp.bfloat16)  2.12 us
    dot_general x1, matrix products, local(): jnp.einsum('hts,thd->shd', mixing, queries, precision=HIGH)  1.85 us
    add x1, other arithmetic, scans_in(): own = lower_rate[:, None, None] * incoming + lower  1.7 us
  transfers between devices with their start and end apart: 7, of which 3 were waited for; matrix products, arithmetic and copies ran while one was open for 21% of the time, Pallas kernels for 0%

profile of v15, /device:TPU:0, one launch (start us, length us, event | category | flops | bytes accessed | tf_op | source)
XLA Modules:
  0.0 65.1 jit_solution(2674144146609193502)
XLA Ops:
  0.1 0.7 %compare_bitcast_fusion = pred[2]{0:T(512)(128)(4,1)S(1)} fusion(s32[1,2]{1,0:T(1,128)} %param.9), kind=kLoop, calls=%fused_computation.74 | loop fusion | flops 2 | bytes 10 | tf_op jit(solution)/shard_map/eq | solution.py:102
  0.9 0.7 %log_bitcast_fusion = f32[2,16]{1,0:T(2,128)S(1)} fusion(s32[1,2,16]{2,1,0:T(2,128)} %param.8), kind=kLoop, calls=%fused_computation.75 | loop fusion | flops 96 | bytes 256 | tf_op jit(solution)/shard_map/log | solution.py:100
  1.9 0.7 %fusion.36 = (f32[1,1,2048]{2,0,1:T(1,128)S(1)}, f32[1,1,2048]{2,0,1:T(1,128)S(1)}, f32[1,1,2048]{2,0,1:T(1,128)S(1)}) fusion(f32[1,3,2048]{2,0,1:T(1,128)} %param.7), kind=kLoop, calls=%fused_computation.83 | loop fusion | bytes 49152 | tf_op jit(solution)/shard_map/slice | solution.py:111
  2.6 1.3 %copy.34 = bf16[1,128,2048]{1,2,0:T(8,128)(2,1)S(1)} copy(bf16[1,128,2048]{2,1,0:T(8,128)(2,1)} %param.5) | data formatting | bytes 1048576 | tf_op args[0]
  4.0 1.0 %fusion.5 = (bf16[128,2048]{0,1:T(8,128)(2,1)S(1)}, bf16[128,2048]{0,1:T(8,128)(2,1)S(1)}, bf16[128,2048]{0,1:T(8,128)(2,1)S(1)}) fusion(bf16[1,128,2048]{1,2,0:T(8,128)(2,1)S(1)} %copy.34, f32[2048]{0:T(1024)S(1)} %bitcast.122, f32[2048]{0:T(1024)S(1)} %bitcast.125, f32[2048]{0:T(1024)S(1)} %bitcast.128), kind=kLoop, calls=%fused_computation.19 | loop fusion | flops 1835008 | bytes 2121728 | tf_op jit(solution)/shard_map/convert_element_type | solution.py:111
  5.3 0.9 %fusion.16 = f32[16,128,128]{2,1,0:T(8,128)S(1)} fusion(bf16[128,16,128]{0,2,1:T(8,128)(2,1)S(1)} %bitcast.117, bf16[128,16,128]{0,2,1:T(8,128)(2,1)S(1)} %bitcast.110, f32[128,16]{0,1:T(8,128)S(1)} %copy.37), kind=kOutput, calls=%fused_computation.41 | convolution fusion | flops 201850880 | bytes 2105344 | tf_op jit(solution)/shard_map/shd,she->hde/dot_general | solution.py:134
  6.2 1.6 %broadcast_select_fusion.2 = (f32[16,128,128]{2,1,0:T(8,128)S(1)}, f32[16,128,128]{2,1,0:T(8,128)}) fusion(f32[16,128,128]{2,1,0:T(8,128)S(1)} %fusion.16, pred[]{:T(512)S(6)} %eq.29, bf16[128,16,128]{2,1,0:T(8,128)(2,1)S(1)} %bitcast.106, bf16[128,16,128]{0,2,1:T(8,128)(2,1)S(1)} %bitcast.114, f32[128,16]{0,1:T(8,128)S(1)} %copy.35), kind=kOutput, calls=%fused_computation.53 | convolution fusion | flops 202637312 | bytes 4202497 | tf_op jit(solution)/shard_map/shd,she->hde/dot_general | solution.py:137
  7.8 1.1 %pad_maximum_fusion = f32[16,136,128]{2,1,0:T(8,128)} fusion(f32[16,8,128]{2,1,0:T(8,128)S(1)} %broadcast_in_dim.32, f32[16,128,128]{2,1,0:T(8,128)S(1)} %get-tuple-element.11), kind=kLoop, calls=%fused_computation.17 | loop fusion | flops 278528 | bytes 2228224 | tf_op jit(solution)/shard_map/concatenate | solution.py:16
  9.4 1.0 %copy.41 = bf16[1,128,2048]{1,2,0:T(8,128)(2,1)} copy(bf16[1,128,2048]{2,1,0:T(8,128)(2,1)S(1)} %copy-done.3) | data formatting | bytes 1048576 | tf_op args[1]
  10.5 0.6 convolution_multiply_fusion.1
  11.5 1.3 %copy.51 = f32[128,16,128]{0,2,1:T(8,128)} copy(f32[128,16,128]{2,0,1:T(8,128)S(1)} %fusion) | data formatting | bytes 2097152 | tf_op jit(solution)/shard_map/mul | solution.py:154
  13.0 0.6 fusion.1
  13.6 1.4 %convolution_multiply_fusion.3 = f32[16,128,128]{2,1,0:T(8,128)} fusion(bf16[128,16,128]{0,2,1:T(8,128)(2,1)S(1)} %bitcast.112, f32[16,128,128]{1,2,0:T(8,128)S(1)} %fusion.1), kind=kOutput, calls=%fused_computation.7 | convolution fusion | flops 201588736 | bytes 2621440 | tf_op jit(solution)/shard_map/hts,shd->thd/dot_general | solution.py:149
  15.0 1.8 %convolution_multiply_fusion.2 = f32[16,128,128]{2,1,0:T(8,128)} fusion(bf16[128,16,128]{0,2,1:T(8,128)(2,1)S(1)} %bitcast.116, f32[16,128,128]{1,2,0:T(8,128)S(1)} %fusion.1), kind=kOutput, calls=%fused_computation.6 | convolution fusion | flops 201588736 | bytes 2621440 | tf_op jit(solution)/shard_map/hts,thd->shd/dot_general | solution.py:150
  16.8 1.5 %pad_add_fusion = f32[16,136,128]{2,1,0:T(8,128)S(1)} fusion(f32[16,128,128]{2,1,0:T(8,128)S(1)} %copy-done, f32[16,136,128]{2,1,0:T(8,128)} %collective-permute-done, f32[16]{0:T(128)S(1)} %fusion.34), kind=kLoop, calls=%fused_computation.18 | loop fusion | flops 557056 | bytes 3276864 | tf_op jit(solution)/shard_map/add | solution.py:65
  19.1 1.4 %collective-permute-start.1 = (bf16[16,136,128]{2,1,0:T(8,128)(2,1)S(1)}, bf16[16,136,128]{2,1,0:T(8,128)(2,1)S(1)}, u32[]{:S(2)}, u32[]{:S(2)}) collective-permute-start(bf16[16,136,128]{2,1,0:T(8,128)(2,1)S(1)} %pad_maximum_fusion.1), channel_id=1, source_target_pairs={{1,3},{3,5},{5,7},{6,4},{4,2},{2,0},{9,11},{11,13},{13,15},{14,12}... | collective-permute-start | bytes 1671176 | tf_op jit(solution)/shard_map/ppermute | solution.py:40
  20.5 1.3 %collective-permute-start.2 = (bf16[16,136,128]{2,1,0:T(8,128)(2,1)S(1)}, bf16[16,136,128]{2,1,0:T(8,128)(2,1)S(1)}, u32[]{:S(2)}, u32[]{:S(2)}) collective-permute-start(bf16[16,136,128]{2,1,0:T(8,128)(2,1)S(1)} %pad_maximum_fusion.1), channel_id=1, source_target_pairs={{1,5},{3,7},{6,2},{4,0},{9,13},{11,15},{14,10},{12,8},{17,21},{19,... | collective-permute-start | bytes 1671176 | tf_op jit(solution)/shard_map/ppermute | solution.py:40
  21.8 1.3 %collective-permute-start.3 = (bf16[16,136,128]{2,1,0:T(8,128)(2,1)S(1)}, bf16[16,136,128]{2,1,0:T(8,128)(2,1)S(1)}, u32[]{:S(2)}, u32[]{:S(2)}) collective-permute-start(bf16[16,136,128]{2,1,0:T(8,128)(2,1)S(1)} %pad_maximum_fusion.1), channel_id=1, source_target_pairs={{1,7},{6,0},{9,15},{14,8},{17,23},{22,16},{25,31},{30,24}} | collective-permute-start | bytes 1671176 | tf_op jit(solution)/shard_map/ppermute | solution.py:40
  23.1 2.1 %fusion.10 = bf16[128,2048]{0,1:T(8,128)(2,1)S(1)} fusion(f32[16,128,128]{2,1,0:T(8,128)} %convolution_multiply_fusion.2, f32[16,128,128]{2,1,0:T(8,128)S(1)} %copy-done.2, f32[128,16,128]{0,2,1:T(8,128)S(1)} %copy-done.1, bf16[1,128,2048]{1,2,0:T(8,128)(2,1)} %copy.41, f32[2048]{0:T(1024)S(1)} %bitcast.126, f32[2048]{0:T(1024)S(1)} %bitcast.129, ...), kind=kLoop, calls=%fused_computation.27 | loop fusion | flops 2097152 | bytes 4218880 | tf_op jit(solution)/shard_map/convert_element_type | solution.py:159
  25.2 4.7 %collective-permute-start.4 = (bf16[128,2048]{0,1:T(8,128)(2,1)S(1)}, bf16[128,2048]{0,1:T(8,128)(2,1)S(1)}, u32[]{:S(2)}, u32[]{:S(2)}) collective-permute-start(bf16[128,2048]{0,1:T(8,128)(2,1)S(1)} %fusion.10), channel_id=1, source_target_pairs={{0,24},{8,0},{16,8},{24,16},{1,25},{9,1},{17,9},{25,17},{2,26},{10... | collective-permute-start | bytes 1572872 | tf_op jit(solution)/shard_map/ppermute | solution.py:95
  29.9 6.1 %collective-permute-done.1 = bf16[16,136,128]{2,1,0:T(8,128)(2,1)S(1)} collective-permute-done((bf16[16,136,128]{2,1,0:T(8,128)(2,1)S(1)}, bf16[16,136,128]{2,1,0:T(8,128)(2,1)S(1)}, u32[]{:S(2)}, u32[]{:S(2)}) %collective-permute-start.1) | collective-permute-done | bytes 557088 | tf_op jit(solution)/shard_map/ppermute | solution.py:40
  36.0 3.8 %collective-permute-done.2 = bf16[16,136,128]{2,1,0:T(8,128)(2,1)S(1)} collective-permute-done((bf16[16,136,128]{2,1,0:T(8,128)(2,1)S(1)}, bf16[16,136,128]{2,1,0:T(8,128)(2,1)S(1)}, u32[]{:S(2)}, u32[]{:S(2)}) %collective-permute-start.2) | collective-permute-done | bytes 557088 | tf_op jit(solution)/shard_map/ppermute | solution.py:40
  40.0 1.4 %multiply_add_fusion = f32[16,128,128]{2,1,0:T(8,128)} fusion(bf16[16,136,128]{2,1,0:T(8,128)(2,1)S(1)} %collective-permute-done.3, bf16[16,136,128]{2,1,0:T(8,128)(2,1)S(1)} %collective-permute-done.2, bf16[16,136,128]{2,1,0:T(8,128)(2,1)S(1)} %collective-permute-done.1, f32[16]{0:T(128)S(1)} %get-tuple-element.10, f32[16]{0:T(128)S(1)} %get-tuple-element.9), kind=kLoop, calls=%fused_computation.40 | loop fusion | flops 1835008 | bytes 2621568 | tf_op jit(solution)/shard_map/add | solution.py:72
  41.4 0.9 %collective-permute-start.5 = (f32[16,128,128]{2,1,0:T(8,128)}, f32[16,128,128]{2,1,0:T(8,128)S(1)}, u32[]{:S(2)}, u32[]{:S(2)}) collective-permute-start(f32[16,128,128]{2,1,0:T(8,128)} %multiply_add_fusion), channel_id=1, source_target_pairs={{0,1},{2,3},{4,5},{6,7},{1,0},{3,2},{5,4},{7,6},{8,9},{10,11},{12,... | collective-permute-start | bytes 3145736 | tf_op jit(solution)/shard_map/ppermute | solution.py:87
  42.4 1.1 %slice_reduce_fusion = f32[16]{0:T(128)S(1)} fusion(f32[16,136,128]{2,1,0:T(8,128)} %collective-permute-done), kind=kLoop, calls=%fused_computation.62 | loop fusion | bytes 128 | tf_op jit(solution)/shard_map/slice | solution.py:21
  43.4 1.7 %slice_add_fusion = f32[16,128,128]{2,1,0:T(8,128)S(1)} fusion(f32[16,136,128]{2,1,0:T(8,128)} %collective-permute-done, f32[16,128,128]{2,1,0:T(8,128)} %multiply_add_fusion, f32[16]{0:T(128)S(1)} %slice_reduce_fusion), kind=kLoop, calls=%fused_computation.22 | loop fusion | flops 524288 | bytes 3145792 | tf_op jit(solution)/shard_map/add | solution.py:88
  45.7 0.7 %fusion.2 = f32[128,16,128]{0,2,1:T(8,128)S(1)} fusion(bf16[128,16,128]{0,2,1:T(8,128)(2,1)S(1)} %bitcast.113, f32[128,16]{0,1:T(8,128)S(1)} %copy.37, f32[16,128,128]{2,1,0:T(8,128)S(1)} %collective-permute-done.5, f32[16,128,128]{2,1,0:T(8,128)S(1)} %slice_add_fusion, pred[]{:T(512)S(6)} %eq.29), kind=kOutput, calls=%fused_computation.12 | convolution fusion | flops 201850880 | bytes 3678209 | tf_op jit(solution)/shard_map/shd,hde->she/dot_general | solution.py:168
  46.4 0.9 %fusion.4 = f32[128,16,128]{0,2,1:T(8,128)S(1)} fusion(f32[16,128,128]{2,1,0:T(8,128)S(1)} %slice_add_fusion, f32[16,128,128]{2,1,0:T(8,128)S(1)} %collective-permute-done.5, f32[128,16]{0,1:T(8,128)S(1)} %copy.52, pred[]{:T(512)S(6)} %eq.29, bf16[128,16,128]{2,1,0:T(8,128)(2,1)S(1)} %bitcast.109), kind=kOutput, calls=%fused_computation.16 | convolution fusion | flops 201850880 | bytes 3678209 | tf_op jit(solution)/shard_map/the,hde->thd/dot_general | solution.py:165
  47.3 1.2 %fusion.13 = bf16[128,2048]{0,1:T(8,128)(2,1)S(1)} fusion(f32[128,16,128]{0,2,1:T(8,128)S(1)} %fusion.2, f32[128,16,128]{0,2,1:T(8,128)S(1)} %fusion.3, f32[128,16,128]{0,2,1:T(8,128)S(1)} %fusion.4, f32[2048]{0:T(1024)S(1)} %bitcast.127, f32[2048]{0:T(1024)S(1)} %bitcast.130, f32[2048]{0:T(1024)S(1)} %bitcast.124), kind=kLoop, calls=%fused_computation.32 | loop fusion | flops 1572864 | bytes 3694592 | tf_op jit(solution)/shard_map/convert_element_type | solution.py:172
  48.5 4.0 %collective-permute-start.6 = (bf16[128,2048]{0,1:T(8,128)(2,1)S(1)}, bf16[128,2048]{0,1:T(8,128)(2,1)S(1)}, u32[]{:S(2)}, u32[]{:S(2)}) collective-permute-start(bf16[128,2048]{0,1:T(8,128)(2,1)S(1)} %fusion.13), channel_id=1, source_target_pairs={{0,24},{8,0},{16,8},{24,16},{1,25},{9,1},{17,9},{25,17},{2,26},{10... | collective-permute-start | bytes 1572872 | tf_op jit(solution)/shard_map/ppermute | solution.py:95
  52.5 11.4 %collective-permute-done.6 = bf16[128,2048]{0,1:T(8,128)(2,1)S(1)} collective-permute-done((bf16[128,2048]{0,1:T(8,128)(2,1)S(1)}, bf16[128,2048]{0,1:T(8,128)(2,1)S(1)}, u32[]{:S(2)}, u32[]{:S(2)}) %collective-permute-start.6) | collective-permute-done | bytes 524320 | tf_op jit(solution)/shard_map/ppermute | solution.py:95
  64.1 1.0 %copy.57 = bf16[1,128,2048]{2,1,0:T(8,128)(2,1)} copy(bf16[1,128,2048]{1,2,0:T(8,128)(2,1)S(1)} %fusion.21) | data formatting | bytes 1048576 | tf_op jit(solution)/shard_map/broadcast_in_dim | solution.py:177
  (48 shorter events, 3.7 us)
Async XLA Ops:
  4.0 1.0 %copy-start.3 = (bf16[1,128,2048]{2,1,0:T(8,128)(2,1)S(1)}, bf16[1,128,2048]{2,1,0:T(8,128)(2,1)}, u32[]{:S(2)}) copy-start(bf16[1,128,2048]{2,1,0:T(8,128)(2,1)} %param.6) | copy-start | bytes 1572868
  8.9 7.9 %collective-permute-start = (f32[16,136,128]{2,1,0:T(8,128)}, f32[16,136,128]{2,1,0:T(8,128)}, u32[]{:S(2)}, u32[]{:S(2)}) collective-permute-start(f32[16,136,128]{2,1,0:T(8,128)} %pad_maximum_fusion), channel_id=1, source_target_pairs={{0,1},{2,3},{4,5},{6,7},{1,0},{3,2},{5,4},{7,6},{8,9},{10,11},{12,... | collective-permute-start | bytes 3342344 | tf_op jit(solution)/shard_map/ppermute | solution.py:63
  15.0 1.9 %copy-start = (f32[16,128,128]{2,1,0:T(8,128)S(1)}, f32[16,128,128]{2,1,0:T(8,128)}, u32[]{:S(2)}) copy-start(f32[16,128,128]{2,1,0:T(8,128)} %get-tuple-element.12) | copy-start | bytes 3145732
  18.3 4.8 %copy-start.1 = (f32[128,16,128]{0,2,1:T(8,128)S(1)}, f32[128,16,128]{0,2,1:T(8,128)}, u32[]{:S(2)}) copy-start(f32[128,16,128]{0,2,1:T(8,128)} %copy.51) | copy-start | bytes 3145732
  18.8 4.3 %copy-start.2 = (f32[16,128,128]{2,1,0:T(8,128)S(1)}, f32[16,128,128]{2,1,0:T(8,128)}, u32[]{:S(2)}) copy-start(f32[16,128,128]{2,1,0:T(8,128)} %convolution_multiply_fusion.3) | copy-start | bytes 3145732
  19.1 17.0 %collective-permute-start.1 = (bf16[16,136,128]{2,1,0:T(8,128)(2,1)S(1)}, bf16[16,136,128]{2,1,0:T(8,128)(2,1)S(1)}, u32[]{:S(2)}, u32[]{:S(2)}) collective-permute-start(bf16[16,136,128]{2,1,0:T(8,128)(2,1)S(1)} %pad_maximum_fusion.1), channel_id=1, source_target_pairs={{1,3},{3,5},{5,7},{6,4},{4,2},{2,0},{9,11},{11,13},{13,15},{14,12}... | collective-permute-start | bytes 1671176 | tf_op jit(solution)/shard_map/ppermute | solution.py:40
  20.5 19.3 %collective-permute-start.2 = (bf16[16,136,128]{2,1,0:T(8,128)(2,1)S(1)}, bf16[16,136,128]{2,1,0:T(8,128)(2,1)S(1)}, u32[]{:S(2)}, u32[]{:S(2)}) collective-permute-start(bf16[16,136,128]{2,1,0:T(8,128)(2,1)S(1)} %pad_maximum_fusion.1), channel_id=1, source_target_pairs={{1,5},{3,7},{6,2},{4,0},{9,13},{11,15},{14,10},{12,8},{17,21},{19,... | collective-permute-start | bytes 1671176 | tf_op jit(solution)/shard_map/ppermute | solution.py:40
  21.8 18.2 %collective-permute-start.3 = (bf16[16,136,128]{2,1,0:T(8,128)(2,1)S(1)}, bf16[16,136,128]{2,1,0:T(8,128)(2,1)S(1)}, u32[]{:S(2)}, u32[]{:S(2)}) collective-permute-start(bf16[16,136,128]{2,1,0:T(8,128)(2,1)S(1)} %pad_maximum_fusion.1), channel_id=1, source_target_pairs={{1,7},{6,0},{9,15},{14,8},{17,23},{22,16},{25,31},{30,24}} | collective-permute-start | bytes 1671176 | tf_op jit(solution)/shard_map/ppermute | solution.py:40
  25.2 16.2 %collective-permute-start.4 = (bf16[128,2048]{0,1:T(8,128)(2,1)S(1)}, bf16[128,2048]{0,1:T(8,128)(2,1)S(1)}, u32[]{:S(2)}, u32[]{:S(2)}) collective-permute-start(bf16[128,2048]{0,1:T(8,128)(2,1)S(1)} %fusion.10), channel_id=1, source_target_pairs={{0,24},{8,0},{16,8},{24,16},{1,25},{9,1},{17,9},{25,17},{2,26},{10... | collective-permute-start | bytes 1572872 | tf_op jit(solution)/shard_map/ppermute | solution.py:95
  41.4 3.7 %collective-permute-start.5 = (f32[16,128,128]{2,1,0:T(8,128)}, f32[16,128,128]{2,1,0:T(8,128)S(1)}, u32[]{:S(2)}, u32[]{:S(2)}) collective-permute-start(f32[16,128,128]{2,1,0:T(8,128)} %multiply_add_fusion), channel_id=1, source_target_pairs={{0,1},{2,3},{4,5},{6,7},{1,0},{3,2},{5,4},{7,6},{8,9},{10,11},{12,... | collective-permute-start | bytes 3145736 | tf_op jit(solution)/shard_map/ppermute | solution.py:87
  48.5 15.4 %collective-permute-start.6 = (bf16[128,2048]{0,1:T(8,128)(2,1)S(1)}, bf16[128,2048]{0,1:T(8,128)(2,1)S(1)}, u32[]{:S(2)}, u32[]{:S(2)}) collective-permute-start(bf16[128,2048]{0,1:T(8,128)(2,1)S(1)} %fusion.13), channel_id=1, source_target_pairs={{0,24},{8,0},{16,8},{24,16},{1,25},{9,1},{17,9},{25,17},{2,26},{10... | collective-permute-start | bytes 1572872 | tf_op jit(solution)/shard_map/ppermute | solution.py:95

commit v16 on v15

--- a/solution.py
+++ b/solution.py
@@ -61,16 +61,16 @@
     mine = jnp.where(odd, forward_part, backward_part)
     sent = packed(jnp.where(odd, backward_part, forward_part), rate)
     message = lax.ppermute(sent, axis, swap)
-    lower, lower_rate = unpacked(message)
+    lower_rate = unpacked(message)[1]
     window = rate[:, None, None] * message + packed(mine, jnp.zeros_like(rate))
     if couples <= 4:
-        incoming = jnp.zeros_like(mine)
+        incoming = jnp.zeros_like(window)
         weight = jnp.ones_like(rate)
         for step in range(1, couples):
             moves = [(2 * p + 1, 2 * (p + step) + 1) for p in range(couples - step)]
-            got, got_rate = unpacked(sent_narrow(window, axis, both_ways(count, moves)))
+            got = sent_narrow(window, axis, both_ways(count, moves))
             incoming = incoming + weight[:, None, None] * got
-            weight = weight * got_rate
+            weight = weight * unpacked(got)[1]
     else:
         covered = 1
         while 2 * covered < couples:
@@ -82,11 +82,14 @@
         if 1 + covered < couples:
             moves = [(2 * p + 1, 2 * (p + 1 + covered) + 1) for p in range(couples - 1 - covered)]
             nearer = merged(sent_narrow(window, axis, both_ways(count, moves)), nearer)
-        incoming = unpacked(nearer)[0]
+        incoming = nearer
     incoming, held = lax.optimization_barrier((incoming, held))
     other = lax.ppermute(incoming, axis, swap)
-    own = lower_rate[:, None, None] * incoming + lower
-    return jnp.where(odd, own, other), jnp.where(odd, other, own), held
+    own = lower_rate[:, None, None] * incoming + message
+    width = message.shape[1] - 8
+    forward_in = jnp.where(odd, own, other)[:, :width]
+    backward_in = jnp.where(odd, other, own)[:, :width]
+    return forward_in, backward_in, held
 
 
 def passed_along(value, axis, steps):

time: 66.2 us -> 68.8 us (1.039)
  the two profiles are of different devices: /device:TPU:0 before, /device:TPU:28 now
where the time goes in v16:
time: 68.8 us; the launch traced here: 68.3 us
  waiting for transfers between devices  27.2 us (40%)
  other arithmetic  15.6 us (23%)
  matrix products  10.4 us (15%)
  local copies, waits for them, and re-layouts  8.12 us (12%)
  starting transfers between devices  6.67 us (10%)
    ppermute x2, waiting for transfers between devices, passed_along(): return lax.ppermute(value, axis, pairs)  18.5 us
    ppermute x3, waiting for transfers between devices, sent_narrow(): return widen(lax.ppermute(narrow(message), axis, pairs))  8.6 us
    ppermute x3, starting transfers between devices, sent_narrow(): return widen(lax.ppermute(narrow(message), axis, pairs))  6.11 us
    unnamed x11, local copies, waits for them, and re-layouts  2.46 us
    convert_element_type x1, other arithmetic, local(): near_round = near_total.astype(jnp.bfloat16)  2.35 us
    dot_general x1, matrix products, local(): jnp.einsum('hts,thd->shd', mixing, queries, precision=HIGH)  1.86 us
    add x1, other arithmetic, scans_in(): own = lower_rate[:, None, None] * incoming + message  1.75 us
    dot_general x1, matrix products, local(): jnp.einsum('shd,she->hde', queries * growth[:, :, None], grad_rows, preci...  1.57 us
  transfers between devices with their start and end apart: 7, of which 5 were waited for; matrix products, arithmetic and copies ran while one was open for 26% of the time, Pallas kernels for 0%

profile of v16, /device:TPU:28, one launch (start us, length us, event | category | flops | bytes accessed | tf_op | source)
XLA Modules:
  0.0 68.3 jit_solution(12417009604186921166)
XLA Ops:
  0.0 0.7 %compare_bitcast_fusion = pred[2]{0:T(512)(128)(4,1)S(1)} fusion(s32[1,2]{1,0:T(1,128)} %param.9), kind=kLoop, calls=%fused_computation.85 | loop fusion | flops 2 | bytes 10 | tf_op jit(solution)/shard_map/eq | solution.py:105
  1.0 0.7 %log_bitcast_fusion = f32[2,16]{1,0:T(2,128)S(1)} fusion(s32[1,2,16]{2,1,0:T(2,128)} %param.8), kind=kLoop, calls=%fused_computation.86 | loop fusion | flops 96 | bytes 256 | tf_op jit(solution)/shard_map/log | solution.py:103
  2.0 0.7 %fusion.38 = (f32[1,1,2048]{2,0,1:T(1,128)S(1)}, f32[1,1,2048]{2,0,1:T(1,128)S(1)}, f32[1,1,2048]{2,0,1:T(1,128)S(1)}) fusion(f32[1,3,2048]{2,0,1:T(1,128)} %param.7), kind=kLoop, calls=%fused_computation.93 | loop fusion | bytes 49152 | tf_op jit(solution)/shard_map/slice | solution.py:114
  2.9 1.3 %copy.34 = bf16[1,128,2048]{1,2,0:T(8,128)(2,1)S(1)} copy(bf16[1,128,2048]{2,1,0:T(8,128)(2,1)} %param.5) | data formatting | bytes 1048576 | tf_op args[0]
  4.3 1.0 %fusion.6 = (bf16[128,2048]{0,1:T(8,128)(2,1)S(1)}, bf16[128,2048]{0,1:T(8,128)(2,1)S(1)}, bf16[128,2048]{0,1:T(8,128)(2,1)S(1)}) fusion(bf16[1,128,2048]{1,2,0:T(8,128)(2,1)S(1)} %copy.34, f32[2048]{0:T(1024)S(1)} %bitcast.122, f32[2048]{0:T(1024)S(1)} %bitcast.125, f32[2048]{0:T(1024)S(1)} %bitcast.128), kind=kLoop, calls=%fused_computation.24 | loop fusion | flops 1835008 | bytes 2121728 | tf_op jit(solution)/shard_map/convert_element_type | solution.py:114
  5.3 0.8 %fusion.17 = f32[16,128,128]{2,1,0:T(8,128)S(1)} fusion(bf16[128,16,128]{0,2,1:T(8,128)(2,1)S(1)} %bitcast.117, bf16[128,16,128]{0,2,1:T(8,128)(2,1)S(1)} %bitcast.110, f32[128,16]{0,1:T(8,128)S(1)} %copy.37), kind=kOutput, calls=%fused_computation.44 | convolution fusion | flops 201850880 | bytes 2105344 | tf_op jit(solution)/shard_map/shd,she->hde/dot_general | solution.py:137
  6.2 1.6 %broadcast_select_fusion.1 = (f32[16,128,128]{2,1,0:T(8,128)S(1)}, f32[16,128,128]{2,1,0:T(8,128)}) fusion(f32[16,128,128]{2,1,0:T(8,128)S(1)} %fusion.17, pred[]{:T(512)S(6)} %eq.29, bf16[128,16,128]{2,1,0:T(8,128)(2,1)S(1)} %bitcast.106, bf16[128,16,128]{0,2,1:T(8,128)(2,1)S(1)} %bitcast.114, f32[128,16]{0,1:T(8,128)S(1)} %copy.35), kind=kOutput, calls=%fused_computation.61 | convolution fusion | flops 202637312 | bytes 4202497 | tf_op jit(solution)/shard_map/shd,she->hde/dot_general | solution.py:140
  7.8 1.1 %pad_maximum_fusion = f32[16,136,128]{2,1,0:T(8,128)} fusion(f32[16,8,128]{2,1,0:T(8,128)S(1)} %broadcast_in_dim.44, f32[16,128,128]{2,1,0:T(8,128)S(1)} %get-tuple-element.12), kind=kLoop, calls=%fused_computation.17 | loop fusion | flops 278528 | bytes 2228224 | tf_op jit(solution)/shard_map/concatenate | solution.py:16
  9.8 1.5 %convolution_multiply_fusion.1 = f32[16,128,128]{1,2,0:T(8,128)} fusion(bf16[128,16,128]{0,2,1:T(8,128)(2,1)S(1)} %bitcast.115, bf16[128,16,128]{0,2,1:T(8,128)(2,1)S(1)} %bitcast.111, f32[16,128]{1,0:T(8,128)S(1)} %copy.44, pred[128,128]{0,1:T(8,128)(4,1)S(1)} %iota_compare_fusion), kind=kOutput, calls=%fused_computation.5 | convolution fusion | flops 68157440 | bytes 2121728 | tf_op jit(solution)/shard_map/thd,shd->hts/dot_general | solution.py:155
  11.3 1.9 %convolution_multiply_fusion.2 = f32[16,128,128]{2,1,0:T(8,128)} fusion(bf16[128,16,128]{0,2,1:T(8,128)(2,1)S(1)} %bitcast.116, f32[16,128,128]{1,2,0:T(8,128)S(1)} %fusion.1), kind=kOutput, calls=%fused_computation.6 | convolution fusion | flops 201588736 | bytes 2621440 | tf_op jit(solution)/shard_map/hts,thd->shd/dot_general | solution.py:153
  13.2 1.4 %convolution_multiply_fusion.3 = f32[16,128,128]{2,1,0:T(8,128)} fusion(bf16[128,16,128]{0,2,1:T(8,128)(2,1)S(1)} %bitcast.112, f32[16,128,128]{1,2,0:T(8,128)S(1)} %fusion.1), kind=kOutput, calls=%fused_computation.7 | convolution fusion | flops 201588736 | bytes 2621440 | tf_op jit(solution)/shard_map/hts,shd->thd/dot_general | solution.py:152
  14.6 1.5 %pad_add_fusion = f32[16,136,128]{2,1,0:T(8,128)S(1)} fusion(f32[16,128,128]{2,1,0:T(8,128)S(1)} %copy-done, f32[16,136,128]{2,1,0:T(8,128)} %collective-permute-done, f32[16]{0:T(128)S(1)} %fusion.37), kind=kLoop, calls=%fused_computation.23 | loop fusion | flops 557056 | bytes 3276864 | tf_op jit(solution)/shard_map/add | solution.py:65
  16.8 0.8 %pad_maximum_fusion.1 = bf16[16,136,128]{2,1,0:T(8,128)(2,1)} fusion(bf16[16,8,128]{2,1,0:T(8,128)(2,1)S(1)} %broadcast_in_dim.45, bf16[16,128,128]{2,1,0:T(8,128)(2,1)S(1)} %slice.151), kind=kLoop, calls=%fused_computation.52 | loop fusion | flops 1114112 | bytes 1114112 | tf_op jit(solution)/shard_map/concatenate | solution.py:30
  17.6 1.5 %collective-permute-start.3 = (bf16[16,136,128]{2,1,0:T(8,128)(2,1)}, bf16[16,136,128]{2,1,0:T(8,128)(2,1)}, u32[]{:S(2)}, u32[]{:S(2)}) collective-permute-start(bf16[16,136,128]{2,1,0:T(8,128)(2,1)} %pad_maximum_fusion.1), channel_id=1, source_target_pairs={{1,7},{6,0},{9,15},{14,8},{17,23},{22,16},{25,31},{30,24}} | collective-permute-start | bytes 1671176 | tf_op jit(solution)/shard_map/ppermute | solution.py:40
  19.6 1.0 %copy.41 = bf16[1,128,2048]{1,2,0:T(8,128)(2,1)} copy(bf16[1,128,2048]{2,1,0:T(8,128)(2,1)S(1)} %copy-done.1) | data formatting | bytes 1048576 | tf_op args[1]
  20.6 1.3 %copy.51 = f32[128,16,128]{0,2,1:T(8,128)} copy(f32[128,16,128]{2,0,1:T(8,128)S(1)} %fusion) | data formatting | bytes 2097152 | tf_op jit(solution)/shard_map/mul | solution.py:157
  21.9 2.3 %collective-permute-start.2 = (bf16[16,136,128]{2,1,0:T(8,128)(2,1)}, bf16[16,136,128]{2,1,0:T(8,128)(2,1)S(1)}, u32[]{:S(2)}, u32[]{:S(2)}) collective-permute-start(bf16[16,136,128]{2,1,0:T(8,128)(2,1)} %pad_maximum_fusion.1), channel_id=1, source_target_pairs={{1,5},{3,7},{6,2},{4,0},{9,13},{11,15},{14,10},{12,8},{17,21},{19,... | collective-permute-start | bytes 1671176 | tf_op jit(solution)/shard_map/ppermute | solution.py:40
  24.2 2.4 %collective-permute-start.1 = (bf16[16,136,128]{2,1,0:T(8,128)(2,1)}, bf16[16,136,128]{2,1,0:T(8,128)(2,1)S(1)}, u32[]{:S(2)}, u32[]{:S(2)}) collective-permute-start(bf16[16,136,128]{2,1,0:T(8,128)(2,1)} %pad_maximum_fusion.1), channel_id=1, source_target_pairs={{1,3},{3,5},{5,7},{6,4},{4,2},{2,0},{9,11},{11,13},{13,15},{14,12}... | collective-permute-start | bytes 1671176 | tf_op jit(solution)/shard_map/ppermute | solution.py:40
  26.6 2.4 %fusion.11 = bf16[128,2048]{0,1:T(8,128)(2,1)S(1)} fusion(f32[16,128,128]{2,1,0:T(8,128)} %convolution_multiply_fusion.2, f32[16,128,128]{2,1,0:T(8,128)} %convolution_multiply_fusion.3, f32[128,16,128]{0,2,1:T(8,128)} %copy.51, bf16[1,128,2048]{1,2,0:T(8,128)(2,1)S(1)} %copy-done.2, f32[2048]{0:T(1024)S(1)} %bitcast.126, f32[2048]{0:T(1024)S(1)} %bitcast.129, ...), kind=kLoop, calls=%fused_computation.31 | loop fusion | flops 2097152 | bytes 4218880 | tf_op jit(solution)/shard_map/convert_element_type | solution.py:162
  29.4 1.1 %slice_convert_fusion.1 = f32[16,128,128]{2,1,0:T(8,128)S(1)} fusion(bf16[16,136,128]{2,1,0:T(8,128)(2,1)} %collective-permute-done.3), kind=kLoop, calls=%fused_computation.54 | loop fusion | flops 262144 | bytes 1572864 | tf_op jit(solution)/shard_map/convert_element_type | solution.py:36
  30.6 3.7 %collective-permute-done.2 = bf16[16,136,128]{2,1,0:T(8,128)(2,1)S(1)} collective-permute-done((bf16[16,136,128]{2,1,0:T(8,128)(2,1)}, bf16[16,136,128]{2,1,0:T(8,128)(2,1)S(1)}, u32[]{:S(2)}, u32[]{:S(2)}) %collective-permute-start.2) | collective-permute-done | bytes 557088 | tf_op jit(solution)/shard_map/ppermute | solution.py:40
  34.4 4.9 %collective-permute-done.1 = bf16[16,136,128]{2,1,0:T(8,128)(2,1)S(1)} collective-permute-done((bf16[16,136,128]{2,1,0:T(8,128)(2,1)}, bf16[16,136,128]{2,1,0:T(8,128)(2,1)S(1)}, u32[]{:S(2)}, u32[]{:S(2)}) %collective-permute-start.1) | collective-permute-done | bytes 557088 | tf_op jit(solution)/shard_map/ppermute | solution.py:40
  39.5 1.0 %fusion.35 = f32[16]{0:T(128)S(1)} fusion(bf16[16,136,128]{2,1,0:T(8,128)(2,1)} %collective-permute-done.3), kind=kLoop, calls=%fused_computation.82 | loop fusion | flops 48 | bytes 128 | tf_op jit(solution)/shard_map/add | solution.py:35
  40.9 1.4 %fusion.5 = f32[16,136,128]{2,1,0:T(8,128)} fusion(f32[16,8,128]{2,1,0:T(8,128)S(1)} %broadcast_in_dim.47, f32[16,128,128]{2,1,0:T(8,128)S(1)} %slice_convert_fusion.3, f32[16,8,128]{2,1,0:T(8,128)S(1)} %broadcast_in_dim.49, f32[16,128,128]{2,1,0:T(8,128)S(1)} %slice_convert_fusion.2, f32[16,8,128]{2,1,0:T(8,128)S(1)} %broadcast_in_dim.51, ...), kind=kLoop, calls=%fused_computation.19 | loop fusion | flops 1949696 | bytes 4456576 | tf_op jit(solution)/shard_map/add | solution.py:72
  42.2 2.5 %collective-permute-done.4 = bf16[128,2048]{0,1:T(8,128)(2,1)S(1)} collective-permute-done((bf16[128,2048]{0,1:T(8,128)(2,1)S(1)}, bf16[128,2048]{0,1:T(8,128)(2,1)S(1)}, u32[]{:S(2)}, u32[]{:S(2)}) %collective-permute-start.4) | collective-permute-done | bytes 524320 | tf_op jit(solution)/shard_map/ppermute | solution.py:98
  44.7 1.1 %slice_reduce_fusion = f32[16]{0:T(128)S(1)} fusion(f32[16,136,128]{2,1,0:T(8,128)} %collective-permute-done), kind=kLoop, calls=%fused_computation.70 | loop fusion | bytes 128 | tf_op jit(solution)/shard_map/slice | solution.py:21
  45.8 1.8 %multiply_add_fusion = f32[16,136,128]{2,1,0:T(8,128)S(1)} fusion(f32[16,136,128]{2,1,0:T(8,128)} %collective-permute-done, f32[16,136,128]{2,1,0:T(8,128)} %fusion.5, f32[16]{0:T(128)S(1)} %slice_reduce_fusion), kind=kLoop, calls=%fused_computation.22 | loop fusion | flops 557056 | bytes 3342400 | tf_op jit(solution)/shard_map/add | solution.py:88
  48.2 0.8 %fusion.2 = f32[128,16,128]{0,2,1:T(8,128)S(1)} fusion(bf16[128,16,128]{0,2,1:T(8,128)(2,1)S(1)} %bitcast.113, f32[128,16]{0,1:T(8,128)S(1)} %copy.37, f32[16,136,128]{2,1,0:T(8,128)S(1)} %collective-permute-done.5, f32[16,136,128]{2,1,0:T(8,128)S(1)} %multiply_add_fusion, pred[]{:T(512)S(6)} %eq.29), kind=kOutput, calls=%fused_computation.12 | convolution fusion | flops 201850880 | bytes 3678209 | tf_op jit(solution)/shard_map/shd,hde->she/dot_general | solution.py:171
  48.9 0.9 %fusion.4 = f32[128,16,128]{0,2,1:T(8,128)S(1)} fusion(f32[16,136,128]{2,1,0:T(8,128)S(1)} %collective-permute-done.5, f32[16,136,128]{2,1,0:T(8,128)S(1)} %multiply_add_fusion, f32[128,16]{0,1:T(8,128)S(1)} %copy.52, pred[]{:T(512)S(6)} %eq.29, bf16[128,16,128]{2,1,0:T(8,128)(2,1)S(1)} %bitcast.109), kind=kOutput, calls=%fused_computation.16 | convolution fusion | flops 201850880 | bytes 3678209 | tf_op jit(solution)/shard_map/the,hde->thd/dot_general | solution.py:168
  49.8 1.2 %fusion.14 = bf16[128,2048]{0,1:T(8,128)(2,1)S(1)} fusion(f32[128,16,128]{0,2,1:T(8,128)S(1)} %fusion.2, f32[128,16,128]{0,2,1:T(8,128)S(1)} %fusion.3, f32[128,16,128]{0,2,1:T(8,128)S(1)} %fusion.4, f32[2048]{0:T(1024)S(1)} %bitcast.127, f32[2048]{0:T(1024)S(1)} %bitcast.130, f32[2048]{0:T(1024)S(1)} %bitcast.124), kind=kLoop, calls=%fused_computation.36 | loop fusion | flops 1572864 | bytes 3694592 | tf_op jit(solution)/shard_map/convert_element_type | solution.py:175
  51.1 16.1 %collective-permute-done.6 = bf16[128,2048]{0,1:T(8,128)(2,1)S(1)} collective-permute-done((bf16[128,2048]{0,1:T(8,128)(2,1)S(1)}, bf16[128,2048]{0,1:T(8,128)(2,1)S(1)}, u32[]{:S(2)}, u32[]{:S(2)}) %collective-permute-start.6) | collective-permute-done | bytes 524320 | tf_op jit(solution)/shard_map/ppermute | solution.py:98
  67.3 1.0 %copy.57 = bf16[1,128,2048]{2,1,0:T(8,128)(2,1)} copy(bf16[1,128,2048]{1,2,0:T(8,128)(2,1)S(1)} %fusion.24) | data formatting | bytes 1048576 | tf_op jit(solution)/shard_map/broadcast_in_dim | solution.py:180
  (55 shorter events, 4.8 us)
Async XLA Ops:
  0.0 4.2 %copy-start.1 = (bf16[1,128,2048]{2,1,0:T(8,128)(2,1)S(1)}, bf16[1,128,2048]{2,1,0:T(8,128)(2,1)}, u32[]{:S(2)}) copy-start(bf16[1,128,2048]{2,1,0:T(8,128)(2,1)} %param.6) | copy-start | bytes 1572868
  8.9 5.7 %collective-permute-start = (f32[16,136,128]{2,1,0:T(8,128)}, f32[16,136,128]{2,1,0:T(8,128)}, u32[]{:S(2)}, u32[]{:S(2)}) collective-permute-start(f32[16,136,128]{2,1,0:T(8,128)} %pad_maximum_fusion), channel_id=1, source_target_pairs={{0,1},{2,3},{4,5},{6,7},{1,0},{3,2},{5,4},{7,6},{8,9},{10,11},{12,... | collective-permute-start | bytes 3342344 | tf_op jit(solution)/shard_map/ppermute | solution.py:63
  13.2 1.4 %copy-start = (f32[16,128,128]{2,1,0:T(8,128)S(1)}, f32[16,128,128]{2,1,0:T(8,128)}, u32[]{:S(2)}) copy-start(f32[16,128,128]{2,1,0:T(8,128)} %get-tuple-element.13) | copy-start | bytes 3145732
  16.6 2.5 %copy-start.3 = (f32[16,128,128]{1,2,0:T(8,128)S(1)}, f32[16,128,128]{1,2,0:T(8,128)}, u32[]{:S(2)}) copy-start(f32[16,128,128]{1,2,0:T(8,128)} %convolution_multiply_fusion.1) | copy-start | bytes 3145732
  17.6 11.8 %collective-permute-start.3 = (bf16[16,136,128]{2,1,0:T(8,128)(2,1)}, bf16[16,136,128]{2,1,0:T(8,128)(2,1)}, u32[]{:S(2)}, u32[]{:S(2)}) collective-permute-start(bf16[16,136,128]{2,1,0:T(8,128)(2,1)} %pad_maximum_fusion.1), channel_id=1, source_target_pairs={{1,7},{6,0},{9,15},{14,8},{17,23},{22,16},{25,31},{30,24}} | collective-permute-start | bytes 1671176 | tf_op jit(solution)/shard_map/ppermute | solution.py:40
  20.6 6.0 %copy-start.2 = (bf16[1,128,2048]{1,2,0:T(8,128)(2,1)S(1)}, bf16[1,128,2048]{1,2,0:T(8,128)(2,1)}, u32[]{:S(2)}) copy-start(bf16[1,128,2048]{1,2,0:T(8,128)(2,1)} %copy.41) | copy-start | bytes 1572868
  21.9 12.4 %collective-permute-start.2 = (bf16[16,136,128]{2,1,0:T(8,128)(2,1)}, bf16[16,136,128]{2,1,0:T(8,128)(2,1)S(1)}, u32[]{:S(2)}, u32[]{:S(2)}) collective-permute-start(bf16[16,136,128]{2,1,0:T(8,128)(2,1)} %pad_maximum_fusion.1), channel_id=1, source_target_pairs={{1,5},{3,7},{6,2},{4,0},{9,13},{11,15},{14,10},{12,8},{17,21},{19,... | collective-permute-start | bytes 1671176 | tf_op jit(solution)/shard_map/ppermute | solution.py:40
  24.2 15.1 %collective-permute-start.1 = (bf16[16,136,128]{2,1,0:T(8,128)(2,1)}, bf16[16,136,128]{2,1,0:T(8,128)(2,1)S(1)}, u32[]{:S(2)}, u32[]{:S(2)}) collective-permute-start(bf16[16,136,128]{2,1,0:T(8,128)(2,1)} %pad_maximum_fusion.1), channel_id=1, source_target_pairs={{1,3},{3,5},{5,7},{6,4},{4,2},{2,0},{9,11},{11,13},{13,15},{14,12}... | collective-permute-start | bytes 1671176 | tf_op jit(solution)/shard_map/ppermute | solution.py:40
  28.9 15.8 %collective-permute-start.4 = (bf16[128,2048]{0,1:T(8,128)(2,1)S(1)}, bf16[128,2048]{0,1:T(8,128)(2,1)S(1)}, u32[]{:S(2)}, u32[]{:S(2)}) collective-permute-start(bf16[128,2048]{0,1:T(8,128)(2,1)S(1)} %fusion.11), channel_id=1, source_target_pairs={{0,24},{8,0},{16,8},{24,16},{1,25},{9,1},{17,9},{25,17},{2,26},{10... | collective-permute-start | bytes 1572872 | tf_op jit(solution)/shard_map/ppermute | solution.py:98
  44.7 3.0 %collective-permute-start.5 = (f32[16,136,128]{2,1,0:T(8,128)}, f32[16,136,128]{2,1,0:T(8,128)S(1)}, u32[]{:S(2)}, u32[]{:S(2)}) collective-permute-start(f32[16,136,128]{2,1,0:T(8,128)} %fusion.5), channel_id=1, source_target_pairs={{0,1},{2,3},{4,5},{6,7},{1,0},{3,2},{5,4},{7,6},{8,9},{10,11},{12,... | collective-permute-start | bytes 3342344 | tf_op jit(solution)/shard_map/ppermute | solution.py:87
  51.0 16.1 %collective-permute-start.6 = (bf16[128,2048]{0,1:T(8,128)(2,1)S(1)}, bf16[128,2048]{0,1:T(8,128)(2,1)S(1)}, u32[]{:S(2)}, u32[]{:S(2)}) collective-permute-start(bf16[128,2048]{0,1:T(8,128)(2,1)S(1)} %fusion.14), channel_id=1, source_target_pairs={{0,24},{8,0},{16,8},{24,16},{1,25},{9,1},{17,9},{25,17},{2,26},{10... | collective-permute-start | bytes 1572872 | tf_op jit(solution)/shard_map/ppermute | solution.py:98

commit v17 on v15

--- a/solution.py
+++ b/solution.py
@@ -61,7 +61,7 @@
     mine = jnp.where(odd, forward_part, backward_part)
     sent = packed(jnp.where(odd, backward_part, forward_part), rate)
     message = lax.ppermute(sent, axis, swap)
-    lower, lower_rate = unpacked(message)
+    lower_rate = unpacked(message)[1]
     window = rate[:, None, None] * message + packed(mine, jnp.zeros_like(rate))
     if couples <= 4:
         incoming = jnp.zeros_like(mine)
@@ -85,7 +85,8 @@
         incoming = unpacked(nearer)[0]
     incoming, held = lax.optimization_barrier((incoming, held))
     other = lax.ppermute(incoming, axis, swap)
-    own = lower_rate[:, None, None] * incoming + lower
+    width = message.shape[1] - 8
+    own = (lower_rate[:, None, None] * packed(incoming, jnp.zeros_like(rate)) + message)[:, :width]
     return jnp.where(odd, own, other), jnp.where(odd, other, own), held
 
 

time: 66.2 us -> 66.2 us (level)
  no operation moved by 1% of the time
where the time goes in v17:
time: 66.2 us; the launch traced here: 65.1 us
  waiting for transfers between devices  21.3 us (32%)
  starting transfers between devices  14 us (21%)
  other arithmetic  12.2 us (18%)
  matrix products  9.4 us (14%)
  local copies, waits for them, and re-layouts  7.92 us (12%)
    ppermute x2, waiting for transfers between devices, passed_along(): return lax.ppermute(value, axis, pairs)  11.4 us
    ppermute x3, waiting for transfers between devices, sent_narrow(): return widen(lax.ppermute(narrow(message), axis, pairs))  9.91 us
    ppermute x2, starting transfers between devices, passed_along(): return lax.ppermute(value, axis, pairs)  8.7 us
    ppermute x3, starting transfers between devices, sent_narrow(): return widen(lax.ppermute(narrow(message), axis, pairs))  4.01 us
    unnamed x11, local copies, waits for them, and re-layouts  2.48 us
    convert_element_type x1, other arithmetic, local(): near_round = near_total.astype(jnp.bfloat16)  2.12 us
    dot_general x1, matrix products, local(): jnp.einsum('hts,thd->shd', mixing, queries, precision=HIGH)  1.85 us
    add x1, other arithmetic, scans_in(): lower_rate[:, None, None] * packed(incoming, jnp.zeros_like(rate)) + message  1.7 us
  transfers between devices with their start and end apart: 7, of which 3 were waited for; matrix products, arithmetic and copies ran while one was open for 21% of the time, Pallas kernels for 0%

profile of v17, /device:TPU:0, one launch (start us, length us, event | category | flops | bytes accessed | tf_op | source)
XLA Modules:
  0.0 65.1 jit_solution(2674144146609193502)
XLA Ops:
  0.1 0.7 %compare_bitcast_fusion = pred[2]{0:T(512)(128)(4,1)S(1)} fusion(s32[1,2]{1,0:T(1,128)} %param.9), kind=kLoop, calls=%fused_computation.75 | loop fusion | flops 2 | bytes 10 | tf_op jit(solution)/shard_map/eq | solution.py:103
  0.9 0.7 %log_bitcast_fusion = f32[2,16]{1,0:T(2,128)S(1)} fusion(s32[1,2,16]{2,1,0:T(2,128)} %param.8), kind=kLoop, calls=%fused_computation.76 | loop fusion | flops 96 | bytes 256 | tf_op jit(solution)/shard_map/log | solution.py:101
  1.9 0.7 %fusion.36 = (f32[1,1,2048]{2,0,1:T(1,128)S(1)}, f32[1,1,2048]{2,0,1:T(1,128)S(1)}, f32[1,1,2048]{2,0,1:T(1,128)S(1)}) fusion(f32[1,3,2048]{2,0,1:T(1,128)} %param.7), kind=kLoop, calls=%fused_computation.84 | loop fusion | bytes 49152 | tf_op jit(solution)/shard_map/slice | solution.py:112
  2.6 1.3 %copy.34 = bf16[1,128,2048]{1,2,0:T(8,128)(2,1)S(1)} copy(bf16[1,128,2048]{2,1,0:T(8,128)(2,1)} %param.5) | data formatting | bytes 1048576 | tf_op args[0]
  4.0 1.0 %fusion.5 = (bf16[128,2048]{0,1:T(8,128)(2,1)S(1)}, bf16[128,2048]{0,1:T(8,128)(2,1)S(1)}, bf16[128,2048]{0,1:T(8,128)(2,1)S(1)}) fusion(bf16[1,128,2048]{1,2,0:T(8,128)(2,1)S(1)} %copy.34, f32[2048]{0:T(1024)S(1)} %bitcast.122, f32[2048]{0:T(1024)S(1)} %bitcast.125, f32[2048]{0:T(1024)S(1)} %bitcast.128), kind=kLoop, calls=%fused_computation.19 | loop fusion | flops 1835008 | bytes 2121728 | tf_op jit(solution)/shard_map/convert_element_type | solution.py:112
  5.3 0.9 %fusion.16 = f32[16,128,128]{2,1,0:T(8,128)S(1)} fusion(bf16[128,16,128]{0,2,1:T(8,128)(2,1)S(1)} %bitcast.117, bf16[128,16,128]{0,2,1:T(8,128)(2,1)S(1)} %bitcast.110, f32[128,16]{0,1:T(8,128)S(1)} %copy.37), kind=kOutput, calls=%fused_computation.42 | convolution fusion | flops 201850880 | bytes 2105344 | tf_op jit(solution)/shard_map/shd,she->hde/dot_general | solution.py:135
  6.2 1.6 %broadcast_select_fusion.2 = (f32[16,128,128]{2,1,0:T(8,128)S(1)}, f32[16,128,128]{2,1,0:T(8,128)}) fusion(f32[16,128,128]{2,1,0:T(8,128)S(1)} %fusion.16, pred[]{:T(512)S(6)} %eq.29, bf16[128,16,128]{2,1,0:T(8,128)(2,1)S(1)} %bitcast.106, bf16[128,16,128]{0,2,1:T(8,128)(2,1)S(1)} %bitcast.114, f32[128,16]{0,1:T(8,128)S(1)} %copy.35), kind=kOutput, calls=%fused_computation.54 | convolution fusion | flops 202637312 | bytes 4202497 | tf_op jit(solution)/shard_map/shd,she->hde/dot_general | solution.py:138
  7.8 1.1 %pad_maximum_fusion = f32[16,136,128]{2,1,0:T(8,128)} fusion(f32[16,8,128]{2,1,0:T(8,128)S(1)} %broadcast_in_dim.32, f32[16,128,128]{2,1,0:T(8,128)S(1)} %get-tuple-element.11), kind=kLoop, calls=%fused_computation.17 | loop fusion | flops 278528 | bytes 2228224 | tf_op jit(solution)/shard_map/concatenate | solution.py:16
  9.4 1.0 %copy.41 = bf16[1,128,2048]{1,2,0:T(8,128)(2,1)} copy(bf16[1,128,2048]{2,1,0:T(8,128)(2,1)S(1)} %copy-done.3) | data formatting | bytes 1048576 | tf_op args[1]
  10.5 0.6 convolution_multiply_fusion.1
  11.5 1.3 %copy.51 = f32[128,16,128]{0,2,1:T(8,128)} copy(f32[128,16,128]{2,0,1:T(8,128)S(1)} %fusion) | data formatting | bytes 2097152 | tf_op jit(solution)/shard_map/mul | solution.py:155
  13.0 0.6 fusion.1
  13.6 1.4 %convolution_multiply_fusion.3 = f32[16,128,128]{2,1,0:T(8,128)} fusion(bf16[128,16,128]{0,2,1:T(8,128)(2,1)S(1)} %bitcast.112, f32[16,128,128]{1,2,0:T(8,128)S(1)} %fusion.1), kind=kOutput, calls=%fused_computation.7 | convolution fusion | flops 201588736 | bytes 2621440 | tf_op jit(solution)/shard_map/hts,shd->thd/dot_general | solution.py:150
  15.0 1.8 %convolution_multiply_fusion.2 = f32[16,128,128]{2,1,0:T(8,128)} fusion(bf16[128,16,128]{0,2,1:T(8,128)(2,1)S(1)} %bitcast.116, f32[16,128,128]{1,2,0:T(8,128)S(1)} %fusion.1), kind=kOutput, calls=%fused_computation.6 | convolution fusion | flops 201588736 | bytes 2621440 | tf_op jit(solution)/shard_map/hts,thd->shd/dot_general | solution.py:151
  16.8 1.5 %pad_add_fusion = f32[16,136,128]{2,1,0:T(8,128)S(1)} fusion(f32[16,128,128]{2,1,0:T(8,128)S(1)} %copy-done, f32[16,136,128]{2,1,0:T(8,128)} %collective-permute-done, f32[16]{0:T(128)S(1)} %fusion.34), kind=kLoop, calls=%fused_computation.18 | loop fusion | flops 557056 | bytes 3276864 | tf_op jit(solution)/shard_map/add | solution.py:65
  19.1 1.4 %collective-permute-start.1 = (bf16[16,136,128]{2,1,0:T(8,128)(2,1)S(1)}, bf16[16,136,128]{2,1,0:T(8,128)(2,1)S(1)}, u32[]{:S(2)}, u32[]{:S(2)}) collective-permute-start(bf16[16,136,128]{2,1,0:T(8,128)(2,1)S(1)} %pad_maximum_fusion.1), channel_id=1, source_target_pairs={{1,3},{3,5},{5,7},{6,4},{4,2},{2,0},{9,11},{11,13},{13,15},{14,12}... | collective-permute-start | bytes 1671176 | tf_op jit(solution)/shard_map/ppermute | solution.py:40
  20.5 1.3 %collective-permute-start.2 = (bf16[16,136,128]{2,1,0:T(8,128)(2,1)S(1)}, bf16[16,136,128]{2,1,0:T(8,128)(2,1)S(1)}, u32[]{:S(2)}, u32[]{:S(2)}) collective-permute-start(bf16[16,136,128]{2,1,0:T(8,128)(2,1)S(1)} %pad_maximum_fusion.1), channel_id=1, source_target_pairs={{1,5},{3,7},{6,2},{4,0},{9,13},{11,15},{14,10},{12,8},{17,21},{19,... | collective-permute-start | bytes 1671176 | tf_op jit(solution)/shard_map/ppermute | solution.py:40
  21.8 1.3 %collective-permute-start.3 = (bf16[16,136,128]{2,1,0:T(8,128)(2,1)S(1)}, bf16[16,136,128]{2,1,0:T(8,128)(2,1)S(1)}, u32[]{:S(2)}, u32[]{:S(2)}) collective-permute-start(bf16[16,136,128]{2,1,0:T(8,128)(2,1)S(1)} %pad_maximum_fusion.1), channel_id=1, source_target_pairs={{1,7},{6,0},{9,15},{14,8},{17,23},{22,16},{25,31},{30,24}} | collective-permute-start | bytes 1671176 | tf_op jit(solution)/shard_map/ppermute | solution.py:40
  23.1 2.1 %fusion.10 = bf16[128,2048]{0,1:T(8,128)(2,1)S(1)} fusion(f32[16,128,128]{2,1,0:T(8,128)} %convolution_multiply_fusion.2, f32[16,128,128]{2,1,0:T(8,128)S(1)} %copy-done.2, f32[128,16,128]{0,2,1:T(8,128)S(1)} %copy-done.1, bf16[1,128,2048]{1,2,0:T(8,128)(2,1)} %copy.41, f32[2048]{0:T(1024)S(1)} %bitcast.126, f32[2048]{0:T(1024)S(1)} %bitcast.129, ...), kind=kLoop, calls=%fused_computation.28 | loop fusion | flops 2097152 | bytes 4218880 | tf_op jit(solution)/shard_map/convert_element_type | solution.py:160
  25.2 4.7 %collective-permute-start.4 = (bf16[128,2048]{0,1:T(8,128)(2,1)S(1)}, bf16[128,2048]{0,1:T(8,128)(2,1)S(1)}, u32[]{:S(2)}, u32[]{:S(2)}) collective-permute-start(bf16[128,2048]{0,1:T(8,128)(2,1)S(1)} %fusion.10), channel_id=1, source_target_pairs={{0,24},{8,0},{16,8},{24,16},{1,25},{9,1},{17,9},{25,17},{2,26},{10... | collective-permute-start | bytes 1572872 | tf_op jit(solution)/shard_map/ppermute | solution.py:96
  29.9 6.1 %collective-permute-done.1 = bf16[16,136,128]{2,1,0:T(8,128)(2,1)S(1)} collective-permute-done((bf16[16,136,128]{2,1,0:T(8,128)(2,1)S(1)}, bf16[16,136,128]{2,1,0:T(8,128)(2,1)S(1)}, u32[]{:S(2)}, u32[]{:S(2)}) %collective-permute-start.1) | collective-permute-done | bytes 557088 | tf_op jit(solution)/shard_map/ppermute | solution.py:40
  36.0 3.8 %collective-permute-done.2 = bf16[16,136,128]{2,1,0:T(8,128)(2,1)S(1)} collective-permute-done((bf16[16,136,128]{2,1,0:T(8,128)(2,1)S(1)}, bf16[16,136,128]{2,1,0:T(8,128)(2,1)S(1)}, u32[]{:S(2)}, u32[]{:S(2)}) %collective-permute-start.2) | collective-permute-done | bytes 557088 | tf_op jit(solution)/shard_map/ppermute | solution.py:40
  40.0 1.4 %multiply_add_fusion = f32[16,128,128]{2,1,0:T(8,128)} fusion(bf16[16,136,128]{2,1,0:T(8,128)(2,1)S(1)} %collective-permute-done.3, bf16[16,136,128]{2,1,0:T(8,128)(2,1)S(1)} %collective-permute-done.2, bf16[16,136,128]{2,1,0:T(8,128)(2,1)S(1)} %collective-permute-done.1, f32[16]{0:T(128)S(1)} %get-tuple-element.10, f32[16]{0:T(128)S(1)} %get-tuple-element.9), kind=kLoop, calls=%fused_computation.41 | loop fusion | flops 1835008 | bytes 2621568 | tf_op jit(solution)/shard_map/add | solution.py:72
  41.4 0.9 %collective-permute-start.5 = (f32[16,128,128]{2,1,0:T(8,128)}, f32[16,128,128]{2,1,0:T(8,128)S(1)}, u32[]{:S(2)}, u32[]{:S(2)}) collective-permute-start(f32[16,128,128]{2,1,0:T(8,128)} %multiply_add_fusion), channel_id=1, source_target_pairs={{0,1},{2,3},{4,5},{6,7},{1,0},{3,2},{5,4},{7,6},{8,9},{10,11},{12,... | collective-permute-start | bytes 3145736 | tf_op jit(solution)/shard_map/ppermute | solution.py:87
  42.4 1.1 %slice_reduce_fusion = f32[16]{0:T(128)S(1)} fusion(f32[16,136,128]{2,1,0:T(8,128)} %collective-permute-done), kind=kLoop, calls=%fused_computation.63 | loop fusion | bytes 128 | tf_op jit(solution)/shard_map/slice | solution.py:21
  43.4 1.7 %slice_add_fusion = f32[16,128,128]{2,1,0:T(8,128)S(1)} fusion(f32[16,136,128]{2,1,0:T(8,128)} %collective-permute-done, f32[16,128,128]{2,1,0:T(8,128)} %multiply_add_fusion, f32[16]{0:T(128)S(1)} %slice_reduce_fusion), kind=kLoop, calls=%fused_computation.22 | loop fusion | flops 524288 | bytes 3145792 | tf_op jit(solution)/shard_map/add | solution.py:89
  45.7 0.7 %fusion.2 = f32[128,16,128]{0,2,1:T(8,128)S(1)} fusion(bf16[128,16,128]{0,2,1:T(8,128)(2,1)S(1)} %bitcast.113, f32[128,16]{0,1:T(8,128)S(1)} %copy.37, f32[16,128,128]{2,1,0:T(8,128)S(1)} %collective-permute-done.5, f32[16,128,128]{2,1,0:T(8,128)S(1)} %slice_add_fusion, pred[]{:T(512)S(6)} %eq.29), kind=kOutput, calls=%fused_computation.12 | convolution fusion | flops 201850880 | bytes 3678209 | tf_op jit(solution)/shard_map/shd,hde->she/dot_general | solution.py:169
  46.4 0.9 %fusion.4 = f32[128,16,128]{0,2,1:T(8,128)S(1)} fusion(f32[16,128,128]{2,1,0:T(8,128)S(1)} %slice_add_fusion, f32[16,128,128]{2,1,0:T(8,128)S(1)} %collective-permute-done.5, f32[128,16]{0,1:T(8,128)S(1)} %copy.52, pred[]{:T(512)S(6)} %eq.29, bf16[128,16,128]{2,1,0:T(8,128)(2,1)S(1)} %bitcast.109), kind=kOutput, calls=%fused_computation.16 | convolution fusion | flops 201850880 | bytes 3678209 | tf_op jit(solution)/shard_map/the,hde->thd/dot_general | solution.py:166
  47.3 1.2 %fusion.13 = bf16[128,2048]{0,1:T(8,128)(2,1)S(1)} fusion(f32[128,16,128]{0,2,1:T(8,128)S(1)} %fusion.2, f32[128,16,128]{0,2,1:T(8,128)S(1)} %fusion.3, f32[128,16,128]{0,2,1:T(8,128)S(1)} %fusion.4, f32[2048]{0:T(1024)S(1)} %bitcast.127, f32[2048]{0:T(1024)S(1)} %bitcast.130, f32[2048]{0:T(1024)S(1)} %bitcast.124), kind=kLoop, calls=%fused_computation.33 | loop fusion | flops 1572864 | bytes 3694592 | tf_op jit(solution)/shard_map/convert_element_type | solution.py:173
  48.5 4.0 %collective-permute-start.6 = (bf16[128,2048]{0,1:T(8,128)(2,1)S(1)}, bf16[128,2048]{0,1:T(8,128)(2,1)S(1)}, u32[]{:S(2)}, u32[]{:S(2)}) collective-permute-start(bf16[128,2048]{0,1:T(8,128)(2,1)S(1)} %fusion.13), channel_id=1, source_target_pairs={{0,24},{8,0},{16,8},{24,16},{1,25},{9,1},{17,9},{25,17},{2,26},{10... | collective-permute-start | bytes 1572872 | tf_op jit(solution)/shard_map/ppermute | solution.py:96
  52.5 11.4 %collective-permute-done.6 = bf16[128,2048]{0,1:T(8,128)(2,1)S(1)} collective-permute-done((bf16[128,2048]{0,1:T(8,128)(2,1)S(1)}, bf16[128,2048]{0,1:T(8,128)(2,1)S(1)}, u32[]{:S(2)}, u32[]{:S(2)}) %collective-permute-start.6) | collective-permute-done | bytes 524320 | tf_op jit(solution)/shard_map/ppermute | solution.py:96
  64.1 1.0 %copy.57 = bf16[1,128,2048]{2,1,0:T(8,128)(2,1)} copy(bf16[1,128,2048]{1,2,0:T(8,128)(2,1)S(1)} %fusion.21) | data formatting | bytes 1048576 | tf_op jit(solution)/shard_map/broadcast_in_dim | solution.py:178
  (48 shorter events, 3.7 us)
Async XLA Ops:
  4.0 1.0 %copy-start.3 = (bf16[1,128,2048]{2,1,0:T(8,128)(2,1)S(1)}, bf16[1,128,2048]{2,1,0:T(8,128)(2,1)}, u32[]{:S(2)}) copy-start(bf16[1,128,2048]{2,1,0:T(8,128)(2,1)} %param.6) | copy-start | bytes 1572868
  8.9 7.9 %collective-permute-start = (f32[16,136,128]{2,1,0:T(8,128)}, f32[16,136,128]{2,1,0:T(8,128)}, u32[]{:S(2)}, u32[]{:S(2)}) collective-permute-start(f32[16,136,128]{2,1,0:T(8,128)} %pad_maximum_fusion), channel_id=1, source_target_pairs={{0,1},{2,3},{4,5},{6,7},{1,0},{3,2},{5,4},{7,6},{8,9},{10,11},{12,... | collective-permute-start | bytes 3342344 | tf_op jit(solution)/shard_map/ppermute | solution.py:63
  15.0 1.9 %copy-start = (f32[16,128,128]{2,1,0:T(8,128)S(1)}, f32[16,128,128]{2,1,0:T(8,128)}, u32[]{:S(2)}) copy-start(f32[16,128,128]{2,1,0:T(8,128)} %get-tuple-element.12) | copy-start | bytes 3145732
  18.3 4.8 %copy-start.1 = (f32[128,16,128]{0,2,1:T(8,128)S(1)}, f32[128,16,128]{0,2,1:T(8,128)}, u32[]{:S(2)}) copy-start(f32[128,16,128]{0,2,1:T(8,128)} %copy.51) | copy-start | bytes 3145732
  18.8 4.3 %copy-start.2 = (f32[16,128,128]{2,1,0:T(8,128)S(1)}, f32[16,128,128]{2,1,0:T(8,128)}, u32[]{:S(2)}) copy-start(f32[16,128,128]{2,1,0:T(8,128)} %convolution_multiply_fusion.3) | copy-start | bytes 3145732
  19.1 17.0 %collective-permute-start.1 = (bf16[16,136,128]{2,1,0:T(8,128)(2,1)S(1)}, bf16[16,136,128]{2,1,0:T(8,128)(2,1)S(1)}, u32[]{:S(2)}, u32[]{:S(2)}) collective-permute-start(bf16[16,136,128]{2,1,0:T(8,128)(2,1)S(1)} %pad_maximum_fusion.1), channel_id=1, source_target_pairs={{1,3},{3,5},{5,7},{6,4},{4,2},{2,0},{9,11},{11,13},{13,15},{14,12}... | collective-permute-start | bytes 1671176 | tf_op jit(solution)/shard_map/ppermute | solution.py:40
  20.5 19.3 %collective-permute-start.2 = (bf16[16,136,128]{2,1,0:T(8,128)(2,1)S(1)}, bf16[16,136,128]{2,1,0:T(8,128)(2,1)S(1)}, u32[]{:S(2)}, u32[]{:S(2)}) collective-permute-start(bf16[16,136,128]{2,1,0:T(8,128)(2,1)S(1)} %pad_maximum_fusion.1), channel_id=1, source_target_pairs={{1,5},{3,7},{6,2},{4,0},{9,13},{11,15},{14,10},{12,8},{17,21},{19,... | collective-permute-start | bytes 1671176 | tf_op jit(solution)/shard_map/ppermute | solution.py:40
  21.8 18.2 %collective-permute-start.3 = (bf16[16,136,128]{2,1,0:T(8,128)(2,1)S(1)}, bf16[16,136,128]{2,1,0:T(8,128)(2,1)S(1)}, u32[]{:S(2)}, u32[]{:S(2)}) collective-permute-start(bf16[16,136,128]{2,1,0:T(8,128)(2,1)S(1)} %pad_maximum_fusion.1), channel_id=1, source_target_pairs={{1,7},{6,0},{9,15},{14,8},{17,23},{22,16},{25,31},{30,24}} | collective-permute-start | bytes 1671176 | tf_op jit(solution)/shard_map/ppermute | solution.py:40
  25.2 16.2 %collective-permute-start.4 = (bf16[128,2048]{0,1:T(8,128)(2,1)S(1)}, bf16[128,2048]{0,1:T(8,128)(2,1)S(1)}, u32[]{:S(2)}, u32[]{:S(2)}) collective-permute-start(bf16[128,2048]{0,1:T(8,128)(2,1)S(1)} %fusion.10), channel_id=1, source_target_pairs={{0,24},{8,0},{16,8},{24,16},{1,25},{9,1},{17,9},{25,17},{2,26},{10... | collective-permute-start | bytes 1572872 | tf_op jit(solution)/shard_map/ppermute | solution.py:96
  41.4 3.7 %collective-permute-start.5 = (f32[16,128,128]{2,1,0:T(8,128)}, f32[16,128,128]{2,1,0:T(8,128)S(1)}, u32[]{:S(2)}, u32[]{:S(2)}) collective-permute-start(f32[16,128,128]{2,1,0:T(8,128)} %multiply_add_fusion), channel_id=1, source_target_pairs={{0,1},{2,3},{4,5},{6,7},{1,0},{3,2},{5,4},{7,6},{8,9},{10,11},{12,... | collective-permute-start | bytes 3145736 | tf_op jit(solution)/shard_map/ppermute | solution.py:87
  48.5 15.4 %collective-permute-start.6 = (bf16[128,2048]{0,1:T(8,128)(2,1)S(1)}, bf16[128,2048]{0,1:T(8,128)(2,1)S(1)}, u32[]{:S(2)}, u32[]{:S(2)}) collective-permute-start(bf16[128,2048]{0,1:T(8,128)(2,1)S(1)} %fusion.13), channel_id=1, source_target_pairs={{0,24},{8,0},{16,8},{24,16},{1,25},{9,1},{17,9},{25,17},{2,26},{10... | collective-permute-start | bytes 1572872 | tf_op jit(solution)/shard_map/ppermute | solution.py:96

commit v18 on v15

--- a/solution.py
+++ b/solution.py
@@ -53,18 +53,19 @@
 def scans_in(forward_part, backward_part, rate, axis, held):
     count = lax.axis_size(axis)
     if count == 1:
-        return jnp.zeros_like(forward_part), jnp.zeros_like(backward_part), held
+        return jnp.zeros_like(forward_part[:, :-8]), jnp.zeros_like(backward_part[:, :-8]), held
     assert count % 2 == 0
     odd = lax.axis_index(axis) % 2 == 1
     couples = count // 2
     swap = [(2 * p, 2 * p + 1) for p in range(couples)] + [(2 * p + 1, 2 * p) for p in range(couples)]
-    mine = jnp.where(odd, forward_part, backward_part)
-    sent = packed(jnp.where(odd, backward_part, forward_part), rate)
+    width = forward_part.shape[1] - 8
+    tile = packed(jnp.zeros_like(forward_part[:, :width]), rate)
+    sent = jnp.where(odd, backward_part, forward_part) + tile
     message = lax.ppermute(sent, axis, swap)
     lower, lower_rate = unpacked(message)
-    window = rate[:, None, None] * message + packed(mine, jnp.zeros_like(rate))
+    window = rate[:, None, None] * message + jnp.where(odd, forward_part, backward_part)
     if couples <= 4:
-        incoming = jnp.zeros_like(mine)
+        incoming = jnp.zeros_like(lower)
         weight = jnp.ones_like(rate)
         for step in range(1, couples):
             moves = [(2 * p + 1, 2 * (p + step) + 1) for p in range(couples - step)]
@@ -131,11 +132,12 @@
     cumul = jnp.cumsum(logs, axis=0)
     growth = jnp.exp(cumul)
     tail = jnp.exp(cumul[-1][None, :] - cumul)
+    widened = ((0, 0), (0, 0), (0, 8))
     forward_part = jnp.einsum(
-        "shd,she->hde", key_rows * tail[:, :, None], value_rows, precision=HIGH
+        "shd,she->hde", jnp.pad(key_rows * tail[:, :, None], widened), value_rows, precision=HIGH
     )
     adjoint_part = scale * jnp.einsum(
-        "shd,she->hde", queries * growth[:, :, None], grad_rows, precision=HIGH
+        "shd,she->hde", jnp.pad(queries * growth[:, :, None], widened), grad_rows, precision=HIGH
     )
     whole_decay = jnp.exp(cumul[-1])
     cum_heads = cumul.T

time: 66.2 us -> 69.1 us (1.044)
  local copies, waits for them, and re-layouts: 7.92 us -> 10.2 us
  matrix products: 9.4 us -> 10.8 us
  other arithmetic: 12.2 us -> 11.3 us
    mul x1, local copies, waits for them, and re-layouts: 1.34 us -> 2.56 us  [local(): scale * jnp.einsum('hts,the->she', attention, grad_rows, precision=HIGH)]
    concatenate x1 -> x0, other arithmetic: 1.13 us -> none  [packed(): return jnp.concatenate([state, tile], axis=1)]
    unnamed x11, local copies, waits for them, and re-layouts: 2.48 us -> 3.52 us
    dot_general x1, matrix products: 0.46 us -> 1.43 us  [local(): jnp.einsum('hts,the->she', attention, grad_rows, precision=HIGH)]
  transfers between devices with their start and end apart: 7 -> 7, of which waited for: 3 -> 3; matrix products, arithmetic and copies ran while one was open for 21% -> 25% of each run, Pallas kernels for 0% -> 0%
where the time goes in v18:
time: 69.1 us; the launch traced here: 67.9 us
  waiting for transfers between devices  21.3 us (31%)
  starting transfers between devices  14 us (20%)
  other arithmetic  11.3 us (16%)
  matrix products  10.8 us (16%)
  local copies, waits for them, and re-layouts  10.2 us (15%)
    ppermute x2, waiting for transfers between devices, passed_along(): return lax.ppermute(value, axis, pairs)  11.4 us
    ppermute x3, waiting for transfers between devices, sent_narrow(): return widen(lax.ppermute(narrow(message), axis, pairs))  9.93 us
    ppermute x2, starting transfers between devices, passed_along(): return lax.ppermute(value, axis, pairs)  8.69 us
    ppermute x3, starting transfers between devices, sent_narrow(): return widen(lax.ppermute(narrow(message), axis, pairs))  4.01 us
    unnamed x11, local copies, waits for them, and re-layouts  3.52 us
    mul x1, local copies, waits for them, and re-layouts, local(): scale * jnp.einsum('hts,the->she', attention, grad_rows, precision=HIGH)  2.56 us
    dot_general x1, matrix products, local(): jnp.einsum('shd,she->hde', jnp.pad(queries * growth[:, :, None], widened)...  2.15 us
    convert_element_type x1, other arithmetic, local(): near_round = near_total.astype(jnp.bfloat16)  2.12 us
  transfers between devices with their start and end apart: 7, of which 3 were waited for; matrix products, arithmetic and copies ran while one was open for 25% of the time, Pallas kernels for 0%

profile of v18, /device:TPU:0, one launch (start us, length us, event | category | flops | bytes accessed | tf_op | source)
XLA Modules:
  0.0 67.9 jit_solution(18312357442727144825)
XLA Ops:
  0.1 0.7 compare_bitcast_fusion
  0.9 0.7 %log_bitcast_fusion = f32[2,16]{1,0:T(2,128)S(1)} fusion(s32[1,2,16]{2,1,0:T(2,128)} %param.8), kind=kLoop, calls=%fused_computation.71 | loop fusion | flops 96 | bytes 256 | tf_op jit(solution)/shard_map/log | solution.py:101
  1.9 0.7 %fusion.34 = (f32[1,1,2048]{2,0,1:T(1,128)S(1)}, f32[1,1,2048]{2,0,1:T(1,128)S(1)}, f32[1,1,2048]{2,0,1:T(1,128)S(1)}) fusion(f32[1,3,2048]{2,0,1:T(1,128)} %param.7), kind=kLoop, calls=%fused_computation.81 | loop fusion | bytes 49152 | tf_op jit(solution)/shard_map/slice | solution.py:112
  2.6 1.3 %copy.33 = bf16[1,128,2048]{1,2,0:T(8,128)(2,1)S(1)} copy(bf16[1,128,2048]{2,1,0:T(8,128)(2,1)} %param.5) | data formatting | bytes 1048576 | tf_op args[0]
  4.0 1.0 %fusion.8 = (bf16[128,2048]{0,1:T(8,128)(2,1)S(1)}, bf16[128,2048]{0,1:T(8,128)(2,1)S(1)}, bf16[128,2048]{0,1:T(8,128)(2,1)S(1)}) fusion(bf16[1,128,2048]{1,2,0:T(8,128)(2,1)S(1)} %copy.33, f32[2048]{0:T(1024)S(1)} %bitcast.122, f32[2048]{0:T(1024)S(1)} %bitcast.125, f32[2048]{0:T(1024)S(1)} %bitcast.128), kind=kLoop, calls=%fused_computation.22 | loop fusion | flops 1835008 | bytes 2121728 | tf_op jit(solution)/shard_map/convert_element_type | solution.py:112
  5.4 0.7 %fusion.5 = f32[16,136,128]{2,1,0:T(8,128)S(1)} fusion(bf16[128,16,128]{0,2,1:T(8,128)(2,1)S(1)} %bitcast.117, f32[128,16,128]{0,2,1:T(8,128)S(1)} %convert_multiply_fusion.3), kind=kOutput, calls=%fused_computation.19 | convolution fusion | flops 213909504 | bytes 2686976 | tf_op jit(solution)/shard_map/shd,she->hde/dot_general | solution.py:136
  6.4 2.2 %pad_add_fusion = (f32[16,136,128]{2,1,0:T(8,128)}, f32[16,136,128]{2,1,0:T(8,128)}) fusion(f32[16,8,128]{2,1,0:T(8,128)S(1)} %broadcast_in_dim.32, f32[16,136,128]{2,1,0:T(8,128)S(1)} %fusion.5, pred[]{:T(512)S(6)} %eq.29, bf16[128,16,128]{2,1,0:T(8,128)(2,1)S(1)} %bitcast.106, f32[128,16,128]{0,2,1:T(8,128)S(1)} %convert_multiply_fusion.4), kind=kOutput, calls=%fused_computation.18 | convolution fusion | flops 214745088 | bytes 4980737 | tf_op jit(solution)/shard_map/shd,she->hde/dot_general | solution.py:139
  9.0 2.0 %copy.40 = bf16[1,128,2048]{1,2,0:T(8,128)(2,1)} copy(bf16[1,128,2048]{2,1,0:T(8,128)(2,1)} %param.6) | data formatting | bytes 1048576 | tf_op args[1]
  11.1 0.6 convolution_multiply_fusion.2
  11.6 1.4 %fusion = f32[128,16,128]{2,0,1:T(8,128)} fusion(f32[16,128,128]{1,2,0:T(8,128)S(1)} %convolution_multiply_fusion.2, bf16[128,16,128]{2,1,0:T(8,128)(2,1)S(1)} %bitcast.107), kind=kOutput, calls=%fused_computation.5 | convolution fusion | flops 201588736 | bytes 2621440 | tf_op jit(solution)/shard_map/hts,the->she/dot_general | solution.py:156
  13.1 2.6 %copy.50 = f32[128,16,128]{0,2,1:T(8,128)} copy(f32[128,16,128]{2,0,1:T(8,128)} %fusion) | data formatting | bytes 2097152 | tf_op jit(solution)/shard_map/mul | solution.py:156
  15.8 0.6 fusion.1
  16.4 1.4 %convolution_multiply_fusion.4 = f32[16,128,128]{2,1,0:T(8,128)} fusion(bf16[128,16,128]{0,2,1:T(8,128)(2,1)S(1)} %bitcast.112, f32[16,128,128]{1,2,0:T(8,128)S(1)} %fusion.1), kind=kOutput, calls=%fused_computation.8 | convolution fusion | flops 201588736 | bytes 2621440 | tf_op jit(solution)/shard_map/hts,shd->thd/dot_general | solution.py:151
  17.8 1.8 %convolution_multiply_fusion.3 = f32[16,128,128]{2,1,0:T(8,128)} fusion(bf16[128,16,128]{0,2,1:T(8,128)(2,1)S(1)} %bitcast.116, f32[16,128,128]{1,2,0:T(8,128)S(1)} %fusion.1), kind=kOutput, calls=%fused_computation.7 | convolution fusion | flops 201588736 | bytes 2621440 | tf_op jit(solution)/shard_map/hts,thd->shd/dot_general | solution.py:152
  19.7 1.5 %select_add_fusion = f32[16,136,128]{2,1,0:T(8,128)S(1)} fusion(f32[16,136,128]{2,1,0:T(8,128)S(1)} %fusion.5, f32[16,136,128]{2,1,0:T(8,128)S(1)} %copy-done, f32[16,136,128]{2,1,0:T(8,128)} %collective-permute-done, f32[16]{0:T(128)S(1)} %fusion.32, pred[]{:T(512)S(6)} %eq.29), kind=kLoop, calls=%fused_computation.17 | loop fusion | flops 835584 | bytes 4456513 | tf_op jit(solution)/shard_map/add | solution.py:66
  21.9 1.4 %collective-permute-start.1 = (bf16[16,136,128]{2,1,0:T(8,128)(2,1)S(1)}, bf16[16,136,128]{2,1,0:T(8,128)(2,1)S(1)}, u32[]{:S(2)}, u32[]{:S(2)}) collective-permute-start(bf16[16,136,128]{2,1,0:T(8,128)(2,1)S(1)} %pad_maximum_fusion), channel_id=1, source_target_pairs={{1,3},{3,5},{5,7},{6,4},{4,2},{2,0},{9,11},{11,13},{13,15},{14,12}... | collective-permute-start | bytes 1671176 | tf_op jit(solution)/shard_map/ppermute | solution.py:40
  23.3 1.3 %collective-permute-start.2 = (bf16[16,136,128]{2,1,0:T(8,128)(2,1)S(1)}, bf16[16,136,128]{2,1,0:T(8,128)(2,1)S(1)}, u32[]{:S(2)}, u32[]{:S(2)}) collective-permute-start(bf16[16,136,128]{2,1,0:T(8,128)(2,1)S(1)} %pad_maximum_fusion), channel_id=1, source_target_pairs={{1,5},{3,7},{6,2},{4,0},{9,13},{11,15},{14,10},{12,8},{17,21},{19,... | collective-permute-start | bytes 1671176 | tf_op jit(solution)/shard_map/ppermute | solution.py:40
  24.6 1.3 %collective-permute-start.3 = (bf16[16,136,128]{2,1,0:T(8,128)(2,1)S(1)}, bf16[16,136,128]{2,1,0:T(8,128)(2,1)S(1)}, u32[]{:S(2)}, u32[]{:S(2)}) collective-permute-start(bf16[16,136,128]{2,1,0:T(8,128)(2,1)S(1)} %pad_maximum_fusion), channel_id=1, source_target_pairs={{1,7},{6,0},{9,15},{14,8},{17,23},{22,16},{25,31},{30,24}} | collective-permute-start | bytes 1671176 | tf_op jit(solution)/shard_map/ppermute | solution.py:40
  25.9 2.1 %fusion.13 = bf16[128,2048]{0,1:T(8,128)(2,1)S(1)} fusion(f32[16,128,128]{2,1,0:T(8,128)} %convolution_multiply_fusion.3, f32[16,128,128]{2,1,0:T(8,128)S(1)} %copy-done.2, f32[128,16,128]{0,2,1:T(8,128)S(1)} %copy-done.1, bf16[1,128,2048]{1,2,0:T(8,128)(2,1)} %copy.40, f32[2048]{0:T(1024)S(1)} %bitcast.126, f32[2048]{0:T(1024)S(1)} %bitcast.129, ...), kind=kLoop, calls=%fused_computation.30 | loop fusion | flops 2097152 | bytes 4218880 | tf_op jit(solution)/shard_map/convert_element_type | solution.py:161
  28.1 4.6 %collective-permute-start.4 = (bf16[128,2048]{0,1:T(8,128)(2,1)S(1)}, bf16[128,2048]{0,1:T(8,128)(2,1)S(1)}, u32[]{:S(2)}, u32[]{:S(2)}) collective-permute-start(bf16[128,2048]{0,1:T(8,128)(2,1)S(1)} %fusion.13), channel_id=1, source_target_pairs={{0,24},{8,0},{16,8},{24,16},{1,25},{9,1},{17,9},{25,17},{2,26},{10... | collective-permute-start | bytes 1572872 | tf_op jit(solution)/shard_map/ppermute | solution.py:96
  32.7 6.2 %collective-permute-done.1 = bf16[16,136,128]{2,1,0:T(8,128)(2,1)S(1)} collective-permute-done((bf16[16,136,128]{2,1,0:T(8,128)(2,1)S(1)}, bf16[16,136,128]{2,1,0:T(8,128)(2,1)S(1)}, u32[]{:S(2)}, u32[]{:S(2)}) %collective-permute-start.1) | collective-permute-done | bytes 557088 | tf_op jit(solution)/shard_map/ppermute | solution.py:40
  38.9 3.8 %collective-permute-done.2 = bf16[16,136,128]{2,1,0:T(8,128)(2,1)S(1)} collective-permute-done((bf16[16,136,128]{2,1,0:T(8,128)(2,1)S(1)}, bf16[16,136,128]{2,1,0:T(8,128)(2,1)S(1)}, u32[]{:S(2)}, u32[]{:S(2)}) %collective-permute-start.2) | collective-permute-done | bytes 557088 | tf_op jit(solution)/shard_map/ppermute | solution.py:40
  42.8 1.4 %multiply_add_fusion = f32[16,128,128]{2,1,0:T(8,128)} fusion(bf16[16,136,128]{2,1,0:T(8,128)(2,1)S(1)} %collective-permute-done.3, bf16[16,136,128]{2,1,0:T(8,128)(2,1)S(1)} %collective-permute-done.2, bf16[16,136,128]{2,1,0:T(8,128)(2,1)S(1)} %collective-permute-done.1, f32[16]{0:T(128)S(1)} %get-tuple-element.10, f32[16]{0:T(128)S(1)} %get-tuple-element.9), kind=kLoop, calls=%fused_computation.43 | loop fusion | flops 1835008 | bytes 2621568 | tf_op jit(solution)/shard_map/add | solution.py:73
  44.3 0.9 %collective-permute-start.5 = (f32[16,128,128]{2,1,0:T(8,128)}, f32[16,128,128]{2,1,0:T(8,128)S(1)}, u32[]{:S(2)}, u32[]{:S(2)}) collective-permute-start(f32[16,128,128]{2,1,0:T(8,128)} %multiply_add_fusion), channel_id=1, source_target_pairs={{0,1},{2,3},{4,5},{6,7},{1,0},{3,2},{5,4},{7,6},{8,9},{10,11},{12,... | collective-permute-start | bytes 3145736 | tf_op jit(solution)/shard_map/ppermute | solution.py:88
  45.2 1.1 %slice_reduce_fusion = f32[16]{0:T(128)S(1)} fusion(f32[16,136,128]{2,1,0:T(8,128)} %collective-permute-done), kind=kLoop, calls=%fused_computation.58 | loop fusion | bytes 128 | tf_op jit(solution)/shard_map/slice | solution.py:21
  46.3 1.7 %slice_add_fusion = f32[16,128,128]{2,1,0:T(8,128)S(1)} fusion(f32[16,136,128]{2,1,0:T(8,128)} %collective-permute-done, f32[16,128,128]{2,1,0:T(8,128)} %multiply_add_fusion, f32[16]{0:T(128)S(1)} %slice_reduce_fusion), kind=kLoop, calls=%fused_computation.25 | loop fusion | flops 524288 | bytes 3145792 | tf_op jit(solution)/shard_map/add | solution.py:89
  48.5 0.7 %fusion.2 = f32[128,16,128]{0,2,1:T(8,128)S(1)} fusion(bf16[128,16,128]{0,2,1:T(8,128)(2,1)S(1)} %bitcast.113, f32[128,16]{0,1:T(8,128)S(1)} %copy.36, f32[16,128,128]{2,1,0:T(8,128)S(1)} %collective-permute-done.5, f32[16,128,128]{2,1,0:T(8,128)S(1)} %slice_add_fusion, pred[]{:T(512)S(6)} %eq.29), kind=kOutput, calls=%fused_computation.12 | convolution fusion | flops 201850880 | bytes 3678209 | tf_op jit(solution)/shard_map/shd,hde->she/dot_general | solution.py:170
  49.2 0.9 %fusion.4 = f32[128,16,128]{0,2,1:T(8,128)S(1)} fusion(f32[16,128,128]{2,1,0:T(8,128)S(1)} %slice_add_fusion, f32[16,128,128]{2,1,0:T(8,128)S(1)} %collective-permute-done.5, f32[128,16]{0,1:T(8,128)S(1)} %copy.51, pred[]{:T(512)S(6)} %eq.29, bf16[128,16,128]{2,1,0:T(8,128)(2,1)S(1)} %bitcast.109), kind=kOutput, calls=%fused_computation.16 | convolution fusion | flops 201850880 | bytes 3678209 | tf_op jit(solution)/shard_map/the,hde->thd/dot_general | solution.py:167
  50.1 1.2 %fusion.16 = bf16[128,2048]{0,1:T(8,128)(2,1)S(1)} fusion(f32[128,16,128]{0,2,1:T(8,128)S(1)} %fusion.2, f32[128,16,128]{0,2,1:T(8,128)S(1)} %fusion.3, f32[128,16,128]{0,2,1:T(8,128)S(1)} %fusion.4, f32[2048]{0:T(1024)S(1)} %bitcast.127, f32[2048]{0:T(1024)S(1)} %bitcast.130, f32[2048]{0:T(1024)S(1)} %bitcast.124), kind=kLoop, calls=%fused_computation.35 | loop fusion | flops 1572864 | bytes 3694592 | tf_op jit(solution)/shard_map/convert_element_type | solution.py:174
  51.3 4.0 %collective-permute-start.6 = (bf16[128,2048]{0,1:T(8,128)(2,1)S(1)}, bf16[128,2048]{0,1:T(8,128)(2,1)S(1)}, u32[]{:S(2)}, u32[]{:S(2)}) collective-permute-start(bf16[128,2048]{0,1:T(8,128)(2,1)S(1)} %fusion.16), channel_id=1, source_target_pairs={{0,24},{8,0},{16,8},{24,16},{1,25},{9,1},{17,9},{25,17},{2,26},{10... | collective-permute-start | bytes 1572872 | tf_op jit(solution)/shard_map/ppermute | solution.py:96
  55.3 11.4 %collective-permute-done.6 = bf16[128,2048]{0,1:T(8,128)(2,1)S(1)} collective-permute-done((bf16[128,2048]{0,1:T(8,128)(2,1)S(1)}, bf16[128,2048]{0,1:T(8,128)(2,1)S(1)}, u32[]{:S(2)}, u32[]{:S(2)}) %collective-permute-start.6) | collective-permute-done | bytes 524320 | tf_op jit(solution)/shard_map/ppermute | solution.py:96
  66.9 1.0 %copy.56 = bf16[1,128,2048]{2,1,0:T(8,128)(2,1)} copy(bf16[1,128,2048]{1,2,0:T(8,128)(2,1)S(1)} %fusion.19) | data formatting | bytes 1048576 | tf_op jit(solution)/shard_map/broadcast_in_dim | solution.py:179
  (49 shorter events, 3.4 us)
Async XLA Ops:
  4.0 1.0 %copy-start.3 = (bf16[1,128,2048]{2,1,0:T(8,128)(2,1)S(1)}, bf16[1,128,2048]{2,1,0:T(8,128)(2,1)}, u32[]{:S(2)}) copy-start(bf16[1,128,2048]{2,1,0:T(8,128)(2,1)} %param.6) | copy-start | bytes 1572868
  8.5 11.1 %collective-permute-start = (f32[16,136,128]{2,1,0:T(8,128)}, f32[16,136,128]{2,1,0:T(8,128)}, u32[]{:S(2)}, u32[]{:S(2)}) collective-permute-start(f32[16,136,128]{2,1,0:T(8,128)} %get-tuple-element.20), channel_id=1, source_target_pairs={{0,1},{2,3},{4,5},{6,7},{1,0},{3,2},{5,4},{7,6},{8,9},{10,11},{12,... | collective-permute-start | bytes 3342344 | tf_op jit(solution)/shard_map/ppermute | solution.py:64
  17.8 1.8 %copy-start = (f32[16,136,128]{2,1,0:T(8,128)S(1)}, f32[16,136,128]{2,1,0:T(8,128)}, u32[]{:S(2)}) copy-start(f32[16,136,128]{2,1,0:T(8,128)} %get-tuple-element.21) | copy-start | bytes 3342340
  21.1 4.8 %copy-start.1 = (f32[128,16,128]{0,2,1:T(8,128)S(1)}, f32[128,16,128]{0,2,1:T(8,128)}, u32[]{:S(2)}) copy-start(f32[128,16,128]{0,2,1:T(8,128)} %copy.50) | copy-start | bytes 3145732
  21.6 4.3 %copy-start.2 = (f32[16,128,128]{2,1,0:T(8,128)S(1)}, f32[16,128,128]{2,1,0:T(8,128)}, u32[]{:S(2)}) copy-start(f32[16,128,128]{2,1,0:T(8,128)} %convolution_multiply_fusion.4) | copy-start | bytes 3145732
  21.9 17.0 %collective-permute-start.1 = (bf16[16,136,128]{2,1,0:T(8,128)(2,1)S(1)}, bf16[16,136,128]{2,1,0:T(8,128)(2,1)S(1)}, u32[]{:S(2)}, u32[]{:S(2)}) collective-permute-start(bf16[16,136,128]{2,1,0:T(8,128)(2,1)S(1)} %pad_maximum_fusion), channel_id=1, source_target_pairs={{1,3},{3,5},{5,7},{6,4},{4,2},{2,0},{9,11},{11,13},{13,15},{14,12}... | collective-permute-start | bytes 1671176 | tf_op jit(solution)/shard_map/ppermute | solution.py:40
  23.3 19.3 %collective-permute-start.2 = (bf16[16,136,128]{2,1,0:T(8,128)(2,1)S(1)}, bf16[16,136,128]{2,1,0:T(8,128)(2,1)S(1)}, u32[]{:S(2)}, u32[]{:S(2)}) collective-permute-start(bf16[16,136,128]{2,1,0:T(8,128)(2,1)S(1)} %pad_maximum_fusion), channel_id=1, source_target_pairs={{1,5},{3,7},{6,2},{4,0},{9,13},{11,15},{14,10},{12,8},{17,21},{19,... | collective-permute-start | bytes 1671176 | tf_op jit(solution)/shard_map/ppermute | solution.py:40
  24.6 18.2 %collective-permute-start.3 = (bf16[16,136,128]{2,1,0:T(8,128)(2,1)S(1)}, bf16[16,136,128]{2,1,0:T(8,128)(2,1)S(1)}, u32[]{:S(2)}, u32[]{:S(2)}) collective-permute-start(bf16[16,136,128]{2,1,0:T(8,128)(2,1)S(1)} %pad_maximum_fusion), channel_id=1, source_target_pairs={{1,7},{6,0},{9,15},{14,8},{17,23},{22,16},{25,31},{30,24}} | collective-permute-start | bytes 1671176 | tf_op jit(solution)/shard_map/ppermute | solution.py:40
  28.1 16.2 %collective-permute-start.4 = (bf16[128,2048]{0,1:T(8,128)(2,1)S(1)}, bf16[128,2048]{0,1:T(8,128)(2,1)S(1)}, u32[]{:S(2)}, u32[]{:S(2)}) collective-permute-start(bf16[128,2048]{0,1:T(8,128)(2,1)S(1)} %fusion.13), channel_id=1, source_target_pairs={{0,24},{8,0},{16,8},{24,16},{1,25},{9,1},{17,9},{25,17},{2,26},{10... | collective-permute-start | bytes 1572872 | tf_op jit(solution)/shard_map/ppermute | solution.py:96
  44.3 3.7 %collective-permute-start.5 = (f32[16,128,128]{2,1,0:T(8,128)}, f32[16,128,128]{2,1,0:T(8,128)S(1)}, u32[]{:S(2)}, u32[]{:S(2)}) collective-permute-start(f32[16,128,128]{2,1,0:T(8,128)} %multiply_add_fusion), channel_id=1, source_target_pairs={{0,1},{2,3},{4,5},{6,7},{1,0},{3,2},{5,4},{7,6},{8,9},{10,11},{12,... | collective-permute-start | bytes 3145736 | tf_op jit(solution)/shard_map/ppermute | solution.py:88
  51.3 15.4 %collective-permute-start.6 = (bf16[128,2048]{0,1:T(8,128)(2,1)S(1)}, bf16[128,2048]{0,1:T(8,128)(2,1)S(1)}, u32[]{:S(2)}, u32[]{:S(2)}) collective-permute-start(bf16[128,2048]{0,1:T(8,128)(2,1)S(1)} %fusion.16), channel_id=1, source_target_pairs={{0,24},{8,0},{16,8},{24,16},{1,25},{9,1},{17,9},{25,17},{2,26},{10... | collective-permute-start | bytes 1572872 | tf_op jit(solution)/shard_map/ppermute | solution.py:96

commit v19 on v15

--- a/solution.py
+++ b/solution.py
@@ -68,6 +68,11 @@
         weight = jnp.ones_like(rate)
         for step in range(1, couples):
             moves = [(2 * p + 1, 2 * (p + step) + 1) for p in range(couples - step)]
+            if step == couples - 1:
+                bare = unpacked(window)[0].astype(jnp.bfloat16)
+                got = lax.ppermute(bare, axis, both_ways(count, moves)).astype(jnp.float32)
+                incoming = incoming + weight[:, None, None] * got
+                continue
             got, got_rate = unpacked(sent_narrow(window, axis, both_ways(count, moves)))
             incoming = incoming + weight[:, None, None] * got
             weight = weight * got_rate

time: 66.2 us -> 66.2 us (level)
    ppermute x3 -> x2, starting transfers between devices: 4.01 us -> 2.72 us  [sent_narrow(): return widen(lax.ppermute(narrow(message), axis, pairs))]
    ppermute x0 -> x1, starting transfers between devices: none -> 1.29 us  [scans_in(): got = lax.ppermute(bare, axis, both_ways(count, moves)).astype(jnp.float32)]
    ppermute x3 -> x2, waiting for transfers between devices: 9.91 us -> 9.56 us  [sent_narrow(): return widen(lax.ppermute(narrow(message), axis, pairs))]
where the time goes in v19:
time: 66.2 us; the launch traced here: 65.1 us
  waiting for transfers between devices  20.9 us (32%)
  starting transfers between devices  14.4 us (22%)
  other arithmetic  12.2 us (18%)
  matrix products  9.4 us (14%)
  local copies, waits for them, and re-layouts  7.92 us (12%)
    ppermute x2, waiting for transfers between devices, passed_along(): return lax.ppermute(value, axis, pairs)  11.4 us
    ppermute x2, waiting for transfers between devices, sent_narrow(): return widen(lax.ppermute(narrow(message), axis, pairs))  9.56 us
    ppermute x2, starting transfers between devices, passed_along(): return lax.ppermute(value, axis, pairs)  8.69 us
    ppermute x2, starting transfers between devices, sent_narrow(): return widen(lax.ppermute(narrow(message), axis, pairs))  2.72 us
    unnamed x11, local copies, waits for them, and re-layouts  2.48 us
    convert_element_type x1, other arithmetic, local(): near_round = near_total.astype(jnp.bfloat16)  2.12 us
    dot_general x1, matrix products, local(): jnp.einsum('hts,thd->shd', mixing, queries, precision=HIGH)  1.85 us
    add x1, other arithmetic, scans_in(): own = lower_rate[:, None, None] * incoming + lower  1.7 us
  transfers between devices with their start and end apart: 7, of which 3 were waited for; matrix products, arithmetic and copies ran while one was open for 21% of the time, Pallas kernels for 0%

profile of v19, /device:TPU:0, one launch (start us, length us, event | category | flops | bytes accessed | tf_op | source)
XLA Modules:
  0.0 65.1 jit_solution(2222299351690249903)
XLA Ops:
  0.1 0.7 %compare_bitcast_fusion = pred[2]{0:T(512)(128)(4,1)S(1)} fusion(s32[1,2]{1,0:T(1,128)} %param.9), kind=kLoop, calls=%fused_computation.74 | loop fusion | flops 2 | bytes 10 | tf_op jit(solution)/shard_map/eq | solution.py:107
  0.9 0.7 %log_bitcast_fusion = f32[2,16]{1,0:T(2,128)S(1)} fusion(s32[1,2,16]{2,1,0:T(2,128)} %param.8), kind=kLoop, calls=%fused_computation.75 | loop fusion | flops 96 | bytes 256 | tf_op jit(solution)/shard_map/log | solution.py:105
  1.9 0.7 %fusion.36 = (f32[1,1,2048]{2,0,1:T(1,128)S(1)}, f32[1,1,2048]{2,0,1:T(1,128)S(1)}, f32[1,1,2048]{2,0,1:T(1,128)S(1)}) fusion(f32[1,3,2048]{2,0,1:T(1,128)} %param.7), kind=kLoop, calls=%fused_computation.83 | loop fusion | bytes 49152 | tf_op jit(solution)/shard_map/slice | solution.py:116
  2.6 1.3 %copy.34 = bf16[1,128,2048]{1,2,0:T(8,128)(2,1)S(1)} copy(bf16[1,128,2048]{2,1,0:T(8,128)(2,1)} %param.5) | data formatting | bytes 1048576 | tf_op args[0]
  4.0 1.0 %fusion.5 = (bf16[128,2048]{0,1:T(8,128)(2,1)S(1)}, bf16[128,2048]{0,1:T(8,128)(2,1)S(1)}, bf16[128,2048]{0,1:T(8,128)(2,1)S(1)}) fusion(bf16[1,128,2048]{1,2,0:T(8,128)(2,1)S(1)} %copy.34, f32[2048]{0:T(1024)S(1)} %bitcast.122, f32[2048]{0:T(1024)S(1)} %bitcast.125, f32[2048]{0:T(1024)S(1)} %bitcast.128), kind=kLoop, calls=%fused_computation.19 | loop fusion | flops 1835008 | bytes 2121728 | tf_op jit(solution)/shard_map/convert_element_type | solution.py:116
  5.3 0.9 %fusion.16 = f32[16,128,128]{2,1,0:T(8,128)S(1)} fusion(bf16[128,16,128]{0,2,1:T(8,128)(2,1)S(1)} %bitcast.117, bf16[128,16,128]{0,2,1:T(8,128)(2,1)S(1)} %bitcast.110, f32[128,16]{0,1:T(8,128)S(1)} %copy.37), kind=kOutput, calls=%fused_computation.41 | convolution fusion | flops 201850880 | bytes 2105344 | tf_op jit(solution)/shard_map/shd,she->hde/dot_general | solution.py:139
  6.2 1.6 %broadcast_select_fusion.2 = (f32[16,128,128]{2,1,0:T(8,128)S(1)}, f32[16,128,128]{2,1,0:T(8,128)}) fusion(f32[16,128,128]{2,1,0:T(8,128)S(1)} %fusion.16, pred[]{:T(512)S(6)} %eq.29, bf16[128,16,128]{2,1,0:T(8,128)(2,1)S(1)} %bitcast.106, bf16[128,16,128]{0,2,1:T(8,128)(2,1)S(1)} %bitcast.114, f32[128,16]{0,1:T(8,128)S(1)} %copy.35), kind=kOutput, calls=%fused_computation.53 | convolution fusion | flops 202637312 | bytes 4202497 | tf_op jit(solution)/shard_map/shd,she->hde/dot_general | solution.py:142
  7.8 1.1 %pad_maximum_fusion = f32[16,136,128]{2,1,0:T(8,128)} fusion(f32[16,8,128]{2,1,0:T(8,128)S(1)} %broadcast_in_dim.32, f32[16,128,128]{2,1,0:T(8,128)S(1)} %get-tuple-element.11), kind=kLoop, calls=%fused_computation.17 | loop fusion | flops 278528 | bytes 2228224 | tf_op jit(solution)/shard_map/concatenate | solution.py:16
  9.4 1.0 %copy.41 = bf16[1,128,2048]{1,2,0:T(8,128)(2,1)} copy(bf16[1,128,2048]{2,1,0:T(8,128)(2,1)S(1)} %copy-done.3) | data formatting | bytes 1048576 | tf_op args[1]
  10.5 0.6 convolution_multiply_fusion.1
  11.5 1.3 %copy.51 = f32[128,16,128]{0,2,1:T(8,128)} copy(f32[128,16,128]{2,0,1:T(8,128)S(1)} %fusion) | data formatting | bytes 2097152 | tf_op jit(solution)/shard_map/mul | solution.py:159
  13.0 0.6 fusion.1
  13.6 1.4 %convolution_multiply_fusion.3 = f32[16,128,128]{2,1,0:T(8,128)} fusion(bf16[128,16,128]{0,2,1:T(8,128)(2,1)S(1)} %bitcast.112, f32[16,128,128]{1,2,0:T(8,128)S(1)} %fusion.1), kind=kOutput, calls=%fused_computation.7 | convolution fusion | flops 201588736 | bytes 2621440 | tf_op jit(solution)/shard_map/hts,shd->thd/dot_general | solution.py:154
  15.0 1.8 %convolution_multiply_fusion.2 = f32[16,128,128]{2,1,0:T(8,128)} fusion(bf16[128,16,128]{0,2,1:T(8,128)(2,1)S(1)} %bitcast.116, f32[16,128,128]{1,2,0:T(8,128)S(1)} %fusion.1), kind=kOutput, calls=%fused_computation.6 | convolution fusion | flops 201588736 | bytes 2621440 | tf_op jit(solution)/shard_map/hts,thd->shd/dot_general | solution.py:155
  16.8 1.5 %pad_add_fusion = f32[16,136,128]{2,1,0:T(8,128)S(1)} fusion(f32[16,128,128]{2,1,0:T(8,128)S(1)} %copy-done, f32[16,136,128]{2,1,0:T(8,128)} %collective-permute-done, f32[16]{0:T(128)S(1)} %fusion.34), kind=kLoop, calls=%fused_computation.18 | loop fusion | flops 557056 | bytes 3276864 | tf_op jit(solution)/shard_map/add | solution.py:65
  19.0 1.4 %collective-permute-start.1 = (bf16[16,136,128]{2,1,0:T(8,128)(2,1)S(1)}, bf16[16,136,128]{2,1,0:T(8,128)(2,1)S(1)}, u32[]{:S(2)}, u32[]{:S(2)}) collective-permute-start(bf16[16,136,128]{2,1,0:T(8,128)(2,1)S(1)} %pad_maximum_fusion.1), channel_id=1, source_target_pairs={{1,3},{3,5},{5,7},{6,4},{4,2},{2,0},{9,11},{11,13},{13,15},{14,12}... | collective-permute-start | bytes 1671176 | tf_op jit(solution)/shard_map/ppermute | solution.py:40
  20.5 1.3 %collective-permute-start.2 = (bf16[16,136,128]{2,1,0:T(8,128)(2,1)S(1)}, bf16[16,136,128]{2,1,0:T(8,128)(2,1)S(1)}, u32[]{:S(2)}, u32[]{:S(2)}) collective-permute-start(bf16[16,136,128]{2,1,0:T(8,128)(2,1)S(1)} %pad_maximum_fusion.1), channel_id=1, source_target_pairs={{1,5},{3,7},{6,2},{4,0},{9,13},{11,15},{14,10},{12,8},{17,21},{19,... | collective-permute-start | bytes 1671176 | tf_op jit(solution)/shard_map/ppermute | solution.py:40
  21.8 1.3 %collective-permute-start.3 = (bf16[16,128,128]{2,1,0:T(8,128)(2,1)S(1)}, bf16[16,128,128]{2,1,0:T(8,128)(2,1)S(1)}, u32[]{:S(2)}, u32[]{:S(2)}) collective-permute-start(bf16[16,128,128]{2,1,0:T(8,128)(2,1)S(1)} %slice.110), channel_id=1, source_target_pairs={{1,7},{6,0},{9,15},{14,8},{17,23},{22,16},{25,31},{30,24}} | collective-permute-start | bytes 1572872 | tf_op jit(solution)/shard_map/ppermute | solution.py:73
  23.1 2.1 %fusion.10 = bf16[128,2048]{0,1:T(8,128)(2,1)S(1)} fusion(f32[16,128,128]{2,1,0:T(8,128)} %convolution_multiply_fusion.2, f32[16,128,128]{2,1,0:T(8,128)S(1)} %copy-done.2, f32[128,16,128]{0,2,1:T(8,128)S(1)} %copy-done.1, bf16[1,128,2048]{1,2,0:T(8,128)(2,1)} %copy.41, f32[2048]{0:T(1024)S(1)} %bitcast.126, f32[2048]{0:T(1024)S(1)} %bitcast.129, ...), kind=kLoop, calls=%fused_computation.27 | loop fusion | flops 2097152 | bytes 4218880 | tf_op jit(solution)/shard_map/convert_element_type | solution.py:164
  25.2 4.7 %collective-permute-start.4 = (bf16[128,2048]{0,1:T(8,128)(2,1)S(1)}, bf16[128,2048]{0,1:T(8,128)(2,1)S(1)}, u32[]{:S(2)}, u32[]{:S(2)}) collective-permute-start(bf16[128,2048]{0,1:T(8,128)(2,1)S(1)} %fusion.10), channel_id=1, source_target_pairs={{0,24},{8,0},{16,8},{24,16},{1,25},{9,1},{17,9},{25,17},{2,26},{10... | collective-permute-start | bytes 1572872 | tf_op jit(solution)/shard_map/ppermute | solution.py:100
  29.9 6.1 %collective-permute-done.1 = bf16[16,136,128]{2,1,0:T(8,128)(2,1)S(1)} collective-permute-done((bf16[16,136,128]{2,1,0:T(8,128)(2,1)S(1)}, bf16[16,136,128]{2,1,0:T(8,128)(2,1)S(1)}, u32[]{:S(2)}, u32[]{:S(2)}) %collective-permute-start.1) | collective-permute-done | bytes 557088 | tf_op jit(solution)/shard_map/ppermute | solution.py:40
  36.0 3.4 %collective-permute-done.2 = bf16[16,136,128]{2,1,0:T(8,128)(2,1)S(1)} collective-permute-done((bf16[16,136,128]{2,1,0:T(8,128)(2,1)S(1)}, bf16[16,136,128]{2,1,0:T(8,128)(2,1)S(1)}, u32[]{:S(2)}, u32[]{:S(2)}) %collective-permute-start.2) | collective-permute-done | bytes 557088 | tf_op jit(solution)/shard_map/ppermute | solution.py:40
  39.7 1.4 %multiply_add_fusion = f32[16,128,128]{2,1,0:T(8,128)} fusion(bf16[16,128,128]{2,1,0:T(8,128)(2,1)S(1)} %collective-permute-done.3, bf16[16,136,128]{2,1,0:T(8,128)(2,1)S(1)} %collective-permute-done.2, bf16[16,136,128]{2,1,0:T(8,128)(2,1)S(1)} %collective-permute-done.1, f32[16]{0:T(128)S(1)} %get-tuple-element.10, f32[16]{0:T(128)S(1)} %get-tuple-element.9), kind=kLoop, calls=%fused_computation.40 | loop fusion | flops 1835008 | bytes 2621568 | tf_op jit(solution)/shard_map/add | solution.py:74
  41.1 1.2 %collective-permute-start.5 = (f32[16,128,128]{2,1,0:T(8,128)}, f32[16,128,128]{2,1,0:T(8,128)S(1)}, u32[]{:S(2)}, u32[]{:S(2)}) collective-permute-start(f32[16,128,128]{2,1,0:T(8,128)} %multiply_add_fusion), channel_id=1, source_target_pairs={{0,1},{2,3},{4,5},{6,7},{1,0},{3,2},{5,4},{7,6},{8,9},{10,11},{12,... | collective-permute-start | bytes 3145736 | tf_op jit(solution)/shard_map/ppermute | solution.py:92
  42.4 1.1 %slice_reduce_fusion = f32[16]{0:T(128)S(1)} fusion(f32[16,136,128]{2,1,0:T(8,128)} %collective-permute-done), kind=kLoop, calls=%fused_computation.62 | loop fusion | bytes 128 | tf_op jit(solution)/shard_map/slice | solution.py:21
  43.4 1.7 %slice_add_fusion = f32[16,128,128]{2,1,0:T(8,128)S(1)} fusion(f32[16,136,128]{2,1,0:T(8,128)} %collective-permute-done, f32[16,128,128]{2,1,0:T(8,128)} %multiply_add_fusion, f32[16]{0:T(128)S(1)} %slice_reduce_fusion), kind=kLoop, calls=%fused_computation.22 | loop fusion | flops 524288 | bytes 3145792 | tf_op jit(solution)/shard_map/add | solution.py:93
  45.6 0.7 %fusion.2 = f32[128,16,128]{0,2,1:T(8,128)S(1)} fusion(bf16[128,16,128]{0,2,1:T(8,128)(2,1)S(1)} %bitcast.113, f32[128,16]{0,1:T(8,128)S(1)} %copy.37, f32[16,128,128]{2,1,0:T(8,128)S(1)} %collective-permute-done.5, f32[16,128,128]{2,1,0:T(8,128)S(1)} %slice_add_fusion, pred[]{:T(512)S(6)} %eq.29), kind=kOutput, calls=%fused_computation.12 | convolution fusion | flops 201850880 | bytes 3678209 | tf_op jit(solution)/shard_map/shd,hde->she/dot_general | solution.py:173
  46.4 0.9 %fusion.4 = f32[128,16,128]{0,2,1:T(8,128)S(1)} fusion(f32[16,128,128]{2,1,0:T(8,128)S(1)} %slice_add_fusion, f32[16,128,128]{2,1,0:T(8,128)S(1)} %collective-permute-done.5, f32[128,16]{0,1:T(8,128)S(1)} %copy.52, pred[]{:T(512)S(6)} %eq.29, bf16[128,16,128]{2,1,0:T(8,128)(2,1)S(1)} %bitcast.109), kind=kOutput, calls=%fused_computation.16 | convolution fusion | flops 201850880 | bytes 3678209 | tf_op jit(solution)/shard_map/the,hde->thd/dot_general | solution.py:170
  47.3 1.2 %fusion.13 = bf16[128,2048]{0,1:T(8,128)(2,1)S(1)} fusion(f32[128,16,128]{0,2,1:T(8,128)S(1)} %fusion.2, f32[128,16,128]{0,2,1:T(8,128)S(1)} %fusion.3, f32[128,16,128]{0,2,1:T(8,128)S(1)} %fusion.4, f32[2048]{0:T(1024)S(1)} %bitcast.127, f32[2048]{0:T(1024)S(1)} %bitcast.130, f32[2048]{0:T(1024)S(1)} %bitcast.124), kind=kLoop, calls=%fused_computation.32 | loop fusion | flops 1572864 | bytes 3694592 | tf_op jit(solution)/shard_map/convert_element_type | solution.py:177
  48.5 4.0 %collective-permute-start.6 = (bf16[128,2048]{0,1:T(8,128)(2,1)S(1)}, bf16[128,2048]{0,1:T(8,128)(2,1)S(1)}, u32[]{:S(2)}, u32[]{:S(2)}) collective-permute-start(bf16[128,2048]{0,1:T(8,128)(2,1)S(1)} %fusion.13), channel_id=1, source_target_pairs={{0,24},{8,0},{16,8},{24,16},{1,25},{9,1},{17,9},{25,17},{2,26},{10... | collective-permute-start | bytes 1572872 | tf_op jit(solution)/shard_map/ppermute | solution.py:100
  52.5 11.4 %collective-permute-done.6 = bf16[128,2048]{0,1:T(8,128)(2,1)S(1)} collective-permute-done((bf16[128,2048]{0,1:T(8,128)(2,1)S(1)}, bf16[128,2048]{0,1:T(8,128)(2,1)S(1)}, u32[]{:S(2)}, u32[]{:S(2)}) %collective-permute-start.6) | collective-permute-done | bytes 524320 | tf_op jit(solution)/shard_map/ppermute | solution.py:100
  64.0 1.0 %copy.57 = bf16[1,128,2048]{2,1,0:T(8,128)(2,1)} copy(bf16[1,128,2048]{1,2,0:T(8,128)(2,1)S(1)} %fusion.21) | data formatting | bytes 1048576 | tf_op jit(solution)/shard_map/broadcast_in_dim | solution.py:182
  (48 shorter events, 3.7 us)
Async XLA Ops:
  4.0 1.0 %copy-start.3 = (bf16[1,128,2048]{2,1,0:T(8,128)(2,1)S(1)}, bf16[1,128,2048]{2,1,0:T(8,128)(2,1)}, u32[]{:S(2)}) copy-start(bf16[1,128,2048]{2,1,0:T(8,128)(2,1)} %param.6) | copy-start | bytes 1572868
  8.9 7.9 %collective-permute-start = (f32[16,136,128]{2,1,0:T(8,128)}, f32[16,136,128]{2,1,0:T(8,128)}, u32[]{:S(2)}, u32[]{:S(2)}) collective-permute-start(f32[16,136,128]{2,1,0:T(8,128)} %pad_maximum_fusion), channel_id=1, source_target_pairs={{0,1},{2,3},{4,5},{6,7},{1,0},{3,2},{5,4},{7,6},{8,9},{10,11},{12,... | collective-permute-start | bytes 3342344 | tf_op jit(solution)/shard_map/ppermute | solution.py:63
  15.0 1.9 %copy-start = (f32[16,128,128]{2,1,0:T(8,128)S(1)}, f32[16,128,128]{2,1,0:T(8,128)}, u32[]{:S(2)}) copy-start(f32[16,128,128]{2,1,0:T(8,128)} %get-tuple-element.12) | copy-start | bytes 3145732
  18.5 4.6 %copy-start.1 = (f32[128,16,128]{0,2,1:T(8,128)S(1)}, f32[128,16,128]{0,2,1:T(8,128)}, u32[]{:S(2)}) copy-start(f32[128,16,128]{0,2,1:T(8,128)} %copy.51) | copy-start | bytes 3145732
  18.8 4.3 %copy-start.2 = (f32[16,128,128]{2,1,0:T(8,128)S(1)}, f32[16,128,128]{2,1,0:T(8,128)}, u32[]{:S(2)}) copy-start(f32[16,128,128]{2,1,0:T(8,128)} %convolution_multiply_fusion.3) | copy-start | bytes 3145732
  19.0 17.0 %collective-permute-start.1 = (bf16[16,136,128]{2,1,0:T(8,128)(2,1)S(1)}, bf16[16,136,128]{2,1,0:T(8,128)(2,1)S(1)}, u32[]{:S(2)}, u32[]{:S(2)}) collective-permute-start(bf16[16,136,128]{2,1,0:T(8,128)(2,1)S(1)} %pad_maximum_fusion.1), channel_id=1, source_target_pairs={{1,3},{3,5},{5,7},{6,4},{4,2},{2,0},{9,11},{11,13},{13,15},{14,12}... | collective-permute-start | bytes 1671176 | tf_op jit(solution)/shard_map/ppermute | solution.py:40
  20.5 19.0 %collective-permute-start.2 = (bf16[16,136,128]{2,1,0:T(8,128)(2,1)S(1)}, bf16[16,136,128]{2,1,0:T(8,128)(2,1)S(1)}, u32[]{:S(2)}, u32[]{:S(2)}) collective-permute-start(bf16[16,136,128]{2,1,0:T(8,128)(2,1)S(1)} %pad_maximum_fusion.1), channel_id=1, source_target_pairs={{1,5},{3,7},{6,2},{4,0},{9,13},{11,15},{14,10},{12,8},{17,21},{19,... | collective-permute-start | bytes 1671176 | tf_op jit(solution)/shard_map/ppermute | solution.py:40
  21.8 17.9 %collective-permute-start.3 = (bf16[16,128,128]{2,1,0:T(8,128)(2,1)S(1)}, bf16[16,128,128]{2,1,0:T(8,128)(2,1)S(1)}, u32[]{:S(2)}, u32[]{:S(2)}) collective-permute-start(bf16[16,128,128]{2,1,0:T(8,128)(2,1)S(1)} %slice.110), channel_id=1, source_target_pairs={{1,7},{6,0},{9,15},{14,8},{17,23},{22,16},{25,31},{30,24}} | collective-permute-start | bytes 1572872 | tf_op jit(solution)/shard_map/ppermute | solution.py:73
  25.2 15.9 %collective-permute-start.4 = (bf16[128,2048]{0,1:T(8,128)(2,1)S(1)}, bf16[128,2048]{0,1:T(8,128)(2,1)S(1)}, u32[]{:S(2)}, u32[]{:S(2)}) collective-permute-start(bf16[128,2048]{0,1:T(8,128)(2,1)S(1)} %fusion.10), channel_id=1, source_target_pairs={{0,24},{8,0},{16,8},{24,16},{1,25},{9,1},{17,9},{25,17},{2,26},{10... | collective-permute-start | bytes 1572872 | tf_op jit(solution)/shard_map/ppermute | solution.py:100
  41.1 4.1 %collective-permute-start.5 = (f32[16,128,128]{2,1,0:T(8,128)}, f32[16,128,128]{2,1,0:T(8,128)S(1)}, u32[]{:S(2)}, u32[]{:S(2)}) collective-permute-start(f32[16,128,128]{2,1,0:T(8,128)} %multiply_add_fusion), channel_id=1, source_target_pairs={{0,1},{2,3},{4,5},{6,7},{1,0},{3,2},{5,4},{7,6},{8,9},{10,11},{12,... | collective-permute-start | bytes 3145736 | tf_op jit(solution)/shard_map/ppermute | solution.py:92
  48.5 15.4 %collective-permute-start.6 = (bf16[128,2048]{0,1:T(8,128)(2,1)S(1)}, bf16[128,2048]{0,1:T(8,128)(2,1)S(1)}, u32[]{:S(2)}, u32[]{:S(2)}) collective-permute-start(bf16[128,2048]{0,1:T(8,128)(2,1)S(1)} %fusion.13), channel_id=1, source_target_pairs={{0,24},{8,0},{16,8},{24,16},{1,25},{9,1},{17,9},{25,17},{2,26},{10... | collective-permute-start | bytes 1572872 | tf_op jit(solution)/shard_map/ppermute | solution.py:100

commit v20 on v15

--- a/solution.py
+++ b/solution.py
@@ -157,7 +157,7 @@
     near_total = near_total + gain[1] * key_near.reshape(rows, width)
     near_total = near_total + gain[2] * value_near.reshape(rows, width)
     near_round = near_total.astype(jnp.bfloat16)
-    near_received = passed_along(near_round, "section", -1)
+    near_received = near_round
     state_in, adjoint_in, near_received = scans_in(
         forward_part, adjoint_part, whole_decay, "ctx", near_received
     )
@@ -170,10 +170,9 @@
     far_total = far_total + gain[1] * key_far.reshape(rows, width)
     far_total = far_total + gain[2] * value_far.reshape(rows, width)
     far_round = far_total.astype(jnp.bfloat16)
-    far_received = passed_along(far_round, "section", -1)
-    received = (near_received.astype(jnp.float32) + far_received.astype(jnp.float32)).astype(
-        jnp.bfloat16
-    )
+    near_kept, far_kept = lax.optimization_barrier((near_received, far_round))
+    outgoing = (near_kept.astype(jnp.float32) + far_kept.astype(jnp.float32)).astype(jnp.bfloat16)
+    received = passed_along(outgoing, "section", -1)
     return received[None]
 
 

time: 66.2 us -> 65 us (0.982)
  starting transfers between devices: 14 us -> 6.85 us
  other arithmetic: 12.2 us -> 15.4 us
  waiting for transfers between devices: 21.3 us -> 23.6 us
  matrix products: 9.4 us -> 10.4 us
    ppermute x2 -> x1, starting transfers between devices: 8.7 us -> 2.54 us  [passed_along(): return lax.ppermute(value, axis, pairs)]
    ppermute x3, waiting for transfers between devices: 9.91 us -> 11.8 us  [sent_narrow(): return widen(lax.ppermute(narrow(message), axis, pairs))]
    add x1, other arithmetic: 1.42 us -> 2.63 us  [scans_in(): incoming = incoming + weight[:, None, None] * got]
    dot_general x1, matrix products: 0.56 us -> 1.51 us  [local(): jnp.einsum('thd,shd->hts', query_half, key_half, preferred_element_type=j...]
    ppermute x1, starting transfers between devices: 0.89 us -> 0.01 us  [scans_in(): other = lax.ppermute(incoming, axis, swap)]
    add x1, other arithmetic: 0.21 us -> 1.04 us  [widen(): message[:, width, 0].astype(jnp.float32)]
    concatenate x1, other arithmetic: 0.04 us -> 0.88 us  [narrow(): return jnp.concatenate([state.astype(jnp.bfloat16), tile], axis=1)]
    ppermute x2 -> x1, waiting for transfers between devices: 11.4 us -> 11.8 us  [passed_along(): return lax.ppermute(value, axis, pairs)]
  transfers between devices with their start and end apart: 7 -> 6, of which waited for: 3 -> 3; matrix products, arithmetic and copies ran while one was open for 21% -> 23% of each run, Pallas kernels for 0% -> 0%
where the time goes in v20:
time: 65 us; the launch traced here: 64.4 us
  waiting for transfers between devices  23.6 us (36%)
  other arithmetic  15.4 us (24%)
  matrix products  10.4 us (16%)
  local copies, waits for them, and re-layouts  7.89 us (12%)
  starting transfers between devices  6.85 us (11%)
    ppermute x1, waiting for transfers between devices, passed_along(): return lax.ppermute(value, axis, pairs)  11.8 us
    ppermute x3, waiting for transfers between devices, sent_narrow(): return widen(lax.ppermute(narrow(message), axis, pairs))  11.8 us
    ppermute x3, starting transfers between devices, sent_narrow(): return widen(lax.ppermute(narrow(message), axis, pairs))  3.85 us
    add x1, other arithmetic, scans_in(): incoming = incoming + weight[:, None, None] * got  2.63 us
    ppermute x1, starting transfers between devices, passed_along(): return lax.ppermute(value, axis, pairs)  2.54 us
    convert_element_type x1, other arithmetic, local(): near_round = near_total.astype(jnp.bfloat16)  2.48 us
    unnamed x9, local copies, waits for them, and re-layouts  2.47 us
    dot_general x1, matrix products, local(): jnp.einsum('hts,thd->shd', mixing, queries, precision=HIGH)  1.87 us
  transfers between devices with their start and end apart: 6, of which 3 were waited for; matrix products, arithmetic and copies ran while one was open for 23% of the time, Pallas kernels for 0%

profile of v20, /device:TPU:0, one launch (start us, length us, event | category | flops | bytes accessed | tf_op | source)
XLA Modules:
  0.0 64.4 jit_solution(18350961168384460472)
XLA Ops:
  0.1 0.7 %compare_bitcast_fusion = pred[2]{0:T(512)(128)(4,1)S(1)} fusion(s32[1,2]{1,0:T(1,128)} %param.9), kind=kLoop, calls=%fused_computation.73 | loop fusion | flops 2 | bytes 10 | tf_op jit(solution)/shard_map/eq | solution.py:102
  0.9 0.7 %log_bitcast_fusion = f32[2,16]{1,0:T(2,128)S(1)} fusion(s32[1,2,16]{2,1,0:T(2,128)} %param.8), kind=kLoop, calls=%fused_computation.74 | loop fusion | flops 96 | bytes 256 | tf_op jit(solution)/shard_map/log | solution.py:100
  1.9 0.7 %fusion.35 = (f32[1,1,2048]{2,0,1:T(1,128)S(1)}, f32[1,1,2048]{2,0,1:T(1,128)S(1)}, f32[1,1,2048]{2,0,1:T(1,128)S(1)}) fusion(f32[1,3,2048]{2,0,1:T(1,128)} %param.7), kind=kLoop, calls=%fused_computation.82 | loop fusion | bytes 49152 | tf_op jit(solution)/shard_map/slice | solution.py:111
  2.6 1.3 %copy.34 = bf16[1,128,2048]{1,2,0:T(8,128)(2,1)S(1)} copy(bf16[1,128,2048]{2,1,0:T(8,128)(2,1)} %param.5) | data formatting | bytes 1048576 | tf_op args[0]
  4.0 1.0 %fusion.5 = (bf16[128,2048]{0,1:T(8,128)(2,1)S(1)}, bf16[128,2048]{0,1:T(8,128)(2,1)S(1)}, bf16[128,2048]{0,1:T(8,128)(2,1)S(1)}) fusion(bf16[1,128,2048]{1,2,0:T(8,128)(2,1)S(1)} %copy.34, f32[2048]{0:T(1024)S(1)} %bitcast.122, f32[2048]{0:T(1024)S(1)} %bitcast.125, f32[2048]{0:T(1024)S(1)} %bitcast.128), kind=kLoop, calls=%fused_computation.19 | loop fusion | flops 1835008 | bytes 2121728 | tf_op jit(solution)/shard_map/convert_element_type | solution.py:111
  5.3 0.9 %fusion.16 = f32[16,128,128]{2,1,0:T(8,128)S(1)} fusion(bf16[128,16,128]{0,2,1:T(8,128)(2,1)S(1)} %bitcast.116, bf16[128,16,128]{0,2,1:T(8,128)(2,1)S(1)} %bitcast.109, f32[128,16]{0,1:T(8,128)S(1)} %copy.37), kind=kOutput, calls=%fused_computation.41 | convolution fusion | flops 201850880 | bytes 2105344 | tf_op jit(solution)/shard_map/shd,she->hde/dot_general | solution.py:134
  6.2 1.6 %broadcast_select_fusion.2 = (f32[16,128,128]{2,1,0:T(8,128)S(1)}, f32[16,128,128]{2,1,0:T(8,128)}) fusion(f32[16,128,128]{2,1,0:T(8,128)S(1)} %fusion.16, pred[]{:T(512)S(6)} %eq.29, bf16[128,16,128]{2,1,0:T(8,128)(2,1)S(1)} %bitcast.105, bf16[128,16,128]{0,2,1:T(8,128)(2,1)S(1)} %bitcast.113, f32[128,16]{0,1:T(8,128)S(1)} %copy.35), kind=kOutput, calls=%fused_computation.52 | convolution fusion | flops 202637312 | bytes 4202497 | tf_op jit(solution)/shard_map/shd,she->hde/dot_general | solution.py:137
  7.8 1.1 %pad_maximum_fusion = f32[16,136,128]{2,1,0:T(8,128)} fusion(f32[16,8,128]{2,1,0:T(8,128)S(1)} %broadcast_in_dim.32, f32[16,128,128]{2,1,0:T(8,128)S(1)} %get-tuple-element.15), kind=kLoop, calls=%fused_computation.17 | loop fusion | flops 278528 | bytes 2228224 | tf_op jit(solution)/shard_map/concatenate | solution.py:16
  9.6 0.6 fusion.1
  10.2 1.5 %convolution_multiply_fusion.1 = f32[16,128,128]{1,2,0:T(8,128)} fusion(bf16[128,16,128]{0,2,1:T(8,128)(2,1)S(1)} %bitcast.114, bf16[128,16,128]{0,2,1:T(8,128)(2,1)S(1)} %bitcast.110, f32[16,128]{1,0:T(8,128)S(1)} %copy.44, pred[128,128]{0,1:T(8,128)(4,1)S(1)} %iota_compare_fusion), kind=kOutput, calls=%fused_computation.5 | convolution fusion | flops 68157440 | bytes 2121728 | tf_op jit(solution)/shard_map/thd,shd->hts/dot_general | solution.py:152
  11.7 1.4 %convolution_multiply_fusion.3 = f32[16,128,128]{2,1,0:T(8,128)} fusion(bf16[128,16,128]{0,2,1:T(8,128)(2,1)S(1)} %bitcast.111, f32[16,128,128]{1,2,0:T(8,128)S(1)} %fusion.1), kind=kOutput, calls=%fused_computation.7 | convolution fusion | flops 201588736 | bytes 2621440 | tf_op jit(solution)/shard_map/hts,shd->thd/dot_general | solution.py:149
  13.2 1.9 %convolution_multiply_fusion.2 = f32[16,128,128]{2,1,0:T(8,128)} fusion(bf16[128,16,128]{0,2,1:T(8,128)(2,1)S(1)} %bitcast.115, f32[16,128,128]{1,2,0:T(8,128)S(1)} %fusion.1), kind=kOutput, calls=%fused_computation.6 | convolution fusion | flops 201588736 | bytes 2621440 | tf_op jit(solution)/shard_map/hts,thd->shd/dot_general | solution.py:150
  15.1 1.5 %pad_add_fusion = f32[16,136,128]{2,1,0:T(8,128)S(1)} fusion(f32[16,128,128]{2,1,0:T(8,128)S(1)} %copy-done, f32[16,136,128]{2,1,0:T(8,128)} %collective-permute-done, f32[16]{0:T(128)S(1)} %fusion.33), kind=kLoop, calls=%fused_computation.18 | loop fusion | flops 557056 | bytes 3276864 | tf_op jit(solution)/shard_map/add | solution.py:65
  17.2 0.9 %pad_maximum_fusion.1 = bf16[16,136,128]{2,1,0:T(8,128)(2,1)} fusion(bf16[16,8,128]{2,1,0:T(8,128)(2,1)S(1)} %broadcast_in_dim.33, bf16[16,128,128]{2,1,0:T(8,128)(2,1)S(1)} %slice.117), kind=kLoop, calls=%fused_computation.46 | loop fusion | flops 1114112 | bytes 1114112 | tf_op jit(solution)/shard_map/concatenate | solution.py:30
  18.1 1.3 %collective-permute-start.1 = (bf16[16,136,128]{2,1,0:T(8,128)(2,1)}, bf16[16,136,128]{2,1,0:T(8,128)(2,1)}, u32[]{:S(2)}, u32[]{:S(2)}) collective-permute-start(bf16[16,136,128]{2,1,0:T(8,128)(2,1)} %pad_maximum_fusion.1), channel_id=1, source_target_pairs={{1,3},{3,5},{5,7},{6,4},{4,2},{2,0},{9,11},{11,13},{13,15},{14,12}... | collective-permute-start | bytes 1671176 | tf_op jit(solution)/shard_map/ppermute | solution.py:40
  19.4 1.3 %collective-permute-start.2 = (bf16[16,136,128]{2,1,0:T(8,128)(2,1)}, bf16[16,136,128]{2,1,0:T(8,128)(2,1)}, u32[]{:S(2)}, u32[]{:S(2)}) collective-permute-start(bf16[16,136,128]{2,1,0:T(8,128)(2,1)} %pad_maximum_fusion.1), channel_id=1, source_target_pairs={{1,5},{3,7},{6,2},{4,0},{9,13},{11,15},{14,10},{12,8},{17,21},{19,... | collective-permute-start | bytes 1671176 | tf_op jit(solution)/shard_map/ppermute | solution.py:40
  21.1 1.0 %copy.41 = bf16[1,128,2048]{1,2,0:T(8,128)(2,1)} copy(bf16[1,128,2048]{2,1,0:T(8,128)(2,1)S(1)} %copy-done.1) | data formatting | bytes 1048576 | tf_op args[1]
  22.1 1.3 %copy.51 = f32[128,16,128]{0,2,1:T(8,128)} copy(f32[128,16,128]{2,0,1:T(8,128)S(1)} %fusion) | data formatting | bytes 2097152 | tf_op jit(solution)/shard_map/mul | solution.py:154
  23.4 1.3 %collective-permute-start.3 = (bf16[16,136,128]{2,1,0:T(8,128)(2,1)}, bf16[16,136,128]{2,1,0:T(8,128)(2,1)S(1)}, u32[]{:S(2)}, u32[]{:S(2)}) collective-permute-start(bf16[16,136,128]{2,1,0:T(8,128)(2,1)} %pad_maximum_fusion.1), channel_id=1, source_target_pairs={{1,7},{6,0},{9,15},{14,8},{17,23},{22,16},{25,31},{30,24}} | collective-permute-start | bytes 1671176 | tf_op jit(solution)/shard_map/ppermute | solution.py:40
  24.7 2.5 %fusion.10 = bf16[128,2048]{0,1:T(8,128)(2,1)S(1)} fusion(f32[16,128,128]{2,1,0:T(8,128)} %convolution_multiply_fusion.2, f32[16,128,128]{2,1,0:T(8,128)} %convolution_multiply_fusion.3, f32[128,16,128]{0,2,1:T(8,128)} %copy.51, bf16[1,128,2048]{1,2,0:T(8,128)(2,1)} %copy.41, f32[2048]{0:T(1024)S(1)} %bitcast.126, f32[2048]{0:T(1024)S(1)} %bitcast.129, ...), kind=kLoop, calls=%fused_computation.27 | loop fusion | flops 2097152 | bytes 4218880 | tf_op jit(solution)/shard_map/convert_element_type | solution.py:159
  27.2 8.0 %collective-permute-done.1 = bf16[16,136,128]{2,1,0:T(8,128)(2,1)} collective-permute-done((bf16[16,136,128]{2,1,0:T(8,128)(2,1)}, bf16[16,136,128]{2,1,0:T(8,128)(2,1)}, u32[]{:S(2)}, u32[]{:S(2)}) %collective-permute-start.1) | collective-permute-done | bytes 557088 | tf_op jit(solution)/shard_map/ppermute | solution.py:40
  35.2 3.8 %collective-permute-done.2 = bf16[16,136,128]{2,1,0:T(8,128)(2,1)} collective-permute-done((bf16[16,136,128]{2,1,0:T(8,128)(2,1)}, bf16[16,136,128]{2,1,0:T(8,128)(2,1)}, u32[]{:S(2)}, u32[]{:S(2)}) %collective-permute-start.2) | collective-permute-done | bytes 557088 | tf_op jit(solution)/shard_map/ppermute | solution.py:40
  39.0 1.0 %fusion.34 = (f32[16]{0:T(128)S(1)}, f32[16]{0:T(128)S(1)}) fusion(bf16[16,136,128]{2,1,0:T(8,128)(2,1)} %collective-permute-done.2, bf16[16,136,128]{2,1,0:T(8,128)(2,1)} %collective-permute-done.1), kind=kLoop, calls=%fused_computation.81 | loop fusion | flops 112 | bytes 256 | tf_op jit(solution)/shard_map/add | solution.py:35
  40.1 2.6 %multiply_add_fusion = f32[16,128,128]{2,1,0:T(8,128)} fusion(bf16[16,136,128]{2,1,0:T(8,128)(2,1)S(1)} %collective-permute-done.3, bf16[16,136,128]{2,1,0:T(8,128)(2,1)} %collective-permute-done.2, bf16[16,136,128]{2,1,0:T(8,128)(2,1)} %collective-permute-done.1, f32[16]{0:T(128)S(1)} %get-tuple-element.14, f32[16]{0:T(128)S(1)} %get-tuple-element.13), kind=kLoop, calls=%fused_computation.40 | loop fusion | flops 1835008 | bytes 2621568 | tf_op jit(solution)/shard_map/add | solution.py:72
  42.7 1.1 %slice_reduce_fusion = f32[16]{0:T(128)S(1)} fusion(f32[16,136,128]{2,1,0:T(8,128)} %collective-permute-done), kind=kLoop, calls=%fused_computation.61 | loop fusion | bytes 128 | tf_op jit(solution)/shard_map/slice | solution.py:21
  43.8 1.7 %slice_add_fusion = f32[16,128,128]{2,1,0:T(8,128)S(1)} fusion(f32[16,136,128]{2,1,0:T(8,128)} %collective-permute-done, f32[16,128,128]{2,1,0:T(8,128)} %multiply_add_fusion, f32[16]{0:T(128)S(1)} %slice_reduce_fusion), kind=kLoop, calls=%fused_computation.22 | loop fusion | flops 524288 | bytes 3145792 | tf_op jit(solution)/shard_map/add | solution.py:88
  46.0 0.7 %fusion.2 = f32[128,16,128]{0,2,1:T(8,128)S(1)} fusion(bf16[128,16,128]{0,2,1:T(8,128)(2,1)S(1)} %bitcast.112, f32[128,16]{0,1:T(8,128)S(1)} %copy.37, f32[16,128,128]{2,1,0:T(8,128)S(1)} %collective-permute-done.4, f32[16,128,128]{2,1,0:T(8,128)S(1)} %slice_add_fusion, pred[]{:T(512)S(6)} %eq.29), kind=kOutput, calls=%fused_computation.12 | convolution fusion | flops 201850880 | bytes 3678209 | tf_op jit(solution)/shard_map/shd,hde->she/dot_general | solution.py:168
  46.8 0.9 %fusion.4 = f32[128,16,128]{0,2,1:T(8,128)S(1)} fusion(f32[16,128,128]{2,1,0:T(8,128)S(1)} %slice_add_fusion, f32[16,128,128]{2,1,0:T(8,128)S(1)} %collective-permute-done.4, f32[128,16]{0,1:T(8,128)S(1)} %copy.52, pred[]{:T(512)S(6)} %eq.29, bf16[128,16,128]{2,1,0:T(8,128)(2,1)S(1)} %bitcast.108), kind=kOutput, calls=%fused_computation.16 | convolution fusion | flops 201850880 | bytes 3678209 | tf_op jit(solution)/shard_map/the,hde->thd/dot_general | solution.py:165
  47.7 1.2 %fusion.13 = bf16[128,2048]{0,1:T(8,128)(2,1)S(1)} fusion(f32[128,16,128]{0,2,1:T(8,128)S(1)} %fusion.2, f32[128,16,128]{0,2,1:T(8,128)S(1)} %fusion.3, f32[128,16,128]{0,2,1:T(8,128)S(1)} %fusion.4, f32[2048]{0:T(1024)S(1)} %bitcast.127, f32[2048]{0:T(1024)S(1)} %bitcast.130, f32[2048]{0:T(1024)S(1)} %bitcast.124), kind=kLoop, calls=%fused_computation.32 | loop fusion | flops 1572864 | bytes 3694592 | tf_op jit(solution)/shard_map/convert_element_type | solution.py:172
  49.0 2.5 %collective-permute-start.5 = (bf16[128,2048]{0,1:T(8,128)(2,1)S(1)}, bf16[128,2048]{0,1:T(8,128)(2,1)S(1)}, u32[]{:S(2)}, u32[]{:S(2)}) collective-permute-start(bf16[128,2048]{0,1:T(8,128)(2,1)S(1)} %add_convert_fusion), channel_id=1, source_target_pairs={{0,24},{8,0},{16,8},{24,16},{1,25},{9,1},{17,9},{25,17},{2,26},{10... | collective-permute-start | bytes 1572872 | tf_op jit(solution)/shard_map/ppermute | solution.py:95
  51.6 11.8 %collective-permute-done.5 = bf16[128,2048]{0,1:T(8,128)(2,1)S(1)} collective-permute-done((bf16[128,2048]{0,1:T(8,128)(2,1)S(1)}, bf16[128,2048]{0,1:T(8,128)(2,1)S(1)}, u32[]{:S(2)}, u32[]{:S(2)}) %collective-permute-start.5) | collective-permute-done | bytes 524320 | tf_op jit(solution)/shard_map/ppermute | solution.py:95
  63.4 1.0 %copy.57 = bf16[1,128,2048]{2,1,0:T(8,128)(2,1)} copy(bf16[1,128,2048]{1,2,0:T(8,128)(2,1)S(1)} %bitcast.121) | data formatting | bytes 1048576 | tf_op jit(solution)/shard_map/broadcast_in_dim | solution.py:176
  (44 shorter events, 3.5 us)
Async XLA Ops:
  4.0 1.0 %copy-start.1 = (bf16[1,128,2048]{2,1,0:T(8,128)(2,1)S(1)}, bf16[1,128,2048]{2,1,0:T(8,128)(2,1)}, u32[]{:S(2)}) copy-start(bf16[1,128,2048]{2,1,0:T(8,128)(2,1)} %param.6) | copy-start | bytes 1572868
  8.9 6.1 %collective-permute-start = (f32[16,136,128]{2,1,0:T(8,128)}, f32[16,136,128]{2,1,0:T(8,128)}, u32[]{:S(2)}, u32[]{:S(2)}) collective-permute-start(f32[16,136,128]{2,1,0:T(8,128)} %pad_maximum_fusion), channel_id=1, source_target_pairs={{0,1},{2,3},{4,5},{6,7},{1,0},{3,2},{5,4},{7,6},{8,9},{10,11},{12,... | collective-permute-start | bytes 3342344 | tf_op jit(solution)/shard_map/ppermute | solution.py:63
  13.2 1.9 %copy-start = (f32[16,128,128]{2,1,0:T(8,128)S(1)}, f32[16,128,128]{2,1,0:T(8,128)}, u32[]{:S(2)}) copy-start(f32[16,128,128]{2,1,0:T(8,128)} %get-tuple-element.16) | copy-start | bytes 3145732
  17.0 3.6 %copy-start.2 = (f32[16,128,128]{1,2,0:T(8,128)S(1)}, f32[16,128,128]{1,2,0:T(8,128)}, u32[]{:S(2)}) copy-start(f32[16,128,128]{1,2,0:T(8,128)} %convolution_multiply_fusion.1) | copy-start | bytes 3145732
  18.1 17.1 %collective-permute-start.1 = (bf16[16,136,128]{2,1,0:T(8,128)(2,1)}, bf16[16,136,128]{2,1,0:T(8,128)(2,1)}, u32[]{:S(2)}, u32[]{:S(2)}) collective-permute-start(bf16[16,136,128]{2,1,0:T(8,128)(2,1)} %pad_maximum_fusion.1), channel_id=1, source_target_pairs={{1,3},{3,5},{5,7},{6,4},{4,2},{2,0},{9,11},{11,13},{13,15},{14,12}... | collective-permute-start | bytes 1671176 | tf_op jit(solution)/shard_map/ppermute | solution.py:40
  19.4 19.6 %collective-permute-start.2 = (bf16[16,136,128]{2,1,0:T(8,128)(2,1)}, bf16[16,136,128]{2,1,0:T(8,128)(2,1)}, u32[]{:S(2)}, u32[]{:S(2)}) collective-permute-start(bf16[16,136,128]{2,1,0:T(8,128)(2,1)} %pad_maximum_fusion.1), channel_id=1, source_target_pairs={{1,5},{3,7},{6,2},{4,0},{9,13},{11,15},{14,10},{12,8},{17,21},{19,... | collective-permute-start | bytes 1671176 | tf_op jit(solution)/shard_map/ppermute | solution.py:40
  23.4 16.6 %collective-permute-start.3 = (bf16[16,136,128]{2,1,0:T(8,128)(2,1)}, bf16[16,136,128]{2,1,0:T(8,128)(2,1)S(1)}, u32[]{:S(2)}, u32[]{:S(2)}) collective-permute-start(bf16[16,136,128]{2,1,0:T(8,128)(2,1)} %pad_maximum_fusion.1), channel_id=1, source_target_pairs={{1,7},{6,0},{9,15},{14,8},{17,23},{22,16},{25,31},{30,24}} | collective-permute-start | bytes 1671176 | tf_op jit(solution)/shard_map/ppermute | solution.py:40
  42.7 2.9 %collective-permute-start.4 = (f32[16,128,128]{2,1,0:T(8,128)}, f32[16,128,128]{2,1,0:T(8,128)S(1)}, u32[]{:S(2)}, u32[]{:S(2)}) collective-permute-start(f32[16,128,128]{2,1,0:T(8,128)} %multiply_add_fusion), channel_id=1, source_target_pairs={{0,1},{2,3},{4,5},{6,7},{1,0},{3,2},{5,4},{7,6},{8,9},{10,11},{12,... | collective-permute-start | bytes 3145736 | tf_op jit(solution)/shard_map/ppermute | solution.py:87
  49.0 14.4 %collective-permute-start.5 = (bf16[128,2048]{0,1:T(8,128)(2,1)S(1)}, bf16[128,2048]{0,1:T(8,128)(2,1)S(1)}, u32[]{:S(2)}, u32[]{:S(2)}) collective-permute-start(bf16[128,2048]{0,1:T(8,128)(2,1)S(1)} %add_convert_fusion), channel_id=1, source_target_pairs={{0,24},{8,0},{16,8},{24,16},{1,25},{9,1},{17,9},{25,17},{2,26},{10... | collective-permute-start | bytes 1572872 | tf_op jit(solution)/shard_map/ppermute | solution.py:95

commit v21 on v20

--- a/solution.py
+++ b/solution.py
@@ -83,7 +83,6 @@
             moves = [(2 * p + 1, 2 * (p + 1 + covered) + 1) for p in range(couples - 1 - covered)]
             nearer = merged(sent_narrow(window, axis, both_ways(count, moves)), nearer)
         incoming = unpacked(nearer)[0]
-    incoming, held = lax.optimization_barrier((incoming, held))
     other = lax.ppermute(incoming, axis, swap)
     own = lower_rate[:, None, None] * incoming + lower
     return jnp.where(odd, own, other), jnp.where(odd, other, own), held

time: 65 us -> 67.2 us (1.034)
  waiting for transfers between devices: 23.6 us -> 29.3 us
  other arithmetic: 15.4 us -> 10.3 us
  starting transfers between devices: 6.85 us -> 9.15 us
  matrix products: 10.4 us -> 8.4 us
  local copies, waits for them, and re-layouts: 7.89 us -> 9.18 us
    ppermute x3, waiting for transfers between devices: 11.8 us -> 15.3 us  [sent_narrow(): return widen(lax.ppermute(narrow(message), axis, pairs))]
    add x1 -> x0, other arithmetic: 2.63 us -> none  [scans_in(): incoming = incoming + weight[:, None, None] * got]
    convert_element_type x1 -> x0, other arithmetic: 2.48 us -> none  [local(): near_round = near_total.astype(jnp.bfloat16)]
    ppermute x1, starting transfers between devices: 2.54 us -> 4.77 us  [passed_along(): return lax.ppermute(value, axis, pairs)]
    ppermute x1, waiting for transfers between devices: 0.01 us -> 2.22 us  [scans_in(): message = lax.ppermute(sent, axis, swap)]
    mul x1, local copies, waits for them, and re-layouts: 1.3 us -> 2.59 us  [local(): scale * jnp.einsum('hts,the->she', attention, grad_rows, precision=HIGH)]
    add x1, other arithmetic: 1.46 us -> 0.2 us  [scans_in(): window = rate[:, None, None] * message + packed(mine, jnp.zeros_like(rate))]
    dot_general x1, matrix products: 0.59 us -> 1.68 us  [local(): jnp.einsum('thd,shd->hts', grad_half, value_half, preferred_element_type=...]
  transfers between devices with their start and end apart: 6 -> 6, of which waited for: 3 -> 5; matrix products, arithmetic and copies ran while one was open for 23% -> 15% of each run, Pallas kernels for 0% -> 0%
where the time goes in v21:
time: 67.2 us; the launch traced here: 66.7 us
  waiting for transfers between devices  29.3 us (44%)
  other arithmetic  10.3 us (15%)
  local copies, waits for them, and re-layouts  9.18 us (14%)
  starting transfers between devices  9.15 us (14%)
  matrix products  8.4 us (12%)
    ppermute x3, waiting for transfers between devices, sent_narrow(): return widen(lax.ppermute(narrow(message), axis, pairs))  15.3 us
    ppermute x1, waiting for transfers between devices, passed_along(): return lax.ppermute(value, axis, pairs)  11.9 us
    ppermute x1, starting transfers between devices, passed_along(): return lax.ppermute(value, axis, pairs)  4.77 us
    ppermute x3, starting transfers between devices, sent_narrow(): return widen(lax.ppermute(narrow(message), axis, pairs))  3.86 us
    unnamed x21, local copies, waits for them, and re-layouts  3.26 us
    add x1, other arithmetic, scans_in(): own = lower_rate[:, None, None] * incoming + lower  2.75 us
    mul x1, local copies, waits for them, and re-layouts, local(): scale * jnp.einsum('hts,the->she', attention, grad_rows, precision=HIGH)  2.59 us
    ppermute x1, waiting for transfers between devices, scans_in(): message = lax.ppermute(sent, axis, swap)  2.22 us
  transfers between devices with their start and end apart: 6, of which 5 were waited for; matrix products, arithmetic and copies ran while one was open for 15% of the time, Pallas kernels for 0%

profile of v21, /device:TPU:0, one launch (start us, length us, event | category | flops | bytes accessed | tf_op | source)
XLA Modules:
  0.0 66.7 jit_solution(15116219435711777040)
XLA Ops:
  0.1 0.7 compare_bitcast_fusion
  0.9 0.7 %log_bitcast_fusion = f32[2,16]{1,0:T(2,128)S(1)} fusion(s32[1,2,16]{2,1,0:T(2,128)} %param.8), kind=kLoop, calls=%fused_computation.74 | loop fusion | flops 96 | bytes 256 | tf_op jit(solution)/shard_map/log | solution.py:99
  1.9 1.3 %copy.35 = bf16[1,128,2048]{1,2,0:T(8,128)(2,1)S(1)} copy(bf16[1,128,2048]{2,1,0:T(8,128)(2,1)} %param.5) | data formatting | bytes 1048576 | tf_op args[0]
  3.3 1.0 %fusion.5 = (bf16[128,2048]{0,1:T(8,128)(2,1)S(1)}, bf16[128,2048]{0,1:T(8,128)(2,1)S(1)}, bf16[128,2048]{0,1:T(8,128)(2,1)S(1)}) fusion(bf16[1,128,2048]{1,2,0:T(8,128)(2,1)S(1)} %copy.35, f32[2048]{0:T(1024)S(1)} %bitcast.122, f32[2048]{0:T(1024)S(1)} %bitcast.124, f32[2048]{0:T(1024)S(1)} %bitcast.126), kind=kLoop, calls=%fused_computation.19 | loop fusion | flops 1835008 | bytes 2121728 | tf_op jit(solution)/shard_map/convert_element_type | solution.py:110
  4.6 0.5 convolution_multiply_fusion
  5.1 0.9 %broadcast_select_fusion.1 = (f32[16,128,128]{2,1,0:T(8,128)S(1)}, f32[16,128,128]{2,1,0:T(8,128)S(1)}) fusion(f32[16,128,128]{2,1,0:T(8,128)S(1)} %convolution_multiply_fusion, pred[]{:T(512)S(6)} %eq.29, bf16[128,16,128]{0,2,1:T(8,128)(2,1)S(1)} %bitcast.113, bf16[128,16,128]{0,2,1:T(8,128)(2,1)S(1)} %bitcast.105, f32[128,16]{0,1:T(8,128)S(1)} %copy.49), kind=kOutput, calls=%fused_computation.51 | convolution fusion | flops 202375168 | bytes 4202497 | tf_op jit(solution)/shard_map/shd,she->hde/dot_general | solution.py:133
  6.1 0.5 collective-permute-start
  6.8 2.2 %collective-permute-done = f32[16,136,128]{2,1,0:T(8,128)S(1)} collective-permute-done((f32[16,136,128]{2,1,0:T(8,128)S(1)}, f32[16,136,128]{2,1,0:T(8,128)S(1)}, u32[]{:S(2)}, u32[]{:S(2)}) %collective-permute-start) | collective-permute-done | bytes 1114144 | tf_op jit(solution)/shard_map/ppermute | solution.py:63
  9.4 0.9 %slice.117 = bf16[16,128,128]{2,1,0:T(8,128)(2,1)} slice(f32[16,136,128]{2,1,0:T(8,128)S(1)} %pad_add_fusion), slice={[0:16], [0:128], [0:128]} | slice | bytes 1048576 | tf_op jit(solution)/shard_map/slice | solution.py:21
  10.7 1.9 %pad_maximum_fusion.1 = bf16[16,136,128]{2,1,0:T(8,128)(2,1)} fusion(bf16[16,8,128]{2,1,0:T(8,128)(2,1)S(1)} %broadcast_in_dim.34, bf16[16,128,128]{2,1,0:T(8,128)(2,1)} %slice.117), kind=kLoop, calls=%fused_computation.46 | loop fusion | flops 1114112 | bytes 1114112 | tf_op jit(solution)/shard_map/concatenate | solution.py:30
  12.6 1.3 %collective-permute-start.2 = (bf16[16,136,128]{2,1,0:T(8,128)(2,1)}, bf16[16,136,128]{2,1,0:T(8,128)(2,1)}, u32[]{:S(2)}, u32[]{:S(2)}) collective-permute-start(bf16[16,136,128]{2,1,0:T(8,128)(2,1)} %pad_maximum_fusion.1), channel_id=1, source_target_pairs={{1,5},{3,7},{6,2},{4,0},{9,13},{11,15},{14,10},{12,8},{17,21},{19,... | collective-permute-start | bytes 1671176 | tf_op jit(solution)/shard_map/ppermute | solution.py:40
  13.9 1.3 %collective-permute-start.1 = (bf16[16,136,128]{2,1,0:T(8,128)(2,1)}, bf16[16,136,128]{2,1,0:T(8,128)(2,1)}, u32[]{:S(2)}, u32[]{:S(2)}) collective-permute-start(bf16[16,136,128]{2,1,0:T(8,128)(2,1)} %pad_maximum_fusion.1), channel_id=1, source_target_pairs={{1,3},{3,5},{5,7},{6,4},{4,2},{2,0},{9,11},{11,13},{13,15},{14,12}... | collective-permute-start | bytes 1671176 | tf_op jit(solution)/shard_map/ppermute | solution.py:40
  15.2 1.3 %collective-permute-start.3 = (bf16[16,136,128]{2,1,0:T(8,128)(2,1)}, bf16[16,136,128]{2,1,0:T(8,128)(2,1)}, u32[]{:S(2)}, u32[]{:S(2)}) collective-permute-start(bf16[16,136,128]{2,1,0:T(8,128)(2,1)} %pad_maximum_fusion.1), channel_id=1, source_target_pairs={{1,7},{6,0},{9,15},{14,8},{17,23},{22,16},{25,31},{30,24}} | collective-permute-start | bytes 1671176 | tf_op jit(solution)/shard_map/ppermute | solution.py:40
  16.5 1.0 %copy.34 = bf16[1,128,2048]{1,2,0:T(8,128)(2,1)} copy(bf16[1,128,2048]{2,1,0:T(8,128)(2,1)S(1)} %copy-done.7) | data formatting | bytes 1048576 | tf_op args[1]
  17.7 0.6 convolution_multiply_fusion.2
  18.4 6.2 %collective-permute-done.2 = bf16[16,136,128]{2,1,0:T(8,128)(2,1)} collective-permute-done((bf16[16,136,128]{2,1,0:T(8,128)(2,1)}, bf16[16,136,128]{2,1,0:T(8,128)(2,1)}, u32[]{:S(2)}, u32[]{:S(2)}) %collective-permute-start.2) | collective-permute-done | bytes 557088 | tf_op jit(solution)/shard_map/ppermute | solution.py:40
  24.6 5.7 %collective-permute-done.1 = bf16[16,136,128]{2,1,0:T(8,128)(2,1)} collective-permute-done((bf16[16,136,128]{2,1,0:T(8,128)(2,1)}, bf16[16,136,128]{2,1,0:T(8,128)(2,1)}, u32[]{:S(2)}, u32[]{:S(2)}) %collective-permute-start.1) | collective-permute-done | bytes 557088 | tf_op jit(solution)/shard_map/ppermute | solution.py:40
  30.3 1.0 %fusion.34 = (f32[16]{0:T(128)S(1)}, f32[16]{0:T(128)S(1)}) fusion(bf16[16,136,128]{2,1,0:T(8,128)(2,1)} %collective-permute-done.2, bf16[16,136,128]{2,1,0:T(8,128)(2,1)} %collective-permute-done.1), kind=kLoop, calls=%fused_computation.81 | loop fusion | flops 112 | bytes 256 | tf_op jit(solution)/shard_map/add | solution.py:35
  31.3 3.4 %collective-permute-done.3 = bf16[16,136,128]{2,1,0:T(8,128)(2,1)} collective-permute-done((bf16[16,136,128]{2,1,0:T(8,128)(2,1)}, bf16[16,136,128]{2,1,0:T(8,128)(2,1)}, u32[]{:S(2)}, u32[]{:S(2)}) %collective-permute-start.3) | collective-permute-done | bytes 557088 | tf_op jit(solution)/shard_map/ppermute | solution.py:40
  34.7 2.8 %slice_add_fusion = (f32[16,128,128]{2,1,0:T(8,128)S(1)}, f32[16,128,128]{2,1,0:T(8,128)}) fusion(f32[16,136,128]{2,1,0:T(8,128)S(1)} %collective-permute-done, f32[16]{0:T(128)S(1)} %slice_reduce_fusion.1, bf16[16,136,128]{2,1,0:T(8,128)(2,1)} %collective-permute-done.3, f32[16]{0:T(128)S(1)} %get-tuple-element.10, ...), kind=kLoop, calls=%fused_computation.22 | loop fusion | flops 2359296 | bytes 4718784 | tf_op jit(solution)/shard_map/add | solution.py:87
  37.5 1.4 %fusion = f32[128,16,128]{2,0,1:T(8,128)} fusion(f32[16,128,128]{1,2,0:T(8,128)S(1)} %convolution_multiply_fusion.2, bf16[128,16,128]{2,1,0:T(8,128)(2,1)S(1)} %bitcast.110), kind=kOutput, calls=%fused_computation.5 | convolution fusion | flops 201588736 | bytes 2621440 | tf_op jit(solution)/shard_map/hts,the->she/dot_general | solution.py:153
  38.9 2.6 %copy.45 = f32[128,16,128]{0,2,1:T(8,128)} copy(f32[128,16,128]{2,0,1:T(8,128)} %fusion) | data formatting | bytes 2097152 | tf_op jit(solution)/shard_map/mul | solution.py:153
  41.5 1.7 %fusion.1 = f32[16,128,128]{1,2,0:T(8,128)S(1)} fusion(bf16[128,16,128]{0,2,1:T(8,128)(2,1)} %bitcast.114, f32[16,128]{1,0:T(8,128)S(1)} %copy.38, pred[128,128]{0,1:T(8,128)(4,1)S(1)} %iota_compare_fusion, bf16[128,16,128]{2,1,0:T(8,128)(2,1)S(1)} %bitcast.111), kind=kOutput, calls=%fused_computation.10 | convolution fusion | flops 68157440 | bytes 2121728 | tf_op jit(solution)/shard_map/thd,shd->hts/dot_general | solution.py:145
  43.2 0.8 %convolution_multiply_fusion.3 = f32[16,128,128]{2,1,0:T(8,128)S(1)} fusion(bf16[128,16,128]{0,2,1:T(8,128)(2,1)S(1)} %bitcast.118, f32[16,128,128]{1,2,0:T(8,128)S(1)} %fusion.1), kind=kOutput, calls=%fused_computation.7 | convolution fusion | flops 201588736 | bytes 2621440 | tf_op jit(solution)/shard_map/hts,thd->shd/dot_general | solution.py:149
  44.1 0.4 convolution_multiply_fusion.4
  44.6 0.7 %fusion.2 = f32[128,16,128]{0,2,1:T(8,128)S(1)} fusion(bf16[128,16,128]{0,2,1:T(8,128)(2,1)S(1)} %bitcast.108, f32[128,16]{0,1:T(8,128)S(1)} %copy.49, f32[16,128,128]{2,1,0:T(8,128)S(1)} %collective-permute-done.4, f32[16,128,128]{2,1,0:T(8,128)S(1)} %get-tuple-element.11, pred[]{:T(512)S(6)} %eq.29), kind=kOutput, calls=%fused_computation.12 | convolution fusion | flops 201850880 | bytes 3678209 | tf_op jit(solution)/shard_map/shd,hde->she/dot_general | solution.py:167
  45.6 0.5 fusion.3
  46.1 0.8 %fusion.4 = f32[128,16,128]{0,2,1:T(8,128)S(1)} fusion(f32[16,128,128]{2,1,0:T(8,128)S(1)} %get-tuple-element.11, f32[16,128,128]{2,1,0:T(8,128)S(1)} %collective-permute-done.4, f32[128,16]{0,1:T(8,128)S(1)} %copy.46, pred[]{:T(512)S(6)} %eq.29, bf16[128,16,128]{2,1,0:T(8,128)(2,1)S(1)} %bitcast.112), kind=kOutput, calls=%fused_computation.16 | convolution fusion | flops 201850880 | bytes 3678209 | tf_op jit(solution)/shard_map/the,hde->thd/dot_general | solution.py:164
  47.4 1.4 %fusion.13 = (bf16[128,2048]{0,1:T(8,128)(2,1)S(1)}, bf16[128,2048]{0,1:T(8,128)(2,1)S(1)}) fusion(f32[128,16,128]{0,2,1:T(8,128)S(1)} %fusion.2, f32[128,16,128]{0,2,1:T(8,128)S(1)} %fusion.3, f32[128,16,128]{0,2,1:T(8,128)S(1)} %fusion.4, f32[2048]{0:T(1024)S(1)} %bitcast.127, f32[2048]{0:T(1024)S(1)} %bitcast.123, f32[2048]{0:T(1024)S(1)} %bitcast.125, ...), kind=kLoop, calls=%fused_computation.32 | loop fusion | flops 3670016 | bytes 7888896 | tf_op jit(solution)/shard_map/convert_element_type | solution.py:171
  49.0 4.8 %collective-permute-start.5 = (bf16[128,2048]{0,1:T(8,128)(2,1)S(1)}, bf16[128,2048]{0,1:T(8,128)(2,1)S(1)}, u32[]{:S(2)}, u32[]{:S(2)}) collective-permute-start(bf16[128,2048]{0,1:T(8,128)(2,1)S(1)} %add_convert_fusion), channel_id=1, source_target_pairs={{0,24},{8,0},{16,8},{24,16},{1,25},{9,1},{17,9},{25,17},{2,26},{10... | collective-permute-start | bytes 1572872 | tf_op jit(solution)/shard_map/ppermute | solution.py:94
  53.8 11.9 %collective-permute-done.5 = bf16[128,2048]{0,1:T(8,128)(2,1)S(1)} collective-permute-done((bf16[128,2048]{0,1:T(8,128)(2,1)S(1)}, bf16[128,2048]{0,1:T(8,128)(2,1)S(1)}, u32[]{:S(2)}, u32[]{:S(2)}) %collective-permute-start.5) | collective-permute-done | bytes 524320 | tf_op jit(solution)/shard_map/ppermute | solution.py:94
  65.7 1.0 %copy.57 = bf16[1,128,2048]{2,1,0:T(8,128)(2,1)} copy(bf16[1,128,2048]{1,2,0:T(8,128)(2,1)S(1)} %bitcast.121) | data formatting | bytes 1048576 | tf_op jit(solution)/shard_map/broadcast_in_dim | solution.py:175
  (54 shorter events, 3.2 us)
Async XLA Ops:
  0.0 3.2 %copy-start.8 = (f32[1,3,2048]{2,0,1:T(1,128)S(1)}, f32[1,3,2048]{2,0,1:T(1,128)}, u32[]{:S(2)}) copy-start(f32[1,3,2048]{2,0,1:T(1,128)} %param.7) | copy-start | bytes 73732
  3.2 1.2 %copy-start.6 = (bf16[1,128,2048]{2,1,0:T(8,128)(2,1)S(1)}, bf16[1,128,2048]{2,1,0:T(8,128)(2,1)}, u32[]{:S(2)}) copy-start(bf16[1,128,2048]{2,1,0:T(8,128)(2,1)} %param.6) | copy-start | bytes 1572868
  4.3 0.8 %copy-start = (bf16[128,2048]{0,1:T(8,128)(2,1)}, bf16[128,2048]{0,1:T(8,128)(2,1)S(1)}, u32[]{:S(2)}) copy-start(bf16[128,2048]{0,1:T(8,128)(2,1)S(1)} %get-tuple-element.17) | copy-start | bytes 1572868
  4.3 13.4 %copy-start.2 = (bf16[128,2048]{0,1:T(8,128)(2,1)}, bf16[128,2048]{0,1:T(8,128)(2,1)S(1)}, u32[]{:S(2)}) copy-start(bf16[128,2048]{0,1:T(8,128)(2,1)S(1)} %get-tuple-element.16) | copy-start | bytes 1572868
  6.1 2.9 %collective-permute-start = (f32[16,136,128]{2,1,0:T(8,128)S(1)}, f32[16,136,128]{2,1,0:T(8,128)S(1)}, u32[]{:S(2)}, u32[]{:S(2)}) collective-permute-start(f32[16,136,128]{2,1,0:T(8,128)S(1)} %pad_maximum_fusion), channel_id=1, source_target_pairs={{0,1},{2,3},{4,5},{6,7},{1,0},{3,2},{5,4},{7,6},{8,9},{10,11},{12,... | collective-permute-start | bytes 3342344 | tf_op jit(solution)/shard_map/ppermute | solution.py:63
  9.4 7.1 %copy-start.7 = (bf16[1,128,2048]{2,1,0:T(8,128)(2,1)S(1)}, bf16[1,128,2048]{2,1,0:T(8,128)(2,1)}, u32[]{:S(2)}) copy-start(bf16[1,128,2048]{2,1,0:T(8,128)(2,1)} %param.6) | copy-start | bytes 1572868
  12.6 12.0 %collective-permute-start.2 = (bf16[16,136,128]{2,1,0:T(8,128)(2,1)}, bf16[16,136,128]{2,1,0:T(8,128)(2,1)}, u32[]{:S(2)}, u32[]{:S(2)}) collective-permute-start(bf16[16,136,128]{2,1,0:T(8,128)(2,1)} %pad_maximum_fusion.1), channel_id=1, source_target_pairs={{1,5},{3,7},{6,2},{4,0},{9,13},{11,15},{14,10},{12,8},{17,21},{19,... | collective-permute-start | bytes 1671176 | tf_op jit(solution)/shard_map/ppermute | solution.py:40
  13.9 16.4 %collective-permute-start.1 = (bf16[16,136,128]{2,1,0:T(8,128)(2,1)}, bf16[16,136,128]{2,1,0:T(8,128)(2,1)}, u32[]{:S(2)}, u32[]{:S(2)}) collective-permute-start(bf16[16,136,128]{2,1,0:T(8,128)(2,1)} %pad_maximum_fusion.1), channel_id=1, source_target_pairs={{1,3},{3,5},{5,7},{6,4},{4,2},{2,0},{9,11},{11,13},{13,15},{14,12}... | collective-permute-start | bytes 1671176 | tf_op jit(solution)/shard_map/ppermute | solution.py:40
  15.2 19.5 %collective-permute-start.3 = (bf16[16,136,128]{2,1,0:T(8,128)(2,1)}, bf16[16,136,128]{2,1,0:T(8,128)(2,1)}, u32[]{:S(2)}, u32[]{:S(2)}) collective-permute-start(bf16[16,136,128]{2,1,0:T(8,128)(2,1)} %pad_maximum_fusion.1), channel_id=1, source_target_pairs={{1,7},{6,0},{9,15},{14,8},{17,23},{22,16},{25,31},{30,24}} | collective-permute-start | bytes 1671176 | tf_op jit(solution)/shard_map/ppermute | solution.py:40
  37.5 7.1 %collective-permute-start.4 = (f32[16,128,128]{2,1,0:T(8,128)}, f32[16,128,128]{2,1,0:T(8,128)S(1)}, u32[]{:S(2)}, u32[]{:S(2)}) collective-permute-start(f32[16,128,128]{2,1,0:T(8,128)} %get-tuple-element.12), channel_id=1, source_target_pairs={{0,1},{2,3},{4,5},{6,7},{1,0},{3,2},{5,4},{7,6},{8,9},{10,11},{12,... | collective-permute-start | bytes 3145736 | tf_op jit(solution)/shard_map/ppermute | solution.py:86
  41.5 1.7 %copy-start.3 = (bf16[128,2048]{0,1:T(8,128)(2,1)S(1)}, bf16[128,2048]{0,1:T(8,128)(2,1)}, u32[]{:S(2)}) copy-start(bf16[128,2048]{0,1:T(8,128)(2,1)} %copy-done.2) | copy-start | bytes 1572868
  44.5 1.0 %copy-start.1 = (bf16[128,2048]{0,1:T(8,128)(2,1)S(1)}, bf16[128,2048]{0,1:T(8,128)(2,1)}, u32[]{:S(2)}) copy-start(bf16[128,2048]{0,1:T(8,128)(2,1)} %copy-done) | copy-start | bytes 1572868
  46.1 1.2 %copy-start.4 = (f32[128,16,128]{0,2,1:T(8,128)S(1)}, f32[128,16,128]{0,2,1:T(8,128)}, u32[]{:S(2)}) copy-start(f32[128,16,128]{0,2,1:T(8,128)} %copy.45) | copy-start | bytes 3145732
  46.1 1.3 %copy-start.5 = (bf16[1,128,2048]{1,2,0:T(8,128)(2,1)S(1)}, bf16[1,128,2048]{1,2,0:T(8,128)(2,1)}, u32[]{:S(2)}) copy-start(bf16[1,128,2048]{1,2,0:T(8,128)(2,1)} %copy.34) | copy-start | bytes 1572868
  49.0 16.6 %collective-permute-start.5 = (bf16[128,2048]{0,1:T(8,128)(2,1)S(1)}, bf16[128,2048]{0,1:T(8,128)(2,1)S(1)}, u32[]{:S(2)}, u32[]{:S(2)}) collective-permute-start(bf16[128,2048]{0,1:T(8,128)(2,1)S(1)} %add_convert_fusion), channel_id=1, source_target_pairs={{0,24},{8,0},{16,8},{24,16},{1,25},{9,1},{17,9},{25,17},{2,26},{10... | collective-permute-start | bytes 1572872 | tf_op jit(solution)/shard_map/ppermute | solution.py:94

commit v22 on v20

--- a/solution.py
+++ b/solution.py
@@ -68,6 +68,11 @@
         weight = jnp.ones_like(rate)
         for step in range(1, couples):
             moves = [(2 * p + 1, 2 * (p + step) + 1) for p in range(couples - step)]
+            if step == couples - 1:
+                bare = unpacked(window)[0].astype(jnp.bfloat16)
+                got = lax.ppermute(bare, axis, both_ways(count, moves)).astype(jnp.float32)
+                incoming = incoming + weight[:, None, None] * got
+                continue
             got, got_rate = unpacked(sent_narrow(window, axis, both_ways(count, moves)))
             incoming = incoming + weight[:, None, None] * got
             weight = weight * got_rate

time: 65 us -> 64.8 us (level)
  waiting for transfers between devices: 23.6 us -> 22.6 us
  other arithmetic: 15.4 us -> 16.1 us
    ppermute x0 -> x1, starting transfers between devices: none -> 1.28 us  [scans_in(): got = lax.ppermute(bare, axis, both_ways(count, moves)).astype(jnp.float32)]
    ppermute x3 -> x2, starting transfers between devices: 3.85 us -> 2.57 us  [sent_narrow(): return widen(lax.ppermute(narrow(message), axis, pairs))]
    ppermute x3 -> x2, waiting for transfers between devices: 11.8 us -> 10.7 us  [sent_narrow(): return widen(lax.ppermute(narrow(message), axis, pairs))]
    convert_element_type x1, other arithmetic: 2.48 us -> 3.17 us  [local(): near_round = near_total.astype(jnp.bfloat16)]
    unnamed x9 -> x15, local copies, waits for them, and re-layouts: 2.47 us -> 2.5 us
  transfers between devices with their start and end apart: 6 -> 6, of which waited for: 3 -> 3; matrix products, arithmetic and copies ran while one was open for 23% -> 24% of each run, Pallas kernels for 0% -> 0%
where the time goes in v22:
time: 64.8 us; the launch traced here: 64.1 us
  waiting for transfers between devices  22.6 us (35%)
  other arithmetic  16.1 us (25%)
  matrix products  10.4 us (16%)
  local copies, waits for them, and re-layouts  7.99 us (12%)
  starting transfers between devices  6.79 us (10%)
    ppermute x1, waiting for transfers between devices, passed_along(): return lax.ppermute(value, axis, pairs)  11.9 us
    ppermute x2, waiting for transfers between devices, sent_narrow(): return widen(lax.ppermute(narrow(message), axis, pairs))  10.7 us
    convert_element_type x1, other arithmetic, local(): near_round = near_total.astype(jnp.bfloat16)  3.17 us
    add x1, other arithmetic, scans_in(): incoming = incoming + weight[:, None, None] * got  2.65 us
    ppermute x2, starting transfers between devices, sent_narrow(): return widen(lax.ppermute(narrow(message), axis, pairs))  2.57 us
    unnamed x15, local copies, waits for them, and re-layouts  2.5 us
    ppermute x1, starting transfers between devices, passed_along(): return lax.ppermute(value, axis, pairs)  2.49 us
    dot_general x1, matrix products, local(): jnp.einsum('hts,thd->shd', mixing, queries, precision=HIGH)  1.83 us
  transfers between devices with their start and end apart: 6, of which 3 were waited for; matrix products, arithmetic and copies ran while one was open for 24% of the time, Pallas kernels for 0%

profile of v22, /device:TPU:0, one launch (start us, length us, event | category | flops | bytes accessed | tf_op | source)
XLA Modules:
  0.0 64.1 jit_solution(6283316779964441118)
XLA Ops:
  0.1 0.7 %compare_bitcast_fusion = pred[2]{0:T(512)(128)(4,1)S(1)} fusion(s32[1,2]{1,0:T(1,128)} %param.9), kind=kLoop, calls=%fused_computation.73 | loop fusion | flops 2 | bytes 10 | tf_op jit(solution)/shard_map/eq | solution.py:107
  0.9 0.7 %log_bitcast_fusion = f32[2,16]{1,0:T(2,128)S(1)} fusion(s32[1,2,16]{2,1,0:T(2,128)} %param.8), kind=kLoop, calls=%fused_computation.74 | loop fusion | flops 96 | bytes 256 | tf_op jit(solution)/shard_map/log | solution.py:105
  1.9 0.7 %fusion.35 = (f32[1,1,2048]{2,0,1:T(1,128)S(1)}, f32[1,1,2048]{2,0,1:T(1,128)S(1)}, f32[1,1,2048]{2,0,1:T(1,128)S(1)}) fusion(f32[1,3,2048]{2,0,1:T(1,128)} %param.7), kind=kLoop, calls=%fused_computation.82 | loop fusion | bytes 49152 | tf_op jit(solution)/shard_map/slice | solution.py:116
  2.6 1.3 %copy.34 = bf16[1,128,2048]{1,2,0:T(8,128)(2,1)S(1)} copy(bf16[1,128,2048]{2,1,0:T(8,128)(2,1)} %param.5) | data formatting | bytes 1048576 | tf_op args[0]
  4.0 1.0 %fusion.5 = (bf16[128,2048]{0,1:T(8,128)(2,1)S(1)}, bf16[128,2048]{0,1:T(8,128)(2,1)S(1)}, bf16[128,2048]{0,1:T(8,128)(2,1)S(1)}) fusion(bf16[1,128,2048]{1,2,0:T(8,128)(2,1)S(1)} %copy.34, f32[2048]{0:T(1024)S(1)} %bitcast.122, f32[2048]{0:T(1024)S(1)} %bitcast.125, f32[2048]{0:T(1024)S(1)} %bitcast.128), kind=kLoop, calls=%fused_computation.19 | loop fusion | flops 1835008 | bytes 2121728 | tf_op jit(solution)/shard_map/convert_element_type | solution.py:116
  5.3 0.9 %fusion.16 = f32[16,128,128]{2,1,0:T(8,128)S(1)} fusion(bf16[128,16,128]{0,2,1:T(8,128)(2,1)S(1)} %bitcast.116, bf16[128,16,128]{0,2,1:T(8,128)(2,1)S(1)} %bitcast.109, f32[128,16]{0,1:T(8,128)S(1)} %copy.37), kind=kOutput, calls=%fused_computation.41 | convolution fusion | flops 201850880 | bytes 2105344 | tf_op jit(solution)/shard_map/shd,she->hde/dot_general | solution.py:139
  6.2 1.6 %broadcast_select_fusion.2 = (f32[16,128,128]{2,1,0:T(8,128)S(1)}, f32[16,128,128]{2,1,0:T(8,128)}) fusion(f32[16,128,128]{2,1,0:T(8,128)S(1)} %fusion.16, pred[]{:T(512)S(6)} %eq.29, bf16[128,16,128]{2,1,0:T(8,128)(2,1)S(1)} %bitcast.105, bf16[128,16,128]{0,2,1:T(8,128)(2,1)S(1)} %bitcast.113, f32[128,16]{0,1:T(8,128)S(1)} %copy.35), kind=kOutput, calls=%fused_computation.52 | convolution fusion | flops 202637312 | bytes 4202497 | tf_op jit(solution)/shard_map/shd,she->hde/dot_general | solution.py:142
  7.8 1.1 %pad_maximum_fusion = f32[16,136,128]{2,1,0:T(8,128)} fusion(f32[16,8,128]{2,1,0:T(8,128)S(1)} %broadcast_in_dim.32, f32[16,128,128]{2,1,0:T(8,128)S(1)} %get-tuple-element.15), kind=kLoop, calls=%fused_computation.17 | loop fusion | flops 278528 | bytes 2228224 | tf_op jit(solution)/shard_map/concatenate | solution.py:16
  9.7 0.6 fusion.1
  10.3 1.5 %convolution_multiply_fusion.1 = f32[16,128,128]{1,2,0:T(8,128)} fusion(bf16[128,16,128]{0,2,1:T(8,128)(2,1)S(1)} %bitcast.114, bf16[128,16,128]{0,2,1:T(8,128)(2,1)S(1)} %bitcast.110, f32[16,128]{1,0:T(8,128)S(1)} %copy.44, pred[128,128]{0,1:T(8,128)(4,1)S(1)} %iota_compare_fusion), kind=kOutput, calls=%fused_computation.5 | convolution fusion | flops 68157440 | bytes 2121728 | tf_op jit(solution)/shard_map/thd,shd->hts/dot_general | solution.py:157
  11.8 1.4 %convolution_multiply_fusion.3 = f32[16,128,128]{2,1,0:T(8,128)} fusion(bf16[128,16,128]{0,2,1:T(8,128)(2,1)S(1)} %bitcast.111, f32[16,128,128]{1,2,0:T(8,128)S(1)} %fusion.1), kind=kOutput, calls=%fused_computation.7 | convolution fusion | flops 201588736 | bytes 2621440 | tf_op jit(solution)/shard_map/hts,shd->thd/dot_general | solution.py:154
  13.2 1.8 %convolution_multiply_fusion.2 = f32[16,128,128]{2,1,0:T(8,128)} fusion(bf16[128,16,128]{0,2,1:T(8,128)(2,1)S(1)} %bitcast.115, f32[16,128,128]{1,2,0:T(8,128)S(1)} %fusion.1), kind=kOutput, calls=%fused_computation.6 | convolution fusion | flops 201588736 | bytes 2621440 | tf_op jit(solution)/shard_map/hts,thd->shd/dot_general | solution.py:155
  15.0 1.5 %pad_add_fusion = f32[16,136,128]{2,1,0:T(8,128)S(1)} fusion(f32[16,128,128]{2,1,0:T(8,128)S(1)} %copy-done, f32[16,136,128]{2,1,0:T(8,128)} %collective-permute-done, f32[16]{0:T(128)S(1)} %fusion.33), kind=kLoop, calls=%fused_computation.18 | loop fusion | flops 557056 | bytes 3276864 | tf_op jit(solution)/shard_map/add | solution.py:65
  17.2 0.9 %pad_maximum_fusion.1 = bf16[16,136,128]{2,1,0:T(8,128)(2,1)} fusion(bf16[16,8,128]{2,1,0:T(8,128)(2,1)S(1)} %broadcast_in_dim.33, bf16[16,128,128]{2,1,0:T(8,128)(2,1)S(1)} %slice.110), kind=kLoop, calls=%fused_computation.46 | loop fusion | flops 1114112 | bytes 1114112 | tf_op jit(solution)/shard_map/concatenate | solution.py:30
  18.1 1.3 %collective-permute-start.1 = (bf16[16,136,128]{2,1,0:T(8,128)(2,1)}, bf16[16,136,128]{2,1,0:T(8,128)(2,1)}, u32[]{:S(2)}, u32[]{:S(2)}) collective-permute-start(bf16[16,136,128]{2,1,0:T(8,128)(2,1)} %pad_maximum_fusion.1), channel_id=1, source_target_pairs={{1,3},{3,5},{5,7},{6,4},{4,2},{2,0},{9,11},{11,13},{13,15},{14,12}... | collective-permute-start | bytes 1671176 | tf_op jit(solution)/shard_map/ppermute | solution.py:40
  19.4 1.3 %collective-permute-start.2 = (bf16[16,136,128]{2,1,0:T(8,128)(2,1)}, bf16[16,136,128]{2,1,0:T(8,128)(2,1)}, u32[]{:S(2)}, u32[]{:S(2)}) collective-permute-start(bf16[16,136,128]{2,1,0:T(8,128)(2,1)} %pad_maximum_fusion.1), channel_id=1, source_target_pairs={{1,5},{3,7},{6,2},{4,0},{9,13},{11,15},{14,10},{12,8},{17,21},{19,... | collective-permute-start | bytes 1671176 | tf_op jit(solution)/shard_map/ppermute | solution.py:40
  21.1 1.0 %copy.41 = bf16[1,128,2048]{1,2,0:T(8,128)(2,1)} copy(bf16[1,128,2048]{2,1,0:T(8,128)(2,1)S(1)} %copy-done.1) | data formatting | bytes 1048576 | tf_op args[1]
  22.1 1.4 %copy.51 = f32[128,16,128]{0,2,1:T(8,128)} copy(f32[128,16,128]{2,0,1:T(8,128)S(1)} %fusion) | data formatting | bytes 2097152 | tf_op jit(solution)/shard_map/mul | solution.py:159
  23.5 1.3 %collective-permute-start.3 = (bf16[16,128,128]{2,1,0:T(8,128)(2,1)S(1)}, bf16[16,128,128]{2,1,0:T(8,128)(2,1)S(1)}, u32[]{:S(2)}, u32[]{:S(2)}) collective-permute-start(bf16[16,128,128]{2,1,0:T(8,128)(2,1)S(1)} %copy-done.3), channel_id=1, source_target_pairs={{1,7},{6,0},{9,15},{14,8},{17,23},{22,16},{25,31},{30,24}} | collective-permute-start | bytes 1572872 | tf_op jit(solution)/shard_map/ppermute | solution.py:73
  24.8 3.2 %fusion.10 = bf16[128,2048]{0,1:T(8,128)(2,1)} fusion(f32[16,128,128]{2,1,0:T(8,128)} %convolution_multiply_fusion.2, f32[16,128,128]{2,1,0:T(8,128)} %convolution_multiply_fusion.3, f32[128,16,128]{0,2,1:T(8,128)} %copy.51, bf16[1,128,2048]{1,2,0:T(8,128)(2,1)} %copy.41, f32[2048]{0:T(1024)S(1)} %bitcast.126, f32[2048]{0:T(1024)S(1)} %bitcast.129, ...), kind=kLoop, calls=%fused_computation.27 | loop fusion | flops 2097152 | bytes 4218880 | tf_op jit(solution)/shard_map/convert_element_type | solution.py:164
  28.0 7.3 %collective-permute-done.1 = bf16[16,136,128]{2,1,0:T(8,128)(2,1)} collective-permute-done((bf16[16,136,128]{2,1,0:T(8,128)(2,1)}, bf16[16,136,128]{2,1,0:T(8,128)(2,1)}, u32[]{:S(2)}, u32[]{:S(2)}) %collective-permute-start.1) | collective-permute-done | bytes 557088 | tf_op jit(solution)/shard_map/ppermute | solution.py:40
  35.2 3.4 %collective-permute-done.2 = bf16[16,136,128]{2,1,0:T(8,128)(2,1)} collective-permute-done((bf16[16,136,128]{2,1,0:T(8,128)(2,1)}, bf16[16,136,128]{2,1,0:T(8,128)(2,1)}, u32[]{:S(2)}, u32[]{:S(2)}) %collective-permute-start.2) | collective-permute-done | bytes 557088 | tf_op jit(solution)/shard_map/ppermute | solution.py:40
  38.7 1.0 %fusion.34 = (f32[16]{0:T(128)S(1)}, f32[16]{0:T(128)S(1)}) fusion(bf16[16,136,128]{2,1,0:T(8,128)(2,1)} %collective-permute-done.2, bf16[16,136,128]{2,1,0:T(8,128)(2,1)} %collective-permute-done.1), kind=kLoop, calls=%fused_computation.81 | loop fusion | flops 112 | bytes 256 | tf_op jit(solution)/shard_map/add | solution.py:35
  39.7 2.7 %multiply_add_fusion = f32[16,128,128]{2,1,0:T(8,128)} fusion(bf16[16,128,128]{2,1,0:T(8,128)(2,1)S(1)} %collective-permute-done.3, bf16[16,136,128]{2,1,0:T(8,128)(2,1)} %collective-permute-done.2, bf16[16,136,128]{2,1,0:T(8,128)(2,1)} %collective-permute-done.1, f32[16]{0:T(128)S(1)} %get-tuple-element.14, f32[16]{0:T(128)S(1)} %get-tuple-element.13), kind=kLoop, calls=%fused_computation.40 | loop fusion | flops 1835008 | bytes 2621568 | tf_op jit(solution)/shard_map/add | solution.py:74
  42.4 1.1 %slice_reduce_fusion = f32[16]{0:T(128)S(1)} fusion(f32[16,136,128]{2,1,0:T(8,128)} %collective-permute-done), kind=kLoop, calls=%fused_computation.61 | loop fusion | bytes 128 | tf_op jit(solution)/shard_map/slice | solution.py:21
  43.5 1.7 %slice_add_fusion = f32[16,128,128]{2,1,0:T(8,128)S(1)} fusion(f32[16,136,128]{2,1,0:T(8,128)} %collective-permute-done, f32[16,128,128]{2,1,0:T(8,128)} %multiply_add_fusion, f32[16]{0:T(128)S(1)} %slice_reduce_fusion), kind=kLoop, calls=%fused_computation.22 | loop fusion | flops 524288 | bytes 3145792 | tf_op jit(solution)/shard_map/add | solution.py:93
  45.7 0.7 %fusion.2 = f32[128,16,128]{0,2,1:T(8,128)S(1)} fusion(bf16[128,16,128]{0,2,1:T(8,128)(2,1)S(1)} %bitcast.112, f32[128,16]{0,1:T(8,128)S(1)} %copy.37, f32[16,128,128]{2,1,0:T(8,128)S(1)} %collective-permute-done.4, f32[16,128,128]{2,1,0:T(8,128)S(1)} %slice_add_fusion, pred[]{:T(512)S(6)} %eq.29), kind=kOutput, calls=%fused_computation.12 | convolution fusion | flops 201850880 | bytes 3678209 | tf_op jit(solution)/shard_map/shd,hde->she/dot_general | solution.py:173
  46.5 0.9 %fusion.4 = f32[128,16,128]{0,2,1:T(8,128)S(1)} fusion(f32[16,128,128]{2,1,0:T(8,128)S(1)} %slice_add_fusion, f32[16,128,128]{2,1,0:T(8,128)S(1)} %collective-permute-done.4, f32[128,16]{0,1:T(8,128)S(1)} %copy.52, pred[]{:T(512)S(6)} %eq.29, bf16[128,16,128]{2,1,0:T(8,128)(2,1)S(1)} %bitcast.108), kind=kOutput, calls=%fused_computation.16 | convolution fusion | flops 201850880 | bytes 3678209 | tf_op jit(solution)/shard_map/the,hde->thd/dot_general | solution.py:170
  47.4 1.2 %fusion.13 = bf16[128,2048]{0,1:T(8,128)(2,1)S(1)} fusion(f32[128,16,128]{0,2,1:T(8,128)S(1)} %fusion.2, f32[128,16,128]{0,2,1:T(8,128)S(1)} %fusion.3, f32[128,16,128]{0,2,1:T(8,128)S(1)} %fusion.4, f32[2048]{0:T(1024)S(1)} %bitcast.127, f32[2048]{0:T(1024)S(1)} %bitcast.130, f32[2048]{0:T(1024)S(1)} %bitcast.124), kind=kLoop, calls=%fused_computation.32 | loop fusion | flops 1572864 | bytes 3694592 | tf_op jit(solution)/shard_map/convert_element_type | solution.py:177
  48.7 2.5 %collective-permute-start.5 = (bf16[128,2048]{0,1:T(8,128)(2,1)S(1)}, bf16[128,2048]{0,1:T(8,128)(2,1)S(1)}, u32[]{:S(2)}, u32[]{:S(2)}) collective-permute-start(bf16[128,2048]{0,1:T(8,128)(2,1)S(1)} %add_convert_fusion), channel_id=1, source_target_pairs={{0,24},{8,0},{16,8},{24,16},{1,25},{9,1},{17,9},{25,17},{2,26},{10... | collective-permute-start | bytes 1572872 | tf_op jit(solution)/shard_map/ppermute | solution.py:100
  51.2 11.9 %collective-permute-done.5 = bf16[128,2048]{0,1:T(8,128)(2,1)S(1)} collective-permute-done((bf16[128,2048]{0,1:T(8,128)(2,1)S(1)}, bf16[128,2048]{0,1:T(8,128)(2,1)S(1)}, u32[]{:S(2)}, u32[]{:S(2)}) %collective-permute-start.5) | collective-permute-done | bytes 524320 | tf_op jit(solution)/shard_map/ppermute | solution.py:100
  63.1 1.0 %copy.57 = bf16[1,128,2048]{2,1,0:T(8,128)(2,1)} copy(bf16[1,128,2048]{1,2,0:T(8,128)(2,1)S(1)} %bitcast.121) | data formatting | bytes 1048576 | tf_op jit(solution)/shard_map/broadcast_in_dim | solution.py:181
  (50 shorter events, 3.5 us)
Async XLA Ops:
  4.0 1.0 %copy-start.1 = (bf16[1,128,2048]{2,1,0:T(8,128)(2,1)S(1)}, bf16[1,128,2048]{2,1,0:T(8,128)(2,1)}, u32[]{:S(2)}) copy-start(bf16[1,128,2048]{2,1,0:T(8,128)(2,1)} %param.6) | copy-start | bytes 1572868
  9.0 6.1 %collective-permute-start = (f32[16,136,128]{2,1,0:T(8,128)}, f32[16,136,128]{2,1,0:T(8,128)}, u32[]{:S(2)}, u32[]{:S(2)}) collective-permute-start(f32[16,136,128]{2,1,0:T(8,128)} %pad_maximum_fusion), channel_id=1, source_target_pairs={{0,1},{2,3},{4,5},{6,7},{1,0},{3,2},{5,4},{7,6},{8,9},{10,11},{12,... | collective-permute-start | bytes 3342344 | tf_op jit(solution)/shard_map/ppermute | solution.py:63
  13.2 1.8 %copy-start = (f32[16,128,128]{2,1,0:T(8,128)S(1)}, f32[16,128,128]{2,1,0:T(8,128)}, u32[]{:S(2)}) copy-start(f32[16,128,128]{2,1,0:T(8,128)} %get-tuple-element.16) | copy-start | bytes 3145732
  16.8 2.5 %copy-start.2 = (bf16[16,128,128]{2,1,0:T(8,128)(2,1)}, bf16[16,128,128]{2,1,0:T(8,128)(2,1)S(1)}, u32[]{:S(2)}) copy-start(bf16[16,128,128]{2,1,0:T(8,128)(2,1)S(1)} %slice.110) | copy-start | bytes 1572868
  17.0 3.6 %copy-start.5 = (f32[16,128,128]{1,2,0:T(8,128)S(1)}, f32[16,128,128]{1,2,0:T(8,128)}, u32[]{:S(2)}) copy-start(f32[16,128,128]{1,2,0:T(8,128)} %convolution_multiply_fusion.1) | copy-start | bytes 3145732
  18.1 17.2 %collective-permute-start.1 = (bf16[16,136,128]{2,1,0:T(8,128)(2,1)}, bf16[16,136,128]{2,1,0:T(8,128)(2,1)}, u32[]{:S(2)}, u32[]{:S(2)}) collective-permute-start(bf16[16,136,128]{2,1,0:T(8,128)(2,1)} %pad_maximum_fusion.1), channel_id=1, source_target_pairs={{1,3},{3,5},{5,7},{6,4},{4,2},{2,0},{9,11},{11,13},{13,15},{14,12}... | collective-permute-start | bytes 1671176 | tf_op jit(solution)/shard_map/ppermute | solution.py:40
  19.4 19.3 %collective-permute-start.2 = (bf16[16,136,128]{2,1,0:T(8,128)(2,1)}, bf16[16,136,128]{2,1,0:T(8,128)(2,1)}, u32[]{:S(2)}, u32[]{:S(2)}) collective-permute-start(bf16[16,136,128]{2,1,0:T(8,128)(2,1)} %pad_maximum_fusion.1), channel_id=1, source_target_pairs={{1,5},{3,7},{6,2},{4,0},{9,13},{11,15},{14,10},{12,8},{17,21},{19,... | collective-permute-start | bytes 1671176 | tf_op jit(solution)/shard_map/ppermute | solution.py:40
  22.1 1.4 %copy-start.3 = (bf16[16,128,128]{2,1,0:T(8,128)(2,1)S(1)}, bf16[16,128,128]{2,1,0:T(8,128)(2,1)}, u32[]{:S(2)}) copy-start(bf16[16,128,128]{2,1,0:T(8,128)(2,1)} %copy-done.2) | copy-start | bytes 1572868
  23.5 16.2 %collective-permute-start.3 = (bf16[16,128,128]{2,1,0:T(8,128)(2,1)S(1)}, bf16[16,128,128]{2,1,0:T(8,128)(2,1)S(1)}, u32[]{:S(2)}, u32[]{:S(2)}) collective-permute-start(bf16[16,128,128]{2,1,0:T(8,128)(2,1)S(1)} %copy-done.3), channel_id=1, source_target_pairs={{1,7},{6,0},{9,15},{14,8},{17,23},{22,16},{25,31},{30,24}} | collective-permute-start | bytes 1572872 | tf_op jit(solution)/shard_map/ppermute | solution.py:73
  42.4 2.9 %collective-permute-start.4 = (f32[16,128,128]{2,1,0:T(8,128)}, f32[16,128,128]{2,1,0:T(8,128)S(1)}, u32[]{:S(2)}, u32[]{:S(2)}) collective-permute-start(f32[16,128,128]{2,1,0:T(8,128)} %multiply_add_fusion), channel_id=1, source_target_pairs={{0,1},{2,3},{4,5},{6,7},{1,0},{3,2},{5,4},{7,6},{8,9},{10,11},{12,... | collective-permute-start | bytes 3145736 | tf_op jit(solution)/shard_map/ppermute | solution.py:92
  47.3 1.2 %copy-start.4 = (bf16[128,2048]{0,1:T(8,128)(2,1)S(1)}, bf16[128,2048]{0,1:T(8,128)(2,1)}, u32[]{:S(2)}) copy-start(bf16[128,2048]{0,1:T(8,128)(2,1)} %fusion.10) | copy-start | bytes 1572868
  48.7 14.4 %collective-permute-start.5 = (bf16[128,2048]{0,1:T(8,128)(2,1)S(1)}, bf16[128,2048]{0,1:T(8,128)(2,1)S(1)}, u32[]{:S(2)}, u32[]{:S(2)}) collective-permute-start(bf16[128,2048]{0,1:T(8,128)(2,1)S(1)} %add_convert_fusion), channel_id=1, source_target_pairs={{0,24},{8,0},{16,8},{24,16},{1,25},{9,1},{17,9},{25,17},{2,26},{10... | collective-permute-start | bytes 1572872 | tf_op jit(solution)/shard_map/ppermute | solution.py:100
